TPU v7x, 32 devices: a whole 2x2x4 slice. The times are simulated.
32 devices in a mesh: grp: 2 (over x), blk: 16 (over z, y, core).
Axes of the slice: x: 2, y: 2, z: 4, core: 2. Of those that a mesh axis runs over, the one named last changes fastest.
Arguments:
- queries: bfloat16 [512, 2048], P(('grp', 'blk')), parts along dimension 0, may hold values from 0 to 2, as said below
- library: bfloat16 [24576, 2048], P(('grp', 'blk')), parts along dimension 0, may hold values from 0 to 2, as said below
- assays: bfloat16 [24576, 256], P(('grp', 'blk')), parts along dimension 0, may hold values from -14 to 14
Outputs:
- smoothed: float32 [512, 256], P(('grp', 'blk')), parts along dimension 0
There are 2 independent parts, one for each index of `grp`. A program takes and returns all parts, laid end to end along the dimension named above; each array names one. Nothing has to cross between parts.
Inputs may be any that keep to these rules, and one draw needn't show every extreme that they name: `queries`: nonnegative fingerprint features. `library`: nonnegative fingerprint features.
All inputs are finite; a program needn't handle non-finite values.
Results may differ from a plain program's by a relative error of at most 0.002.
Values may be sent and summed in bfloat16 or wider, within the bound.
No kernel may reach another device: no remote copies, remote signals or barrier semaphores. Data moves between devices by JAX's collectives and lax.ppermute only.
A program may use at most 64 MiB of HBM per device.

v0:
```python
import jax
import jax.numpy as jnp
from jax import lax
from jax.sharding import PartitionSpec as P

EPS = 1e-05
TAU = 0.05


def shifted(shard, axis, by):
    count = lax.axis_size(axis)
    return lax.ppermute(shard, axis, [(i, (i + by) % count) for i in range(count)])


def weighted_sums(block, library, lib_sq, zvals):
    blockf = block.astype(jnp.float32)
    q_sq = jnp.sum(blockf * blockf, axis=1)
    inner = lax.dot_general(
        block, library, (((1,), (1,)), ((), ())), preferred_element_type=jnp.float32
    )
    tanimoto = inner / (q_sq[:, None] + lib_sq[None, :] - inner)
    weight = jnp.exp((tanimoto - 1.0) / TAU)
    numer = jnp.dot(weight.astype(jnp.bfloat16), zvals, preferred_element_type=jnp.float32)
    denom = jnp.sum(weight, axis=1)
    return (numer, denom)


def shards(queries, library, assays):
    values = assays.astype(jnp.float32)
    col_sum, col_sq = lax.psum((jnp.sum(values, axis=0), jnp.sum(values * values, axis=0)), "blk")
    total = library.shape[0] * lax.axis_size("blk")
    mean = col_sum / total
    spread = col_sq / total - mean * mean
    zvals = ((values - mean) * lax.rsqrt(spread + EPS)).astype(jnp.bfloat16)
    lib_sq = jnp.sum(jnp.square(library.astype(jnp.float32)), axis=1)

    def advance(index, state):
        block, numer, denom = state
        part_num, part_den = weighted_sums(block, library, lib_sq, zvals)
        moved = shifted(block, "blk", 1)
        numer, denom = shifted((numer + part_num, denom + part_den), "blk", 1)
        return (moved, numer, denom)

    start = (
        queries,
        jnp.zeros((queries.shape[0], zvals.shape[1]), jnp.float32),
        jnp.zeros((queries.shape[0],), jnp.float32),
    )
    block, numer, denom = lax.fori_loop(0, lax.axis_size("blk"), advance, start)
    return numer / denom[:, None]


def solution(mesh):
    return jax.shard_map(
        shards,
        mesh=mesh,
        in_specs=(P(("grp", "blk"), None), P(("grp", "blk"), None), P(("grp", "blk"), None)),
        out_specs=P(("grp", "blk"), None),
        check_vma=False,
    )
```

profile of v0, /device:TPU:0, one launch (start us, length us, event | category | flops | bytes accessed | tf_op | source)
XLA Modules:
  0.0 160.2 jit_solution(12168928565363730623)
XLA Ops:
  0.0 1.3 convert_reduce_fusion
  1.3 35.0 %all-reduce = (f32[256]{0:T(256)S(1)}, f32[256]{0:T(256)S(1)}) all-reduce(f32[256]{0:T(256)S(1)} %get-tuple-element.98, f32[256]{0:T(256)S(1)} %get-tuple-element.97), channel_id=1, replica_groups=mesh['grp'=2,'blk'=16] {'blk'}, use_global_device_ids=true, to_apply=%region_4.0 | all-reduce | flops 512 | bytes 4096 | tf_op jit(solution)/shard_map/psum | solution.py:30
  36.3 2.6 %multiply_reduce_fusion.1 = f32[768]{0:T(1024)S(1)} fusion(bf16[768,2048]{1,0:T(8,128)(2,1)} %param.6), kind=kLoop, calls=%fused_computation.8 | loop fusion | flops 4717824 | bytes 3148800 | tf_op jit(solution)/shard_map/reduce_sum | solution.py:35
  38.9 0.8 fusion.7
  39.7 119.8 %while.16 = (s32[]{:T(128)}, bf16[16,2048]{1,0:T(8,128)(2,1)S(1)}, f32[16,256]{1,0:T(8,128)S(1)}, f32[16]{0:T(128)S(1)}, bf16[768,2048]{1,0:T(8,128)(2,1)S(1)}, ...) while((s32[]{:T(128)}, bf16[16,2048]{1,0:T(8,128)(2,1)S(1)}, f32[16,256]{1,0:T(8,128)S(1)}, ...), condition=%wide.region_8.0_spmd, body=%wide.region_5.0_spmd.sunk | while | flops 56872944 | bytes 5839785 | solution.py:49
  39.8 0.1 multiply_reduce_fusion.3
  40.0 1.1 fusion.21
  41.0 0.2 convolution_add_fusion.2
  41.4 5.9 %collective-permute-done.2 = f32[16]{0:T(128)S(1)} collective-permute-done((f32[16]{0:T(128)S(1)}, f32[16]{0:T(128)S(1)}, u32[]{:S(2)}, u32[]{:S(2)}) %collective-permute-start.2) | collective-permute-done | bytes 96 | tf_op jit(solution)/shard_map/while/body/eval_jaxpr/ppermute | solution.py:12
  47.3 0.1 multiply_reduce_fusion.3
  47.5 1.1 fusion.21
  48.5 0.2 convolution_add_fusion.2
  48.9 5.9 %collective-permute-done.2 = f32[16]{0:T(128)S(1)} collective-permute-done((f32[16]{0:T(128)S(1)}, f32[16]{0:T(128)S(1)}, u32[]{:S(2)}, u32[]{:S(2)}) %collective-permute-start.2) | collective-permute-done | bytes 96 | tf_op jit(solution)/shard_map/while/body/eval_jaxpr/ppermute | solution.py:12
  54.8 0.1 multiply_reduce_fusion.3
  54.9 1.1 fusion.21
  56.0 0.2 convolution_add_fusion.2
  56.3 5.9 %collective-permute-done.2 = f32[16]{0:T(128)S(1)} collective-permute-done((f32[16]{0:T(128)S(1)}, f32[16]{0:T(128)S(1)}, u32[]{:S(2)}, u32[]{:S(2)}) %collective-permute-start.2) | collective-permute-done | bytes 96 | tf_op jit(solution)/shard_map/while/body/eval_jaxpr/ppermute | solution.py:12
  62.3 0.1 multiply_reduce_fusion.3
  62.4 1.1 fusion.21
  63.5 0.2 convolution_add_fusion.2
  63.8 5.9 %collective-permute-done.2 = f32[16]{0:T(128)S(1)} collective-permute-done((f32[16]{0:T(128)S(1)}, f32[16]{0:T(128)S(1)}, u32[]{:S(2)}, u32[]{:S(2)}) %collective-permute-start.2) | collective-permute-done | bytes 96 | tf_op jit(solution)/shard_map/while/body/eval_jaxpr/ppermute | solution.py:12
  69.8 0.1 multiply_reduce_fusion.3
  69.9 1.1 fusion.21
  71.0 0.2 convolution_add_fusion.2
  71.3 5.9 %collective-permute-done.2 = f32[16]{0:T(128)S(1)} collective-permute-done((f32[16]{0:T(128)S(1)}, f32[16]{0:T(128)S(1)}, u32[]{:S(2)}, u32[]{:S(2)}) %collective-permute-start.2) | collective-permute-done | bytes 96 | tf_op jit(solution)/shard_map/while/body/eval_jaxpr/ppermute | solution.py:12
  77.3 0.1 multiply_reduce_fusion.3
  77.4 1.1 fusion.21
  78.5 0.2 convolution_add_fusion.2
  78.8 5.9 %collective-permute-done.2 = f32[16]{0:T(128)S(1)} collective-permute-done((f32[16]{0:T(128)S(1)}, f32[16]{0:T(128)S(1)}, u32[]{:S(2)}, u32[]{:S(2)}) %collective-permute-start.2) | collective-permute-done | bytes 96 | tf_op jit(solution)/shard_map/while/body/eval_jaxpr/ppermute | solution.py:12
  84.8 0.1 multiply_reduce_fusion.3
  84.9 1.1 fusion.21
  85.9 0.2 convolution_add_fusion.2
  86.3 5.9 %collective-permute-done.2 = f32[16]{0:T(128)S(1)} collective-permute-done((f32[16]{0:T(128)S(1)}, f32[16]{0:T(128)S(1)}, u32[]{:S(2)}, u32[]{:S(2)}) %collective-permute-start.2) | collective-permute-done | bytes 96 | tf_op jit(solution)/shard_map/while/body/eval_jaxpr/ppermute | solution.py:12
  92.2 0.1 multiply_reduce_fusion.3
  92.4 1.1 fusion.21
  93.4 0.2 convolution_add_fusion.2
  93.8 5.9 %collective-permute-done.2 = f32[16]{0:T(128)S(1)} collective-permute-done((f32[16]{0:T(128)S(1)}, f32[16]{0:T(128)S(1)}, u32[]{:S(2)}, u32[]{:S(2)}) %collective-permute-start.2) | collective-permute-done | bytes 96 | tf_op jit(solution)/shard_map/while/body/eval_jaxpr/ppermute | solution.py:12
  99.7 0.1 multiply_reduce_fusion.3
  99.9 1.1 fusion.21
  100.9 0.2 convolution_add_fusion.2
  101.2 5.9 %collective-permute-done.2 = f32[16]{0:T(128)S(1)} collective-permute-done((f32[16]{0:T(128)S(1)}, f32[16]{0:T(128)S(1)}, u32[]{:S(2)}, u32[]{:S(2)}) %collective-permute-start.2) | collective-permute-done | bytes 96 | tf_op jit(solution)/shard_map/while/body/eval_jaxpr/ppermute | solution.py:12
  107.2 0.1 multiply_reduce_fusion.3
  107.3 1.1 fusion.21
  108.4 0.2 convolution_add_fusion.2
  108.7 5.9 %collective-permute-done.2 = f32[16]{0:T(128)S(1)} collective-permute-done((f32[16]{0:T(128)S(1)}, f32[16]{0:T(128)S(1)}, u32[]{:S(2)}, u32[]{:S(2)}) %collective-permute-start.2) | collective-permute-done | bytes 96 | tf_op jit(solution)/shard_map/while/body/eval_jaxpr/ppermute | solution.py:12
  114.8 1.1 fusion.21
  115.9 0.2 convolution_add_fusion.2
  116.2 5.9 %collective-permute-done.2 = f32[16]{0:T(128)S(1)} collective-permute-done((f32[16]{0:T(128)S(1)}, f32[16]{0:T(128)S(1)}, u32[]{:S(2)}, u32[]{:S(2)}) %collective-permute-start.2) | collective-permute-done | bytes 96 | tf_op jit(solution)/shard_map/while/body/eval_jaxpr/ppermute | solution.py:12
  122.3 1.1 fusion.21
  123.4 0.2 convolution_add_fusion.2
  123.7 5.9 %collective-permute-done.2 = f32[16]{0:T(128)S(1)} collective-permute-done((f32[16]{0:T(128)S(1)}, f32[16]{0:T(128)S(1)}, u32[]{:S(2)}, u32[]{:S(2)}) %collective-permute-start.2) | collective-permute-done | bytes 96 | tf_op jit(solution)/shard_map/while/body/eval_jaxpr/ppermute | solution.py:12
  129.8 1.1 fusion.21
  130.9 0.2 convolution_add_fusion.2
  131.2 5.9 %collective-permute-done.2 = f32[16]{0:T(128)S(1)} collective-permute-done((f32[16]{0:T(128)S(1)}, f32[16]{0:T(128)S(1)}, u32[]{:S(2)}, u32[]{:S(2)}) %collective-permute-start.2) | collective-permute-done | bytes 96 | tf_op jit(solution)/shard_map/while/body/eval_jaxpr/ppermute | solution.py:12
  137.3 1.1 fusion.21
  138.3 0.2 convolution_add_fusion.2
  138.7 5.9 %collective-permute-done.2 = f32[16]{0:T(128)S(1)} collective-permute-done((f32[16]{0:T(128)S(1)}, f32[16]{0:T(128)S(1)}, u32[]{:S(2)}, u32[]{:S(2)}) %collective-permute-start.2) | collective-permute-done | bytes 96 | tf_op jit(solution)/shard_map/while/body/eval_jaxpr/ppermute | solution.py:12
  144.8 1.1 fusion.21
  145.8 0.2 convolution_add_fusion.2
  146.2 5.9 %collective-permute-done.2 = f32[16]{0:T(128)S(1)} collective-permute-done((f32[16]{0:T(128)S(1)}, f32[16]{0:T(128)S(1)}, u32[]{:S(2)}, u32[]{:S(2)}) %collective-permute-start.2) | collective-permute-done | bytes 96 | tf_op jit(solution)/shard_map/while/body/eval_jaxpr/ppermute | solution.py:12
  152.2 1.1 fusion.21
  153.3 0.2 convolution_add_fusion.2
  153.6 5.9 %collective-permute-done.2 = f32[16]{0:T(128)S(1)} collective-permute-done((f32[16]{0:T(128)S(1)}, f32[16]{0:T(128)S(1)}, u32[]{:S(2)}, u32[]{:S(2)}) %collective-permute-start.2) | collective-permute-done | bytes 96 | tf_op jit(solution)/shard_map/while/body/eval_jaxpr/ppermute | solution.py:12
  159.5 0.7 broadcast_divide_fusion
  (159 shorter events, 3.6 us)
Async XLA Ops:
  0.0 39.7 %copy-start = (bf16[768,2048]{1,0:T(8,128)(2,1)S(1)}, bf16[768,2048]{1,0:T(8,128)(2,1)}, u32[]{:S(2)}) copy-start(bf16[768,2048]{1,0:T(8,128)(2,1)} %param.6) | copy-start | bytes 9437188
  0.0 39.7 %copy-start.2 = (bf16[16,2048]{1,0:T(8,128)(2,1)S(1)}, bf16[16,2048]{1,0:T(8,128)(2,1)}, u32[]{:S(2)}) copy-start(bf16[16,2048]{1,0:T(8,128)(2,1)} %param.5) | copy-start | bytes 196612
  36.3 2.6 %copy-start.3 = (bf16[768,256]{1,0:T(8,128)(2,1)S(1)}, bf16[768,256]{1,0:T(8,128)(2,1)}, u32[]{:S(2)}) copy-start(bf16[768,256]{1,0:T(8,128)(2,1)} %param.7) | copy-start | bytes 1179652
  39.8 1.3 copy-start.1
  39.8 7.5 %collective-permute-start = (bf16[16,2048]{1,0:T(8,128)(2,1)S(1)}, bf16[16,2048]{1,0:T(8,128)(2,1)S(1)}, u32[]{:S(2)}, u32[]{:S(2)}) collective-permute-start(bf16[16,2048]{1,0:T(8,128)(2,1)S(1)} %copy.9), channel_id=1, source_target_pairs={{0,1},{1,2},{2,3},{3,4},{4,5},{5,6},{6,7},{7,8},{8,9},{9,10},{10,1... | collective-permute-start | bytes 196616 | tf_op jit(solution)/shard_map/while/body/eval_jaxpr/ppermute | solution.py:12
  41.2 6.0 %collective-permute-start.1 = (f32[16,256]{1,0:T(8,128)S(1)}, f32[16,256]{1,0:T(8,128)S(1)}, u32[]{:S(2)}, u32[]{:S(2)}) collective-permute-start(f32[16,256]{1,0:T(8,128)S(1)} %convolution_add_fusion.2), channel_id=1, source_target_pairs={{0,1},{1,2},{2,3},{3,4},{4,5},{5,6},{6,7},{7,8},{8,9},{9,10},{10,1... | collective-permute-start | bytes 49160 | tf_op jit(solution)/shard_map/while/body/eval_jaxpr/ppermute | solution.py:12
  41.3 5.9 %collective-permute-start.2 = (f32[16]{0:T(128)S(1)}, f32[16]{0:T(128)S(1)}, u32[]{:S(2)}, u32[]{:S(2)}) collective-permute-start(f32[16]{0:T(128)S(1)} %add.94), channel_id=1, source_target_pairs={{0,1},{1,2},{2,3},{3,4},{4,5},{5,6},{6,7},{7,8},{8,9},{9,10},{10,1... | collective-permute-start | bytes 200 | tf_op jit(solution)/shard_map/while/body/eval_jaxpr/ppermute | solution.py:12
  47.2 1.3 copy-start.1
  47.3 7.5 %collective-permute-start = (bf16[16,2048]{1,0:T(8,128)(2,1)S(1)}, bf16[16,2048]{1,0:T(8,128)(2,1)S(1)}, u32[]{:S(2)}, u32[]{:S(2)}) collective-permute-start(bf16[16,2048]{1,0:T(8,128)(2,1)S(1)} %copy.9), channel_id=1, source_target_pairs={{0,1},{1,2},{2,3},{3,4},{4,5},{5,6},{6,7},{7,8},{8,9},{9,10},{10,1... | collective-permute-start | bytes 196616 | tf_op jit(solution)/shard_map/while/body/eval_jaxpr/ppermute | solution.py:12
  48.7 6.0 %collective-permute-start.1 = (f32[16,256]{1,0:T(8,128)S(1)}, f32[16,256]{1,0:T(8,128)S(1)}, u32[]{:S(2)}, u32[]{:S(2)}) collective-permute-start(f32[16,256]{1,0:T(8,128)S(1)} %convolution_add_fusion.2), channel_id=1, source_target_pairs={{0,1},{1,2},{2,3},{3,4},{4,5},{5,6},{6,7},{7,8},{8,9},{9,10},{10,1... | collective-permute-start | bytes 49160 | tf_op jit(solution)/shard_map/while/body/eval_jaxpr/ppermute | solution.py:12
  48.8 5.9 %collective-permute-start.2 = (f32[16]{0:T(128)S(1)}, f32[16]{0:T(128)S(1)}, u32[]{:S(2)}, u32[]{:S(2)}) collective-permute-start(f32[16]{0:T(128)S(1)} %add.94), channel_id=1, source_target_pairs={{0,1},{1,2},{2,3},{3,4},{4,5},{5,6},{6,7},{7,8},{8,9},{9,10},{10,1... | collective-permute-start | bytes 200 | tf_op jit(solution)/shard_map/while/body/eval_jaxpr/ppermute | solution.py:12
  54.7 1.3 copy-start.1
  54.8 7.5 %collective-permute-start = (bf16[16,2048]{1,0:T(8,128)(2,1)S(1)}, bf16[16,2048]{1,0:T(8,128)(2,1)S(1)}, u32[]{:S(2)}, u32[]{:S(2)}) collective-permute-start(bf16[16,2048]{1,0:T(8,128)(2,1)S(1)} %copy.9), channel_id=1, source_target_pairs={{0,1},{1,2},{2,3},{3,4},{4,5},{5,6},{6,7},{7,8},{8,9},{9,10},{10,1... | collective-permute-start | bytes 196616 | tf_op jit(solution)/shard_map/while/body/eval_jaxpr/ppermute | solution.py:12
  56.2 6.0 %collective-permute-start.1 = (f32[16,256]{1,0:T(8,128)S(1)}, f32[16,256]{1,0:T(8,128)S(1)}, u32[]{:S(2)}, u32[]{:S(2)}) collective-permute-start(f32[16,256]{1,0:T(8,128)S(1)} %convolution_add_fusion.2), channel_id=1, source_target_pairs={{0,1},{1,2},{2,3},{3,4},{4,5},{5,6},{6,7},{7,8},{8,9},{9,10},{10,1... | collective-permute-start | bytes 49160 | tf_op jit(solution)/shard_map/while/body/eval_jaxpr/ppermute | solution.py:12
  56.3 5.9 %collective-permute-start.2 = (f32[16]{0:T(128)S(1)}, f32[16]{0:T(128)S(1)}, u32[]{:S(2)}, u32[]{:S(2)}) collective-permute-start(f32[16]{0:T(128)S(1)} %add.94), channel_id=1, source_target_pairs={{0,1},{1,2},{2,3},{3,4},{4,5},{5,6},{6,7},{7,8},{8,9},{9,10},{10,1... | collective-permute-start | bytes 200 | tf_op jit(solution)/shard_map/while/body/eval_jaxpr/ppermute | solution.py:12
  62.2 1.3 copy-start.1
  62.2 7.5 %collective-permute-start = (bf16[16,2048]{1,0:T(8,128)(2,1)S(1)}, bf16[16,2048]{1,0:T(8,128)(2,1)S(1)}, u32[]{:S(2)}, u32[]{:S(2)}) collective-permute-start(bf16[16,2048]{1,0:T(8,128)(2,1)S(1)} %copy.9), channel_id=1, source_target_pairs={{0,1},{1,2},{2,3},{3,4},{4,5},{5,6},{6,7},{7,8},{8,9},{9,10},{10,1... | collective-permute-start | bytes 196616 | tf_op jit(solution)/shard_map/while/body/eval_jaxpr/ppermute | solution.py:12
  63.7 6.0 %collective-permute-start.1 = (f32[16,256]{1,0:T(8,128)S(1)}, f32[16,256]{1,0:T(8,128)S(1)}, u32[]{:S(2)}, u32[]{:S(2)}) collective-permute-start(f32[16,256]{1,0:T(8,128)S(1)} %convolution_add_fusion.2), channel_id=1, source_target_pairs={{0,1},{1,2},{2,3},{3,4},{4,5},{5,6},{6,7},{7,8},{8,9},{9,10},{10,1... | collective-permute-start | bytes 49160 | tf_op jit(solution)/shard_map/while/body/eval_jaxpr/ppermute | solution.py:12
  63.8 5.9 %collective-permute-start.2 = (f32[16]{0:T(128)S(1)}, f32[16]{0:T(128)S(1)}, u32[]{:S(2)}, u32[]{:S(2)}) collective-permute-start(f32[16]{0:T(128)S(1)} %add.94), channel_id=1, source_target_pairs={{0,1},{1,2},{2,3},{3,4},{4,5},{5,6},{6,7},{7,8},{8,9},{9,10},{10,1... | collective-permute-start | bytes 200 | tf_op jit(solution)/shard_map/while/body/eval_jaxpr/ppermute | solution.py:12
  69.7 1.3 copy-start.1
  69.7 7.5 %collective-permute-start = (bf16[16,2048]{1,0:T(8,128)(2,1)S(1)}, bf16[16,2048]{1,0:T(8,128)(2,1)S(1)}, u32[]{:S(2)}, u32[]{:S(2)}) collective-permute-start(bf16[16,2048]{1,0:T(8,128)(2,1)S(1)} %copy.9), channel_id=1, source_target_pairs={{0,1},{1,2},{2,3},{3,4},{4,5},{5,6},{6,7},{7,8},{8,9},{9,10},{10,1... | collective-permute-start | bytes 196616 | tf_op jit(solution)/shard_map/while/body/eval_jaxpr/ppermute | solution.py:12
  71.2 6.0 %collective-permute-start.1 = (f32[16,256]{1,0:T(8,128)S(1)}, f32[16,256]{1,0:T(8,128)S(1)}, u32[]{:S(2)}, u32[]{:S(2)}) collective-permute-start(f32[16,256]{1,0:T(8,128)S(1)} %convolution_add_fusion.2), channel_id=1, source_target_pairs={{0,1},{1,2},{2,3},{3,4},{4,5},{5,6},{6,7},{7,8},{8,9},{9,10},{10,1... | collective-permute-start | bytes 49160 | tf_op jit(solution)/shard_map/while/body/eval_jaxpr/ppermute | solution.py:12
  71.2 5.9 %collective-permute-start.2 = (f32[16]{0:T(128)S(1)}, f32[16]{0:T(128)S(1)}, u32[]{:S(2)}, u32[]{:S(2)}) collective-permute-start(f32[16]{0:T(128)S(1)} %add.94), channel_id=1, source_target_pairs={{0,1},{1,2},{2,3},{3,4},{4,5},{5,6},{6,7},{7,8},{8,9},{9,10},{10,1... | collective-permute-start | bytes 200 | tf_op jit(solution)/shard_map/while/body/eval_jaxpr/ppermute | solution.py:12
  77.2 1.3 copy-start.1
  77.2 7.5 %collective-permute-start = (bf16[16,2048]{1,0:T(8,128)(2,1)S(1)}, bf16[16,2048]{1,0:T(8,128)(2,1)S(1)}, u32[]{:S(2)}, u32[]{:S(2)}) collective-permute-start(bf16[16,2048]{1,0:T(8,128)(2,1)S(1)} %copy.9), channel_id=1, source_target_pairs={{0,1},{1,2},{2,3},{3,4},{4,5},{5,6},{6,7},{7,8},{8,9},{9,10},{10,1... | collective-permute-start | bytes 196616 | tf_op jit(solution)/shard_map/while/body/eval_jaxpr/ppermute | solution.py:12
  78.7 6.0 %collective-permute-start.1 = (f32[16,256]{1,0:T(8,128)S(1)}, f32[16,256]{1,0:T(8,128)S(1)}, u32[]{:S(2)}, u32[]{:S(2)}) collective-permute-start(f32[16,256]{1,0:T(8,128)S(1)} %convolution_add_fusion.2), channel_id=1, source_target_pairs={{0,1},{1,2},{2,3},{3,4},{4,5},{5,6},{6,7},{7,8},{8,9},{9,10},{10,1... | collective-permute-start | bytes 49160 | tf_op jit(solution)/shard_map/while/body/eval_jaxpr/ppermute | solution.py:12
  78.7 5.9 %collective-permute-start.2 = (f32[16]{0:T(128)S(1)}, f32[16]{0:T(128)S(1)}, u32[]{:S(2)}, u32[]{:S(2)}) collective-permute-start(f32[16]{0:T(128)S(1)} %add.94), channel_id=1, source_target_pairs={{0,1},{1,2},{2,3},{3,4},{4,5},{5,6},{6,7},{7,8},{8,9},{9,10},{10,1... | collective-permute-start | bytes 200 | tf_op jit(solution)/shard_map/while/body/eval_jaxpr/ppermute | solution.py:12
  84.7 1.3 copy-start.1
  84.7 7.5 %collective-permute-start = (bf16[16,2048]{1,0:T(8,128)(2,1)S(1)}, bf16[16,2048]{1,0:T(8,128)(2,1)S(1)}, u32[]{:S(2)}, u32[]{:S(2)}) collective-permute-start(bf16[16,2048]{1,0:T(8,128)(2,1)S(1)} %copy.9), channel_id=1, source_target_pairs={{0,1},{1,2},{2,3},{3,4},{4,5},{5,6},{6,7},{7,8},{8,9},{9,10},{10,1... | collective-permute-start | bytes 196616 | tf_op jit(solution)/shard_map/while/body/eval_jaxpr/ppermute | solution.py:12
  86.1 6.0 %collective-permute-start.1 = (f32[16,256]{1,0:T(8,128)S(1)}, f32[16,256]{1,0:T(8,128)S(1)}, u32[]{:S(2)}, u32[]{:S(2)}) collective-permute-start(f32[16,256]{1,0:T(8,128)S(1)} %convolution_add_fusion.2), channel_id=1, source_target_pairs={{0,1},{1,2},{2,3},{3,4},{4,5},{5,6},{6,7},{7,8},{8,9},{9,10},{10,1... | collective-permute-start | bytes 49160 | tf_op jit(solution)/shard_map/while/body/eval_jaxpr/ppermute | solution.py:12
  86.2 5.9 %collective-permute-start.2 = (f32[16]{0:T(128)S(1)}, f32[16]{0:T(128)S(1)}, u32[]{:S(2)}, u32[]{:S(2)}) collective-permute-start(f32[16]{0:T(128)S(1)} %add.94), channel_id=1, source_target_pairs={{0,1},{1,2},{2,3},{3,4},{4,5},{5,6},{6,7},{7,8},{8,9},{9,10},{10,1... | collective-permute-start | bytes 200 | tf_op jit(solution)/shard_map/while/body/eval_jaxpr/ppermute | solution.py:12
  92.2 1.3 copy-start.1
  92.2 7.5 %collective-permute-start = (bf16[16,2048]{1,0:T(8,128)(2,1)S(1)}, bf16[16,2048]{1,0:T(8,128)(2,1)S(1)}, u32[]{:S(2)}, u32[]{:S(2)}) collective-permute-start(bf16[16,2048]{1,0:T(8,128)(2,1)S(1)} %copy.9), channel_id=1, source_target_pairs={{0,1},{1,2},{2,3},{3,4},{4,5},{5,6},{6,7},{7,8},{8,9},{9,10},{10,1... | collective-permute-start | bytes 196616 | tf_op jit(solution)/shard_map/while/body/eval_jaxpr/ppermute | solution.py:12
  93.6 6.0 %collective-permute-start.1 = (f32[16,256]{1,0:T(8,128)S(1)}, f32[16,256]{1,0:T(8,128)S(1)}, u32[]{:S(2)}, u32[]{:S(2)}) collective-permute-start(f32[16,256]{1,0:T(8,128)S(1)} %convolution_add_fusion.2), channel_id=1, source_target_pairs={{0,1},{1,2},{2,3},{3,4},{4,5},{5,6},{6,7},{7,8},{8,9},{9,10},{10,1... | collective-permute-start | bytes 49160 | tf_op jit(solution)/shard_map/while/body/eval_jaxpr/ppermute | solution.py:12
  93.7 5.9 %collective-permute-start.2 = (f32[16]{0:T(128)S(1)}, f32[16]{0:T(128)S(1)}, u32[]{:S(2)}, u32[]{:S(2)}) collective-permute-start(f32[16]{0:T(128)S(1)} %add.94), channel_id=1, source_target_pairs={{0,1},{1,2},{2,3},{3,4},{4,5},{5,6},{6,7},{7,8},{8,9},{9,10},{10,1... | collective-permute-start | bytes 200 | tf_op jit(solution)/shard_map/while/body/eval_jaxpr/ppermute | solution.py:12
  99.6 1.3 copy-start.1
  99.7 7.5 %collective-permute-start = (bf16[16,2048]{1,0:T(8,128)(2,1)S(1)}, bf16[16,2048]{1,0:T(8,128)(2,1)S(1)}, u32[]{:S(2)}, u32[]{:S(2)}) collective-permute-start(bf16[16,2048]{1,0:T(8,128)(2,1)S(1)} %copy.9), channel_id=1, source_target_pairs={{0,1},{1,2},{2,3},{3,4},{4,5},{5,6},{6,7},{7,8},{8,9},{9,10},{10,1... | collective-permute-start | bytes 196616 | tf_op jit(solution)/shard_map/while/body/eval_jaxpr/ppermute | solution.py:12
  101.1 6.0 %collective-permute-start.1 = (f32[16,256]{1,0:T(8,128)S(1)}, f32[16,256]{1,0:T(8,128)S(1)}, u32[]{:S(2)}, u32[]{:S(2)}) collective-permute-start(f32[16,256]{1,0:T(8,128)S(1)} %convolution_add_fusion.2), channel_id=1, source_target_pairs={{0,1},{1,2},{2,3},{3,4},{4,5},{5,6},{6,7},{7,8},{8,9},{9,10},{10,1... | collective-permute-start | bytes 49160 | tf_op jit(solution)/shard_map/while/body/eval_jaxpr/ppermute | solution.py:12
  101.2 5.9 %collective-permute-start.2 = (f32[16]{0:T(128)S(1)}, f32[16]{0:T(128)S(1)}, u32[]{:S(2)}, u32[]{:S(2)}) collective-permute-start(f32[16]{0:T(128)S(1)} %add.94), channel_id=1, source_target_pairs={{0,1},{1,2},{2,3},{3,4},{4,5},{5,6},{6,7},{7,8},{8,9},{9,10},{10,1... | collective-permute-start | bytes 200 | tf_op jit(solution)/shard_map/while/body/eval_jaxpr/ppermute | solution.py:12
  107.1 1.3 copy-start.1
  107.1 7.5 %collective-permute-start = (bf16[16,2048]{1,0:T(8,128)(2,1)S(1)}, bf16[16,2048]{1,0:T(8,128)(2,1)S(1)}, u32[]{:S(2)}, u32[]{:S(2)}) collective-permute-start(bf16[16,2048]{1,0:T(8,128)(2,1)S(1)} %copy.9), channel_id=1, source_target_pairs={{0,1},{1,2},{2,3},{3,4},{4,5},{5,6},{6,7},{7,8},{8,9},{9,10},{10,1... | collective-permute-start | bytes 196616 | tf_op jit(solution)/shard_map/while/body/eval_jaxpr/ppermute | solution.py:12
  108.6 6.0 %collective-permute-start.1 = (f32[16,256]{1,0:T(8,128)S(1)}, f32[16,256]{1,0:T(8,128)S(1)}, u32[]{:S(2)}, u32[]{:S(2)}) collective-permute-start(f32[16,256]{1,0:T(8,128)S(1)} %convolution_add_fusion.2), channel_id=1, source_target_pairs={{0,1},{1,2},{2,3},{3,4},{4,5},{5,6},{6,7},{7,8},{8,9},{9,10},{10,1... | collective-permute-start | bytes 49160 | tf_op jit(solution)/shard_map/while/body/eval_jaxpr/ppermute | solution.py:12
  108.7 5.9 %collective-permute-start.2 = (f32[16]{0:T(128)S(1)}, f32[16]{0:T(128)S(1)}, u32[]{:S(2)}, u32[]{:S(2)}) collective-permute-start(f32[16]{0:T(128)S(1)} %add.94), channel_id=1, source_target_pairs={{0,1},{1,2},{2,3},{3,4},{4,5},{5,6},{6,7},{7,8},{8,9},{9,10},{10,1... | collective-permute-start | bytes 200 | tf_op jit(solution)/shard_map/while/body/eval_jaxpr/ppermute | solution.py:12
  114.6 1.3 copy-start.1
  114.6 7.5 %collective-permute-start = (bf16[16,2048]{1,0:T(8,128)(2,1)S(1)}, bf16[16,2048]{1,0:T(8,128)(2,1)S(1)}, u32[]{:S(2)}, u32[]{:S(2)}) collective-permute-start(bf16[16,2048]{1,0:T(8,128)(2,1)S(1)} %copy.9), channel_id=1, source_target_pairs={{0,1},{1,2},{2,3},{3,4},{4,5},{5,6},{6,7},{7,8},{8,9},{9,10},{10,1... | collective-permute-start | bytes 196616 | tf_op jit(solution)/shard_map/while/body/eval_jaxpr/ppermute | solution.py:12
  116.1 6.0 %collective-permute-start.1 = (f32[16,256]{1,0:T(8,128)S(1)}, f32[16,256]{1,0:T(8,128)S(1)}, u32[]{:S(2)}, u32[]{:S(2)}) collective-permute-start(f32[16,256]{1,0:T(8,128)S(1)} %convolution_add_fusion.2), channel_id=1, source_target_pairs={{0,1},{1,2},{2,3},{3,4},{4,5},{5,6},{6,7},{7,8},{8,9},{9,10},{10,1... | collective-permute-start | bytes 49160 | tf_op jit(solution)/shard_map/while/body/eval_jaxpr/ppermute | solution.py:12
  116.1 5.9 %collective-permute-start.2 = (f32[16]{0:T(128)S(1)}, f32[16]{0:T(128)S(1)}, u32[]{:S(2)}, u32[]{:S(2)}) collective-permute-start(f32[16]{0:T(128)S(1)} %add.94), channel_id=1, source_target_pairs={{0,1},{1,2},{2,3},{3,4},{4,5},{5,6},{6,7},{7,8},{8,9},{9,10},{10,1... | collective-permute-start | bytes 200 | tf_op jit(solution)/shard_map/while/body/eval_jaxpr/ppermute | solution.py:12
  122.1 1.3 copy-start.1
  122.1 7.5 %collective-permute-start = (bf16[16,2048]{1,0:T(8,128)(2,1)S(1)}, bf16[16,2048]{1,0:T(8,128)(2,1)S(1)}, u32[]{:S(2)}, u32[]{:S(2)}) collective-permute-start(bf16[16,2048]{1,0:T(8,128)(2,1)S(1)} %copy.9), channel_id=1, source_target_pairs={{0,1},{1,2},{2,3},{3,4},{4,5},{5,6},{6,7},{7,8},{8,9},{9,10},{10,1... | collective-permute-start | bytes 196616 | tf_op jit(solution)/shard_map/while/body/eval_jaxpr/ppermute | solution.py:12
  123.6 6.0 %collective-permute-start.1 = (f32[16,256]{1,0:T(8,128)S(1)}, f32[16,256]{1,0:T(8,128)S(1)}, u32[]{:S(2)}, u32[]{:S(2)}) collective-permute-start(f32[16,256]{1,0:T(8,128)S(1)} %convolution_add_fusion.2), channel_id=1, source_target_pairs={{0,1},{1,2},{2,3},{3,4},{4,5},{5,6},{6,7},{7,8},{8,9},{9,10},{10,1... | collective-permute-start | bytes 49160 | tf_op jit(solution)/shard_map/while/body/eval_jaxpr/ppermute | solution.py:12
  123.6 5.9 %collective-permute-start.2 = (f32[16]{0:T(128)S(1)}, f32[16]{0:T(128)S(1)}, u32[]{:S(2)}, u32[]{:S(2)}) collective-permute-start(f32[16]{0:T(128)S(1)} %add.94), channel_id=1, source_target_pairs={{0,1},{1,2},{2,3},{3,4},{4,5},{5,6},{6,7},{7,8},{8,9},{9,10},{10,1... | collective-permute-start | bytes 200 | tf_op jit(solution)/shard_map/while/body/eval_jaxpr/ppermute | solution.py:12
  129.6 1.3 copy-start.1
  129.6 7.5 %collective-permute-start = (bf16[16,2048]{1,0:T(8,128)(2,1)S(1)}, bf16[16,2048]{1,0:T(8,128)(2,1)S(1)}, u32[]{:S(2)}, u32[]{:S(2)}) collective-permute-start(bf16[16,2048]{1,0:T(8,128)(2,1)S(1)} %copy.9), channel_id=1, source_target_pairs={{0,1},{1,2},{2,3},{3,4},{4,5},{5,6},{6,7},{7,8},{8,9},{9,10},{10,1... | collective-permute-start | bytes 196616 | tf_op jit(solution)/shard_map/while/body/eval_jaxpr/ppermute | solution.py:12
  131.1 6.0 %collective-permute-start.1 = (f32[16,256]{1,0:T(8,128)S(1)}, f32[16,256]{1,0:T(8,128)S(1)}, u32[]{:S(2)}, u32[]{:S(2)}) collective-permute-start(f32[16,256]{1,0:T(8,128)S(1)} %convolution_add_fusion.2), channel_id=1, source_target_pairs={{0,1},{1,2},{2,3},{3,4},{4,5},{5,6},{6,7},{7,8},{8,9},{9,10},{10,1... | collective-permute-start | bytes 49160 | tf_op jit(solution)/shard_map/while/body/eval_jaxpr/ppermute | solution.py:12
  131.1 5.9 %collective-permute-start.2 = (f32[16]{0:T(128)S(1)}, f32[16]{0:T(128)S(1)}, u32[]{:S(2)}, u32[]{:S(2)}) collective-permute-start(f32[16]{0:T(128)S(1)} %add.94), channel_id=1, source_target_pairs={{0,1},{1,2},{2,3},{3,4},{4,5},{5,6},{6,7},{7,8},{8,9},{9,10},{10,1... | collective-permute-start | bytes 200 | tf_op jit(solution)/shard_map/while/body/eval_jaxpr/ppermute | solution.py:12
  137.1 7.5 %collective-permute-start = (bf16[16,2048]{1,0:T(8,128)(2,1)S(1)}, bf16[16,2048]{1,0:T(8,128)(2,1)S(1)}, u32[]{:S(2)}, u32[]{:S(2)}) collective-permute-start(bf16[16,2048]{1,0:T(8,128)(2,1)S(1)} %copy.9), channel_id=1, source_target_pairs={{0,1},{1,2},{2,3},{3,4},{4,5},{5,6},{6,7},{7,8},{8,9},{9,10},{10,1... | collective-permute-start | bytes 196616 | tf_op jit(solution)/shard_map/while/body/eval_jaxpr/ppermute | solution.py:12
  138.5 6.0 %collective-permute-start.1 = (f32[16,256]{1,0:T(8,128)S(1)}, f32[16,256]{1,0:T(8,128)S(1)}, u32[]{:S(2)}, u32[]{:S(2)}) collective-permute-start(f32[16,256]{1,0:T(8,128)S(1)} %convolution_add_fusion.2), channel_id=1, source_target_pairs={{0,1},{1,2},{2,3},{3,4},{4,5},{5,6},{6,7},{7,8},{8,9},{9,10},{10,1... | collective-permute-start | bytes 49160 | tf_op jit(solution)/shard_map/while/body/eval_jaxpr/ppermute | solution.py:12
  138.6 5.9 %collective-permute-start.2 = (f32[16]{0:T(128)S(1)}, f32[16]{0:T(128)S(1)}, u32[]{:S(2)}, u32[]{:S(2)}) collective-permute-start(f32[16]{0:T(128)S(1)} %add.94), channel_id=1, source_target_pairs={{0,1},{1,2},{2,3},{3,4},{4,5},{5,6},{6,7},{7,8},{8,9},{9,10},{10,1... | collective-permute-start | bytes 200 | tf_op jit(solution)/shard_map/while/body/eval_jaxpr/ppermute | solution.py:12
  144.6 7.5 %collective-permute-start = (bf16[16,2048]{1,0:T(8,128)(2,1)S(1)}, bf16[16,2048]{1,0:T(8,128)(2,1)S(1)}, u32[]{:S(2)}, u32[]{:S(2)}) collective-permute-start(bf16[16,2048]{1,0:T(8,128)(2,1)S(1)} %copy.9), channel_id=1, source_target_pairs={{0,1},{1,2},{2,3},{3,4},{4,5},{5,6},{6,7},{7,8},{8,9},{9,10},{10,1... | collective-permute-start | bytes 196616 | tf_op jit(solution)/shard_map/while/body/eval_jaxpr/ppermute | solution.py:12
  146.0 6.0 %collective-permute-start.1 = (f32[16,256]{1,0:T(8,128)S(1)}, f32[16,256]{1,0:T(8,128)S(1)}, u32[]{:S(2)}, u32[]{:S(2)}) collective-permute-start(f32[16,256]{1,0:T(8,128)S(1)} %convolution_add_fusion.2), channel_id=1, source_target_pairs={{0,1},{1,2},{2,3},{3,4},{4,5},{5,6},{6,7},{7,8},{8,9},{9,10},{10,1... | collective-permute-start | bytes 49160 | tf_op jit(solution)/shard_map/while/body/eval_jaxpr/ppermute | solution.py:12
  146.1 5.9 %collective-permute-start.2 = (f32[16]{0:T(128)S(1)}, f32[16]{0:T(128)S(1)}, u32[]{:S(2)}, u32[]{:S(2)}) collective-permute-start(f32[16]{0:T(128)S(1)} %add.94), channel_id=1, source_target_pairs={{0,1},{1,2},{2,3},{3,4},{4,5},{5,6},{6,7},{7,8},{8,9},{9,10},{10,1... | collective-permute-start | bytes 200 | tf_op jit(solution)/shard_map/while/body/eval_jaxpr/ppermute | solution.py:12
  152.1 7.5 %collective-permute-start = (bf16[16,2048]{1,0:T(8,128)(2,1)S(1)}, bf16[16,2048]{1,0:T(8,128)(2,1)S(1)}, u32[]{:S(2)}, u32[]{:S(2)}) collective-permute-start(bf16[16,2048]{1,0:T(8,128)(2,1)S(1)} %copy.9), channel_id=1, source_target_pairs={{0,1},{1,2},{2,3},{3,4},{4,5},{5,6},{6,7},{7,8},{8,9},{9,10},{10,1... | collective-permute-start | bytes 196616 | tf_op jit(solution)/shard_map/while/body/eval_jaxpr/ppermute | solution.py:12
  153.5 6.0 %collective-permute-start.1 = (f32[16,256]{1,0:T(8,128)S(1)}, f32[16,256]{1,0:T(8,128)S(1)}, u32[]{:S(2)}, u32[]{:S(2)}) collective-permute-start(f32[16,256]{1,0:T(8,128)S(1)} %convolution_add_fusion.2), channel_id=1, source_target_pairs={{0,1},{1,2},{2,3},{3,4},{4,5},{5,6},{6,7},{7,8},{8,9},{9,10},{10,1... | collective-permute-start | bytes 49160 | tf_op jit(solution)/shard_map/while/body/eval_jaxpr/ppermute | solution.py:12
  153.6 5.9 %collective-permute-start.2 = (f32[16]{0:T(128)S(1)}, f32[16]{0:T(128)S(1)}, u32[]{:S(2)}, u32[]{:S(2)}) collective-permute-start(f32[16]{0:T(128)S(1)} %add.94), channel_id=1, source_target_pairs={{0,1},{1,2},{2,3},{3,4},{4,5},{5,6},{6,7},{7,8},{8,9},{9,10},{10,1... | collective-permute-start | bytes 200 | tf_op jit(solution)/shard_map/while/body/eval_jaxpr/ppermute | solution.py:12
  (3 other events, 3.8 us)
where the time goes:
time: 160 us
  waiting for transfers between devices  94 us (59%)
  blocking collectives  35 us (22%)
  matrix products  20.1 us (13%)
  other arithmetic  8 us (5%)
  starting transfers between devices  2.07 us (1%)
    ppermute x48, waiting for transfers between devices, shifted(): lax.ppermute(shard, axis, [(i, (i + by) % count) for i in range(count)])  94 us
    psum x1, blocking collectives, shards(): lax.psum((jnp.sum(values, axis=0), jnp.sum(values * values, axis=0)), 'blk')  35 us
    dot_general x16, matrix products, weighted_sums(): lax.dot_general(block, library, (((1,), (1,)), ((), ())), preferred_eleme...  16.9 us
  transfers between devices with their start and end apart: 48, of which 16 were waited for; matrix products, arithmetic and copies ran while one was open for 14% of the time, Pallas kernels for 0%

commit v1 on v0

v1 whole, which is shorter than its diff:
```python
import jax
import jax.numpy as jnp
from jax import lax
from jax.sharding import PartitionSpec as P

EPS = 1e-05
TAU = 0.05


def split3(x):
    hi = x.astype(jnp.bfloat16)
    rest = x - hi.astype(jnp.float32)
    mid = rest.astype(jnp.bfloat16)
    lo = (rest - mid.astype(jnp.float32)).astype(jnp.bfloat16)
    return jnp.concatenate([hi, mid, lo])


def join3(parts, n):
    parts = parts.astype(jnp.float32)
    return (parts[..., :n] + parts[..., n:2 * n]) + parts[..., 2 * n:3 * n]


def weighted_sums(block, library, lib_sq, zvals):
    blockf = block.astype(jnp.float32)
    q_sq = jnp.sum(blockf * blockf, axis=1)
    inner = lax.dot_general(
        block, library, (((1,), (1,)), ((), ())), preferred_element_type=jnp.float32
    )
    tanimoto = inner / (q_sq[:, None] + lib_sq[None, :] - inner)
    weight = jnp.exp((tanimoto - 1.0) / TAU)
    numer = jnp.dot(weight.astype(jnp.bfloat16), zvals, preferred_element_type=jnp.float32)
    denom = jnp.sum(weight, axis=1)
    return (numer, denom)


def shards(queries, library, assays):
    nblk = lax.axis_size("blk")
    q_dev, feat = queries.shape
    width = assays.shape[1]
    values = assays.astype(jnp.float32)
    partial = jnp.concatenate([jnp.sum(values, axis=0), jnp.sum(values * values, axis=0)])
    coded = split3(partial)
    stat_rows = -(-coded.shape[0] // feat)
    coded = jnp.pad(coded, (0, stat_rows * feat - coded.shape[0])).reshape(stat_rows, feat)

    packet = jnp.concatenate([queries, coded], axis=0)
    gathered = lax.all_gather(packet, "blk", tiled=False)
    everyone = gathered[:, :q_dev, :].reshape(nblk * q_dev, feat)
    stats = join3(gathered[:, q_dev:, :].reshape(nblk, stat_rows * feat), 2 * width)
    stats = jnp.sum(stats, axis=0)

    col_sum, col_sq = stats[:width], stats[width:]
    total = library.shape[0] * nblk
    mean = col_sum / total
    spread = col_sq / total - mean * mean
    zvals = ((values - mean) * lax.rsqrt(spread + EPS)).astype(jnp.bfloat16)
    lib_sq = jnp.sum(jnp.square(library.astype(jnp.float32)), axis=1)

    numer, denom = weighted_sums(everyone, library, lib_sq, zvals)
    den_rows = -(-q_dev // width)
    den_rows += -(q_dev + den_rows) % 8
    den = jnp.pad(denom.reshape(nblk, q_dev), ((0, 0), (0, den_rows * width - q_dev)))
    den = den.reshape(nblk, den_rows, width)
    sums = jnp.concatenate([numer.reshape(nblk, q_dev, width), den], axis=1)
    sums = sums.reshape(nblk * (q_dev + den_rows), width)
    mine = lax.psum_scatter(sums, "blk", scatter_dimension=0, tiled=True)
    own_num = mine[:q_dev]
    own_den = mine[q_dev:].reshape(den_rows * width)[:q_dev]
    return own_num / own_den[:, None]


def solution(mesh):
    return jax.shard_map(
        shards,
        mesh=mesh,
        in_specs=(P(("grp", "blk"), None), P(("grp", "blk"), None), P(("grp", "blk"), None)),
        out_specs=P(("grp", "blk"), None),
        check_vma=False,
    )
```

time: 160 us -> 124 us (0.78)
  blocking collectives: 35 us -> 0 us
  matrix products: 20.1 us -> 3.62 us
  between operations: 0.02 us -> 13.5 us
  other arithmetic: 8 us -> 10.1 us
  starting transfers between devices: 2.07 us -> 0.04 us
    ppermute x48 -> x0, waiting for transfers between devices: 94 us -> none  [shifted(): lax.ppermute(shard, axis, [(i, (i + by) % count) for i in range(count)])]
    reduce_scatter x0 -> x1, waiting for transfers between devices: none -> 54.9 us  [shards(): mine = lax.psum_scatter(sums, 'blk', scatter_dimension=0, tiled=True)]
    all_gather x0 -> x1, waiting for transfers between devices: none -> 40.1 us  [shards(): gathered = lax.all_gather(packet, 'blk', tiled=False)]
    psum x1 -> x0, blocking collectives: 35 us -> none  [shards(): lax.psum((jnp.sum(values, axis=0), jnp.sum(values * values, axis=0)), 'blk')]
    dot_general x16 -> x1, matrix products: 16.9 us -> 3.16 us  [weighted_sums(): lax.dot_general(block, library, (((1,), (1,)), ((), ())), preferred_eleme...]
    dot_general x16 -> x1, matrix products: 3.16 us -> 0.46 us  [weighted_sums(): jnp.dot(weight.astype(jnp.bfloat16), zvals, preferred_element_type=jnp.fl...]
    ppermute x48 -> x0, starting transfers between devices: 2.07 us -> none  [shifted(): lax.ppermute(shard, axis, [(i, (i + by) % count) for i in range(count)])]
  transfers between devices with their start and end apart: 48 -> 2, of which waited for: 16 -> 2; matrix products, arithmetic and copies ran while one was open for 14% -> 2% of each run, Pallas kernels for 0% -> 0%
where the time goes in v1:
time: 124 us; the launch traced here: 123 us
  waiting for transfers between devices  95 us (77%)
  between operations  13.5 us (11%)
  other arithmetic  10.1 us (8%)
  matrix products  3.62 us (3%)
    reduce_scatter x1, waiting for transfers between devices, shards(): mine = lax.psum_scatter(sums, 'blk', scatter_dimension=0, tiled=True)  54.9 us
    all_gather x1, waiting for transfers between devices, shards(): gathered = lax.all_gather(packet, 'blk', tiled=False)  40.1 us
    dot_general x1, matrix products, weighted_sums(): lax.dot_general(block, library, (((1,), (1,)), ((), ())), preferred_eleme...  3.16 us
    reduce_sum x1, other arithmetic, shards(): lib_sq = jnp.sum(jnp.square(library.astype(jnp.float32)), axis=1)  2.57 us
  transfers between devices with their start and end apart: 2, of which 2 were waited for; matrix products, arithmetic and copies ran while one was open for 2% of the time, Pallas kernels for 0%

profile of v1, /device:TPU:0, one launch (start us, length us, event | category | flops | bytes accessed | tf_op | source)
XLA Modules:
  0.0 123.3 jit_solution(13529821399963518893)
XLA Ops:
  6.5 0.0 all-gather.4.cloned.1.call-start
  6.5 1.1 convert_reduce_fusion
  7.7 1.5 %maximum_bitcast_fusion = bf16[1,17,2048]{2,1,0:T(8,128)(2,1)} fusion(bf16[1,2048]{1,0:T(2,128)(2,1)S(1)} %reshape.31, bf16[16,2048]{1,0:T(8,128)(2,1)} %param.3), kind=kLoop, calls=%fused_computation.19 | loop fusion | flops 139264 | bytes 139264
  9.2 0.0 all-gather.4.cloned.1.call-update
  9.2 0.0 reduce-scatter.2.cloned.1.call-start
  9.3 2.6 %multiply_reduce_fusion = f32[768]{0:T(1024)S(1)} fusion(bf16[768,2048]{1,0:T(8,128)(2,1)} %param.4), kind=kLoop, calls=%fused_computation | loop fusion | flops 4717824 | bytes 3148800 | tf_op jit(solution)/shard_map/reduce_sum | solution.py:57
  11.9 40.1 %all-gather.4.cloned.1.call-done = bf16[16,17,2048]{2,1,0:T(8,128)(2,1)} async-done(((bf16[1,17,2048]{2,1,0:T(8,128)(2,1)}), bf16[16,17,2048]{2,1,0:T(8,128)(2,1)}) %all-gather.4.cloned.1.call-update) | async-done | bytes 1114128 | tf_op jit(solution)/shard_map/all_gather | solution.py:47
  52.0 0.0 slice-start
  52.0 1.6 %multiply_reduce_fusion.1 = f32[16,16]{1,0:T(8,128)S(1)} fusion(bf16[16,17,2048]{2,1,0:T(8,128)(2,1)} %all-gather.4.cloned.1.call-done), kind=kLoop, calls=%fused_computation.1 | loop fusion | flops 1572608 | bytes 1049600 | tf_op jit(solution)/shard_map/reduce_sum | solution.py:25
  53.5 0.1 add.34
  53.6 1.1 slice_convert_fusion
  54.9 0.0 slice-done
  54.9 0.0 copy-start
  54.9 3.2 %fusion.19 = (f32[256]{0:T(256)S(1)}, f32[256,768]{1,0:T(8,128)S(1)}) fusion(f32[768]{0:T(1024)S(1)} %multiply_reduce_fusion, f32[256]{0:T(256)S(1)} %add.34, bf16[256,2048]{1,0:T(8,128)(2,1)S(1)} %bitcast.15, bf16[768,2048]{1,0:T(8,128)(2,1)} %param.4), kind=kOutput, calls=%fused_computation.38 | convolution fusion | flops 806485760 | bytes 4985856 | tf_op jit(solution)/shard_map/dot_general | solution.py:26
  58.0 0.1 reshape.34
  58.2 0.0 copy-done
  58.2 0.5 fusion.6
  58.7 0.8 pad_maximum_fusion
  59.4 0.0 reduce-scatter.2.cloned.1.call-update
  59.5 54.9 %reduce-scatter.2.cloned.1.call-done = f32[24,256]{1,0:T(8,128)} async-done(((f32[384,256]{1,0:T(8,128)}), f32[24,256]{1,0:T(8,128)}) %reduce-scatter.2.cloned.1.call-update) | async-done | bytes 24592 | tf_op jit(solution)/shard_map/reduce_scatter | solution.py:66
  114.3 0.7 slice_bitcast_fusion
  115.0 1.4 %slice_divide_fusion = f32[16,256]{1,0:T(8,128)} fusion(f32[24,256]{1,0:T(8,128)} %reduce-scatter.2.cloned.1.call-done, f32[16]{0:T(128)S(1)} %slice.47), kind=kLoop, calls=%fused_computation.23 | loop fusion | flops 4096 | bytes 32832 | tf_op jit(solution)/shard_map/div | solution.py:69
  (11 shorter events, 0.2 us)
Async XLA Ops:
  6.5 45.4 %all-gather.4.cloned.1.call-start = ((), (), s32[]{:S(2)}) async-start(), calls=%async_computation.2 | async-start | bytes 1671168 | tf_op jit(solution)/shard_map/all_gather | solution.py:47
  9.2 105.1 %reduce-scatter.2.cloned.1.call-start = ((), (), s32[]{:S(2)}) async-start(), calls=%async_computation.1 | async-start | bytes 417792 | tf_op jit(solution)/shard_map/reduce_scatter | solution.py:66
  52.0 2.9 %slice-start = ((bf16[16,17,2048]{2,1,0:T(8,128)(2,1)}), bf16[16,16,2048]{2,1,0:T(8,128)(2,1)S(1)}, s32[]{:S(2)}) async-start(bf16[16,17,2048]{2,1,0:T(8,128)(2,1)} %all-gather.4.cloned.1.call-done), calls=%async_computation.3 | async-start | bytes 2097152 | tf_op jit(solution)/shard_map/slice | solution.py:48
  54.9 3.3 %copy-start = (bf16[768,256]{1,0:T(8,128)(2,1)S(1)}, bf16[768,256]{1,0:T(8,128)(2,1)}, u32[]{:S(2)}) copy-start(bf16[768,256]{1,0:T(8,128)(2,1)} %param.5) | copy-start | bytes 1179652
Sparse Core Ops, SparseCore 0:
  9.6 42.3 all-gather.3
  59.6 54.7 reduce-scatter.1

commit v2 on v0

v2 whole, which is shorter than its diff:
```python
import jax
import jax.numpy as jnp
from jax import lax
from jax.sharding import PartitionSpec as P

EPS = 1e-05
TAU = 0.05


def weighted_sums(block, library, lib_sq, zvals):
    blockf = block.astype(jnp.float32)
    q_sq = jnp.sum(blockf * blockf, axis=1)
    inner = lax.dot_general(
        block, library, (((1,), (1,)), ((), ())), preferred_element_type=jnp.float32
    )
    tanimoto = inner / (q_sq[:, None] + lib_sq[None, :] - inner)
    weight = jnp.exp((tanimoto - 1.0) / TAU)
    numer = jnp.dot(weight.astype(jnp.bfloat16), zvals, preferred_element_type=jnp.float32)
    denom = jnp.sum(weight, axis=1)
    return (numer, denom)


def swap(tree, axis, dist):
    count = lax.axis_size(axis)
    return lax.ppermute(tree, axis, [(i, i ^ dist) for i in range(count)])


def shards(queries, library, assays):
    nblk = lax.axis_size("blk")
    q_dev, feat = queries.shape
    width = assays.shape[1]
    values = assays.astype(jnp.float32)
    partial = jnp.concatenate([jnp.sum(values, axis=0), jnp.sum(values * values, axis=0)])

    dists = []
    dist = nblk // 2
    while dist >= 1:
        dists.append(dist)
        dist //= 2
    qbuf, sbuf = queries[None], partial[None]
    for dist in dists:
        q_in, s_in = swap((qbuf, sbuf), "blk", dist)
        qbuf = jnp.concatenate([qbuf, q_in], axis=0)
        sbuf = jnp.concatenate([sbuf, s_in], axis=0)

    stats = jnp.sum(sbuf, axis=0)
    col_sum, col_sq = stats[:width], stats[width:]
    total = library.shape[0] * nblk
    mean = col_sum / total
    spread = col_sq / total - mean * mean
    zvals = ((values - mean) * lax.rsqrt(spread + EPS)).astype(jnp.bfloat16)
    lib_sq = jnp.sum(jnp.square(library.astype(jnp.float32)), axis=1)

    numer, denom = weighted_sums(qbuf.reshape(nblk * q_dev, feat), library, lib_sq, zvals)
    nbuf = numer.reshape(nblk, q_dev, width)
    dbuf = denom.reshape(nblk, q_dev)
    for dist in reversed(dists):
        half = nbuf.shape[0] // 2
        n_in, d_in = swap((nbuf[half:], dbuf[half:]), "blk", dist)
        nbuf = nbuf[:half] + n_in
        dbuf = dbuf[:half] + d_in
    return nbuf[0] / dbuf[0][:, None]


def solution(mesh):
    return jax.shard_map(
        shards,
        mesh=mesh,
        in_specs=(P(("grp", "blk"), None), P(("grp", "blk"), None), P(("grp", "blk"), None)),
        out_specs=P(("grp", "blk"), None),
        check_vma=False,
    )
```

time: 160 us -> 56.6 us (0.35)
  waiting for transfers between devices: 94 us -> 15 us
  blocking collectives: 35 us -> 0 us
  starting transfers between devices: 2.07 us -> 22.8 us
  matrix products: 20.1 us -> 2.96 us
  local copies, waits for them, and re-layouts: 0.18 us -> 4.59 us
  other arithmetic: 8 us -> 10.7 us
    ppermute x48 -> x16, waiting for transfers between devices: 94 us -> 15 us  [swap(): return lax.ppermute(tree, axis, [(i, i ^ dist) for i in range(count)])]
    psum x1 -> x0, blocking collectives: 35 us -> none  [shards(): lax.psum((jnp.sum(values, axis=0), jnp.sum(values * values, axis=0)), 'blk')]
    ppermute x48 -> x16, starting transfers between devices: 2.07 us -> 22.8 us  [swap(): return lax.ppermute(tree, axis, [(i, i ^ dist) for i in range(count)])]
    dot_general x16 -> x1, matrix products: 16.9 us -> 2.51 us  [weighted_sums(): lax.dot_general(block, library, (((1,), (1,)), ((), ())), preferred_eleme...]
    unnamed x6 -> x16, local copies, waits for them, and re-layouts: 0.01 us -> 3.46 us
    dot_general x16 -> x1, matrix products: 3.16 us -> 0.46 us  [weighted_sums(): jnp.dot(weight.astype(jnp.bfloat16), zvals, preferred_element_type=jnp.fl...]
    reduce_sum x0 -> x4, other arithmetic: none -> 2.6 us  [shards(): stats = jnp.sum(sbuf, axis=0)]
  transfers between devices with their start and end apart: 48 -> 16, of which waited for: 16 -> 9; matrix products, arithmetic and copies ran while one was open for 14% -> 19% of each run, Pallas kernels for 0% -> 0%
where the time goes in v2:
time: 56.6 us; the launch traced here: 56.3 us
  starting transfers between devices  22.8 us (40%)
  waiting for transfers between devices  15 us (27%)
  other arithmetic  10.7 us (19%)
  local copies, waits for them, and re-layouts  4.59 us (8%)
  matrix products  2.96 us (5%)
    ppermute x16, starting transfers between devices, swap(): return lax.ppermute(tree, axis, [(i, i ^ dist) for i in range(count)])  22.8 us
    ppermute x16, waiting for transfers between devices, swap(): return lax.ppermute(tree, axis, [(i, i ^ dist) for i in range(count)])  15 us
    unnamed x16, local copies, waits for them, and re-layouts  3.46 us
    reduce_sum x1, other arithmetic, shards(): lib_sq = jnp.sum(jnp.square(library.astype(jnp.float32)), axis=1)  3.16 us
    reduce_sum x4, other arithmetic, shards(): stats = jnp.sum(sbuf, axis=0)  2.6 us
    dot_general x1, matrix products, weighted_sums(): lax.dot_general(block, library, (((1,), (1,)), ((), ())), preferred_eleme...  2.51 us
    reduce_sum x1, other arithmetic, weighted_sums(): q_sq = jnp.sum(blockf * blockf, axis=1)  1.49 us
    reduce_sum x1, other arithmetic, shards(): jnp.sum(values, axis=0)  1.17 us
  transfers between devices with their start and end apart: 16, of which 9 were waited for; matrix products, arithmetic and copies ran while one was open for 19% of the time, Pallas kernels for 0%

profile of v2, /device:TPU:0, one launch (start us, length us, event | category | flops | bytes accessed | tf_op | source)
XLA Modules:
  0.0 56.3 jit_solution(14715964894723115391)
XLA Ops:
  0.0 0.0 copy-start.1
  0.0 1.2 %convert_reduce_fusion = (f32[256]{0:T(256)S(1)}, f32[256]{0:T(256)S(1)}) fusion(bf16[768,256]{1,0:T(8,128)(2,1)} %param.5), kind=kLoop, calls=%fused_computation.4 | loop fusion | flops 785920 | bytes 395264 | tf_op jit(solution)/shard_map/reduce_sum | solution.py:33
  1.2 0.0 copy-start.3
  1.2 0.0 copy-start.4
  1.2 4.1 %collective-permute-start.4 = (f32[1,512]{1,0:T(1,128)S(1)}, f32[1,512]{1,0:T(1,128)S(1)}, u32[]{:S(2)}, u32[]{:S(2)}) collective-permute-start(f32[1,512]{1,0:T(1,128)S(1)} %bitcast.23), channel_id=1, source_target_pairs={{0,8},{1,9},{2,10},{3,11},{4,12},{5,13},{6,14},{7,15},{8,0},{9,1},... | collective-permute-start | bytes 6152 | tf_op jit(solution)/shard_map/ppermute | solution.py:25
  5.3 1.6 %collective-permute-done.4 = f32[1,512]{1,0:T(1,128)S(1)} collective-permute-done((f32[1,512]{1,0:T(1,128)S(1)}, f32[1,512]{1,0:T(1,128)S(1)}, u32[]{:S(2)}, u32[]{:S(2)}) %collective-permute-start.4) | collective-permute-done | bytes 2080 | tf_op jit(solution)/shard_map/ppermute | solution.py:25
  6.9 2.0 %collective-permute-start.5 = (f32[2,512]{1,0:T(2,128)S(1)}, f32[2,512]{1,0:T(2,128)S(1)}, u32[]{:S(2)}, u32[]{:S(2)}) collective-permute-start(f32[2,512]{1,0:T(2,128)S(1)} %pad_maximum_fusion.5), channel_id=1, source_target_pairs={{0,4},{1,5},{2,6},{3,7},{4,0},{5,1},{6,2},{7,3},{8,12},{9,13},{10,... | collective-permute-start | bytes 12296 | tf_op jit(solution)/shard_map/ppermute | solution.py:25
  8.9 0.0 copy-done.3
  8.9 0.0 copy-done.4
  8.9 2.6 %collective-permute-start = (bf16[1,16,2048]{2,1,0:T(8,128)(2,1)}, bf16[1,16,2048]{2,1,0:T(8,128)(2,1)S(1)}, u32[]{:S(2)}, u32[]{:S(2)}) collective-permute-start(bf16[1,16,2048]{2,1,0:T(8,128)(2,1)} %bitcast.16), channel_id=1, source_target_pairs={{0,8},{1,9},{2,10},{3,11},{4,12},{5,13},{6,14},{7,15},{8,0},{9,1},... | collective-permute-start | bytes 196616 | tf_op jit(solution)/shard_map/ppermute | solution.py:25
  11.5 0.0 collective-permute-done.5
  11.5 1.6 %collective-permute-start.6 = (f32[4,512]{1,0:T(4,128)S(1)}, f32[4,512]{1,0:T(4,128)S(1)}, u32[]{:S(2)}, u32[]{:S(2)}) collective-permute-start(f32[4,512]{1,0:T(4,128)S(1)} %pad_maximum_fusion.4), channel_id=1, source_target_pairs={{0,2},{1,3},{2,0},{3,1},{4,6},{5,7},{6,4},{7,5},{8,10},{9,11},{10,... | collective-permute-start | bytes 24584 | tf_op jit(solution)/shard_map/ppermute | solution.py:25
  13.1 1.5 %constant_dynamic-update-slice_fusion.4 = bf16[16,16,2048]{2,1,0:T(8,128)(2,1)} fusion(bf16[16,2048]{1,0:T(8,128)(2,1)} %param.3), kind=kLoop, calls=%fused_computation.29 | loop fusion | bytes 131072
  14.5 0.7 %collective-permute-done.6 = f32[4,512]{1,0:T(4,128)S(1)} collective-permute-done((f32[4,512]{1,0:T(4,128)S(1)}, f32[4,512]{1,0:T(4,128)S(1)}, u32[]{:S(2)}, u32[]{:S(2)}) %collective-permute-start.6) | collective-permute-done | bytes 8224 | tf_op jit(solution)/shard_map/ppermute | solution.py:25
  15.2 0.6 %pad_maximum_fusion.3 = f32[8,512]{1,0:T(8,128)} fusion(f32[4,512]{1,0:T(4,128)S(1)} %collective-permute-done.6, f32[2,512]{1,0:T(2,128)S(1)} %collective-permute-done.5, f32[1,512]{1,0:T(1,128)S(1)} %collective-permute-done.4, f32[1,512]{1,0:T(1,128)S(1)} %bitcast.26), kind=kLoop, calls=%fused_computation.24 | loop fusion | flops 12288 | bytes 32768 | tf_op jit(solution)/shard_map/concatenate | solution.py:44
  15.8 0.0 collective-permute-start.7
  15.8 0.0 collective-permute-done
  15.8 0.9 %pad_maximum_fusion.2 = bf16[2,16,2048]{2,1,0:T(8,128)(2,1)S(1)} fusion(bf16[1,16,2048]{2,1,0:T(8,128)(2,1)S(1)} %collective-permute-done, bf16[1,16,2048]{2,1,0:T(8,128)(2,1)} %bitcast.17), kind=kLoop, calls=%fused_computation.18 | loop fusion | flops 65536 | bytes 262144 | tf_op jit(solution)/shard_map/concatenate | solution.py:43
  16.7 0.0 copy-start
  16.7 1.1 %collective-permute-start.1 = (bf16[2,16,2048]{2,1,0:T(8,128)(2,1)S(1)}, bf16[2,16,2048]{2,1,0:T(8,128)(2,1)S(1)}, u32[]{:S(2)}, u32[]{:S(2)}) collective-permute-start(bf16[2,16,2048]{2,1,0:T(8,128)(2,1)S(1)} %pad_maximum_fusion.2), channel_id=1, source_target_pairs={{0,4},{1,5},{2,6},{3,7},{4,0},{5,1},{6,2},{7,3},{8,12},{9,13},{10,... | collective-permute-start | bytes 393224 | tf_op jit(solution)/shard_map/ppermute | solution.py:25
  17.8 3.2 %multiply_reduce_fusion = f32[768]{0:T(1024)} fusion(bf16[768,2048]{1,0:T(8,128)(2,1)} %param.4), kind=kLoop, calls=%fused_computation | loop fusion | flops 4717824 | bytes 3148800 | tf_op jit(solution)/shard_map/reduce_sum | solution.py:52
  21.0 0.6 %reduce_sum.84 = f32[512]{0:T(512)} reduce(f32[2,512]{1,0:T(2,128)S(1)} %collective-permute-done.5, f32[]{:T(128)} %constant.4.clone.1), dimensions={0}, to_apply=%region_4.0 | reduce | flops 512 | bytes 6148 | tf_op jit(solution)/shard_map/reduce_sum | solution.py:46
  21.5 0.6 %reduce_sum.86 = f32[512]{0:T(512)} reduce(f32[4,512]{1,0:T(4,128)S(1)} %collective-permute-done.6, f32[]{:T(128)} %constant.4.clone.1), dimensions={0}, to_apply=%region_5.0 | reduce | flops 1536 | bytes 10244 | tf_op jit(solution)/shard_map/reduce_sum | solution.py:46
  22.1 0.0 collective-permute-done.7
  22.1 0.7 %reduce_sum.88 = f32[512]{0:T(512)S(1)} reduce(f32[8,512]{1,0:T(8,128)} %collective-permute-done.7, f32[]{:T(128)} %constant.4.clone.1), dimensions={0}, to_apply=%region_6.7 | reduce | flops 3584 | bytes 18436 | tf_op jit(solution)/shard_map/reduce_sum | solution.py:46
  22.9 0.0 collective-permute-done.1
  22.9 0.0 copy-done.1
  22.9 1.6 %collective-permute-start.2 = (bf16[4,16,2048]{2,1,0:T(8,128)(2,1)S(1)}, bf16[4,16,2048]{2,1,0:T(8,128)(2,1)S(1)}, u32[]{:S(2)}, u32[]{:S(2)}) collective-permute-start(bf16[4,16,2048]{2,1,0:T(8,128)(2,1)S(1)} %pad_maximum_fusion.1), channel_id=1, source_target_pairs={{0,2},{1,3},{2,0},{3,1},{4,6},{5,7},{6,4},{7,5},{8,10},{9,11},{10,... | collective-permute-start | bytes 786440 | tf_op jit(solution)/shard_map/ppermute | solution.py:25
  24.5 0.7 %add_add_fusion = f32[512]{0:T(512)S(1)} fusion(f32[512]{0:T(512)S(1)} %reduce_sum.88, f32[512]{0:T(512)} %reduce_sum.86, f32[512]{0:T(512)} %reduce_sum.84, f32[512]{0:T(512)S(1)} %bitcast.22, f32[256]{0:T(256)} %copy-done.4, f32[256]{0:T(256)} %copy-done.3), kind=kLoop, calls=%fused_computation.34 | loop fusion | flops 2560 | bytes 12288 | tf_op jit(solution)/shard_map/reduce_sum | solution.py:46
  25.2 6.4 %collective-permute-done.2 = bf16[4,16,2048]{2,1,0:T(8,128)(2,1)S(1)} collective-permute-done((bf16[4,16,2048]{2,1,0:T(8,128)(2,1)S(1)}, bf16[4,16,2048]{2,1,0:T(8,128)(2,1)S(1)}, u32[]{:S(2)}, u32[]{:S(2)}) %collective-permute-start.2) | collective-permute-done | bytes 262176 | tf_op jit(solution)/shard_map/ppermute | solution.py:25
  31.6 0.1 pad_maximum_fusion
  31.6 0.1 collective-permute-start.3
  31.7 0.6 %constant_dynamic-update-slice_fusion.3 = bf16[16,16,2048]{2,1,0:T(8,128)(2,1)} fusion(bf16[16,16,2048]{2,1,0:T(8,128)(2,1)} %constant_dynamic-update-slice_fusion.4, bf16[1,16,2048]{2,1,0:T(8,128)(2,1)S(1)} %collective-permute-done), kind=kLoop, calls=%fused_computation.28 | loop fusion | bytes 131072
  32.3 0.6 %constant_dynamic-update-slice_fusion.2 = bf16[16,16,2048]{2,1,0:T(8,128)(2,1)} fusion(bf16[16,16,2048]{2,1,0:T(8,128)(2,1)} %constant_dynamic-update-slice_fusion.3, bf16[2,16,2048]{2,1,0:T(8,128)(2,1)S(1)} %collective-permute-done.1), kind=kLoop, calls=%fused_computation.27 | loop fusion | bytes 262144
  33.0 0.7 %constant_dynamic-update-slice_fusion.1 = bf16[16,16,2048]{2,1,0:T(8,128)(2,1)} fusion(bf16[16,16,2048]{2,1,0:T(8,128)(2,1)} %constant_dynamic-update-slice_fusion.2, bf16[4,16,2048]{2,1,0:T(8,128)(2,1)S(1)} %collective-permute-done.2), kind=kLoop, calls=%fused_computation.26 | loop fusion | bytes 524288
  33.7 0.0 collective-permute-done.3
  33.7 0.8 %constant_dynamic-update-slice_fusion = bf16[16,16,2048]{2,1,0:T(8,128)(2,1)} fusion(bf16[16,16,2048]{2,1,0:T(8,128)(2,1)} %constant_dynamic-update-slice_fusion.1, bf16[8,16,2048]{2,1,0:T(8,128)(2,1)S(1)} %collective-permute-done.3), kind=kLoop, calls=%fused_computation.25 | loop fusion | bytes 1048576 | tf_op jit(solution)/shard_map/concatenate | solution.py:43
  34.5 1.5 %multiply_reduce_fusion.1 = f32[16,16]{1,0:T(8,128)S(1)} fusion(bf16[16,16,2048]{2,1,0:T(8,128)(2,1)} %constant_dynamic-update-slice_fusion), kind=kLoop, calls=%fused_computation.1 | loop fusion | flops 1572608 | bytes 1049600 | tf_op jit(solution)/shard_map/reduce_sum | solution.py:12
  36.0 0.1 add.46
  36.1 0.0 copy-done
  36.1 0.0 copy-done.5
  36.1 0.0 copy-start.2
  36.1 2.5 %fusion.13 = (f32[256]{0:T(256)S(1)}, f32[256,768]{1,0:T(8,128)S(1)}) fusion(f32[768]{0:T(1024)S(1)} %copy-done.5, f32[256]{0:T(256)S(1)} %add.46, bf16[256,2048]{1,0:T(8,128)(2,1)} %bitcast.15, bf16[768,2048]{1,0:T(8,128)(2,1)S(1)} %copy-done), kind=kOutput, calls=%fused_computation.39 | convolution fusion | flops 806485760 | bytes 4985856 | tf_op jit(solution)/shard_map/dot_general | solution.py:13
  38.6 0.0 copy-done.2
  38.6 0.5 fusion.6
  39.1 0.6 collective-permute-start.8
  39.7 0.1 slice.97
  39.8 0.0 collective-permute-start.12
  39.8 0.1 slice.95
  39.9 1.1 %collective-permute-done.12 = f32[8,16]{1,0:T(8,128)S(1)} collective-permute-done((f32[8,16]{1,0:T(8,128)S(1)}, f32[8,16]{1,0:T(8,128)S(1)}, u32[]{:S(2)}, u32[]{:S(2)}) %collective-permute-start.12) | collective-permute-done | bytes 544 | tf_op jit(solution)/shard_map/ppermute | solution.py:25
  41.0 1.5 %collective-permute-start.13 = (f32[4,16]{1,0:T(4,128)S(1)}, f32[4,16]{1,0:T(4,128)S(1)}, u32[]{:S(2)}, u32[]{:S(2)}) collective-permute-start(f32[4,16]{1,0:T(4,128)S(1)} %slice.99), channel_id=1, source_target_pairs={{0,2},{1,3},{2,0},{3,1},{4,6},{5,7},{6,4},{7,5},{8,10},{9,11},{10,... | collective-permute-start | bytes 776 | tf_op jit(solution)/shard_map/ppermute | solution.py:25
  42.5 0.0 collective-permute-done.8
  42.5 0.6 %collective-permute-start.9 = (f32[4,16,256]{2,1,0:T(8,128)S(1)}, f32[4,16,256]{2,1,0:T(8,128)S(1)}, u32[]{:S(2)}, u32[]{:S(2)}) collective-permute-start(f32[4,16,256]{2,1,0:T(8,128)S(1)} %slice.107), channel_id=1, source_target_pairs={{0,2},{1,3},{2,0},{3,1},{4,6},{5,7},{6,4},{7,5},{8,10},{9,11},{10,... | collective-permute-start | bytes 196616 | tf_op jit(solution)/shard_map/ppermute | solution.py:25
  43.1 1.5 %collective-permute-done.13 = f32[4,16]{1,0:T(4,128)S(1)} collective-permute-done((f32[4,16]{1,0:T(4,128)S(1)}, f32[4,16]{1,0:T(4,128)S(1)}, u32[]{:S(2)}, u32[]{:S(2)}) %collective-permute-start.13) | collective-permute-done | bytes 288 | tf_op jit(solution)/shard_map/ppermute | solution.py:25
  44.6 1.0 %collective-permute-start.14 = (f32[2,16]{1,0:T(2,128)S(1)}, f32[2,16]{1,0:T(2,128)S(1)}, u32[]{:S(2)}, u32[]{:S(2)}) collective-permute-start(f32[2,16]{1,0:T(2,128)S(1)} %slice.101), channel_id=1, source_target_pairs={{0,4},{1,5},{2,6},{3,7},{4,0},{5,1},{6,2},{7,3},{8,12},{9,13},{10,... | collective-permute-start | bytes 392 | tf_op jit(solution)/shard_map/ppermute | solution.py:25
  45.6 1.3 %collective-permute-done.9 = f32[4,16,256]{2,1,0:T(8,128)S(1)} collective-permute-done((f32[4,16,256]{2,1,0:T(8,128)S(1)}, f32[4,16,256]{2,1,0:T(8,128)S(1)}, u32[]{:S(2)}, u32[]{:S(2)}) %collective-permute-start.9) | collective-permute-done | bytes 65568 | tf_op jit(solution)/shard_map/ppermute | solution.py:25
  46.9 1.1 %collective-permute-start.10 = (f32[2,16,256]{2,1,0:T(8,128)S(1)}, f32[2,16,256]{2,1,0:T(8,128)S(1)}, u32[]{:S(2)}, u32[]{:S(2)}) collective-permute-start(f32[2,16,256]{2,1,0:T(8,128)S(1)} %slice.109), channel_id=1, source_target_pairs={{0,4},{1,5},{2,6},{3,7},{4,0},{5,1},{6,2},{7,3},{8,12},{9,13},{10,... | collective-permute-start | bytes 98312 | tf_op jit(solution)/shard_map/ppermute | solution.py:25
  48.0 0.2 collective-permute-done.14
  48.1 2.4 %collective-permute-start.15 = (f32[1,16]{1,0:T(1,128)S(1)}, f32[1,16]{1,0:T(1,128)S(1)}, u32[]{:S(2)}, u32[]{:S(2)}) collective-permute-start(f32[1,16]{1,0:T(1,128)S(1)} %slice.103), channel_id=1, source_target_pairs={{0,8},{1,9},{2,10},{3,11},{4,12},{5,13},{6,14},{7,15},{8,0},{9,1},... | collective-permute-start | bytes 200 | tf_op jit(solution)/shard_map/ppermute | solution.py:25
  50.6 0.3 collective-permute-done.10
  50.9 2.6 %collective-permute-start.11 = (f32[1,16,256]{2,1,0:T(8,128)S(1)}, f32[1,16,256]{2,1,0:T(8,128)S(1)}, u32[]{:S(2)}, u32[]{:S(2)}) collective-permute-start(f32[1,16,256]{2,1,0:T(8,128)S(1)} %slice.111), channel_id=1, source_target_pairs={{0,8},{1,9},{2,10},{3,11},{4,12},{5,13},{6,14},{7,15},{8,0},{9,1},... | collective-permute-start | bytes 49160 | tf_op jit(solution)/shard_map/ppermute | solution.py:25
  53.4 0.0 collective-permute-done.15
  53.4 2.1 %collective-permute-done.11 = f32[1,16,256]{2,1,0:T(8,128)S(1)} collective-permute-done((f32[1,16,256]{2,1,0:T(8,128)S(1)}, f32[1,16,256]{2,1,0:T(8,128)S(1)}, u32[]{:S(2)}, u32[]{:S(2)}) %collective-permute-start.11) | collective-permute-done | bytes 16416 | tf_op jit(solution)/shard_map/ppermute | solution.py:25
  55.6 0.7 %fusion.12 = f32[16,256]{1,0:T(8,128)} fusion(f32[1,16,256]{2,1,0:T(8,128)S(1)} %collective-permute-done.11, f32[2,16,256]{2,1,0:T(8,128)S(1)} %slice_add_fusion.1, f32[16]{0:T(128)S(1)} %add_bitcast_fusion), kind=kLoop, calls=%fused_computation.23 | loop fusion | flops 8192 | bytes 49216 | tf_op jit(solution)/shard_map/div | solution.py:62
  (21 shorter events, 0.2 us)
Async XLA Ops:
  0.0 22.9 %copy-start.1 = (bf16[16,2048]{1,0:T(8,128)(2,1)S(1)}, bf16[16,2048]{1,0:T(8,128)(2,1)}, u32[]{:S(2)}) copy-start(bf16[16,2048]{1,0:T(8,128)(2,1)} %param.3) | copy-start | bytes 196612
  1.2 7.7 %copy-start.3 = (f32[256]{0:T(256)}, f32[256]{0:T(256)S(1)}, u32[]{:S(2)}) copy-start(f32[256]{0:T(256)S(1)} %get-tuple-element.5) | copy-start | bytes 3076
  1.2 7.7 %copy-start.4 = (f32[256]{0:T(256)}, f32[256]{0:T(256)S(1)}, u32[]{:S(2)}) copy-start(f32[256]{0:T(256)S(1)} %get-tuple-element.6) | copy-start | bytes 3076
  1.2 5.7 %collective-permute-start.4 = (f32[1,512]{1,0:T(1,128)S(1)}, f32[1,512]{1,0:T(1,128)S(1)}, u32[]{:S(2)}, u32[]{:S(2)}) collective-permute-start(f32[1,512]{1,0:T(1,128)S(1)} %bitcast.23), channel_id=1, source_target_pairs={{0,8},{1,9},{2,10},{3,11},{4,12},{5,13},{6,14},{7,15},{8,0},{9,1},... | collective-permute-start | bytes 6152 | tf_op jit(solution)/shard_map/ppermute | solution.py:25
  6.9 4.6 %collective-permute-start.5 = (f32[2,512]{1,0:T(2,128)S(1)}, f32[2,512]{1,0:T(2,128)S(1)}, u32[]{:S(2)}, u32[]{:S(2)}) collective-permute-start(f32[2,512]{1,0:T(2,128)S(1)} %pad_maximum_fusion.5), channel_id=1, source_target_pairs={{0,4},{1,5},{2,6},{3,7},{4,0},{5,1},{6,2},{7,3},{8,12},{9,13},{10,... | collective-permute-start | bytes 12296 | tf_op jit(solution)/shard_map/ppermute | solution.py:25
  8.9 6.9 %collective-permute-start = (bf16[1,16,2048]{2,1,0:T(8,128)(2,1)}, bf16[1,16,2048]{2,1,0:T(8,128)(2,1)S(1)}, u32[]{:S(2)}, u32[]{:S(2)}) collective-permute-start(bf16[1,16,2048]{2,1,0:T(8,128)(2,1)} %bitcast.16), channel_id=1, source_target_pairs={{0,8},{1,9},{2,10},{3,11},{4,12},{5,13},{6,14},{7,15},{8,0},{9,1},... | collective-permute-start | bytes 196616 | tf_op jit(solution)/shard_map/ppermute | solution.py:25
  11.5 3.7 %collective-permute-start.6 = (f32[4,512]{1,0:T(4,128)S(1)}, f32[4,512]{1,0:T(4,128)S(1)}, u32[]{:S(2)}, u32[]{:S(2)}) collective-permute-start(f32[4,512]{1,0:T(4,128)S(1)} %pad_maximum_fusion.4), channel_id=1, source_target_pairs={{0,2},{1,3},{2,0},{3,1},{4,6},{5,7},{6,4},{7,5},{8,10},{9,11},{10,... | collective-permute-start | bytes 24584 | tf_op jit(solution)/shard_map/ppermute | solution.py:25
  15.8 6.3 %collective-permute-start.7 = (f32[8,512]{1,0:T(8,128)}, f32[8,512]{1,0:T(8,128)}, u32[]{:S(2)}, u32[]{:S(2)}) collective-permute-start(f32[8,512]{1,0:T(8,128)} %pad_maximum_fusion.3), channel_id=1, source_target_pairs={{0,1},{1,0},{2,3},{3,2},{4,5},{5,4},{6,7},{7,6},{8,9},{9,8},{10,11... | collective-permute-start | bytes 49160 | tf_op jit(solution)/shard_map/ppermute | solution.py:25
  16.7 19.4 %copy-start = (bf16[768,2048]{1,0:T(8,128)(2,1)S(1)}, bf16[768,2048]{1,0:T(8,128)(2,1)}, u32[]{:S(2)}) copy-start(bf16[768,2048]{1,0:T(8,128)(2,1)} %param.4) | copy-start | bytes 9437188
  16.7 6.2 %collective-permute-start.1 = (bf16[2,16,2048]{2,1,0:T(8,128)(2,1)S(1)}, bf16[2,16,2048]{2,1,0:T(8,128)(2,1)S(1)}, u32[]{:S(2)}, u32[]{:S(2)}) collective-permute-start(bf16[2,16,2048]{2,1,0:T(8,128)(2,1)S(1)} %pad_maximum_fusion.2), channel_id=1, source_target_pairs={{0,4},{1,5},{2,6},{3,7},{4,0},{5,1},{6,2},{7,3},{8,12},{9,13},{10,... | collective-permute-start | bytes 393224 | tf_op jit(solution)/shard_map/ppermute | solution.py:25
  22.1 14.0 %copy-start.5 = (f32[768]{0:T(1024)S(1)}, f32[768]{0:T(1024)}, u32[]{:S(2)}) copy-start(f32[768]{0:T(1024)} %multiply_reduce_fusion) | copy-start | bytes 9220
  22.9 8.6 %collective-permute-start.2 = (bf16[4,16,2048]{2,1,0:T(8,128)(2,1)S(1)}, bf16[4,16,2048]{2,1,0:T(8,128)(2,1)S(1)}, u32[]{:S(2)}, u32[]{:S(2)}) collective-permute-start(bf16[4,16,2048]{2,1,0:T(8,128)(2,1)S(1)} %pad_maximum_fusion.1), channel_id=1, source_target_pairs={{0,2},{1,3},{2,0},{3,1},{4,6},{5,7},{6,4},{7,5},{8,10},{9,11},{10,... | collective-permute-start | bytes 786440 | tf_op jit(solution)/shard_map/ppermute | solution.py:25
  31.6 2.1 %collective-permute-start.3 = (bf16[8,16,2048]{2,1,0:T(8,128)(2,1)S(1)}, bf16[8,16,2048]{2,1,0:T(8,128)(2,1)S(1)}, u32[]{:S(2)}, u32[]{:S(2)}) collective-permute-start(bf16[8,16,2048]{2,1,0:T(8,128)(2,1)S(1)} %pad_maximum_fusion), channel_id=1, source_target_pairs={{0,1},{1,0},{2,3},{3,2},{4,5},{5,4},{6,7},{7,6},{8,9},{9,8},{10,11... | collective-permute-start | bytes 1572872 | tf_op jit(solution)/shard_map/ppermute | solution.py:25
  36.1 2.5 %copy-start.2 = (bf16[768,256]{1,0:T(8,128)(2,1)S(1)}, bf16[768,256]{1,0:T(8,128)(2,1)}, u32[]{:S(2)}) copy-start(bf16[768,256]{1,0:T(8,128)(2,1)} %param.5) | copy-start | bytes 1179652
  39.1 3.4 %collective-permute-start.8 = (f32[8,16,256]{2,1,0:T(8,128)S(1)}, f32[8,16,256]{2,1,0:T(8,128)S(1)}, u32[]{:S(2)}, u32[]{:S(2)}) collective-permute-start(f32[8,16,256]{2,1,0:T(8,128)S(1)} %bitcast.21), channel_id=1, source_target_pairs={{0,1},{1,0},{2,3},{3,2},{4,5},{5,4},{6,7},{7,6},{8,9},{9,8},{10,11... | collective-permute-start | bytes 393224 | tf_op jit(solution)/shard_map/ppermute | solution.py:25
  39.8 1.2 %collective-permute-start.12 = (f32[8,16]{1,0:T(8,128)S(1)}, f32[8,16]{1,0:T(8,128)S(1)}, u32[]{:S(2)}, u32[]{:S(2)}) collective-permute-start(f32[8,16]{1,0:T(8,128)S(1)} %slice.97), channel_id=1, source_target_pairs={{0,1},{1,0},{2,3},{3,2},{4,5},{5,4},{6,7},{7,6},{8,9},{9,8},{10,11... | collective-permute-start | bytes 1544 | tf_op jit(solution)/shard_map/ppermute | solution.py:25
  41.0 3.6 %collective-permute-start.13 = (f32[4,16]{1,0:T(4,128)S(1)}, f32[4,16]{1,0:T(4,128)S(1)}, u32[]{:S(2)}, u32[]{:S(2)}) collective-permute-start(f32[4,16]{1,0:T(4,128)S(1)} %slice.99), channel_id=1, source_target_pairs={{0,2},{1,3},{2,0},{3,1},{4,6},{5,7},{6,4},{7,5},{8,10},{9,11},{10,... | collective-permute-start | bytes 776 | tf_op jit(solution)/shard_map/ppermute | solution.py:25
  42.5 4.3 %collective-permute-start.9 = (f32[4,16,256]{2,1,0:T(8,128)S(1)}, f32[4,16,256]{2,1,0:T(8,128)S(1)}, u32[]{:S(2)}, u32[]{:S(2)}) collective-permute-start(f32[4,16,256]{2,1,0:T(8,128)S(1)} %slice.107), channel_id=1, source_target_pairs={{0,2},{1,3},{2,0},{3,1},{4,6},{5,7},{6,4},{7,5},{8,10},{9,11},{10,... | collective-permute-start | bytes 196616 | tf_op jit(solution)/shard_map/ppermute | solution.py:25
  44.6 3.6 %collective-permute-start.14 = (f32[2,16]{1,0:T(2,128)S(1)}, f32[2,16]{1,0:T(2,128)S(1)}, u32[]{:S(2)}, u32[]{:S(2)}) collective-permute-start(f32[2,16]{1,0:T(2,128)S(1)} %slice.101), channel_id=1, source_target_pairs={{0,4},{1,5},{2,6},{3,7},{4,0},{5,1},{6,2},{7,3},{8,12},{9,13},{10,... | collective-permute-start | bytes 392 | tf_op jit(solution)/shard_map/ppermute | solution.py:25
  46.9 4.0 %collective-permute-start.10 = (f32[2,16,256]{2,1,0:T(8,128)S(1)}, f32[2,16,256]{2,1,0:T(8,128)S(1)}, u32[]{:S(2)}, u32[]{:S(2)}) collective-permute-start(f32[2,16,256]{2,1,0:T(8,128)S(1)} %slice.109), channel_id=1, source_target_pairs={{0,4},{1,5},{2,6},{3,7},{4,0},{5,1},{6,2},{7,3},{8,12},{9,13},{10,... | collective-permute-start | bytes 98312 | tf_op jit(solution)/shard_map/ppermute | solution.py:25
  48.1 5.3 %collective-permute-start.15 = (f32[1,16]{1,0:T(1,128)S(1)}, f32[1,16]{1,0:T(1,128)S(1)}, u32[]{:S(2)}, u32[]{:S(2)}) collective-permute-start(f32[1,16]{1,0:T(1,128)S(1)} %slice.103), channel_id=1, source_target_pairs={{0,8},{1,9},{2,10},{3,11},{4,12},{5,13},{6,14},{7,15},{8,0},{9,1},... | collective-permute-start | bytes 200 | tf_op jit(solution)/shard_map/ppermute | solution.py:25
  50.9 4.7 %collective-permute-start.11 = (f32[1,16,256]{2,1,0:T(8,128)S(1)}, f32[1,16,256]{2,1,0:T(8,128)S(1)}, u32[]{:S(2)}, u32[]{:S(2)}) collective-permute-start(f32[1,16,256]{2,1,0:T(8,128)S(1)} %slice.111), channel_id=1, source_target_pairs={{0,8},{1,9},{2,10},{3,11},{4,12},{5,13},{6,14},{7,15},{8,0},{9,1},... | collective-permute-start | bytes 49160 | tf_op jit(solution)/shard_map/ppermute | solution.py:25

commit v3 on v1

--- a/solution.py
+++ b/solution.py
@@ -8,11 +8,11 @@
 
 
 def split3(x):
-    hi = x.astype(jnp.bfloat16)
-    rest = x - hi.astype(jnp.float32)
-    mid = rest.astype(jnp.bfloat16)
-    lo = (rest - mid.astype(jnp.float32)).astype(jnp.bfloat16)
-    return jnp.concatenate([hi, mid, lo])
+    hi = lax.reduce_precision(x, exponent_bits=8, mantissa_bits=7)
+    rest = x - hi
+    mid = lax.reduce_precision(rest, exponent_bits=8, mantissa_bits=7)
+    lo = rest - mid
+    return jnp.concatenate([hi, mid, lo], axis=-1).astype(jnp.bfloat16)
 
 
 def join3(parts, n):
@@ -39,14 +39,16 @@
     width = assays.shape[1]
     values = assays.astype(jnp.float32)
     partial = jnp.concatenate([jnp.sum(values, axis=0), jnp.sum(values * values, axis=0)])
+
     coded = split3(partial)
-    stat_rows = -(-coded.shape[0] // feat)
-    coded = jnp.pad(coded, (0, stat_rows * feat - coded.shape[0])).reshape(stat_rows, feat)
-
-    packet = jnp.concatenate([queries, coded], axis=0)
-    gathered = lax.all_gather(packet, "blk", tiled=False)
-    everyone = gathered[:, :q_dev, :].reshape(nblk * q_dev, feat)
-    stats = join3(gathered[:, q_dev:, :].reshape(nblk, stat_rows * feat), 2 * width)
+    lanes = -(-coded.shape[0] // q_dev)
+    lanes += -lanes % 128
+    coded = jnp.pad(coded, (0, q_dev * lanes - coded.shape[0])).reshape(q_dev, lanes)
+    packet = jnp.concatenate([queries, coded], axis=1)
+    packets = jnp.broadcast_to(packet[None], (nblk,) + packet.shape)
+    got = lax.all_to_all(packets, "blk", 0, 0, tiled=True)
+    everyone = got[:, :, :feat].reshape(nblk * q_dev, feat)
+    stats = join3(got[:, :, feat:].reshape(nblk, q_dev * lanes), 2 * width)
     stats = jnp.sum(stats, axis=0)
 
     col_sum, col_sq = stats[:width], stats[width:]
@@ -62,8 +64,7 @@
     den = jnp.pad(denom.reshape(nblk, q_dev), ((0, 0), (0, den_rows * width - q_dev)))
     den = den.reshape(nblk, den_rows, width)
     sums = jnp.concatenate([numer.reshape(nblk, q_dev, width), den], axis=1)
-    sums = sums.reshape(nblk * (q_dev + den_rows), width)
-    mine = lax.psum_scatter(sums, "blk", scatter_dimension=0, tiled=True)
+    mine = jnp.sum(lax.all_to_all(sums, "blk", 0, 0, tiled=True), axis=0)
     own_num = mine[:q_dev]
     own_den = mine[q_dev:].reshape(den_rows * width)[:q_dev]
     return own_num / own_den[:, None]

time: 124 us -> 59.2 us (0.48)
  waiting for transfers between devices: 95 us -> 21.4 us
  blocking collectives: 0 us -> 19.1 us
  between operations: 13.5 us -> 0.11 us
  starting transfers between devices: 0.04 us -> 7.41 us
  other arithmetic: 10.1 us -> 5.65 us
    reduce_scatter x1 -> x0, waiting for transfers between devices: 54.9 us -> none  [shards(): mine = lax.psum_scatter(sums, 'blk', scatter_dimension=0, tiled=True)]
    all_gather x1 -> x0, waiting for transfers between devices: 40.1 us -> none  [shards(): gathered = lax.all_gather(packet, 'blk', tiled=False)]
    all_to_all x0 -> x1, waiting for transfers between devices: none -> 21.4 us  [shards(): got = lax.all_to_all(packets, 'blk', 0, 0, tiled=True)]
    all_to_all x0 -> x1, blocking collectives: none -> 19.1 us  [shards(): mine = jnp.sum(lax.all_to_all(sums, 'blk', 0, 0, tiled=True), axis=0)]
    all_to_all x0 -> x1, starting transfers between devices: none -> 7.41 us  [shards(): got = lax.all_to_all(packets, 'blk', 0, 0, tiled=True)]
    unnamed x1 -> x0, other arithmetic: 1.48 us -> none
    reduce_sum x1, other arithmetic: 1.58 us -> 0.26 us  [weighted_sums(): q_sq = jnp.sum(blockf * blockf, axis=1)]
  transfers between devices with their start and end apart: 2 -> 1, of which waited for: 2 -> 1; matrix products, arithmetic and copies ran while one was open for 2% -> 4% of each run, Pallas kernels for 0% -> 0%
where the time goes in v3:
time: 59.2 us; the launch traced here: 58.8 us
  waiting for transfers between devices  21.4 us (36%)
  blocking collectives  19.1 us (32%)
  starting transfers between devices  7.41 us (13%)
  other arithmetic  5.65 us (10%)
  matrix products  3.71 us (6%)
  local copies, waits for them, and re-layouts  1.48 us (2%)
    all_to_all x1, waiting for transfers between devices, shards(): got = lax.all_to_all(packets, 'blk', 0, 0, tiled=True)  21.4 us
    all_to_all x1, blocking collectives, shards(): mine = jnp.sum(lax.all_to_all(sums, 'blk', 0, 0, tiled=True), axis=0)  19.1 us
    all_to_all x1, starting transfers between devices, shards(): got = lax.all_to_all(packets, 'blk', 0, 0, tiled=True)  7.41 us
    dot_general x1, matrix products, weighted_sums(): lax.dot_general(block, library, (((1,), (1,)), ((), ())), preferred_eleme...  3.26 us
    reduce_sum x1, other arithmetic, shards(): lib_sq = jnp.sum(jnp.square(library.astype(jnp.float32)), axis=1)  2.57 us
  transfers between devices with their start and end apart: 1, of which 1 were waited for; matrix products, arithmetic and copies ran while one was open for 4% of the time, Pallas kernels for 0%

profile of v3, /device:TPU:0, one launch (start us, length us, event | category | flops | bytes accessed | tf_op | source)
XLA Modules:
  0.0 58.8 jit_solution(4567109829729102627)
XLA Ops:
  0.0 1.1 %convert_reduce_fusion = (f32[256]{0:T(256)S(1)}, f32[256]{0:T(256)S(1)}) fusion(bf16[768,256]{1,0:T(8,128)(2,1)} %param.5), kind=kLoop, calls=%fused_computation.5 | loop fusion | flops 785920 | bytes 395264 | tf_op jit(solution)/shard_map/reduce_sum | solution.py:41
  1.2 0.8 %pad_maximum_fusion.1 = bf16[16,2176]{1,0:T(8,128)(2,1)S(1)} fusion(bf16[16,128]{1,0:T(8,128)(2,1)S(1)} %fusion.17, bf16[16,2048]{1,0:T(8,128)(2,1)} %param.3), kind=kLoop, calls=%fused_computation.18 | loop fusion | flops 139264 | bytes 139264 | tf_op jit(solution)/shard_map/concatenate | solution.py:47
  2.0 1.1 %broadcast_in_dim.2 = bf16[16,16,2176]{2,1,0:T(8,128)(2,1)} broadcast(bf16[16,2176]{1,0:T(8,128)(2,1)S(1)} %pad_maximum_fusion.1), dimensions={1,2} | broadcast | bytes 1183744 | tf_op jit(solution)/shard_map/broadcast_in_dim | solution.py:48
  3.1 7.4 %all-to-all-start = ((bf16[16,16,2176]{2,1,0:T(8,128)(2,1)}), bf16[16,16,2176]{2,1,0:T(8,128)(2,1)S(1)}, u32[]{:S(2)}, u32[]{:S(2)}) async-start(bf16[16,16,2176]{2,1,0:T(8,128)(2,1)} %broadcast_in_dim.2), calls=%async_computation | async-start | bytes 2228224 | tf_op jit(solution)/shard_map/all_to_all | solution.py:49
  10.5 2.6 %multiply_reduce_fusion = f32[768]{0:T(1024)S(1)} fusion(bf16[768,2048]{1,0:T(8,128)(2,1)} %param.4), kind=kLoop, calls=%fused_computation | loop fusion | flops 4717824 | bytes 3148800 | tf_op jit(solution)/shard_map/reduce_sum | solution.py:59
  13.1 21.4 %all-to-all-done = bf16[16,16,2176]{2,1,0:T(8,128)(2,1)S(1)} async-done(((bf16[16,16,2176]{2,1,0:T(8,128)(2,1)}), bf16[16,16,2176]{2,1,0:T(8,128)(2,1)S(1)}, u32[]{:S(2)}, u32[]{:S(2)}) %all-to-all-start) | async-done | bytes 1114144 | tf_op jit(solution)/shard_map/all_to_all | solution.py:49
  34.5 0.3 multiply_reduce_fusion.1
  34.7 0.1 add.32
  34.9 0.1 slice.40
  35.1 0.0 copy-start
  35.1 3.3 %fusion.19 = (f32[256]{0:T(256)S(1)}, f32[256,768]{1,0:T(8,128)S(1)}) fusion(f32[768]{0:T(1024)S(1)} %multiply_reduce_fusion, f32[256]{0:T(256)S(1)} %add.32, bf16[256,2048]{1,0:T(8,128)(2,1)S(1)} %bitcast.15, bf16[768,2048]{1,0:T(8,128)(2,1)} %param.4), kind=kOutput, calls=%fused_computation.40 | convolution fusion | flops 806485760 | bytes 4985856 | tf_op jit(solution)/shard_map/dot_general | solution.py:26
  38.3 0.1 reshape.32
  38.5 0.0 copy-done
  38.5 0.5 fusion.6
  39.0 19.1 %all_to_all.10 = f32[16,24,256]{2,1,0:T(8,128)S(1)} all-to-all(f32[16,24,256]{2,1,0:T(8,128)S(1)} %pad_maximum_fusion), channel_id=1, replica_groups=mesh['grp'=2,'blk'=16] {'blk'}, dimensions={0} | all-to-all | bytes 786432 | tf_op jit(solution)/shard_map/all_to_all | solution.py:67
  58.2 0.7 %slice_divide_fusion = f32[16,256]{1,0:T(8,128)} fusion(f32[24,256]{1,0:T(8,128)S(1)} %reduce_sum.69, f32[16]{0:T(128)S(1)} %slice.47), kind=kLoop, calls=%fused_computation.23 | loop fusion | flops 4096 | bytes 32832 | tf_op jit(solution)/shard_map/div | solution.py:70
  (13 shorter events, 0.3 us)
Async XLA Ops:
  3.1 31.4 %all-to-all-start = ((bf16[16,16,2176]{2,1,0:T(8,128)(2,1)}), bf16[16,16,2176]{2,1,0:T(8,128)(2,1)S(1)}, u32[]{:S(2)}, u32[]{:S(2)}) async-start(bf16[16,16,2176]{2,1,0:T(8,128)(2,1)} %broadcast_in_dim.2), calls=%async_computation | async-start | bytes 2228224 | tf_op jit(solution)/shard_map/all_to_all | solution.py:49
  35.1 3.4 %copy-start = (bf16[768,256]{1,0:T(8,128)(2,1)S(1)}, bf16[768,256]{1,0:T(8,128)(2,1)}, u32[]{:S(2)}) copy-start(bf16[768,256]{1,0:T(8,128)(2,1)} %param.5) | copy-start | bytes 1179652

commit v4 on v3

--- a/solution.py
+++ b/solution.py
@@ -33,8 +33,47 @@
     return (numer, denom)
 
 
+def swap(x, axis, mask):
+    count = lax.axis_size(axis)
+    return lax.ppermute(x, axis, [(i, i ^ mask) for i in range(count)])
+
+
+def digit_groups(count):
+    bits = []
+    while (1 << len(bits)) < count:
+        bits.append(1 << len(bits))
+    assert (1 << len(bits)) == count
+    return [bits[k:k + 2] for k in range(0, len(bits), 2)]
+
+
+def offsets(group):
+    masks = [0]
+    for bit in group:
+        masks = masks + [m | bit for m in masks]
+    return masks
+
+
+def gather_rounds(packet, axis, groups):
+    buf = packet
+    for group in reversed(groups):
+        parts = [buf] + [swap(buf, axis, m) for m in offsets(group)[1:]]
+        buf = jnp.stack(parts, axis=0)
+    return buf
+
+
+def scatter_rounds(buf, axis, groups):
+    for group in groups:
+        masks = offsets(group)
+        total = buf[0]
+        for k in range(1, len(masks)):
+            total = total + swap(buf[k], axis, masks[k])
+        buf = total
+    return buf
+
+
 def shards(queries, library, assays):
     nblk = lax.axis_size("blk")
+    groups = digit_groups(nblk)
     q_dev, feat = queries.shape
     width = assays.shape[1]
     values = assays.astype(jnp.float32)
@@ -45,8 +84,7 @@
     lanes += -lanes % 128
     coded = jnp.pad(coded, (0, q_dev * lanes - coded.shape[0])).reshape(q_dev, lanes)
     packet = jnp.concatenate([queries, coded], axis=1)
-    packets = jnp.broadcast_to(packet[None], (nblk,) + packet.shape)
-    got = lax.all_to_all(packets, "blk", 0, 0, tiled=True)
+    got = gather_rounds(packet, "blk", groups).reshape(nblk, q_dev, feat + lanes)
     everyone = got[:, :, :feat].reshape(nblk * q_dev, feat)
     stats = join3(got[:, :, feat:].reshape(nblk, q_dev * lanes), 2 * width)
     stats = jnp.sum(stats, axis=0)
@@ -64,7 +102,8 @@
     den = jnp.pad(denom.reshape(nblk, q_dev), ((0, 0), (0, den_rows * width - q_dev)))
     den = den.reshape(nblk, den_rows, width)
     sums = jnp.concatenate([numer.reshape(nblk, q_dev, width), den], axis=1)
-    mine = jnp.sum(lax.all_to_all(sums, "blk", 0, 0, tiled=True), axis=0)
+    sums = sums.reshape(tuple(len(offsets(g)) for g in groups) + sums.shape[1:])
+    mine = scatter_rounds(sums, "blk", groups)
     own_num = mine[:q_dev]
     own_den = mine[q_dev:].reshape(den_rows * width)[:q_dev]
     return own_num / own_den[:, None]

time: 59.2 us -> 51.6 us (0.87)
  blocking collectives: 19.1 us -> 0 us
  starting transfers between devices: 7.41 us -> 14.1 us
  waiting for transfers between devices: 21.4 us -> 24.2 us
  matrix products: 3.71 us -> 4.91 us
  other arithmetic: 5.65 us -> 6.43 us
    ppermute x0 -> x12, waiting for transfers between devices: none -> 24.2 us  [swap(): return lax.ppermute(x, axis, [(i, i ^ mask) for i in range(count)])]
    all_to_all x1 -> x0, waiting for transfers between devices: 21.4 us -> none  [shards(): got = lax.all_to_all(packets, 'blk', 0, 0, tiled=True)]
    all_to_all x1 -> x0, blocking collectives: 19.1 us -> none  [shards(): mine = jnp.sum(lax.all_to_all(sums, 'blk', 0, 0, tiled=True), axis=0)]
    ppermute x0 -> x12, starting transfers between devices: none -> 14.1 us  [swap(): return lax.ppermute(x, axis, [(i, i ^ mask) for i in range(count)])]
    all_to_all x1 -> x0, starting transfers between devices: 7.41 us -> none  [shards(): got = lax.all_to_all(packets, 'blk', 0, 0, tiled=True)]
    dot_general x1, matrix products: 0.46 us -> 1.59 us  [weighted_sums(): jnp.dot(weight.astype(jnp.bfloat16), zvals, preferred_element_type=jnp.fl...]
    another operation x1 -> x4, other arithmetic: 0.02 us -> 1.09 us  [the longest x3 1.07 us: gather_rounds(): buf = jnp.stack(parts, axis=0)]
    broadcast_in_dim x1 -> x0, local copies, waits for them, and re-layouts: 1.07 us -> none  [shards(): packets = jnp.broadcast_to(packet[None], (nblk,) + packet.shape)]
  transfers between devices with their start and end apart: 1 -> 12, of which waited for: 1 -> 8; matrix products, arithmetic and copies ran while one was open for 4% -> 5% of each run, Pallas kernels for 0% -> 0%
where the time goes in v4:
time: 51.6 us; the launch traced here: 51.3 us
  waiting for transfers between devices  24.2 us (47%)
  starting transfers between devices  14.1 us (27%)
  other arithmetic  6.43 us (12%)
  matrix products  4.91 us (10%)
  local copies, waits for them, and re-layouts  1.55 us (3%)
    ppermute x12, waiting for transfers between devices, swap(): return lax.ppermute(x, axis, [(i, i ^ mask) for i in range(count)])  24.2 us
    ppermute x12, starting transfers between devices, swap(): return lax.ppermute(x, axis, [(i, i ^ mask) for i in range(count)])  14.1 us
    dot_general x1, matrix products, weighted_sums(): lax.dot_general(block, library, (((1,), (1,)), ((), ())), preferred_eleme...  3.32 us
    reduce_sum x1, other arithmetic, shards(): lib_sq = jnp.sum(jnp.square(library.astype(jnp.float32)), axis=1)  2.57 us
    dot_general x1, matrix products, weighted_sums(): jnp.dot(weight.astype(jnp.bfloat16), zvals, preferred_element_type=jnp.fl...  1.59 us
    reduce_sum x1, other arithmetic, shards(): jnp.sum(values, axis=0)  1.14 us
    slice x1, local copies, waits for them, and re-layouts, shards(): everyone = got[:, :, :feat].reshape(nblk * q_dev, feat)  1.12 us
    another operation x3, other arithmetic, gather_rounds(): buf = jnp.stack(parts, axis=0)  1.07 us
  transfers between devices with their start and end apart: 12, of which 8 were waited for; matrix products, arithmetic and copies ran while one was open for 5% of the time, Pallas kernels for 0%

profile of v4, /device:TPU:0, one launch (start us, length us, event | category | flops | bytes accessed | tf_op | source)
XLA Modules:
  0.0 51.3 jit_solution(7500605302750829312)
XLA Ops:
  0.0 1.1 %convert_reduce_fusion = (f32[256]{0:T(256)S(1)}, f32[256]{0:T(256)S(1)}) fusion(bf16[768,256]{1,0:T(8,128)(2,1)} %param.5), kind=kLoop, calls=%fused_computation.5 | loop fusion | flops 785920 | bytes 395264 | tf_op jit(solution)/shard_map/reduce_sum | solution.py:80
  1.2 0.9 %fusion.28 = (bf16[1,16,2176]{2,1,0:T(8,128)(2,1)S(1)}, bf16[16,2176]{1,0:T(8,128)(2,1)S(1)}) fusion(bf16[16,128]{1,0:T(8,128)(2,1)S(1)} %fusion.26, bf16[16,2048]{1,0:T(8,128)(2,1)} %param.3), kind=kLoop, calls=%fused_computation.61 | loop fusion | flops 139264 | bytes 208896 | tf_op jit(solution)/shard_map/stack | solution.py:60
  2.0 5.1 %collective-permute-start.2 = (bf16[16,2176]{1,0:T(8,128)(2,1)S(1)}, bf16[16,2176]{1,0:T(8,128)(2,1)S(1)}, u32[]{:S(2)}, u32[]{:S(2)}) collective-permute-start(bf16[16,2176]{1,0:T(8,128)(2,1)S(1)} %get-tuple-element.16), channel_id=1, source_target_pairs={{0,12},{1,13},{2,14},{3,15},{4,8},{5,9},{6,10},{7,11},{8,4},{9,5},... | collective-permute-start | bytes 208904 | tf_op jit(solution)/shard_map/ppermute | solution.py:38
  7.2 0.0 collective-permute-start.1
  7.2 0.6 %collective-permute-start = (bf16[16,2176]{1,0:T(8,128)(2,1)S(1)}, bf16[16,2176]{1,0:T(8,128)(2,1)S(1)}, u32[]{:S(2)}, u32[]{:S(2)}) collective-permute-start(bf16[16,2176]{1,0:T(8,128)(2,1)S(1)} %get-tuple-element.16), channel_id=1, source_target_pairs={{0,4},{1,5},{2,6},{3,7},{4,0},{5,1},{6,2},{7,3},{8,12},{9,13},{10,... | collective-permute-start | bytes 208904 | tf_op jit(solution)/shard_map/ppermute | solution.py:38
  7.8 1.9 %collective-permute-done.2 = bf16[16,2176]{1,0:T(8,128)(2,1)S(1)} collective-permute-done((bf16[16,2176]{1,0:T(8,128)(2,1)S(1)}, bf16[16,2176]{1,0:T(8,128)(2,1)S(1)}, u32[]{:S(2)}, u32[]{:S(2)}) %collective-permute-start.2) | collective-permute-done | bytes 69664 | tf_op jit(solution)/shard_map/ppermute | solution.py:38
  9.7 3.3 %collective-permute-done.1 = bf16[16,2176]{1,0:T(8,128)(2,1)S(1)} collective-permute-done((bf16[16,2176]{1,0:T(8,128)(2,1)S(1)}, bf16[16,2176]{1,0:T(8,128)(2,1)S(1)}, u32[]{:S(2)}, u32[]{:S(2)}) %collective-permute-start.1) | collective-permute-done | bytes 69664 | tf_op jit(solution)/shard_map/ppermute | solution.py:38
  13.1 0.0 collective-permute-done
  13.1 0.1 fusion.31
  13.1 0.9 %collective-permute-start.5 = (bf16[4,16,2176]{2,1,0:T(8,128)(2,1)S(1)}, bf16[4,16,2176]{2,1,0:T(8,128)(2,1)S(1)}, u32[]{:S(2)}, u32[]{:S(2)}) collective-permute-start(bf16[4,16,2176]{2,1,0:T(8,128)(2,1)S(1)} %get-tuple-element.11), channel_id=1, source_target_pairs={{0,3},{1,2},{2,1},{3,0},{4,7},{5,6},{6,5},{7,4},{8,11},{9,10},{10,... | collective-permute-start | bytes 835592 | tf_op jit(solution)/shard_map/ppermute | solution.py:38
  14.0 0.8 %collective-permute-start.4 = (bf16[4,16,2176]{2,1,0:T(8,128)(2,1)S(1)}, bf16[4,16,2176]{2,1,0:T(8,128)(2,1)S(1)}, u32[]{:S(2)}, u32[]{:S(2)}) collective-permute-start(bf16[4,16,2176]{2,1,0:T(8,128)(2,1)S(1)} %get-tuple-element.11), channel_id=1, source_target_pairs={{0,2},{1,3},{2,0},{3,1},{4,6},{5,7},{6,4},{7,5},{8,10},{9,11},{10,... | collective-permute-start | bytes 835592 | tf_op jit(solution)/shard_map/ppermute | solution.py:38
  14.8 0.3 collective-permute-start.3
  15.1 2.6 %multiply_reduce_fusion = f32[768]{0:T(1024)S(1)} fusion(bf16[768,2048]{1,0:T(8,128)(2,1)} %param.4), kind=kLoop, calls=%fused_computation | loop fusion | flops 4717824 | bytes 3148800 | tf_op jit(solution)/shard_map/reduce_sum | solution.py:97
  17.6 4.4 %collective-permute-done.5 = bf16[4,16,2176]{2,1,0:T(8,128)(2,1)S(1)} collective-permute-done((bf16[4,16,2176]{2,1,0:T(8,128)(2,1)S(1)}, bf16[4,16,2176]{2,1,0:T(8,128)(2,1)S(1)}, u32[]{:S(2)}, u32[]{:S(2)}) %collective-permute-start.5) | collective-permute-done | bytes 278560 | tf_op jit(solution)/shard_map/ppermute | solution.py:38
  22.1 6.0 %collective-permute-done.4 = bf16[4,16,2176]{2,1,0:T(8,128)(2,1)S(1)} collective-permute-done((bf16[4,16,2176]{2,1,0:T(8,128)(2,1)S(1)}, bf16[4,16,2176]{2,1,0:T(8,128)(2,1)S(1)}, u32[]{:S(2)}, u32[]{:S(2)}) %collective-permute-start.4) | collective-permute-done | bytes 278560 | tf_op jit(solution)/shard_map/ppermute | solution.py:38
  28.1 0.0 collective-permute-done.3
  28.1 0.2 pad_maximum_fusion
  28.3 0.0 copy-start
  28.3 0.3 multiply_reduce_fusion.1
  28.6 1.1 %slice.76 = bf16[16,16,2048]{2,1,0:T(8,128)(2,1)} slice(bf16[16,16,2176]{2,1,0:T(8,128)(2,1)S(1)} %bitcast.42), slice={[0:16], [0:16], [0:2048]} | slice | bytes 2097152 | tf_op jit(solution)/shard_map/slice | solution.py:88
  29.8 0.6 %slice_multiply_fusion = (f32[256]{0:T(256)S(1)}, f32[256]{0:T(256)}) fusion(f32[512]{0:T(512)S(1)} %fusion.17), kind=kLoop, calls=%fused_computation.60 | loop fusion | flops 1280 | bytes 4096 | tf_op jit(solution)/shard_map/div | solution.py:94
  30.4 0.1 add.50
  30.5 0.1 copy-done
  30.6 0.0 copy-start.1
  30.6 3.3 %fusion.29 = (f32[256]{0:T(256)S(1)}, f32[256,768]{1,0:T(8,128)}) fusion(f32[768]{0:T(1024)S(1)} %multiply_reduce_fusion, f32[256]{0:T(256)S(1)} %add.50, bf16[256,2048]{1,0:T(8,128)(2,1)} %bitcast.47, bf16[768,2048]{1,0:T(8,128)(2,1)S(1)} %copy-done), kind=kOutput, calls=%fused_computation.62 | convolution fusion | flops 806485760 | bytes 4985856 | tf_op jit(solution)/shard_map/dot_general | solution.py:26
  33.9 0.1 reshape.44
  34.1 0.0 copy-done.1
  34.1 1.6 %fusion.6 = f32[256,256]{1,0:T(8,128)S(1)} fusion(bf16[768,256]{1,0:T(8,128)(2,1)S(1)} %copy-done.1, f32[256]{0:T(256)} %get-tuple-element.18, f32[256]{0:T(256)S(1)} %get-tuple-element.17, f32[256,768]{1,0:T(8,128)} %get-tuple-element.23, f32[768]{0:T(1024)S(1)} %multiply_reduce_fusion, f32[256]{0:T(256)S(1)} %add.50), kind=kOutput, calls=%fused_computation.19 | convolution fusion | flops 102629376 | bytes 1447936 | tf_op jit(solution)/shard_map/dot_general | solution.py:31
  35.7 1.0 %collective-permute-start.8 = (f32[4,24,256]{2,1,0:T(8,128)S(1)}, f32[4,24,256]{2,1,0:T(8,128)S(1)}, u32[]{:S(2)}, u32[]{:S(2)}) collective-permute-start(f32[4,24,256]{2,1,0:T(8,128)S(1)} %get-tuple-element.8), channel_id=1, source_target_pairs={{0,3},{1,2},{2,1},{3,0},{4,7},{5,6},{6,5},{7,4},{8,11},{9,10},{10,... | collective-permute-start | bytes 294920 | tf_op jit(solution)/shard_map/ppermute | solution.py:38
  36.8 0.7 %collective-permute-start.7 = (f32[4,24,256]{2,1,0:T(8,128)S(1)}, f32[4,24,256]{2,1,0:T(8,128)S(1)}, u32[]{:S(2)}, u32[]{:S(2)}) collective-permute-start(f32[4,24,256]{2,1,0:T(8,128)S(1)} %get-tuple-element.9), channel_id=1, source_target_pairs={{0,2},{1,3},{2,0},{3,1},{4,6},{5,7},{6,4},{7,5},{8,10},{9,11},{10,... | collective-permute-start | bytes 294920 | tf_op jit(solution)/shard_map/ppermute | solution.py:38
  37.4 0.2 collective-permute-start.6
  37.6 3.0 %collective-permute-done.8 = f32[4,24,256]{2,1,0:T(8,128)S(1)} collective-permute-done((f32[4,24,256]{2,1,0:T(8,128)S(1)}, f32[4,24,256]{2,1,0:T(8,128)S(1)}, u32[]{:S(2)}, u32[]{:S(2)}) %collective-permute-start.8) | collective-permute-done | bytes 98336 | tf_op jit(solution)/shard_map/ppermute | solution.py:38
  40.7 2.3 %collective-permute-done.7 = f32[4,24,256]{2,1,0:T(8,128)S(1)} collective-permute-done((f32[4,24,256]{2,1,0:T(8,128)S(1)}, f32[4,24,256]{2,1,0:T(8,128)S(1)}, u32[]{:S(2)}, u32[]{:S(2)}) %collective-permute-start.7) | collective-permute-done | bytes 98336 | tf_op jit(solution)/shard_map/ppermute | solution.py:38
  43.0 0.0 collective-permute-done.6
  43.0 2.8 %collective-permute-start.11 = (f32[24,256]{1,0:T(8,128)S(1)}, f32[24,256]{1,0:T(8,128)S(1)}, u32[]{:S(2)}, u32[]{:S(2)}) collective-permute-start(f32[24,256]{1,0:T(8,128)S(1)} %get-tuple-element.13), channel_id=1, source_target_pairs={{0,12},{1,13},{2,14},{3,15},{4,8},{5,9},{6,10},{7,11},{8,4},{9,5},... | collective-permute-start | bytes 73736 | tf_op jit(solution)/shard_map/ppermute | solution.py:38
  45.8 0.0 collective-permute-start.10
  45.8 1.7 %collective-permute-start.9 = (f32[24,256]{1,0:T(8,128)S(1)}, f32[24,256]{1,0:T(8,128)S(1)}, u32[]{:S(2)}, u32[]{:S(2)}) collective-permute-start(f32[24,256]{1,0:T(8,128)S(1)} %get-tuple-element.12), channel_id=1, source_target_pairs={{0,4},{1,5},{2,6},{3,7},{4,0},{5,1},{6,2},{7,3},{8,12},{9,13},{10,... | collective-permute-start | bytes 73736 | tf_op jit(solution)/shard_map/ppermute | solution.py:38
  47.5 1.2 %collective-permute-done.11 = f32[24,256]{1,0:T(8,128)S(1)} collective-permute-done((f32[24,256]{1,0:T(8,128)S(1)}, f32[24,256]{1,0:T(8,128)S(1)}, u32[]{:S(2)}, u32[]{:S(2)}) %collective-permute-start.11) | collective-permute-done | bytes 24608 | tf_op jit(solution)/shard_map/ppermute | solution.py:38
  48.7 1.8 %collective-permute-done.10 = f32[24,256]{1,0:T(8,128)S(1)} collective-permute-done((f32[24,256]{1,0:T(8,128)S(1)}, f32[24,256]{1,0:T(8,128)S(1)}, u32[]{:S(2)}, u32[]{:S(2)}) %collective-permute-start.10) | collective-permute-done | bytes 24608 | tf_op jit(solution)/shard_map/ppermute | solution.py:38
  50.5 0.0 collective-permute-done.9
  50.6 0.7 %slice_divide_fusion = f32[16,256]{1,0:T(8,128)} fusion(f32[24,256]{1,0:T(8,128)S(1)} %fusion.20, f32[16]{0:T(128)S(1)} %slice.93), kind=kLoop, calls=%fused_computation.44 | loop fusion | flops 4096 | bytes 32832 | tf_op jit(solution)/shard_map/div | solution.py:109
  (14 shorter events, 0.2 us)
Async XLA Ops:
  2.0 7.7 %collective-permute-start.2 = (bf16[16,2176]{1,0:T(8,128)(2,1)S(1)}, bf16[16,2176]{1,0:T(8,128)(2,1)S(1)}, u32[]{:S(2)}, u32[]{:S(2)}) collective-permute-start(bf16[16,2176]{1,0:T(8,128)(2,1)S(1)} %get-tuple-element.16), channel_id=1, source_target_pairs={{0,12},{1,13},{2,14},{3,15},{4,8},{5,9},{6,10},{7,11},{8,4},{9,5},... | collective-permute-start | bytes 208904 | tf_op jit(solution)/shard_map/ppermute | solution.py:38
  7.2 5.9 %collective-permute-start.1 = (bf16[16,2176]{1,0:T(8,128)(2,1)S(1)}, bf16[16,2176]{1,0:T(8,128)(2,1)S(1)}, u32[]{:S(2)}, u32[]{:S(2)}) collective-permute-start(bf16[16,2176]{1,0:T(8,128)(2,1)S(1)} %get-tuple-element.16), channel_id=1, source_target_pairs={{0,8},{1,9},{2,10},{3,11},{4,12},{5,13},{6,14},{7,15},{8,0},{9,1},... | collective-permute-start | bytes 208904 | tf_op jit(solution)/shard_map/ppermute | solution.py:38
  7.2 5.9 %collective-permute-start = (bf16[16,2176]{1,0:T(8,128)(2,1)S(1)}, bf16[16,2176]{1,0:T(8,128)(2,1)S(1)}, u32[]{:S(2)}, u32[]{:S(2)}) collective-permute-start(bf16[16,2176]{1,0:T(8,128)(2,1)S(1)} %get-tuple-element.16), channel_id=1, source_target_pairs={{0,4},{1,5},{2,6},{3,7},{4,0},{5,1},{6,2},{7,3},{8,12},{9,13},{10,... | collective-permute-start | bytes 208904 | tf_op jit(solution)/shard_map/ppermute | solution.py:38
  13.1 8.9 %collective-permute-start.5 = (bf16[4,16,2176]{2,1,0:T(8,128)(2,1)S(1)}, bf16[4,16,2176]{2,1,0:T(8,128)(2,1)S(1)}, u32[]{:S(2)}, u32[]{:S(2)}) collective-permute-start(bf16[4,16,2176]{2,1,0:T(8,128)(2,1)S(1)} %get-tuple-element.11), channel_id=1, source_target_pairs={{0,3},{1,2},{2,1},{3,0},{4,7},{5,6},{6,5},{7,4},{8,11},{9,10},{10,... | collective-permute-start | bytes 835592 | tf_op jit(solution)/shard_map/ppermute | solution.py:38
  14.0 14.1 %collective-permute-start.4 = (bf16[4,16,2176]{2,1,0:T(8,128)(2,1)S(1)}, bf16[4,16,2176]{2,1,0:T(8,128)(2,1)S(1)}, u32[]{:S(2)}, u32[]{:S(2)}) collective-permute-start(bf16[4,16,2176]{2,1,0:T(8,128)(2,1)S(1)} %get-tuple-element.11), channel_id=1, source_target_pairs={{0,2},{1,3},{2,0},{3,1},{4,6},{5,7},{6,4},{7,5},{8,10},{9,11},{10,... | collective-permute-start | bytes 835592 | tf_op jit(solution)/shard_map/ppermute | solution.py:38
  14.8 13.3 %collective-permute-start.3 = (bf16[4,16,2176]{2,1,0:T(8,128)(2,1)S(1)}, bf16[4,16,2176]{2,1,0:T(8,128)(2,1)S(1)}, u32[]{:S(2)}, u32[]{:S(2)}) collective-permute-start(bf16[4,16,2176]{2,1,0:T(8,128)(2,1)S(1)} %get-tuple-element.11), channel_id=1, source_target_pairs={{0,1},{1,0},{2,3},{3,2},{4,5},{5,4},{6,7},{7,6},{8,9},{9,8},{10,11... | collective-permute-start | bytes 835592 | tf_op jit(solution)/shard_map/ppermute | solution.py:38
  28.3 2.3 %copy-start = (bf16[768,2048]{1,0:T(8,128)(2,1)S(1)}, bf16[768,2048]{1,0:T(8,128)(2,1)}, u32[]{:S(2)}) copy-start(bf16[768,2048]{1,0:T(8,128)(2,1)} %param.4) | copy-start | bytes 9437188
  30.6 3.5 %copy-start.1 = (bf16[768,256]{1,0:T(8,128)(2,1)S(1)}, bf16[768,256]{1,0:T(8,128)(2,1)}, u32[]{:S(2)}) copy-start(bf16[768,256]{1,0:T(8,128)(2,1)} %param.5) | copy-start | bytes 1179652
  35.7 4.9 %collective-permute-start.8 = (f32[4,24,256]{2,1,0:T(8,128)S(1)}, f32[4,24,256]{2,1,0:T(8,128)S(1)}, u32[]{:S(2)}, u32[]{:S(2)}) collective-permute-start(f32[4,24,256]{2,1,0:T(8,128)S(1)} %get-tuple-element.8), channel_id=1, source_target_pairs={{0,3},{1,2},{2,1},{3,0},{4,7},{5,6},{6,5},{7,4},{8,11},{9,10},{10,... | collective-permute-start | bytes 294920 | tf_op jit(solution)/shard_map/ppermute | solution.py:38
  36.8 6.2 %collective-permute-start.7 = (f32[4,24,256]{2,1,0:T(8,128)S(1)}, f32[4,24,256]{2,1,0:T(8,128)S(1)}, u32[]{:S(2)}, u32[]{:S(2)}) collective-permute-start(f32[4,24,256]{2,1,0:T(8,128)S(1)} %get-tuple-element.9), channel_id=1, source_target_pairs={{0,2},{1,3},{2,0},{3,1},{4,6},{5,7},{6,4},{7,5},{8,10},{9,11},{10,... | collective-permute-start | bytes 294920 | tf_op jit(solution)/shard_map/ppermute | solution.py:38
  37.4 5.5 %collective-permute-start.6 = (f32[4,24,256]{2,1,0:T(8,128)S(1)}, f32[4,24,256]{2,1,0:T(8,128)S(1)}, u32[]{:S(2)}, u32[]{:S(2)}) collective-permute-start(f32[4,24,256]{2,1,0:T(8,128)S(1)} %get-tuple-element.7), channel_id=1, source_target_pairs={{0,1},{1,0},{2,3},{3,2},{4,5},{5,4},{6,7},{7,6},{8,9},{9,8},{10,11... | collective-permute-start | bytes 294920 | tf_op jit(solution)/shard_map/ppermute | solution.py:38
  43.0 5.7 %collective-permute-start.11 = (f32[24,256]{1,0:T(8,128)S(1)}, f32[24,256]{1,0:T(8,128)S(1)}, u32[]{:S(2)}, u32[]{:S(2)}) collective-permute-start(f32[24,256]{1,0:T(8,128)S(1)} %get-tuple-element.13), channel_id=1, source_target_pairs={{0,12},{1,13},{2,14},{3,15},{4,8},{5,9},{6,10},{7,11},{8,4},{9,5},... | collective-permute-start | bytes 73736 | tf_op jit(solution)/shard_map/ppermute | solution.py:38
  45.8 4.7 %collective-permute-start.10 = (f32[24,256]{1,0:T(8,128)S(1)}, f32[24,256]{1,0:T(8,128)S(1)}, u32[]{:S(2)}, u32[]{:S(2)}) collective-permute-start(f32[24,256]{1,0:T(8,128)S(1)} %get-tuple-element.14), channel_id=1, source_target_pairs={{0,8},{1,9},{2,10},{3,11},{4,12},{5,13},{6,14},{7,15},{8,0},{9,1},... | collective-permute-start | bytes 73736 | tf_op jit(solution)/shard_map/ppermute | solution.py:38
  45.8 4.7 %collective-permute-start.9 = (f32[24,256]{1,0:T(8,128)S(1)}, f32[24,256]{1,0:T(8,128)S(1)}, u32[]{:S(2)}, u32[]{:S(2)}) collective-permute-start(f32[24,256]{1,0:T(8,128)S(1)} %get-tuple-element.12), channel_id=1, source_target_pairs={{0,4},{1,5},{2,6},{3,7},{4,0},{5,1},{6,2},{7,3},{8,12},{9,13},{10,... | collective-permute-start | bytes 73736 | tf_op jit(solution)/shard_map/ppermute | solution.py:38

commit v5 on v4

--- a/solution.py
+++ b/solution.py
@@ -43,7 +43,12 @@
     while (1 << len(bits)) < count:
         bits.append(1 << len(bits))
     assert (1 << len(bits)) == count
-    return [bits[k:k + 2] for k in range(0, len(bits), 2)]
+    groups = [bits[:1], bits[1:2]]
+    rest = bits[2:]
+    while rest:
+        groups.insert(2, rest[-2:])
+        rest = rest[:-2]
+    return [g for g in groups if g]
 
 
 def offsets(group):

time: 51.6 us -> 47.1 us (0.913)
  waiting for transfers between devices: 24.2 us -> 22 us
  other arithmetic: 6.43 us -> 4.75 us
    ppermute x12 -> x10, waiting for transfers between devices: 24.2 us -> 22 us  [swap(): return lax.ppermute(x, axis, [(i, i ^ mask) for i in range(count)])]
    reduce_sum x1, other arithmetic: 2.57 us -> 0.68 us  [shards(): lib_sq = jnp.sum(jnp.square(library.astype(jnp.float32)), axis=1)]
    ppermute x12 -> x10, starting transfers between devices: 14.1 us -> 13.8 us  [swap(): return lax.ppermute(x, axis, [(i, i ^ mask) for i in range(count)])]
    another operation x3 -> x4, other arithmetic: 1.07 us -> 1.1 us  [gather_rounds(): buf = jnp.stack(parts, axis=0)]
  transfers between devices with their start and end apart: 12 -> 10, of which waited for: 8 -> 9; matrix products, arithmetic and copies ran while one was open for 5% -> 1% of each run, Pallas kernels for 0% -> 0%
where the time goes in v5:
time: 47.1 us; the launch traced here: 46.9 us
  waiting for transfers between devices  22 us (47%)
  starting transfers between devices  13.8 us (29%)
  matrix products  4.88 us (10%)
  other arithmetic  4.75 us (10%)
  local copies, waits for them, and re-layouts  1.39 us (3%)
    ppermute x10, waiting for transfers between devices, swap(): return lax.ppermute(x, axis, [(i, i ^ mask) for i in range(count)])  22 us
    ppermute x10, starting transfers between devices, swap(): return lax.ppermute(x, axis, [(i, i ^ mask) for i in range(count)])  13.8 us
    dot_general x1, matrix products, weighted_sums(): lax.dot_general(block, library, (((1,), (1,)), ((), ())), preferred_eleme...  3.29 us
    dot_general x1, matrix products, weighted_sums(): jnp.dot(weight.astype(jnp.bfloat16), zvals, preferred_element_type=jnp.fl...  1.59 us
    reduce_sum x1, other arithmetic, shards(): jnp.sum(values, axis=0)  1.29 us
    another operation x4, other arithmetic, gather_rounds(): buf = jnp.stack(parts, axis=0)  1.1 us
    slice x1, local copies, waits for them, and re-layouts, shards(): everyone = got[:, :, :feat].reshape(nblk * q_dev, feat)  1.1 us
  transfers between devices with their start and end apart: 10, of which 9 were waited for; matrix products, arithmetic and copies ran while one was open for 1% of the time, Pallas kernels for 0%

profile of v5, /device:TPU:0, one launch (start us, length us, event | category | flops | bytes accessed | tf_op | source)
XLA Modules:
  0.0 46.9 jit_solution(10382738432723244236)
XLA Ops:
  0.0 0.0 copy-start
  0.0 1.3 %convert_reduce_fusion = (f32[256]{0:T(256)S(1)}, f32[256]{0:T(256)S(1)}) fusion(bf16[768,256]{1,0:T(8,128)(2,1)} %param.5), kind=kLoop, calls=%fused_computation.5 | loop fusion | flops 785920 | bytes 395264 | tf_op jit(solution)/shard_map/reduce_sum | solution.py:85
  1.3 0.9 %fusion.24 = (bf16[1,16,2176]{2,1,0:T(8,128)(2,1)S(1)}, bf16[16,2176]{1,0:T(8,128)(2,1)S(1)}) fusion(bf16[16,128]{1,0:T(8,128)(2,1)S(1)} %fusion.22, bf16[16,2048]{1,0:T(8,128)(2,1)} %param.3), kind=kLoop, calls=%fused_computation.56 | loop fusion | flops 139264 | bytes 208896 | tf_op jit(solution)/shard_map/stack | solution.py:65
  2.2 4.1 %collective-permute-start.1 = (bf16[16,2176]{1,0:T(8,128)(2,1)S(1)}, bf16[16,2176]{1,0:T(8,128)(2,1)S(1)}, u32[]{:S(2)}, u32[]{:S(2)}) collective-permute-start(bf16[16,2176]{1,0:T(8,128)(2,1)S(1)} %get-tuple-element.17), channel_id=1, source_target_pairs={{0,8},{1,9},{2,10},{3,11},{4,12},{5,13},{6,14},{7,15},{8,0},{9,1},... | collective-permute-start | bytes 208904 | tf_op jit(solution)/shard_map/ppermute | solution.py:38
  6.3 1.6 %collective-permute-start = (bf16[16,2176]{1,0:T(8,128)(2,1)S(1)}, bf16[16,2176]{1,0:T(8,128)(2,1)S(1)}, u32[]{:S(2)}, u32[]{:S(2)}) collective-permute-start(bf16[16,2176]{1,0:T(8,128)(2,1)S(1)} %get-tuple-element.17), channel_id=1, source_target_pairs={{0,4},{1,5},{2,6},{3,7},{4,0},{5,1},{6,2},{7,3},{8,12},{9,13},{10,... | collective-permute-start | bytes 208904 | tf_op jit(solution)/shard_map/ppermute | solution.py:38
  7.9 0.0 collective-permute-start.2
  7.9 1.6 %collective-permute-done.1 = bf16[16,2176]{1,0:T(8,128)(2,1)S(1)} collective-permute-done((bf16[16,2176]{1,0:T(8,128)(2,1)S(1)}, bf16[16,2176]{1,0:T(8,128)(2,1)S(1)}, u32[]{:S(2)}, u32[]{:S(2)}) %collective-permute-start.1) | collective-permute-done | bytes 69664 | tf_op jit(solution)/shard_map/ppermute | solution.py:38
  9.5 1.1 %collective-permute-done = bf16[16,2176]{1,0:T(8,128)(2,1)S(1)} collective-permute-done((bf16[16,2176]{1,0:T(8,128)(2,1)S(1)}, bf16[16,2176]{1,0:T(8,128)(2,1)S(1)}, u32[]{:S(2)}, u32[]{:S(2)}) %collective-permute-start) | collective-permute-done | bytes 69664 | tf_op jit(solution)/shard_map/ppermute | solution.py:38
  10.6 3.4 %collective-permute-done.2 = bf16[16,2176]{1,0:T(8,128)(2,1)S(1)} collective-permute-done((bf16[16,2176]{1,0:T(8,128)(2,1)S(1)}, bf16[16,2176]{1,0:T(8,128)(2,1)S(1)}, u32[]{:S(2)}, u32[]{:S(2)}) %collective-permute-start.2) | collective-permute-done | bytes 69664 | tf_op jit(solution)/shard_map/ppermute | solution.py:38
  14.0 0.1 fusion.28
  14.1 1.6 %collective-permute-start.3 = (bf16[4,16,2176]{2,1,0:T(8,128)(2,1)S(1)}, bf16[4,16,2176]{2,1,0:T(8,128)(2,1)S(1)}, u32[]{:S(2)}, u32[]{:S(2)}) collective-permute-start(bf16[4,16,2176]{2,1,0:T(8,128)(2,1)S(1)} %get-tuple-element.12), channel_id=1, source_target_pairs={{0,2},{1,3},{2,0},{3,1},{4,6},{5,7},{6,4},{7,5},{8,10},{9,11},{10,... | collective-permute-start | bytes 835592 | tf_op jit(solution)/shard_map/ppermute | solution.py:38
  15.6 5.3 %collective-permute-done.3 = bf16[4,16,2176]{2,1,0:T(8,128)(2,1)S(1)} collective-permute-done((bf16[4,16,2176]{2,1,0:T(8,128)(2,1)S(1)}, bf16[4,16,2176]{2,1,0:T(8,128)(2,1)S(1)}, u32[]{:S(2)}, u32[]{:S(2)}) %collective-permute-start.3) | collective-permute-done | bytes 278560 | tf_op jit(solution)/shard_map/ppermute | solution.py:38
  20.9 0.1 fusion.27
  21.0 0.1 collective-permute-start.4
  21.1 0.0 copy-done
  21.1 0.7 %multiply_reduce_fusion = f32[768]{0:T(1024)S(1)} fusion(bf16[768,2048]{1,0:T(8,128)(2,1)S(1)} %copy-done), kind=kLoop, calls=%fused_computation | loop fusion | flops 4717824 | bytes 3148800 | tf_op jit(solution)/shard_map/reduce_sum | solution.py:102
  21.8 1.3 %collective-permute-done.4 = bf16[2,4,16,2176]{3,2,1,0:T(8,128)(2,1)S(1)} collective-permute-done((bf16[2,4,16,2176]{3,2,1,0:T(8,128)(2,1)S(1)}, bf16[2,4,16,2176]{3,2,1,0:T(8,128)(2,1)S(1)}, u32[]{:S(2)}, u32[]{:S(2)}) %collective-permute-start.4) | collective-permute-done | bytes 557088 | tf_op jit(solution)/shard_map/ppermute | solution.py:38
  23.0 0.1 pad_maximum_fusion
  23.1 0.3 multiply_reduce_fusion.1
  23.4 1.1 %slice.74 = bf16[16,16,2048]{2,1,0:T(8,128)(2,1)} slice(bf16[16,16,2176]{2,1,0:T(8,128)(2,1)S(1)} %bitcast.51), slice={[0:16], [0:16], [0:2048]} | slice | bytes 2097152 | tf_op jit(solution)/shard_map/slice | solution.py:93
  24.5 0.1 add.47
  24.7 0.6 %slice_multiply_fusion = (f32[256]{0:T(256)S(1)}, f32[256]{0:T(256)}) fusion(f32[512]{0:T(512)S(1)} %fusion.13), kind=kLoop, calls=%fused_computation.55 | loop fusion | flops 1280 | bytes 4096 | tf_op jit(solution)/shard_map/div | solution.py:99
  25.3 0.0 copy-start.1
  25.3 3.3 %fusion.25 = (f32[256]{0:T(256)S(1)}, f32[256,768]{1,0:T(8,128)}) fusion(f32[768]{0:T(1024)S(1)} %multiply_reduce_fusion, f32[256]{0:T(256)S(1)} %add.47, bf16[256,2048]{1,0:T(8,128)(2,1)} %bitcast.52, bf16[768,2048]{1,0:T(8,128)(2,1)S(1)} %copy-done), kind=kOutput, calls=%fused_computation.57 | convolution fusion | flops 806485760 | bytes 4985856 | tf_op jit(solution)/shard_map/dot_general | solution.py:26
  28.6 0.1 reshape.40
  28.7 0.0 copy-done.1
  28.7 1.6 %fusion.6 = f32[256,256]{1,0:T(8,128)S(1)} fusion(bf16[768,256]{1,0:T(8,128)(2,1)S(1)} %copy-done.1, f32[256]{0:T(256)} %get-tuple-element.19, f32[256]{0:T(256)S(1)} %get-tuple-element.18, f32[256,768]{1,0:T(8,128)} %get-tuple-element.24, f32[768]{0:T(1024)S(1)} %multiply_reduce_fusion, f32[256]{0:T(256)S(1)} %add.47), kind=kOutput, calls=%fused_computation.14 | convolution fusion | flops 102629376 | bytes 1447936 | tf_op jit(solution)/shard_map/dot_general | solution.py:31
  30.3 0.2 collective-permute-start.5
  30.6 1.3 %collective-permute-done.5 = f32[2,4,24,256]{3,2,1,0:T(8,128)S(1)} collective-permute-done((f32[2,4,24,256]{3,2,1,0:T(8,128)S(1)}, f32[2,4,24,256]{3,2,1,0:T(8,128)S(1)}, u32[]{:S(2)}, u32[]{:S(2)}) %collective-permute-start.5) | collective-permute-done | bytes 196640 | tf_op jit(solution)/shard_map/ppermute | solution.py:38
  31.9 1.6 %collective-permute-start.6 = (f32[4,24,256]{2,1,0:T(8,128)S(1)}, f32[4,24,256]{2,1,0:T(8,128)S(1)}, u32[]{:S(2)}, u32[]{:S(2)}) collective-permute-start(f32[4,24,256]{2,1,0:T(8,128)S(1)} %slice_bitcast_fusion), channel_id=1, source_target_pairs={{0,2},{1,3},{2,0},{3,1},{4,6},{5,7},{6,4},{7,5},{8,10},{9,11},{10,... | collective-permute-start | bytes 294920 | tf_op jit(solution)/shard_map/ppermute | solution.py:38
  33.5 3.3 %collective-permute-done.6 = f32[4,24,256]{2,1,0:T(8,128)S(1)} collective-permute-done((f32[4,24,256]{2,1,0:T(8,128)S(1)}, f32[4,24,256]{2,1,0:T(8,128)S(1)}, u32[]{:S(2)}, u32[]{:S(2)}) %collective-permute-start.6) | collective-permute-done | bytes 98336 | tf_op jit(solution)/shard_map/ppermute | solution.py:38
  36.8 1.1 %collective-permute-start.7 = (f32[24,256]{1,0:T(8,128)S(1)}, f32[24,256]{1,0:T(8,128)S(1)}, u32[]{:S(2)}, u32[]{:S(2)}) collective-permute-start(f32[24,256]{1,0:T(8,128)S(1)} %get-tuple-element.13), channel_id=1, source_target_pairs={{0,4},{1,5},{2,6},{3,7},{4,0},{5,1},{6,2},{7,3},{8,12},{9,13},{10,... | collective-permute-start | bytes 73736 | tf_op jit(solution)/shard_map/ppermute | solution.py:38
  38.0 3.5 %collective-permute-start.9 = (f32[24,256]{1,0:T(8,128)S(1)}, f32[24,256]{1,0:T(8,128)S(1)}, u32[]{:S(2)}, u32[]{:S(2)}) collective-permute-start(f32[24,256]{1,0:T(8,128)S(1)} %get-tuple-element.14), channel_id=1, source_target_pairs={{0,12},{1,13},{2,14},{3,15},{4,8},{5,9},{6,10},{7,11},{8,4},{9,5},... | collective-permute-start | bytes 73736 | tf_op jit(solution)/shard_map/ppermute | solution.py:38
  41.5 0.0 collective-permute-start.8
  41.5 0.0 collective-permute-done.7
  41.5 2.1 %collective-permute-done.9 = f32[24,256]{1,0:T(8,128)S(1)} collective-permute-done((f32[24,256]{1,0:T(8,128)S(1)}, f32[24,256]{1,0:T(8,128)S(1)}, u32[]{:S(2)}, u32[]{:S(2)}) %collective-permute-start.9) | collective-permute-done | bytes 24608 | tf_op jit(solution)/shard_map/ppermute | solution.py:38
  43.6 2.6 %collective-permute-done.8 = f32[24,256]{1,0:T(8,128)S(1)} collective-permute-done((f32[24,256]{1,0:T(8,128)S(1)}, f32[24,256]{1,0:T(8,128)S(1)}, u32[]{:S(2)}, u32[]{:S(2)}) %collective-permute-start.8) | collective-permute-done | bytes 24608 | tf_op jit(solution)/shard_map/ppermute | solution.py:38
  46.3 0.7 %slice_divide_fusion = f32[16,256]{1,0:T(8,128)} fusion(f32[24,256]{1,0:T(8,128)S(1)} %fusion.16, f32[16]{0:T(128)S(1)} %slice.89), kind=kLoop, calls=%fused_computation.39 | loop fusion | flops 4096 | bytes 32832 | tf_op jit(solution)/shard_map/div | solution.py:114
  (16 shorter events, 0.3 us)
Async XLA Ops:
  0.0 21.1 %copy-start = (bf16[768,2048]{1,0:T(8,128)(2,1)S(1)}, bf16[768,2048]{1,0:T(8,128)(2,1)}, u32[]{:S(2)}) copy-start(bf16[768,2048]{1,0:T(8,128)(2,1)} %param.4) | copy-start | bytes 9437188
  2.2 7.3 %collective-permute-start.1 = (bf16[16,2176]{1,0:T(8,128)(2,1)S(1)}, bf16[16,2176]{1,0:T(8,128)(2,1)S(1)}, u32[]{:S(2)}, u32[]{:S(2)}) collective-permute-start(bf16[16,2176]{1,0:T(8,128)(2,1)S(1)} %get-tuple-element.17), channel_id=1, source_target_pairs={{0,8},{1,9},{2,10},{3,11},{4,12},{5,13},{6,14},{7,15},{8,0},{9,1},... | collective-permute-start | bytes 208904 | tf_op jit(solution)/shard_map/ppermute | solution.py:38
  6.3 4.3 %collective-permute-start = (bf16[16,2176]{1,0:T(8,128)(2,1)S(1)}, bf16[16,2176]{1,0:T(8,128)(2,1)S(1)}, u32[]{:S(2)}, u32[]{:S(2)}) collective-permute-start(bf16[16,2176]{1,0:T(8,128)(2,1)S(1)} %get-tuple-element.17), channel_id=1, source_target_pairs={{0,4},{1,5},{2,6},{3,7},{4,0},{5,1},{6,2},{7,3},{8,12},{9,13},{10,... | collective-permute-start | bytes 208904 | tf_op jit(solution)/shard_map/ppermute | solution.py:38
  7.9 6.1 %collective-permute-start.2 = (bf16[16,2176]{1,0:T(8,128)(2,1)S(1)}, bf16[16,2176]{1,0:T(8,128)(2,1)S(1)}, u32[]{:S(2)}, u32[]{:S(2)}) collective-permute-start(bf16[16,2176]{1,0:T(8,128)(2,1)S(1)} %get-tuple-element.17), channel_id=1, source_target_pairs={{0,12},{1,13},{2,14},{3,15},{4,8},{5,9},{6,10},{7,11},{8,4},{9,5},... | collective-permute-start | bytes 208904 | tf_op jit(solution)/shard_map/ppermute | solution.py:38
  14.1 6.9 %collective-permute-start.3 = (bf16[4,16,2176]{2,1,0:T(8,128)(2,1)S(1)}, bf16[4,16,2176]{2,1,0:T(8,128)(2,1)S(1)}, u32[]{:S(2)}, u32[]{:S(2)}) collective-permute-start(bf16[4,16,2176]{2,1,0:T(8,128)(2,1)S(1)} %get-tuple-element.12), channel_id=1, source_target_pairs={{0,2},{1,3},{2,0},{3,1},{4,6},{5,7},{6,4},{7,5},{8,10},{9,11},{10,... | collective-permute-start | bytes 835592 | tf_op jit(solution)/shard_map/ppermute | solution.py:38
  21.0 2.0 %collective-permute-start.4 = (bf16[2,4,16,2176]{3,2,1,0:T(8,128)(2,1)S(1)}, bf16[2,4,16,2176]{3,2,1,0:T(8,128)(2,1)S(1)}, u32[]{:S(2)}, u32[]{:S(2)}) collective-permute-start(bf16[2,4,16,2176]{3,2,1,0:T(8,128)(2,1)S(1)} %get-tuple-element.8), channel_id=1, source_target_pairs={{0,1},{1,0},{2,3},{3,2},{4,5},{5,4},{6,7},{7,6},{8,9},{9,8},{10,11... | collective-permute-start | bytes 1671176 | tf_op jit(solution)/shard_map/ppermute | solution.py:38
  25.3 3.4 %copy-start.1 = (bf16[768,256]{1,0:T(8,128)(2,1)S(1)}, bf16[768,256]{1,0:T(8,128)(2,1)}, u32[]{:S(2)}) copy-start(bf16[768,256]{1,0:T(8,128)(2,1)} %param.5) | copy-start | bytes 1179652
  30.3 1.5 %collective-permute-start.5 = (f32[2,4,24,256]{3,2,1,0:T(8,128)S(1)}, f32[2,4,24,256]{3,2,1,0:T(8,128)S(1)}, u32[]{:S(2)}, u32[]{:S(2)}) collective-permute-start(f32[2,4,24,256]{3,2,1,0:T(8,128)S(1)} %bitcast.61), channel_id=1, source_target_pairs={{0,1},{1,0},{2,3},{3,2},{4,5},{5,4},{6,7},{7,6},{8,9},{9,8},{10,11... | collective-permute-start | bytes 589832 | tf_op jit(solution)/shard_map/ppermute | solution.py:38
  31.9 4.9 %collective-permute-start.6 = (f32[4,24,256]{2,1,0:T(8,128)S(1)}, f32[4,24,256]{2,1,0:T(8,128)S(1)}, u32[]{:S(2)}, u32[]{:S(2)}) collective-permute-start(f32[4,24,256]{2,1,0:T(8,128)S(1)} %slice_bitcast_fusion), channel_id=1, source_target_pairs={{0,2},{1,3},{2,0},{3,1},{4,6},{5,7},{6,4},{7,5},{8,10},{9,11},{10,... | collective-permute-start | bytes 294920 | tf_op jit(solution)/shard_map/ppermute | solution.py:38
  36.8 4.6 %collective-permute-start.7 = (f32[24,256]{1,0:T(8,128)S(1)}, f32[24,256]{1,0:T(8,128)S(1)}, u32[]{:S(2)}, u32[]{:S(2)}) collective-permute-start(f32[24,256]{1,0:T(8,128)S(1)} %get-tuple-element.13), channel_id=1, source_target_pairs={{0,4},{1,5},{2,6},{3,7},{4,0},{5,1},{6,2},{7,3},{8,12},{9,13},{10,... | collective-permute-start | bytes 73736 | tf_op jit(solution)/shard_map/ppermute | solution.py:38
  38.0 5.6 %collective-permute-start.9 = (f32[24,256]{1,0:T(8,128)S(1)}, f32[24,256]{1,0:T(8,128)S(1)}, u32[]{:S(2)}, u32[]{:S(2)}) collective-permute-start(f32[24,256]{1,0:T(8,128)S(1)} %get-tuple-element.14), channel_id=1, source_target_pairs={{0,12},{1,13},{2,14},{3,15},{4,8},{5,9},{6,10},{7,11},{8,4},{9,5},... | collective-permute-start | bytes 73736 | tf_op jit(solution)/shard_map/ppermute | solution.py:38
  41.5 4.7 %collective-permute-start.8 = (f32[24,256]{1,0:T(8,128)S(1)}, f32[24,256]{1,0:T(8,128)S(1)}, u32[]{:S(2)}, u32[]{:S(2)}) collective-permute-start(f32[24,256]{1,0:T(8,128)S(1)} %get-tuple-element.15), channel_id=1, source_target_pairs={{0,8},{1,9},{2,10},{3,11},{4,12},{5,13},{6,14},{7,15},{8,0},{9,1},... | collective-permute-start | bytes 73736 | tf_op jit(solution)/shard_map/ppermute | solution.py:38

commit v6 on v4

--- a/solution.py
+++ b/solution.py
@@ -43,7 +43,7 @@
     while (1 << len(bits)) < count:
         bits.append(1 << len(bits))
     assert (1 << len(bits)) == count
-    return [bits[k:k + 2] for k in range(0, len(bits), 2)]
+    return [[bit] for bit in bits]
 
 
 def offsets(group):

time: 51.6 us -> 48.4 us (0.938)
  other arithmetic: 6.43 us -> 4.77 us
  waiting for transfers between devices: 24.2 us -> 23.1 us
    reduce_sum x1, other arithmetic: 2.57 us -> 0.68 us  [shards(): lib_sq = jnp.sum(jnp.square(library.astype(jnp.float32)), axis=1)]
    ppermute x12 -> x8, waiting for transfers between devices: 24.2 us -> 23.1 us  [swap(): return lax.ppermute(x, axis, [(i, i ^ mask) for i in range(count)])]
    ppermute x12 -> x8, starting transfers between devices: 14.1 us -> 13.9 us  [swap(): return lax.ppermute(x, axis, [(i, i ^ mask) for i in range(count)])]
    another operation x3 -> x5, other arithmetic: 1.07 us -> 1.11 us  [gather_rounds(): buf = jnp.stack(parts, axis=0)]
  transfers between devices with their start and end apart: 12 -> 8, of which waited for: 8 -> 8; matrix products, arithmetic and copies ran while one was open for 5% -> 1% of each run, Pallas kernels for 0% -> 0%
where the time goes in v6:
time: 48.4 us; the launch traced here: 48.3 us
  waiting for transfers between devices  23.1 us (48%)
  starting transfers between devices  13.9 us (29%)
  matrix products  4.89 us (10%)
  other arithmetic  4.77 us (10%)
  local copies, waits for them, and re-layouts  1.41 us (3%)
    ppermute x8, waiting for transfers between devices, swap(): return lax.ppermute(x, axis, [(i, i ^ mask) for i in range(count)])  23.1 us
    ppermute x8, starting transfers between devices, swap(): return lax.ppermute(x, axis, [(i, i ^ mask) for i in range(count)])  13.9 us
    dot_general x1, matrix products, weighted_sums(): lax.dot_general(block, library, (((1,), (1,)), ((), ())), preferred_eleme...  3.3 us
    dot_general x1, matrix products, weighted_sums(): jnp.dot(weight.astype(jnp.bfloat16), zvals, preferred_element_type=jnp.fl...  1.59 us
    reduce_sum x1, other arithmetic, shards(): jnp.sum(values, axis=0)  1.29 us
    another operation x5, other arithmetic, gather_rounds(): buf = jnp.stack(parts, axis=0)  1.11 us
    slice x1, local copies, waits for them, and re-layouts, shards(): everyone = got[:, :, :feat].reshape(nblk * q_dev, feat)  1.11 us
  transfers between devices with their start and end apart: 8, of which 8 were waited for; matrix products, arithmetic and copies ran while one was open for 1% of the time, Pallas kernels for 0%

profile of v6, /device:TPU:0, one launch (start us, length us, event | category | flops | bytes accessed | tf_op | source)
XLA Modules:
  0.0 48.3 jit_solution(3829038738554204573)
XLA Ops:
  0.0 0.0 copy-start
  0.0 1.3 %convert_reduce_fusion = (f32[256]{0:T(256)S(1)}, f32[256]{0:T(256)S(1)}) fusion(bf16[768,256]{1,0:T(8,128)(2,1)} %param.5), kind=kLoop, calls=%fused_computation.5 | loop fusion | flops 785920 | bytes 395264 | tf_op jit(solution)/shard_map/reduce_sum | solution.py:80
  1.3 0.9 %fusion.23 = (bf16[1,16,2176]{2,1,0:T(8,128)(2,1)S(1)}, bf16[16,2176]{1,0:T(8,128)(2,1)S(1)}) fusion(bf16[16,128]{1,0:T(8,128)(2,1)S(1)} %fusion.21, bf16[16,2048]{1,0:T(8,128)(2,1)} %param.3), kind=kLoop, calls=%fused_computation.56 | loop fusion | flops 139264 | bytes 208896 | tf_op jit(solution)/shard_map/stack | solution.py:60
  2.2 4.1 %collective-permute-start = (bf16[16,2176]{1,0:T(8,128)(2,1)S(1)}, bf16[16,2176]{1,0:T(8,128)(2,1)S(1)}, u32[]{:S(2)}, u32[]{:S(2)}) collective-permute-start(bf16[16,2176]{1,0:T(8,128)(2,1)S(1)} %get-tuple-element.16), channel_id=1, source_target_pairs={{0,8},{1,9},{2,10},{3,11},{4,12},{5,13},{6,14},{7,15},{8,0},{9,1},... | collective-permute-start | bytes 208904 | tf_op jit(solution)/shard_map/ppermute | solution.py:38
  6.3 3.8 %collective-permute-done = bf16[16,2176]{1,0:T(8,128)(2,1)S(1)} collective-permute-done((bf16[16,2176]{1,0:T(8,128)(2,1)S(1)}, bf16[16,2176]{1,0:T(8,128)(2,1)S(1)}, u32[]{:S(2)}, u32[]{:S(2)}) %collective-permute-start) | collective-permute-done | bytes 69664 | tf_op jit(solution)/shard_map/ppermute | solution.py:38
  10.1 0.7 %collective-permute-start.1 = (bf16[2,16,2176]{2,1,0:T(8,128)(2,1)S(1)}, bf16[2,16,2176]{2,1,0:T(8,128)(2,1)S(1)}, u32[]{:S(2)}, u32[]{:S(2)}) collective-permute-start(bf16[2,16,2176]{2,1,0:T(8,128)(2,1)S(1)} %get-tuple-element.14), channel_id=1, source_target_pairs={{0,4},{1,5},{2,6},{3,7},{4,0},{5,1},{6,2},{7,3},{8,12},{9,13},{10,... | collective-permute-start | bytes 417800 | tf_op jit(solution)/shard_map/ppermute | solution.py:38
  10.8 4.4 %collective-permute-done.1 = bf16[2,16,2176]{2,1,0:T(8,128)(2,1)S(1)} collective-permute-done((bf16[2,16,2176]{2,1,0:T(8,128)(2,1)S(1)}, bf16[2,16,2176]{2,1,0:T(8,128)(2,1)S(1)}, u32[]{:S(2)}, u32[]{:S(2)}) %collective-permute-start.1) | collective-permute-done | bytes 139296 | tf_op jit(solution)/shard_map/ppermute | solution.py:38
  15.3 1.8 %collective-permute-start.2 = (bf16[2,2,16,2176]{3,2,1,0:T(8,128)(2,1)S(1)}, bf16[2,2,16,2176]{3,2,1,0:T(8,128)(2,1)S(1)}, u32[]{:S(2)}, u32[]{:S(2)}) collective-permute-start(bf16[2,2,16,2176]{3,2,1,0:T(8,128)(2,1)S(1)} %get-tuple-element.12), channel_id=1, source_target_pairs={{0,2},{1,3},{2,0},{3,1},{4,6},{5,7},{6,4},{7,5},{8,10},{9,11},{10,... | collective-permute-start | bytes 835592 | tf_op jit(solution)/shard_map/ppermute | solution.py:38
  17.1 4.8 %collective-permute-done.2 = bf16[2,2,16,2176]{3,2,1,0:T(8,128)(2,1)S(1)} collective-permute-done((bf16[2,2,16,2176]{3,2,1,0:T(8,128)(2,1)S(1)}, bf16[2,2,16,2176]{3,2,1,0:T(8,128)(2,1)S(1)}, u32[]{:S(2)}, u32[]{:S(2)}) %collective-permute-start.2) | collective-permute-done | bytes 278560 | tf_op jit(solution)/shard_map/ppermute | solution.py:38
  21.9 0.1 fusion.28
  22.0 0.1 collective-permute-start.3
  22.1 0.0 copy-done
  22.1 0.7 %multiply_reduce_fusion = f32[768]{0:T(1024)S(1)} fusion(bf16[768,2048]{1,0:T(8,128)(2,1)S(1)} %copy-done), kind=kLoop, calls=%fused_computation | loop fusion | flops 4717824 | bytes 3148800 | tf_op jit(solution)/shard_map/reduce_sum | solution.py:97
  22.8 1.3 %collective-permute-done.3 = bf16[2,2,2,16,2176]{4,3,2,1,0:T(8,128)(2,1)S(1)} collective-permute-done((bf16[2,2,2,16,2176]{4,3,2,1,0:T(8,128)(2,1)S(1)}, bf16[2,2,2,16,2176]{4,3,2,1,0:T(8,128)(2,1)S(1)}, u32[]{:S(2)}, u32[]{:S(2)}) %collective-permute-start.3) | collective-permute-done | bytes 557088 | tf_op jit(solution)/shard_map/ppermute | solution.py:38
  24.0 0.1 pad_maximum_fusion
  24.1 0.3 multiply_reduce_fusion.1
  24.4 1.1 %slice.74 = bf16[16,16,2048]{2,1,0:T(8,128)(2,1)} slice(bf16[16,16,2176]{2,1,0:T(8,128)(2,1)S(1)} %bitcast.50), slice={[0:16], [0:16], [0:2048]} | slice | bytes 2097152 | tf_op jit(solution)/shard_map/slice | solution.py:88
  25.5 0.1 add.44
  25.7 0.6 %slice_multiply_fusion = (f32[256]{0:T(256)S(1)}, f32[256]{0:T(256)}) fusion(f32[512]{0:T(512)S(1)} %fusion.14), kind=kLoop, calls=%fused_computation.55 | loop fusion | flops 1280 | bytes 4096 | tf_op jit(solution)/shard_map/div | solution.py:94
  26.3 0.0 copy-start.1
  26.3 3.3 %fusion.26 = (f32[256]{0:T(256)S(1)}, f32[256,768]{1,0:T(8,128)}) fusion(f32[768]{0:T(1024)S(1)} %multiply_reduce_fusion, f32[256]{0:T(256)S(1)} %add.44, bf16[256,2048]{1,0:T(8,128)(2,1)} %bitcast.51, bf16[768,2048]{1,0:T(8,128)(2,1)S(1)} %copy-done), kind=kOutput, calls=%fused_computation.59 | convolution fusion | flops 806485760 | bytes 4985856 | tf_op jit(solution)/shard_map/dot_general | solution.py:26
  29.6 0.1 reshape.40
  29.7 0.0 copy-done.1
  29.7 1.6 %fusion.6 = f32[256,256]{1,0:T(8,128)S(1)} fusion(bf16[768,256]{1,0:T(8,128)(2,1)S(1)} %copy-done.1, f32[256]{0:T(256)} %get-tuple-element.18, f32[256]{0:T(256)S(1)} %get-tuple-element.17, f32[256,768]{1,0:T(8,128)} %get-tuple-element.23, f32[768]{0:T(1024)S(1)} %multiply_reduce_fusion, f32[256]{0:T(256)S(1)} %add.44), kind=kOutput, calls=%fused_computation.14 | convolution fusion | flops 102629376 | bytes 1447936 | tf_op jit(solution)/shard_map/dot_general | solution.py:31
  31.4 0.2 collective-permute-start.4
  31.6 1.3 %collective-permute-done.4 = f32[2,2,2,24,256]{4,3,2,1,0:T(8,128)S(1)} collective-permute-done((f32[2,2,2,24,256]{4,3,2,1,0:T(8,128)S(1)}, f32[2,2,2,24,256]{4,3,2,1,0:T(8,128)S(1)}, u32[]{:S(2)}, u32[]{:S(2)}) %collective-permute-start.4) | collective-permute-done | bytes 196640 | tf_op jit(solution)/shard_map/ppermute | solution.py:38
  32.9 1.8 %collective-permute-start.5 = (f32[2,2,24,256]{3,2,1,0:T(8,128)S(1)}, f32[2,2,24,256]{3,2,1,0:T(8,128)S(1)}, u32[]{:S(2)}, u32[]{:S(2)}) collective-permute-start(f32[2,2,24,256]{3,2,1,0:T(8,128)S(1)} %slice_bitcast_fusion), channel_id=1, source_target_pairs={{0,2},{1,3},{2,0},{3,1},{4,6},{5,7},{6,4},{7,5},{8,10},{9,11},{10,... | collective-permute-start | bytes 294920 | tf_op jit(solution)/shard_map/ppermute | solution.py:38
  34.7 3.1 %collective-permute-done.5 = f32[2,2,24,256]{3,2,1,0:T(8,128)S(1)} collective-permute-done((f32[2,2,24,256]{3,2,1,0:T(8,128)S(1)}, f32[2,2,24,256]{3,2,1,0:T(8,128)S(1)}, u32[]{:S(2)}, u32[]{:S(2)}) %collective-permute-start.5) | collective-permute-done | bytes 98336 | tf_op jit(solution)/shard_map/ppermute | solution.py:38
  37.8 1.5 %collective-permute-start.6 = (f32[2,24,256]{2,1,0:T(8,128)S(1)}, f32[2,24,256]{2,1,0:T(8,128)S(1)}, u32[]{:S(2)}, u32[]{:S(2)}) collective-permute-start(f32[2,24,256]{2,1,0:T(8,128)S(1)} %slice_bitcast_fusion.2), channel_id=1, source_target_pairs={{0,4},{1,5},{2,6},{3,7},{4,0},{5,1},{6,2},{7,3},{8,12},{9,13},{10,... | collective-permute-start | bytes 147464 | tf_op jit(solution)/shard_map/ppermute | solution.py:38
  39.4 2.6 %collective-permute-done.6 = f32[2,24,256]{2,1,0:T(8,128)S(1)} collective-permute-done((f32[2,24,256]{2,1,0:T(8,128)S(1)}, f32[2,24,256]{2,1,0:T(8,128)S(1)}, u32[]{:S(2)}, u32[]{:S(2)}) %collective-permute-start.6) | collective-permute-done | bytes 49184 | tf_op jit(solution)/shard_map/ppermute | solution.py:38
  42.0 3.7 %collective-permute-start.7 = (f32[24,256]{1,0:T(8,128)S(1)}, f32[24,256]{1,0:T(8,128)S(1)}, u32[]{:S(2)}, u32[]{:S(2)}) collective-permute-start(f32[24,256]{1,0:T(8,128)S(1)} %slice_bitcast_fusion.4), channel_id=1, source_target_pairs={{0,8},{1,9},{2,10},{3,11},{4,12},{5,13},{6,14},{7,15},{8,0},{9,1},... | collective-permute-start | bytes 73736 | tf_op jit(solution)/shard_map/ppermute | solution.py:38
  45.8 1.8 %collective-permute-done.7 = f32[24,256]{1,0:T(8,128)S(1)} collective-permute-done((f32[24,256]{1,0:T(8,128)S(1)}, f32[24,256]{1,0:T(8,128)S(1)}, u32[]{:S(2)}, u32[]{:S(2)}) %collective-permute-start.7) | collective-permute-done | bytes 24608 | tf_op jit(solution)/shard_map/ppermute | solution.py:38
  47.6 0.7 %slice_divide_fusion = f32[16,256]{1,0:T(8,128)} fusion(f32[24,256]{1,0:T(8,128)S(1)} %fusion.15, f32[16]{0:T(128)S(1)} %slice.89), kind=kLoop, calls=%fused_computation.39 | loop fusion | flops 4096 | bytes 32832 | tf_op jit(solution)/shard_map/div | solution.py:109
  (20 shorter events, 0.4 us)
Async XLA Ops:
  0.0 22.1 %copy-start = (bf16[768,2048]{1,0:T(8,128)(2,1)S(1)}, bf16[768,2048]{1,0:T(8,128)(2,1)}, u32[]{:S(2)}) copy-start(bf16[768,2048]{1,0:T(8,128)(2,1)} %param.4) | copy-start | bytes 9437188
  2.2 7.9 %collective-permute-start = (bf16[16,2176]{1,0:T(8,128)(2,1)S(1)}, bf16[16,2176]{1,0:T(8,128)(2,1)S(1)}, u32[]{:S(2)}, u32[]{:S(2)}) collective-permute-start(bf16[16,2176]{1,0:T(8,128)(2,1)S(1)} %get-tuple-element.16), channel_id=1, source_target_pairs={{0,8},{1,9},{2,10},{3,11},{4,12},{5,13},{6,14},{7,15},{8,0},{9,1},... | collective-permute-start | bytes 208904 | tf_op jit(solution)/shard_map/ppermute | solution.py:38
  10.1 5.1 %collective-permute-start.1 = (bf16[2,16,2176]{2,1,0:T(8,128)(2,1)S(1)}, bf16[2,16,2176]{2,1,0:T(8,128)(2,1)S(1)}, u32[]{:S(2)}, u32[]{:S(2)}) collective-permute-start(bf16[2,16,2176]{2,1,0:T(8,128)(2,1)S(1)} %get-tuple-element.14), channel_id=1, source_target_pairs={{0,4},{1,5},{2,6},{3,7},{4,0},{5,1},{6,2},{7,3},{8,12},{9,13},{10,... | collective-permute-start | bytes 417800 | tf_op jit(solution)/shard_map/ppermute | solution.py:38
  15.3 6.6 %collective-permute-start.2 = (bf16[2,2,16,2176]{3,2,1,0:T(8,128)(2,1)S(1)}, bf16[2,2,16,2176]{3,2,1,0:T(8,128)(2,1)S(1)}, u32[]{:S(2)}, u32[]{:S(2)}) collective-permute-start(bf16[2,2,16,2176]{3,2,1,0:T(8,128)(2,1)S(1)} %get-tuple-element.12), channel_id=1, source_target_pairs={{0,2},{1,3},{2,0},{3,1},{4,6},{5,7},{6,4},{7,5},{8,10},{9,11},{10,... | collective-permute-start | bytes 835592 | tf_op jit(solution)/shard_map/ppermute | solution.py:38
  22.0 2.0 %collective-permute-start.3 = (bf16[2,2,2,16,2176]{4,3,2,1,0:T(8,128)(2,1)S(1)}, bf16[2,2,2,16,2176]{4,3,2,1,0:T(8,128)(2,1)S(1)}, u32[]{:S(2)}, u32[]{:S(2)}) collective-permute-start(bf16[2,2,2,16,2176]{4,3,2,1,0:T(8,128)(2,1)S(1)} %get-tuple-element.8), channel_id=1, source_target_pairs={{0,1},{1,0},{2,3},{3,2},{4,5},{5,4},{6,7},{7,6},{8,9},{9,8},{10,11... | collective-permute-start | bytes 1671176 | tf_op jit(solution)/shard_map/ppermute | solution.py:38
  26.3 3.5 %copy-start.1 = (bf16[768,256]{1,0:T(8,128)(2,1)S(1)}, bf16[768,256]{1,0:T(8,128)(2,1)}, u32[]{:S(2)}) copy-start(bf16[768,256]{1,0:T(8,128)(2,1)} %param.5) | copy-start | bytes 1179652
  31.4 1.5 %collective-permute-start.4 = (f32[2,2,2,24,256]{4,3,2,1,0:T(8,128)S(1)}, f32[2,2,2,24,256]{4,3,2,1,0:T(8,128)S(1)}, u32[]{:S(2)}, u32[]{:S(2)}) collective-permute-start(f32[2,2,2,24,256]{4,3,2,1,0:T(8,128)S(1)} %bitcast.60), channel_id=1, source_target_pairs={{0,1},{1,0},{2,3},{3,2},{4,5},{5,4},{6,7},{7,6},{8,9},{9,8},{10,11... | collective-permute-start | bytes 589832 | tf_op jit(solution)/shard_map/ppermute | solution.py:38
  32.9 4.9 %collective-permute-start.5 = (f32[2,2,24,256]{3,2,1,0:T(8,128)S(1)}, f32[2,2,24,256]{3,2,1,0:T(8,128)S(1)}, u32[]{:S(2)}, u32[]{:S(2)}) collective-permute-start(f32[2,2,24,256]{3,2,1,0:T(8,128)S(1)} %slice_bitcast_fusion), channel_id=1, source_target_pairs={{0,2},{1,3},{2,0},{3,1},{4,6},{5,7},{6,4},{7,5},{8,10},{9,11},{10,... | collective-permute-start | bytes 294920 | tf_op jit(solution)/shard_map/ppermute | solution.py:38
  37.8 4.2 %collective-permute-start.6 = (f32[2,24,256]{2,1,0:T(8,128)S(1)}, f32[2,24,256]{2,1,0:T(8,128)S(1)}, u32[]{:S(2)}, u32[]{:S(2)}) collective-permute-start(f32[2,24,256]{2,1,0:T(8,128)S(1)} %slice_bitcast_fusion.2), channel_id=1, source_target_pairs={{0,4},{1,5},{2,6},{3,7},{4,0},{5,1},{6,2},{7,3},{8,12},{9,13},{10,... | collective-permute-start | bytes 147464 | tf_op jit(solution)/shard_map/ppermute | solution.py:38
  42.0 5.5 %collective-permute-start.7 = (f32[24,256]{1,0:T(8,128)S(1)}, f32[24,256]{1,0:T(8,128)S(1)}, u32[]{:S(2)}, u32[]{:S(2)}) collective-permute-start(f32[24,256]{1,0:T(8,128)S(1)} %slice_bitcast_fusion.4), channel_id=1, source_target_pairs={{0,8},{1,9},{2,10},{3,11},{4,12},{5,13},{6,14},{7,15},{8,0},{9,1},... | collective-permute-start | bytes 73736 | tf_op jit(solution)/shard_map/ppermute | solution.py:38

commit v7 on v5

--- a/solution.py
+++ b/solution.py
@@ -20,17 +20,16 @@
     return (parts[..., :n] + parts[..., n:2 * n]) + parts[..., 2 * n:3 * n]
 
 
-def weighted_sums(block, library, lib_sq, zvals):
-    blockf = block.astype(jnp.float32)
+def piece_weights(piece, lib_ext, lib_sq, feat):
+    rows = piece.reshape(-1, piece.shape[-1])
+    blockf = rows[:, :feat].astype(jnp.float32)
     q_sq = jnp.sum(blockf * blockf, axis=1)
     inner = lax.dot_general(
-        block, library, (((1,), (1,)), ((), ())), preferred_element_type=jnp.float32
+        rows, lib_ext, (((1,), (1,)), ((), ())), preferred_element_type=jnp.float32
     )
     tanimoto = inner / (q_sq[:, None] + lib_sq[None, :] - inner)
     weight = jnp.exp((tanimoto - 1.0) / TAU)
-    numer = jnp.dot(weight.astype(jnp.bfloat16), zvals, preferred_element_type=jnp.float32)
-    denom = jnp.sum(weight, axis=1)
-    return (numer, denom)
+    return weight.astype(jnp.bfloat16), jnp.sum(weight, axis=1)
 
 
 def swap(x, axis, mask):
@@ -58,12 +57,16 @@
     return masks
 
 
-def gather_rounds(packet, axis, groups):
-    buf = packet
+def gather_rounds(packet, axis, groups, work):
+    pieces = [packet[None]]
+    results = [work(pieces[0])]
     for group in reversed(groups):
-        parts = [buf] + [swap(buf, axis, m) for m in offsets(group)[1:]]
-        buf = jnp.stack(parts, axis=0)
-    return buf
+        buf = jnp.concatenate(pieces, axis=0) if len(pieces) > 1 else pieces[0]
+        for m in offsets(group)[1:]:
+            got = swap(buf, axis, m)
+            pieces.append(got)
+            results.append(work(got))
+    return jnp.concatenate(pieces, axis=0), results
 
 
 def scatter_rounds(buf, axis, groups):
@@ -89,8 +92,11 @@
     lanes += -lanes % 128
     coded = jnp.pad(coded, (0, q_dev * lanes - coded.shape[0])).reshape(q_dev, lanes)
     packet = jnp.concatenate([queries, coded], axis=1)
-    got = gather_rounds(packet, "blk", groups).reshape(nblk, q_dev, feat + lanes)
-    everyone = got[:, :, :feat].reshape(nblk * q_dev, feat)
+    lib_ext = jnp.pad(library, ((0, 0), (0, lanes)))
+    lib_sq = jnp.sum(jnp.square(library.astype(jnp.float32)), axis=1)
+    got, parts = gather_rounds(
+        packet, "blk", groups, lambda piece: piece_weights(piece, lib_ext, lib_sq, feat)
+    )
     stats = join3(got[:, :, feat:].reshape(nblk, q_dev * lanes), 2 * width)
     stats = jnp.sum(stats, axis=0)
 
@@ -99,9 +105,10 @@
     mean = col_sum / total
     spread = col_sq / total - mean * mean
     zvals = ((values - mean) * lax.rsqrt(spread + EPS)).astype(jnp.bfloat16)
-    lib_sq = jnp.sum(jnp.square(library.astype(jnp.float32)), axis=1)
 
-    numer, denom = weighted_sums(everyone, library, lib_sq, zvals)
+    weight_b = jnp.concatenate([p[0] for p in parts], axis=0)
+    denom = jnp.concatenate([p[1] for p in parts], axis=0)
+    numer = jnp.dot(weight_b, zvals, preferred_element_type=jnp.float32)
     den_rows = -(-q_dev // width)
     den_rows += -(q_dev + den_rows) % 8
     den = jnp.pad(denom.reshape(nblk, q_dev), ((0, 0), (0, den_rows * width - q_dev)))

time: 47.1 us -> 43 us (0.913)
  waiting for transfers between devices: 22 us -> 13.2 us
  other arithmetic: 4.75 us -> 8.14 us
  matrix products: 4.88 us -> 7.13 us
  local copies, waits for them, and re-layouts: 1.39 us -> 0.51 us
    ppermute x10, waiting for transfers between devices: 22 us -> 13.2 us  [swap(): return lax.ppermute(x, axis, [(i, i ^ mask) for i in range(count)])]
    dot_general x2 -> x7, matrix products: 4.88 us -> 7.13 us  [the longest x6 6.83 us: piece_weights(): lax.dot_general(rows, lib_ext, (((1,), (1,)), ((), ())), preferred_elemen...]
    reduce_sum x1, other arithmetic: 0.68 us -> 2.57 us  [shards(): lib_sq = jnp.sum(jnp.square(library.astype(jnp.float32)), axis=1)]
    reduce_sum x1 -> x6, other arithmetic: 0.26 us -> 1.7 us  [piece_weights(): q_sq = jnp.sum(blockf * blockf, axis=1)]
    another operation x5 -> x1, other arithmetic: 1.12 us -> 0.02 us  [the longest x4 1.1 us: gather_rounds(): buf = jnp.stack(parts, axis=0)]
    slice x1 -> x0, local copies, waits for them, and re-layouts: 1.1 us -> none  [shards(): everyone = got[:, :, :feat].reshape(nblk * q_dev, feat)]
    unnamed x0 -> x1, other arithmetic: none -> 0.85 us
    broadcast_in_dim x0 -> x1, other arithmetic: none -> 0.85 us  [gather_rounds(): pieces = [packet[None]]]
  transfers between devices with their start and end apart: 10 -> 10, of which waited for: 9 -> 7; matrix products, arithmetic and copies ran while one was open for 1% -> 25% of each run, Pallas kernels for 0% -> 0%
where the time goes in v7:
time: 43 us; the launch traced here: 42.7 us
  starting transfers between devices  13.5 us (31%)
  waiting for transfers between devices  13.2 us (31%)
  other arithmetic  8.14 us (19%)
  matrix products  7.13 us (17%)
  local copies, waits for them, and re-layouts  0.51 us (1%)
    ppermute x10, starting transfers between devices, swap(): return lax.ppermute(x, axis, [(i, i ^ mask) for i in range(count)])  13.5 us
    ppermute x10, waiting for transfers between devices, swap(): return lax.ppermute(x, axis, [(i, i ^ mask) for i in range(count)])  13.2 us
    dot_general x6, matrix products, piece_weights(): lax.dot_general(rows, lib_ext, (((1,), (1,)), ((), ())), preferred_elemen...  6.83 us
    reduce_sum x1, other arithmetic, shards(): lib_sq = jnp.sum(jnp.square(library.astype(jnp.float32)), axis=1)  2.57 us
    reduce_sum x6, other arithmetic, piece_weights(): q_sq = jnp.sum(blockf * blockf, axis=1)  1.7 us
    reduce_sum x1, other arithmetic, shards(): jnp.sum(values, axis=0)  1.29 us
  transfers between devices with their start and end apart: 10, of which 7 were waited for; matrix products, arithmetic and copies ran while one was open for 25% of the time, Pallas kernels for 0%

profile of v7, /device:TPU:0, one launch (start us, length us, event | category | flops | bytes accessed | tf_op | source)
XLA Modules:
  0.0 42.7 jit_solution(6882680705434179644)
XLA Ops:
  0.0 0.0 copy-start.1
  0.0 0.0 copy-start
  0.0 1.3 %convert_reduce_fusion = (f32[256]{0:T(256)S(1)}, f32[256]{0:T(256)S(1)}) fusion(bf16[768,256]{1,0:T(8,128)(2,1)} %param.5), kind=kLoop, calls=%fused_computation.15 | loop fusion | flops 785920 | bytes 395264 | tf_op jit(solution)/shard_map/reduce_sum | solution.py:88
  1.3 0.8 %fusion.87 = bf16[1,16,2176]{2,1,0:T(8,128)(2,1)S(1)} fusion(bf16[16,128]{1,0:T(8,128)(2,1)S(1)} %fusion.97, bf16[16,2048]{1,0:T(8,128)(2,1)} %param.3), kind=kLoop, calls=%fused_computation.65 | loop fusion | flops 139264 | bytes 139264 | tf_op jit(solution)/shard_map/broadcast_in_dim | solution.py:61
  2.2 3.1 %collective-permute-start = (bf16[1,16,2176]{2,1,0:T(8,128)(2,1)S(1)}, bf16[1,16,2176]{2,1,0:T(8,128)(2,1)S(1)}, u32[]{:S(2)}, u32[]{:S(2)}) collective-permute-start(bf16[1,16,2176]{2,1,0:T(8,128)(2,1)S(1)} %fusion.87), channel_id=1, source_target_pairs={{0,4},{1,5},{2,6},{3,7},{4,0},{5,1},{6,2},{7,3},{8,12},{9,13},{10,... | collective-permute-start | bytes 208904 | tf_op jit(solution)/shard_map/ppermute | solution.py:37
  5.2 2.6 %collective-permute-start.1 = (bf16[1,16,2176]{2,1,0:T(8,128)(2,1)S(1)}, bf16[1,16,2176]{2,1,0:T(8,128)(2,1)S(1)}, u32[]{:S(2)}, u32[]{:S(2)}) collective-permute-start(bf16[1,16,2176]{2,1,0:T(8,128)(2,1)S(1)} %fusion.87), channel_id=1, source_target_pairs={{0,8},{1,9},{2,10},{3,11},{4,12},{5,13},{6,14},{7,15},{8,0},{9,1},... | collective-permute-start | bytes 208904 | tf_op jit(solution)/shard_map/ppermute | solution.py:37
  7.8 0.0 collective-permute-start.2
  7.8 0.8 %constant_dynamic-update-slice_fusion.14 = (bf16[16,16,2176]{2,1,0:T(8,128)(2,1)S(1)}, bf16[8,16,2176]{2,1,0:T(8,128)(2,1)S(1)}) fusion(bf16[16,128]{1,0:T(8,128)(2,1)S(1)} %fusion.97, bf16[16,2048]{1,0:T(8,128)(2,1)} %param.3), kind=kLoop, calls=%fused_computation.80 | loop fusion | flops 139262 | bytes 208896
  8.7 1.0 %multiply_reduce_fusion.6 = f32[16]{0:T(128)S(1)} fusion(bf16[16,2048]{1,0:T(8,128)(2,1)} %param.3), kind=kLoop, calls=%fused_computation.42 | loop fusion | flops 98288 | bytes 65600 | tf_op jit(solution)/shard_map/reduce_sum | solution.py:26
  9.6 2.6 %multiply_reduce_fusion = f32[768]{0:T(1024)S(1)} fusion(bf16[768,2048]{1,0:T(8,128)(2,1)} %param.4), kind=kLoop, calls=%fused_computation | loop fusion | flops 4717824 | bytes 3148800 | tf_op jit(solution)/shard_map/reduce_sum | solution.py:96
  12.2 0.0 copy-done.1
  12.2 0.0 copy-done
  12.2 1.1 %fusion.109 = (f32[16]{0:T(128)S(1)}, bf16[16,768]{1,0:T(8,128)(2,1)S(1)}) fusion(f32[768]{0:T(1024)S(1)} %multiply_reduce_fusion, f32[16]{0:T(128)S(1)} %multiply_reduce_fusion.6, bf16[768,2048]{1,0:T(8,128)(2,1)S(1)} %copy-done, bf16[16,128]{1,0:T(8,128)(2,1)S(1)} %fusion.97, bf16[16,2048]{1,0:T(8,128)(2,1)S(1)} %copy-done.1), kind=kOutput, calls=%fused_computation.118 | convolution fusion | flops 53702640 | bytes 3243136 | tf_op jit(solution)/shard_map/dot_general | solution.py:27
  13.3 0.0 collective-permute-done
  13.3 0.0 collective-permute-done.1
  13.3 0.7 %collective-permute-done.2 = bf16[1,16,2176]{2,1,0:T(8,128)(2,1)S(1)} collective-permute-done((bf16[1,16,2176]{2,1,0:T(8,128)(2,1)S(1)}, bf16[1,16,2176]{2,1,0:T(8,128)(2,1)S(1)}, u32[]{:S(2)}, u32[]{:S(2)}) %collective-permute-start.2) | collective-permute-done | bytes 69664 | tf_op jit(solution)/shard_map/ppermute | solution.py:37
  14.1 1.6 %collective-permute-start.3 = (bf16[4,16,2176]{2,1,0:T(8,128)(2,1)S(1)}, bf16[4,16,2176]{2,1,0:T(8,128)(2,1)S(1)}, u32[]{:S(2)}, u32[]{:S(2)}) collective-permute-start(bf16[4,16,2176]{2,1,0:T(8,128)(2,1)S(1)} %pad_maximum_fusion), channel_id=1, source_target_pairs={{0,2},{1,3},{2,0},{3,1},{4,6},{5,7},{6,4},{7,5},{8,10},{9,11},{10,... | collective-permute-start | bytes 835592 | tf_op jit(solution)/shard_map/ppermute | solution.py:37
  15.7 0.1 multiply_reduce_fusion.5
  15.8 0.1 multiply_reduce_fusion.4
  15.9 0.1 multiply_reduce_fusion.3
  16.1 1.1 %fusion.110 = (f32[16]{0:T(128)S(1)}, bf16[16,768]{1,0:T(8,128)(2,1)S(1)}) fusion(f32[768]{0:T(1024)S(1)} %multiply_reduce_fusion, f32[16]{0:T(128)S(1)} %multiply_reduce_fusion.5, bf16[768,2048]{1,0:T(8,128)(2,1)S(1)} %copy-done, bf16[1,16,2176]{2,1,0:T(8,128)(2,1)S(1)} %collective-permute-done), kind=kOutput, calls=%fused_computation.119 | convolution fusion | flops 53563376 | bytes 3243136 | tf_op jit(solution)/shard_map/dot_general | solution.py:27
  17.1 1.1 %fusion.111 = (f32[16]{0:T(128)S(1)}, bf16[16,768]{1,0:T(8,128)(2,1)S(1)}) fusion(f32[768]{0:T(1024)S(1)} %multiply_reduce_fusion, f32[16]{0:T(128)S(1)} %multiply_reduce_fusion.4, bf16[768,2048]{1,0:T(8,128)(2,1)S(1)} %copy-done, bf16[1,16,2176]{2,1,0:T(8,128)(2,1)S(1)} %collective-permute-done.1), kind=kOutput, calls=%fused_computation.120 | convolution fusion | flops 53563376 | bytes 3243136 | tf_op jit(solution)/shard_map/dot_general | solution.py:27
  18.3 1.1 %fusion.112 = (f32[16]{0:T(128)S(1)}, bf16[16,768]{1,0:T(8,128)(2,1)S(1)}) fusion(f32[768]{0:T(1024)S(1)} %multiply_reduce_fusion, f32[16]{0:T(128)S(1)} %multiply_reduce_fusion.3, bf16[768,2048]{1,0:T(8,128)(2,1)S(1)} %copy-done, bf16[1,16,2176]{2,1,0:T(8,128)(2,1)S(1)} %collective-permute-done.2), kind=kOutput, calls=%fused_computation.121 | convolution fusion | flops 53563376 | bytes 3243136 | tf_op jit(solution)/shard_map/dot_general | solution.py:27
  19.3 2.0 %collective-permute-done.3 = bf16[4,16,2176]{2,1,0:T(8,128)(2,1)S(1)} collective-permute-done((bf16[4,16,2176]{2,1,0:T(8,128)(2,1)S(1)}, bf16[4,16,2176]{2,1,0:T(8,128)(2,1)S(1)}, u32[]{:S(2)}, u32[]{:S(2)}) %collective-permute-start.3) | collective-permute-done | bytes 278560 | tf_op jit(solution)/shard_map/ppermute | solution.py:37
  21.3 0.1 collective-permute-start.4
  21.4 0.2 multiply_reduce_fusion.2
  21.6 1.2 %fusion.113 = (f32[64]{0:T(128)S(1)}, bf16[64,768]{1,0:T(8,128)(2,1)S(1)}) fusion(f32[768]{0:T(1024)S(1)} %multiply_reduce_fusion, f32[64]{0:T(128)S(1)} %multiply_reduce_fusion.2, bf16[64,2176]{1,0:T(8,128)(2,1)S(1)} %bitcast.61, bf16[768,2048]{1,0:T(8,128)(2,1)S(1)} %copy-done), kind=kOutput, calls=%fused_computation.122 | convolution fusion | flops 214253504 | bytes 3526144 | tf_op jit(solution)/shard_map/dot_general | solution.py:27
  22.8 0.5 %collective-permute-done.4 = bf16[8,16,2176]{2,1,0:T(8,128)(2,1)S(1)} collective-permute-done((bf16[8,16,2176]{2,1,0:T(8,128)(2,1)S(1)}, bf16[8,16,2176]{2,1,0:T(8,128)(2,1)S(1)}, u32[]{:S(2)}, u32[]{:S(2)}) %collective-permute-start.4) | collective-permute-done | bytes 557088 | tf_op jit(solution)/shard_map/ppermute | solution.py:37
  23.4 0.1 constant_dynamic-update-slice_fusion.9
  23.5 0.2 multiply_reduce_fusion.1
  23.7 0.0 copy-start.2
  23.7 1.4 %fusion.114 = (f32[128]{0:T(128)S(1)}, bf16[128,768]{1,0:T(8,128)(2,1)S(1)}) fusion(f32[768]{0:T(1024)S(1)} %multiply_reduce_fusion, f32[128]{0:T(128)S(1)} %multiply_reduce_fusion.1, bf16[128,2176]{1,0:T(8,128)(2,1)S(1)} %bitcast.63, bf16[768,2048]{1,0:T(8,128)(2,1)S(1)} %copy-done), kind=kOutput, calls=%fused_computation.123 | convolution fusion | flops 428507008 | bytes 3903488 | tf_op jit(solution)/shard_map/dot_general | solution.py:27
  25.1 0.1 concatenate.35
  25.2 0.1 reshape.55
  25.4 0.0 copy-done.2
  25.4 0.3 fusion.26
  25.7 0.2 collective-permute-start.5
  25.9 1.3 %collective-permute-done.5 = f32[2,4,24,256]{3,2,1,0:T(8,128)S(1)} collective-permute-done((f32[2,4,24,256]{3,2,1,0:T(8,128)S(1)}, f32[2,4,24,256]{3,2,1,0:T(8,128)S(1)}, u32[]{:S(2)}, u32[]{:S(2)}) %collective-permute-start.5) | collective-permute-done | bytes 196640 | tf_op jit(solution)/shard_map/ppermute | solution.py:37
  27.3 1.6 %collective-permute-start.6 = (f32[4,24,256]{2,1,0:T(8,128)S(1)}, f32[4,24,256]{2,1,0:T(8,128)S(1)}, u32[]{:S(2)}, u32[]{:S(2)}) collective-permute-start(f32[4,24,256]{2,1,0:T(8,128)S(1)} %slice_bitcast_fusion), channel_id=1, source_target_pairs={{0,2},{1,3},{2,0},{3,1},{4,6},{5,7},{6,4},{7,5},{8,10},{9,11},{10,... | collective-permute-start | bytes 294920 | tf_op jit(solution)/shard_map/ppermute | solution.py:37
  28.9 3.3 %collective-permute-done.6 = f32[4,24,256]{2,1,0:T(8,128)S(1)} collective-permute-done((f32[4,24,256]{2,1,0:T(8,128)S(1)}, f32[4,24,256]{2,1,0:T(8,128)S(1)}, u32[]{:S(2)}, u32[]{:S(2)}) %collective-permute-start.6) | collective-permute-done | bytes 98336 | tf_op jit(solution)/shard_map/ppermute | solution.py:37
  32.2 0.7 %collective-permute-start.7 = (f32[24,256]{1,0:T(8,128)S(1)}, f32[24,256]{1,0:T(8,128)S(1)}, u32[]{:S(2)}, u32[]{:S(2)}) collective-permute-start(f32[24,256]{1,0:T(8,128)S(1)} %get-tuple-element.11), channel_id=1, source_target_pairs={{0,4},{1,5},{2,6},{3,7},{4,0},{5,1},{6,2},{7,3},{8,12},{9,13},{10,... | collective-permute-start | bytes 73736 | tf_op jit(solution)/shard_map/ppermute | solution.py:37
  32.9 3.5 %collective-permute-start.8 = (f32[24,256]{1,0:T(8,128)S(1)}, f32[24,256]{1,0:T(8,128)S(1)}, u32[]{:S(2)}, u32[]{:S(2)}) collective-permute-start(f32[24,256]{1,0:T(8,128)S(1)} %get-tuple-element.13), channel_id=1, source_target_pairs={{0,8},{1,9},{2,10},{3,11},{4,12},{5,13},{6,14},{7,15},{8,0},{9,1},... | collective-permute-start | bytes 73736 | tf_op jit(solution)/shard_map/ppermute | solution.py:37
  36.4 0.3 collective-permute-start.9
  36.7 0.0 collective-permute-done.7
  36.7 1.5 %collective-permute-done.8 = f32[24,256]{1,0:T(8,128)S(1)} collective-permute-done((f32[24,256]{1,0:T(8,128)S(1)}, f32[24,256]{1,0:T(8,128)S(1)}, u32[]{:S(2)}, u32[]{:S(2)}) %collective-permute-start.8) | collective-permute-done | bytes 24608 | tf_op jit(solution)/shard_map/ppermute | solution.py:37
  38.2 3.8 %collective-permute-done.9 = f32[24,256]{1,0:T(8,128)S(1)} collective-permute-done((f32[24,256]{1,0:T(8,128)S(1)}, f32[24,256]{1,0:T(8,128)S(1)}, u32[]{:S(2)}, u32[]{:S(2)}) %collective-permute-start.9) | collective-permute-done | bytes 24608 | tf_op jit(solution)/shard_map/ppermute | solution.py:37
  42.0 0.7 %slice_divide_fusion = f32[16,256]{1,0:T(8,128)} fusion(f32[24,256]{1,0:T(8,128)S(1)} %fusion.91, f32[16]{0:T(128)S(1)} %slice.109), kind=kLoop, calls=%fused_computation.91 | loop fusion | flops 4096 | bytes 32832 | tf_op jit(solution)/shard_map/div | solution.py:121
  (28 shorter events, 0.5 us)
Async XLA Ops:
  0.0 12.2 %copy-start.1 = (bf16[16,2048]{1,0:T(8,128)(2,1)S(1)}, bf16[16,2048]{1,0:T(8,128)(2,1)}, u32[]{:S(2)}) copy-start(bf16[16,2048]{1,0:T(8,128)(2,1)} %param.3) | copy-start | bytes 196612
  0.0 12.2 %copy-start = (bf16[768,2048]{1,0:T(8,128)(2,1)S(1)}, bf16[768,2048]{1,0:T(8,128)(2,1)}, u32[]{:S(2)}) copy-start(bf16[768,2048]{1,0:T(8,128)(2,1)} %param.4) | copy-start | bytes 9437188
  2.2 11.1 %collective-permute-start = (bf16[1,16,2176]{2,1,0:T(8,128)(2,1)S(1)}, bf16[1,16,2176]{2,1,0:T(8,128)(2,1)S(1)}, u32[]{:S(2)}, u32[]{:S(2)}) collective-permute-start(bf16[1,16,2176]{2,1,0:T(8,128)(2,1)S(1)} %fusion.87), channel_id=1, source_target_pairs={{0,4},{1,5},{2,6},{3,7},{4,0},{5,1},{6,2},{7,3},{8,12},{9,13},{10,... | collective-permute-start | bytes 208904 | tf_op jit(solution)/shard_map/ppermute | solution.py:37
  5.2 8.1 %collective-permute-start.1 = (bf16[1,16,2176]{2,1,0:T(8,128)(2,1)S(1)}, bf16[1,16,2176]{2,1,0:T(8,128)(2,1)S(1)}, u32[]{:S(2)}, u32[]{:S(2)}) collective-permute-start(bf16[1,16,2176]{2,1,0:T(8,128)(2,1)S(1)} %fusion.87), channel_id=1, source_target_pairs={{0,8},{1,9},{2,10},{3,11},{4,12},{5,13},{6,14},{7,15},{8,0},{9,1},... | collective-permute-start | bytes 208904 | tf_op jit(solution)/shard_map/ppermute | solution.py:37
  7.8 6.2 %collective-permute-start.2 = (bf16[1,16,2176]{2,1,0:T(8,128)(2,1)S(1)}, bf16[1,16,2176]{2,1,0:T(8,128)(2,1)S(1)}, u32[]{:S(2)}, u32[]{:S(2)}) collective-permute-start(bf16[1,16,2176]{2,1,0:T(8,128)(2,1)S(1)} %fusion.87), channel_id=1, source_target_pairs={{0,12},{1,13},{2,14},{3,15},{4,8},{5,9},{6,10},{7,11},{8,4},{9,5},... | collective-permute-start | bytes 208904 | tf_op jit(solution)/shard_map/ppermute | solution.py:37
  14.1 7.2 %collective-permute-start.3 = (bf16[4,16,2176]{2,1,0:T(8,128)(2,1)S(1)}, bf16[4,16,2176]{2,1,0:T(8,128)(2,1)S(1)}, u32[]{:S(2)}, u32[]{:S(2)}) collective-permute-start(bf16[4,16,2176]{2,1,0:T(8,128)(2,1)S(1)} %pad_maximum_fusion), channel_id=1, source_target_pairs={{0,2},{1,3},{2,0},{3,1},{4,6},{5,7},{6,4},{7,5},{8,10},{9,11},{10,... | collective-permute-start | bytes 835592 | tf_op jit(solution)/shard_map/ppermute | solution.py:37
  21.3 2.0 %collective-permute-start.4 = (bf16[8,16,2176]{2,1,0:T(8,128)(2,1)S(1)}, bf16[8,16,2176]{2,1,0:T(8,128)(2,1)S(1)}, u32[]{:S(2)}, u32[]{:S(2)}) collective-permute-start(bf16[8,16,2176]{2,1,0:T(8,128)(2,1)S(1)} %get-tuple-element.10), channel_id=1, source_target_pairs={{0,1},{1,0},{2,3},{3,2},{4,5},{5,4},{6,7},{7,6},{8,9},{9,8},{10,11... | collective-permute-start | bytes 1671176 | tf_op jit(solution)/shard_map/ppermute | solution.py:37
  23.7 1.6 %copy-start.2 = (bf16[768,256]{1,0:T(8,128)(2,1)S(1)}, bf16[768,256]{1,0:T(8,128)(2,1)}, u32[]{:S(2)}) copy-start(bf16[768,256]{1,0:T(8,128)(2,1)} %param.5) | copy-start | bytes 1179652
  25.7 1.5 %collective-permute-start.5 = (f32[2,4,24,256]{3,2,1,0:T(8,128)S(1)}, f32[2,4,24,256]{3,2,1,0:T(8,128)S(1)}, u32[]{:S(2)}, u32[]{:S(2)}) collective-permute-start(f32[2,4,24,256]{3,2,1,0:T(8,128)S(1)} %bitcast.73), channel_id=1, source_target_pairs={{0,1},{1,0},{2,3},{3,2},{4,5},{5,4},{6,7},{7,6},{8,9},{9,8},{10,11... | collective-permute-start | bytes 589832 | tf_op jit(solution)/shard_map/ppermute | solution.py:37
  27.3 4.9 %collective-permute-start.6 = (f32[4,24,256]{2,1,0:T(8,128)S(1)}, f32[4,24,256]{2,1,0:T(8,128)S(1)}, u32[]{:S(2)}, u32[]{:S(2)}) collective-permute-start(f32[4,24,256]{2,1,0:T(8,128)S(1)} %slice_bitcast_fusion), channel_id=1, source_target_pairs={{0,2},{1,3},{2,0},{3,1},{4,6},{5,7},{6,4},{7,5},{8,10},{9,11},{10,... | collective-permute-start | bytes 294920 | tf_op jit(solution)/shard_map/ppermute | solution.py:37
  32.2 4.5 %collective-permute-start.7 = (f32[24,256]{1,0:T(8,128)S(1)}, f32[24,256]{1,0:T(8,128)S(1)}, u32[]{:S(2)}, u32[]{:S(2)}) collective-permute-start(f32[24,256]{1,0:T(8,128)S(1)} %get-tuple-element.11), channel_id=1, source_target_pairs={{0,4},{1,5},{2,6},{3,7},{4,0},{5,1},{6,2},{7,3},{8,12},{9,13},{10,... | collective-permute-start | bytes 73736 | tf_op jit(solution)/shard_map/ppermute | solution.py:37
  32.9 5.3 %collective-permute-start.8 = (f32[24,256]{1,0:T(8,128)S(1)}, f32[24,256]{1,0:T(8,128)S(1)}, u32[]{:S(2)}, u32[]{:S(2)}) collective-permute-start(f32[24,256]{1,0:T(8,128)S(1)} %get-tuple-element.13), channel_id=1, source_target_pairs={{0,8},{1,9},{2,10},{3,11},{4,12},{5,13},{6,14},{7,15},{8,0},{9,1},... | collective-permute-start | bytes 73736 | tf_op jit(solution)/shard_map/ppermute | solution.py:37
  36.4 5.6 %collective-permute-start.9 = (f32[24,256]{1,0:T(8,128)S(1)}, f32[24,256]{1,0:T(8,128)S(1)}, u32[]{:S(2)}, u32[]{:S(2)}) collective-permute-start(f32[24,256]{1,0:T(8,128)S(1)} %get-tuple-element.12), channel_id=1, source_target_pairs={{0,12},{1,13},{2,14},{3,15},{4,8},{5,9},{6,10},{7,11},{8,4},{9,5},... | collective-permute-start | bytes 73736 | tf_op jit(solution)/shard_map/ppermute | solution.py:37

commit v8 on v7

--- a/solution.py
+++ b/solution.py
@@ -69,12 +69,21 @@
     return jnp.concatenate(pieces, axis=0), results
 
 
-def scatter_rounds(buf, axis, groups):
+def scatter_rounds(buf, axis, groups, fan=4):
+    rounds = []
     for group in groups:
-        masks = offsets(group)
-        total = buf[0]
+        if rounds and sum(len(g) for g in rounds[-1]) + len(group) <= fan:
+            rounds[-1].append(group)
+        else:
+            rounds.append([group])
+    for take in rounds:
+        masks = [0]
+        for group in take:
+            masks = [a | b for a in masks for b in offsets(group)]
+        flat = buf.reshape((len(masks),) + buf.shape[len(take):])
+        total = flat[0]
         for k in range(1, len(masks)):
-            total = total + swap(buf[k], axis, masks[k])
+            total = total + swap(flat[k], axis, masks[k])
         buf = total
     return buf
 

time: 43 us -> 53.2 us (1.24)
  starting transfers between devices: 13.5 us -> 28.7 us
  waiting for transfers between devices: 13.2 us -> 7.97 us
    ppermute x10 -> x20, starting transfers between devices: 13.5 us -> 28.7 us  [swap(): return lax.ppermute(x, axis, [(i, i ^ mask) for i in range(count)])]
    ppermute x10 -> x20, waiting for transfers between devices: 13.2 us -> 7.97 us  [swap(): return lax.ppermute(x, axis, [(i, i ^ mask) for i in range(count)])]
  transfers between devices with their start and end apart: 10 -> 20, of which waited for: 7 -> 6; matrix products, arithmetic and copies ran while one was open for 25% -> 20% of each run, Pallas kernels for 0% -> 0%
where the time goes in v8:
time: 53.2 us; the launch traced here: 52.6 us
  starting transfers between devices  28.7 us (54%)
  other arithmetic  8.12 us (15%)
  waiting for transfers between devices  7.97 us (15%)
  matrix products  7.13 us (13%)
    ppermute x20, starting transfers between devices, swap(): return lax.ppermute(x, axis, [(i, i ^ mask) for i in range(count)])  28.7 us
    ppermute x20, waiting for transfers between devices, swap(): return lax.ppermute(x, axis, [(i, i ^ mask) for i in range(count)])  7.97 us
    dot_general x6, matrix products, piece_weights(): lax.dot_general(rows, lib_ext, (((1,), (1,)), ((), ())), preferred_elemen...  6.83 us
    reduce_sum x1, other arithmetic, shards(): lib_sq = jnp.sum(jnp.square(library.astype(jnp.float32)), axis=1)  2.57 us
    reduce_sum x6, other arithmetic, piece_weights(): q_sq = jnp.sum(blockf * blockf, axis=1)  1.7 us
    reduce_sum x1, other arithmetic, shards(): jnp.sum(values, axis=0)  1.29 us
  transfers between devices with their start and end apart: 20, of which 6 were waited for; matrix products, arithmetic and copies ran while one was open for 20% of the time, Pallas kernels for 0%

profile of v8, /device:TPU:0, one launch (start us, length us, event | category | flops | bytes accessed | tf_op | source)
XLA Modules:
  0.0 52.6 jit_solution(167112605702920059)
XLA Ops:
  0.0 1.3 %convert_reduce_fusion = (f32[256]{0:T(256)S(1)}, f32[256]{0:T(256)S(1)}) fusion(bf16[768,256]{1,0:T(8,128)(2,1)} %param.5), kind=kLoop, calls=%fused_computation.30 | loop fusion | flops 785920 | bytes 395264 | tf_op jit(solution)/shard_map/reduce_sum | solution.py:97
  1.3 0.8 %fusion.85 = bf16[1,16,2176]{2,1,0:T(8,128)(2,1)S(1)} fusion(bf16[16,128]{1,0:T(8,128)(2,1)S(1)} %fusion.136, bf16[16,2048]{1,0:T(8,128)(2,1)} %param.3), kind=kLoop, calls=%fused_computation.88 | loop fusion | flops 139264 | bytes 139264 | tf_op jit(solution)/shard_map/broadcast_in_dim | solution.py:61
  2.2 3.1 %collective-permute-start = (bf16[1,16,2176]{2,1,0:T(8,128)(2,1)S(1)}, bf16[1,16,2176]{2,1,0:T(8,128)(2,1)S(1)}, u32[]{:S(2)}, u32[]{:S(2)}) collective-permute-start(bf16[1,16,2176]{2,1,0:T(8,128)(2,1)S(1)} %fusion.85), channel_id=1, source_target_pairs={{0,4},{1,5},{2,6},{3,7},{4,0},{5,1},{6,2},{7,3},{8,12},{9,13},{10,... | collective-permute-start | bytes 208904 | tf_op jit(solution)/shard_map/ppermute | solution.py:37
  5.2 2.6 %collective-permute-start.1 = (bf16[1,16,2176]{2,1,0:T(8,128)(2,1)S(1)}, bf16[1,16,2176]{2,1,0:T(8,128)(2,1)S(1)}, u32[]{:S(2)}, u32[]{:S(2)}) collective-permute-start(bf16[1,16,2176]{2,1,0:T(8,128)(2,1)S(1)} %fusion.85), channel_id=1, source_target_pairs={{0,8},{1,9},{2,10},{3,11},{4,12},{5,13},{6,14},{7,15},{8,0},{9,1},... | collective-permute-start | bytes 208904 | tf_op jit(solution)/shard_map/ppermute | solution.py:37
  7.8 0.0 collective-permute-start.2
  7.8 0.8 %constant_dynamic-update-slice_fusion.14 = (bf16[16,16,2176]{2,1,0:T(8,128)(2,1)S(1)}, bf16[8,16,2176]{2,1,0:T(8,128)(2,1)S(1)}) fusion(bf16[16,128]{1,0:T(8,128)(2,1)S(1)} %fusion.136, bf16[16,2048]{1,0:T(8,128)(2,1)} %param.3), kind=kLoop, calls=%fused_computation.103 | loop fusion | flops 139262 | bytes 208896
  8.7 1.0 %multiply_reduce_fusion.6 = f32[16]{0:T(128)S(1)} fusion(bf16[16,2048]{1,0:T(8,128)(2,1)} %param.3), kind=kLoop, calls=%fused_computation.68 | loop fusion | flops 98288 | bytes 65600 | tf_op jit(solution)/shard_map/reduce_sum | solution.py:26
  9.6 2.6 %multiply_reduce_fusion = f32[768]{0:T(1024)S(1)} fusion(bf16[768,2048]{1,0:T(8,128)(2,1)} %param.4), kind=kLoop, calls=%fused_computation | loop fusion | flops 4717824 | bytes 3148800 | tf_op jit(solution)/shard_map/reduce_sum | solution.py:105
  12.2 0.0 copy-done.1
  12.2 0.0 copy-done
  12.2 1.1 %fusion.148 = (f32[16]{0:T(128)S(1)}, bf16[16,768]{1,0:T(8,128)(2,1)S(1)}) fusion(f32[768]{0:T(1024)S(1)} %multiply_reduce_fusion, f32[16]{0:T(128)S(1)} %multiply_reduce_fusion.6, bf16[768,2048]{1,0:T(8,128)(2,1)S(1)} %copy-done, bf16[16,128]{1,0:T(8,128)(2,1)S(1)} %fusion.136, bf16[16,2048]{1,0:T(8,128)(2,1)S(1)} %copy-done.1), kind=kOutput, calls=%fused_computation.180 | convolution fusion | flops 53702640 | bytes 3243136 | tf_op jit(solution)/shard_map/dot_general | solution.py:27
  13.3 0.0 collective-permute-done
  13.3 0.0 collective-permute-done.1
  13.3 0.7 %collective-permute-done.2 = bf16[1,16,2176]{2,1,0:T(8,128)(2,1)S(1)} collective-permute-done((bf16[1,16,2176]{2,1,0:T(8,128)(2,1)S(1)}, bf16[1,16,2176]{2,1,0:T(8,128)(2,1)S(1)}, u32[]{:S(2)}, u32[]{:S(2)}) %collective-permute-start.2) | collective-permute-done | bytes 69664 | tf_op jit(solution)/shard_map/ppermute | solution.py:37
  14.1 1.6 %collective-permute-start.3 = (bf16[4,16,2176]{2,1,0:T(8,128)(2,1)S(1)}, bf16[4,16,2176]{2,1,0:T(8,128)(2,1)S(1)}, u32[]{:S(2)}, u32[]{:S(2)}) collective-permute-start(bf16[4,16,2176]{2,1,0:T(8,128)(2,1)S(1)} %pad_maximum_fusion), channel_id=1, source_target_pairs={{0,2},{1,3},{2,0},{3,1},{4,6},{5,7},{6,4},{7,5},{8,10},{9,11},{10,... | collective-permute-start | bytes 835592 | tf_op jit(solution)/shard_map/ppermute | solution.py:37
  15.7 0.1 multiply_reduce_fusion.5
  15.8 0.1 multiply_reduce_fusion.4
  15.9 0.1 multiply_reduce_fusion.3
  16.1 1.1 %fusion.149 = (f32[16]{0:T(128)S(1)}, bf16[16,768]{1,0:T(8,128)(2,1)S(1)}) fusion(f32[768]{0:T(1024)S(1)} %multiply_reduce_fusion, f32[16]{0:T(128)S(1)} %multiply_reduce_fusion.5, bf16[768,2048]{1,0:T(8,128)(2,1)S(1)} %copy-done, bf16[1,16,2176]{2,1,0:T(8,128)(2,1)S(1)} %collective-permute-done), kind=kOutput, calls=%fused_computation.181 | convolution fusion | flops 53563376 | bytes 3243136 | tf_op jit(solution)/shard_map/dot_general | solution.py:27
  17.1 1.1 %fusion.150 = (f32[16]{0:T(128)S(1)}, bf16[16,768]{1,0:T(8,128)(2,1)S(1)}) fusion(f32[768]{0:T(1024)S(1)} %multiply_reduce_fusion, f32[16]{0:T(128)S(1)} %multiply_reduce_fusion.4, bf16[768,2048]{1,0:T(8,128)(2,1)S(1)} %copy-done, bf16[1,16,2176]{2,1,0:T(8,128)(2,1)S(1)} %collective-permute-done.1), kind=kOutput, calls=%fused_computation.182 | convolution fusion | flops 53563376 | bytes 3243136 | tf_op jit(solution)/shard_map/dot_general | solution.py:27
  18.3 1.1 %fusion.151 = (f32[16]{0:T(128)S(1)}, bf16[16,768]{1,0:T(8,128)(2,1)S(1)}) fusion(f32[768]{0:T(1024)S(1)} %multiply_reduce_fusion, f32[16]{0:T(128)S(1)} %multiply_reduce_fusion.3, bf16[768,2048]{1,0:T(8,128)(2,1)S(1)} %copy-done, bf16[1,16,2176]{2,1,0:T(8,128)(2,1)S(1)} %collective-permute-done.2), kind=kOutput, calls=%fused_computation.183 | convolution fusion | flops 53563376 | bytes 3243136 | tf_op jit(solution)/shard_map/dot_general | solution.py:27
  19.3 2.0 %collective-permute-done.3 = bf16[4,16,2176]{2,1,0:T(8,128)(2,1)S(1)} collective-permute-done((bf16[4,16,2176]{2,1,0:T(8,128)(2,1)S(1)}, bf16[4,16,2176]{2,1,0:T(8,128)(2,1)S(1)}, u32[]{:S(2)}, u32[]{:S(2)}) %collective-permute-start.3) | collective-permute-done | bytes 278560 | tf_op jit(solution)/shard_map/ppermute | solution.py:37
  21.3 0.1 collective-permute-start.4
  21.4 0.2 multiply_reduce_fusion.2
  21.6 1.2 %fusion.152 = (f32[64]{0:T(128)S(1)}, bf16[64,768]{1,0:T(8,128)(2,1)S(1)}) fusion(f32[768]{0:T(1024)S(1)} %multiply_reduce_fusion, f32[64]{0:T(128)S(1)} %multiply_reduce_fusion.2, bf16[64,2176]{1,0:T(8,128)(2,1)S(1)} %bitcast.99, bf16[768,2048]{1,0:T(8,128)(2,1)S(1)} %copy-done), kind=kOutput, calls=%fused_computation.184 | convolution fusion | flops 214253504 | bytes 3526144 | tf_op jit(solution)/shard_map/dot_general | solution.py:27
  22.8 0.5 %collective-permute-done.4 = bf16[8,16,2176]{2,1,0:T(8,128)(2,1)S(1)} collective-permute-done((bf16[8,16,2176]{2,1,0:T(8,128)(2,1)S(1)}, bf16[8,16,2176]{2,1,0:T(8,128)(2,1)S(1)}, u32[]{:S(2)}, u32[]{:S(2)}) %collective-permute-start.4) | collective-permute-done | bytes 557088 | tf_op jit(solution)/shard_map/ppermute | solution.py:37
  23.4 0.1 constant_dynamic-update-slice_fusion.9
  23.5 0.2 multiply_reduce_fusion.1
  23.7 1.4 %fusion.153 = (f32[128]{0:T(128)S(1)}, bf16[128,768]{1,0:T(8,128)(2,1)S(1)}) fusion(f32[768]{0:T(1024)S(1)} %multiply_reduce_fusion, f32[128]{0:T(128)S(1)} %multiply_reduce_fusion.1, bf16[128,2176]{1,0:T(8,128)(2,1)S(1)} %bitcast.104, bf16[768,2048]{1,0:T(8,128)(2,1)S(1)} %copy-done), kind=kOutput, calls=%fused_computation.185 | convolution fusion | flops 428507008 | bytes 3903488 | tf_op jit(solution)/shard_map/dot_general | solution.py:27
  25.1 0.1 concatenate.35
  25.2 0.1 reshape.50
  25.4 0.0 copy-done.2
  25.4 0.3 fusion.26
  25.7 2.9 %collective-permute-start.10 = (f32[24,256]{1,0:T(8,128)S(1)}, f32[24,256]{1,0:T(8,128)S(1)}, u32[]{:S(2)}, u32[]{:S(2)}) collective-permute-start(f32[24,256]{1,0:T(8,128)S(1)} %get-tuple-element.12), channel_id=1, source_target_pairs={{0,10},{1,11},{2,8},{3,9},{4,14},{5,15},{6,12},{7,13},{8,2},{9,3},... | collective-permute-start | bytes 73736 | tf_op jit(solution)/shard_map/ppermute | solution.py:37
  28.6 1.7 %collective-permute-start.11 = (f32[24,256]{1,0:T(8,128)S(1)}, f32[24,256]{1,0:T(8,128)S(1)}, u32[]{:S(2)}, u32[]{:S(2)}) collective-permute-start(f32[24,256]{1,0:T(8,128)S(1)} %get-tuple-element.13), channel_id=1, source_target_pairs={{0,14},{1,15},{2,12},{3,13},{4,10},{5,11},{6,8},{7,9},{8,6},{9,7},... | collective-permute-start | bytes 73736 | tf_op jit(solution)/shard_map/ppermute | solution.py:37
  30.3 0.0 collective-permute-start.12
  30.3 0.6 %collective-permute-start.13 = (f32[24,256]{1,0:T(8,128)S(1)}, f32[24,256]{1,0:T(8,128)S(1)}, u32[]{:S(2)}, u32[]{:S(2)}) collective-permute-start(f32[24,256]{1,0:T(8,128)S(1)} %get-tuple-element.15), channel_id=1, source_target_pairs={{0,5},{1,4},{2,7},{3,6},{4,1},{5,0},{6,3},{7,2},{8,13},{9,12},{10,... | collective-permute-start | bytes 73736 | tf_op jit(solution)/shard_map/ppermute | solution.py:37
  30.9 1.5 %collective-permute-start.5 = (f32[24,256]{1,0:T(8,128)S(1)}, f32[24,256]{1,0:T(8,128)S(1)}, u32[]{:S(2)}, u32[]{:S(2)}) collective-permute-start(f32[24,256]{1,0:T(8,128)S(1)} %get-tuple-element.7), channel_id=1, source_target_pairs={{0,4},{1,5},{2,6},{3,7},{4,0},{5,1},{6,2},{7,3},{8,12},{9,13},{10,... | collective-permute-start | bytes 73736 | tf_op jit(solution)/shard_map/ppermute | solution.py:37
  32.5 0.0 collective-permute-done.10
  32.5 2.0 %collective-permute-start.6 = (f32[24,256]{1,0:T(8,128)S(1)}, f32[24,256]{1,0:T(8,128)S(1)}, u32[]{:S(2)}, u32[]{:S(2)}) collective-permute-start(f32[24,256]{1,0:T(8,128)S(1)} %get-tuple-element.8), channel_id=1, source_target_pairs={{0,8},{1,9},{2,10},{3,11},{4,12},{5,13},{6,14},{7,15},{8,0},{9,1},... | collective-permute-start | bytes 73736 | tf_op jit(solution)/shard_map/ppermute | solution.py:37
  34.5 0.8 %collective-permute-done.11 = f32[24,256]{1,0:T(8,128)S(1)} collective-permute-done((f32[24,256]{1,0:T(8,128)S(1)}, f32[24,256]{1,0:T(8,128)S(1)}, u32[]{:S(2)}, u32[]{:S(2)}) %collective-permute-start.11) | collective-permute-done | bytes 24608 | tf_op jit(solution)/shard_map/ppermute | solution.py:37
  35.3 1.3 %collective-permute-start.7 = (f32[24,256]{1,0:T(8,128)S(1)}, f32[24,256]{1,0:T(8,128)S(1)}, u32[]{:S(2)}, u32[]{:S(2)}) collective-permute-start(f32[24,256]{1,0:T(8,128)S(1)} %get-tuple-element.9), channel_id=1, source_target_pairs={{0,12},{1,13},{2,14},{3,15},{4,8},{5,9},{6,10},{7,11},{8,4},{9,5},... | collective-permute-start | bytes 73736 | tf_op jit(solution)/shard_map/ppermute | solution.py:37
  36.5 0.0 collective-permute-done.12
  36.5 1.1 %collective-permute-start.8 = (f32[24,256]{1,0:T(8,128)S(1)}, f32[24,256]{1,0:T(8,128)S(1)}, u32[]{:S(2)}, u32[]{:S(2)}) collective-permute-start(f32[24,256]{1,0:T(8,128)S(1)} %get-tuple-element.10), channel_id=1, source_target_pairs={{0,2},{1,3},{2,0},{3,1},{4,6},{5,7},{6,4},{7,5},{8,10},{9,11},{10,... | collective-permute-start | bytes 73736 | tf_op jit(solution)/shard_map/ppermute | solution.py:37
  37.6 0.0 collective-permute-done.13
  37.6 0.0 collective-permute-start.9
  37.6 0.0 collective-permute-done.5
  37.6 1.0 %collective-permute-start.14 = (f32[24,256]{1,0:T(8,128)S(1)}, f32[24,256]{1,0:T(8,128)S(1)}, u32[]{:S(2)}, u32[]{:S(2)}) collective-permute-start(f32[24,256]{1,0:T(8,128)S(1)} %get-tuple-element.16), channel_id=1, source_target_pairs={{0,9},{1,8},{2,11},{3,10},{4,13},{5,12},{6,15},{7,14},{8,1},{9,0},... | collective-permute-start | bytes 73736 | tf_op jit(solution)/shard_map/ppermute | solution.py:37
  38.6 0.0 collective-permute-done.6
  38.6 3.5 %collective-permute-start.15 = (f32[24,256]{1,0:T(8,128)S(1)}, f32[24,256]{1,0:T(8,128)S(1)}, u32[]{:S(2)}, u32[]{:S(2)}) collective-permute-start(f32[24,256]{1,0:T(8,128)S(1)} %get-tuple-element.17), channel_id=1, source_target_pairs={{0,13},{1,12},{2,15},{3,14},{4,9},{5,8},{6,11},{7,10},{8,5},{9,4},... | collective-permute-start | bytes 73736 | tf_op jit(solution)/shard_map/ppermute | solution.py:37
  42.1 0.0 collective-permute-done.7
  42.1 0.0 collective-permute-start.16
  42.1 0.0 collective-permute-done.8
  42.1 0.1 collective-permute-start.17
  42.2 0.4 collective-permute-done.9
  42.6 3.3 %collective-permute-start.18 = (f32[24,256]{1,0:T(8,128)S(1)}, f32[24,256]{1,0:T(8,128)S(1)}, u32[]{:S(2)}, u32[]{:S(2)}) collective-permute-start(f32[24,256]{1,0:T(8,128)S(1)} %get-tuple-element.21), channel_id=1, source_target_pairs={{0,11},{1,10},{2,9},{3,8},{4,15},{5,14},{6,13},{7,12},{8,3},{9,2},... | collective-permute-start | bytes 73736 | tf_op jit(solution)/shard_map/ppermute | solution.py:37
  45.9 0.0 collective-permute-done.14
  45.9 2.4 %collective-permute-start.19 = (f32[24,256]{1,0:T(8,128)S(1)}, f32[24,256]{1,0:T(8,128)S(1)}, u32[]{:S(2)}, u32[]{:S(2)}) collective-permute-start(f32[24,256]{1,0:T(8,128)S(1)} %get-tuple-element.20), channel_id=1, source_target_pairs={{0,15},{1,14},{2,13},{3,12},{4,11},{5,10},{6,9},{7,8},{8,7},{9,6},... | collective-permute-start | bytes 73736 | tf_op jit(solution)/shard_map/ppermute | solution.py:37
  48.3 0.0 collective-permute-done.15
  48.3 0.0 collective-permute-done.16
  48.3 0.0 collective-permute-done.17
  48.3 0.0 collective-permute-done.18
  48.3 3.5 %collective-permute-done.19 = f32[24,256]{1,0:T(8,128)S(1)} collective-permute-done((f32[24,256]{1,0:T(8,128)S(1)}, f32[24,256]{1,0:T(8,128)S(1)}, u32[]{:S(2)}, u32[]{:S(2)}) %collective-permute-start.19) | collective-permute-done | bytes 24608 | tf_op jit(solution)/shard_map/ppermute | solution.py:37
  52.0 0.7 %slice_divide_fusion = f32[16,256]{1,0:T(8,128)} fusion(f32[24,256]{1,0:T(8,128)S(1)} %fusion.116, f32[16]{0:T(128)S(1)} %slice.161), kind=kLoop, calls=%fused_computation.153 | loop fusion | flops 4096 | bytes 32832 | tf_op jit(solution)/shard_map/div | solution.py:130
  (28 shorter events, 0.4 us)
Async XLA Ops:
  0.0 12.2 %copy-start.1 = (bf16[16,2048]{1,0:T(8,128)(2,1)S(1)}, bf16[16,2048]{1,0:T(8,128)(2,1)}, u32[]{:S(2)}) copy-start(bf16[16,2048]{1,0:T(8,128)(2,1)} %param.3) | copy-start | bytes 196612
  0.0 12.2 %copy-start = (bf16[768,2048]{1,0:T(8,128)(2,1)S(1)}, bf16[768,2048]{1,0:T(8,128)(2,1)}, u32[]{:S(2)}) copy-start(bf16[768,2048]{1,0:T(8,128)(2,1)} %param.4) | copy-start | bytes 9437188
  2.2 11.1 %collective-permute-start = (bf16[1,16,2176]{2,1,0:T(8,128)(2,1)S(1)}, bf16[1,16,2176]{2,1,0:T(8,128)(2,1)S(1)}, u32[]{:S(2)}, u32[]{:S(2)}) collective-permute-start(bf16[1,16,2176]{2,1,0:T(8,128)(2,1)S(1)} %fusion.85), channel_id=1, source_target_pairs={{0,4},{1,5},{2,6},{3,7},{4,0},{5,1},{6,2},{7,3},{8,12},{9,13},{10,... | collective-permute-start | bytes 208904 | tf_op jit(solution)/shard_map/ppermute | solution.py:37
  5.2 8.1 %collective-permute-start.1 = (bf16[1,16,2176]{2,1,0:T(8,128)(2,1)S(1)}, bf16[1,16,2176]{2,1,0:T(8,128)(2,1)S(1)}, u32[]{:S(2)}, u32[]{:S(2)}) collective-permute-start(bf16[1,16,2176]{2,1,0:T(8,128)(2,1)S(1)} %fusion.85), channel_id=1, source_target_pairs={{0,8},{1,9},{2,10},{3,11},{4,12},{5,13},{6,14},{7,15},{8,0},{9,1},... | collective-permute-start | bytes 208904 | tf_op jit(solution)/shard_map/ppermute | solution.py:37
  7.8 6.2 %collective-permute-start.2 = (bf16[1,16,2176]{2,1,0:T(8,128)(2,1)S(1)}, bf16[1,16,2176]{2,1,0:T(8,128)(2,1)S(1)}, u32[]{:S(2)}, u32[]{:S(2)}) collective-permute-start(bf16[1,16,2176]{2,1,0:T(8,128)(2,1)S(1)} %fusion.85), channel_id=1, source_target_pairs={{0,12},{1,13},{2,14},{3,15},{4,8},{5,9},{6,10},{7,11},{8,4},{9,5},... | collective-permute-start | bytes 208904 | tf_op jit(solution)/shard_map/ppermute | solution.py:37
  14.1 7.2 %collective-permute-start.3 = (bf16[4,16,2176]{2,1,0:T(8,128)(2,1)S(1)}, bf16[4,16,2176]{2,1,0:T(8,128)(2,1)S(1)}, u32[]{:S(2)}, u32[]{:S(2)}) collective-permute-start(bf16[4,16,2176]{2,1,0:T(8,128)(2,1)S(1)} %pad_maximum_fusion), channel_id=1, source_target_pairs={{0,2},{1,3},{2,0},{3,1},{4,6},{5,7},{6,4},{7,5},{8,10},{9,11},{10,... | collective-permute-start | bytes 835592 | tf_op jit(solution)/shard_map/ppermute | solution.py:37
  21.3 2.0 %collective-permute-start.4 = (bf16[8,16,2176]{2,1,0:T(8,128)(2,1)S(1)}, bf16[8,16,2176]{2,1,0:T(8,128)(2,1)S(1)}, u32[]{:S(2)}, u32[]{:S(2)}) collective-permute-start(bf16[8,16,2176]{2,1,0:T(8,128)(2,1)S(1)} %get-tuple-element.23), channel_id=1, source_target_pairs={{0,1},{1,0},{2,3},{3,2},{4,5},{5,4},{6,7},{7,6},{8,9},{9,8},{10,11... | collective-permute-start | bytes 1671176 | tf_op jit(solution)/shard_map/ppermute | solution.py:37
  23.7 1.6 %copy-start.2 = (bf16[768,256]{1,0:T(8,128)(2,1)S(1)}, bf16[768,256]{1,0:T(8,128)(2,1)}, u32[]{:S(2)}) copy-start(bf16[768,256]{1,0:T(8,128)(2,1)} %param.5) | copy-start | bytes 1179652
  25.7 6.8 %collective-permute-start.10 = (f32[24,256]{1,0:T(8,128)S(1)}, f32[24,256]{1,0:T(8,128)S(1)}, u32[]{:S(2)}, u32[]{:S(2)}) collective-permute-start(f32[24,256]{1,0:T(8,128)S(1)} %get-tuple-element.12), channel_id=1, source_target_pairs={{0,10},{1,11},{2,8},{3,9},{4,14},{5,15},{6,12},{7,13},{8,2},{9,3},... | collective-permute-start | bytes 73736 | tf_op jit(solution)/shard_map/ppermute | solution.py:37
  28.6 6.6 %collective-permute-start.11 = (f32[24,256]{1,0:T(8,128)S(1)}, f32[24,256]{1,0:T(8,128)S(1)}, u32[]{:S(2)}, u32[]{:S(2)}) collective-permute-start(f32[24,256]{1,0:T(8,128)S(1)} %get-tuple-element.13), channel_id=1, source_target_pairs={{0,14},{1,15},{2,12},{3,13},{4,10},{5,11},{6,8},{7,9},{8,6},{9,7},... | collective-permute-start | bytes 73736 | tf_op jit(solution)/shard_map/ppermute | solution.py:37
  30.3 6.2 %collective-permute-start.12 = (f32[24,256]{1,0:T(8,128)S(1)}, f32[24,256]{1,0:T(8,128)S(1)}, u32[]{:S(2)}, u32[]{:S(2)}) collective-permute-start(f32[24,256]{1,0:T(8,128)S(1)} %get-tuple-element.14), channel_id=1, source_target_pairs={{0,1},{1,0},{2,3},{3,2},{4,5},{5,4},{6,7},{7,6},{8,9},{9,8},{10,11... | collective-permute-start | bytes 73736 | tf_op jit(solution)/shard_map/ppermute | solution.py:37
  30.3 7.3 %collective-permute-start.13 = (f32[24,256]{1,0:T(8,128)S(1)}, f32[24,256]{1,0:T(8,128)S(1)}, u32[]{:S(2)}, u32[]{:S(2)}) collective-permute-start(f32[24,256]{1,0:T(8,128)S(1)} %get-tuple-element.15), channel_id=1, source_target_pairs={{0,5},{1,4},{2,7},{3,6},{4,1},{5,0},{6,3},{7,2},{8,13},{9,12},{10,... | collective-permute-start | bytes 73736 | tf_op jit(solution)/shard_map/ppermute | solution.py:37
  30.9 6.7 %collective-permute-start.5 = (f32[24,256]{1,0:T(8,128)S(1)}, f32[24,256]{1,0:T(8,128)S(1)}, u32[]{:S(2)}, u32[]{:S(2)}) collective-permute-start(f32[24,256]{1,0:T(8,128)S(1)} %get-tuple-element.7), channel_id=1, source_target_pairs={{0,4},{1,5},{2,6},{3,7},{4,0},{5,1},{6,2},{7,3},{8,12},{9,13},{10,... | collective-permute-start | bytes 73736 | tf_op jit(solution)/shard_map/ppermute | solution.py:37
  32.5 6.1 %collective-permute-start.6 = (f32[24,256]{1,0:T(8,128)S(1)}, f32[24,256]{1,0:T(8,128)S(1)}, u32[]{:S(2)}, u32[]{:S(2)}) collective-permute-start(f32[24,256]{1,0:T(8,128)S(1)} %get-tuple-element.8), channel_id=1, source_target_pairs={{0,8},{1,9},{2,10},{3,11},{4,12},{5,13},{6,14},{7,15},{8,0},{9,1},... | collective-permute-start | bytes 73736 | tf_op jit(solution)/shard_map/ppermute | solution.py:37
  35.3 6.9 %collective-permute-start.7 = (f32[24,256]{1,0:T(8,128)S(1)}, f32[24,256]{1,0:T(8,128)S(1)}, u32[]{:S(2)}, u32[]{:S(2)}) collective-permute-start(f32[24,256]{1,0:T(8,128)S(1)} %get-tuple-element.9), channel_id=1, source_target_pairs={{0,12},{1,13},{2,14},{3,15},{4,8},{5,9},{6,10},{7,11},{8,4},{9,5},... | collective-permute-start | bytes 73736 | tf_op jit(solution)/shard_map/ppermute | solution.py:37
  36.5 5.6 %collective-permute-start.8 = (f32[24,256]{1,0:T(8,128)S(1)}, f32[24,256]{1,0:T(8,128)S(1)}, u32[]{:S(2)}, u32[]{:S(2)}) collective-permute-start(f32[24,256]{1,0:T(8,128)S(1)} %get-tuple-element.10), channel_id=1, source_target_pairs={{0,2},{1,3},{2,0},{3,1},{4,6},{5,7},{6,4},{7,5},{8,10},{9,11},{10,... | collective-permute-start | bytes 73736 | tf_op jit(solution)/shard_map/ppermute | solution.py:37
  37.6 5.0 %collective-permute-start.9 = (f32[24,256]{1,0:T(8,128)S(1)}, f32[24,256]{1,0:T(8,128)S(1)}, u32[]{:S(2)}, u32[]{:S(2)}) collective-permute-start(f32[24,256]{1,0:T(8,128)S(1)} %get-tuple-element.11), channel_id=1, source_target_pairs={{0,6},{1,7},{2,4},{3,5},{4,2},{5,3},{6,0},{7,1},{8,14},{9,15},{10,... | collective-permute-start | bytes 73736 | tf_op jit(solution)/shard_map/ppermute | solution.py:37
  37.6 8.3 %collective-permute-start.14 = (f32[24,256]{1,0:T(8,128)S(1)}, f32[24,256]{1,0:T(8,128)S(1)}, u32[]{:S(2)}, u32[]{:S(2)}) collective-permute-start(f32[24,256]{1,0:T(8,128)S(1)} %get-tuple-element.16), channel_id=1, source_target_pairs={{0,9},{1,8},{2,11},{3,10},{4,13},{5,12},{6,15},{7,14},{8,1},{9,0},... | collective-permute-start | bytes 73736 | tf_op jit(solution)/shard_map/ppermute | solution.py:37
  38.6 9.7 %collective-permute-start.15 = (f32[24,256]{1,0:T(8,128)S(1)}, f32[24,256]{1,0:T(8,128)S(1)}, u32[]{:S(2)}, u32[]{:S(2)}) collective-permute-start(f32[24,256]{1,0:T(8,128)S(1)} %get-tuple-element.17), channel_id=1, source_target_pairs={{0,13},{1,12},{2,15},{3,14},{4,9},{5,8},{6,11},{7,10},{8,5},{9,4},... | collective-permute-start | bytes 73736 | tf_op jit(solution)/shard_map/ppermute | solution.py:37
  42.1 6.2 %collective-permute-start.16 = (f32[24,256]{1,0:T(8,128)S(1)}, f32[24,256]{1,0:T(8,128)S(1)}, u32[]{:S(2)}, u32[]{:S(2)}) collective-permute-start(f32[24,256]{1,0:T(8,128)S(1)} %get-tuple-element.18), channel_id=1, source_target_pairs={{0,3},{1,2},{2,1},{3,0},{4,7},{5,6},{6,5},{7,4},{8,11},{9,10},{10,... | collective-permute-start | bytes 73736 | tf_op jit(solution)/shard_map/ppermute | solution.py:37
  42.1 6.2 %collective-permute-start.17 = (f32[24,256]{1,0:T(8,128)S(1)}, f32[24,256]{1,0:T(8,128)S(1)}, u32[]{:S(2)}, u32[]{:S(2)}) collective-permute-start(f32[24,256]{1,0:T(8,128)S(1)} %get-tuple-element.19), channel_id=1, source_target_pairs={{0,7},{1,6},{2,5},{3,4},{4,3},{5,2},{6,1},{7,0},{8,15},{9,14},{10,... | collective-permute-start | bytes 73736 | tf_op jit(solution)/shard_map/ppermute | solution.py:37
  42.6 5.7 %collective-permute-start.18 = (f32[24,256]{1,0:T(8,128)S(1)}, f32[24,256]{1,0:T(8,128)S(1)}, u32[]{:S(2)}, u32[]{:S(2)}) collective-permute-start(f32[24,256]{1,0:T(8,128)S(1)} %get-tuple-element.21), channel_id=1, source_target_pairs={{0,11},{1,10},{2,9},{3,8},{4,15},{5,14},{6,13},{7,12},{8,3},{9,2},... | collective-permute-start | bytes 73736 | tf_op jit(solution)/shard_map/ppermute | solution.py:37
  45.9 5.9 %collective-permute-start.19 = (f32[24,256]{1,0:T(8,128)S(1)}, f32[24,256]{1,0:T(8,128)S(1)}, u32[]{:S(2)}, u32[]{:S(2)}) collective-permute-start(f32[24,256]{1,0:T(8,128)S(1)} %get-tuple-element.20), channel_id=1, source_target_pairs={{0,15},{1,14},{2,13},{3,12},{4,11},{5,10},{6,9},{7,8},{8,7},{9,6},... | collective-permute-start | bytes 73736 | tf_op jit(solution)/shard_map/ppermute | solution.py:37

commit v9 on v7

--- a/solution.py
+++ b/solution.py
@@ -85,7 +85,11 @@
     q_dev, feat = queries.shape
     width = assays.shape[1]
     values = assays.astype(jnp.float32)
-    partial = jnp.concatenate([jnp.sum(values, axis=0), jnp.sum(values * values, axis=0)])
+    grouped = values.reshape(-1, 8, width)
+    firsts = lax.optimization_barrier(
+        (jnp.sum(grouped, axis=0), jnp.sum(grouped * grouped, axis=0))
+    )
+    partial = jnp.concatenate([jnp.sum(firsts[0], axis=0), jnp.sum(firsts[1], axis=0)])
 
     coded = split3(partial)
     lanes = -(-coded.shape[0] // q_dev)

time: 43 us -> 49.2 us (1.14)
  local copies, waits for them, and re-layouts: 0.51 us -> 3.49 us
  matrix products: 7.13 us -> 9.88 us
  other arithmetic: 8.14 us -> 8.74 us
  waiting for transfers between devices: 13.2 us -> 12.6 us
    dot_general x6, matrix products: 6.83 us -> 8.58 us  [piece_weights(): lax.dot_general(rows, lib_ext, (((1,), (1,)), ((), ())), preferred_elemen...]
    concatenate x1, local copies, waits for them, and re-layouts: 0.02 us -> 1.62 us  [shards(): weight_b = jnp.concatenate([p[0] for p in parts], axis=0)]
    dot_general x1, matrix products: 0.3 us -> 1.3 us  [shards(): numer = jnp.dot(weight_b, zvals, preferred_element_type=jnp.float32)]
    unnamed x19 -> x21, local copies, waits for them, and re-layouts: 0.24 us -> 0.96 us
    concatenate x1, local copies, waits for them, and re-layouts: 0.08 us -> 0.74 us  [shards(): denom = jnp.concatenate([p[1] for p in parts], axis=0)]
    div x1, other arithmetic: 0.01 us -> 0.6 us  [shards(): mean = col_sum / total]
    ppermute x10, waiting for transfers between devices: 13.2 us -> 12.6 us  [swap(): return lax.ppermute(x, axis, [(i, i ^ mask) for i in range(count)])]
    reduce_sum x1 -> x3, other arithmetic: 1.29 us -> 1.31 us  [the longest x1 1.28 us: shards(): jnp.sum(grouped * grouped, axis=0)]
  transfers between devices with their start and end apart: 10 -> 10, of which waited for: 7 -> 6; matrix products, arithmetic and copies ran while one was open for 25% -> 23% of each run, Pallas kernels for 0% -> 0%
where the time goes in v9:
time: 49.2 us; the launch traced here: 48.9 us
  starting transfers between devices  13.9 us (28%)
  waiting for transfers between devices  12.6 us (26%)
  matrix products  9.88 us (20%)
  other arithmetic  8.74 us (18%)
  local copies, waits for them, and re-layouts  3.49 us (7%)
    ppermute x10, starting transfers between devices, swap(): return lax.ppermute(x, axis, [(i, i ^ mask) for i in range(count)])  13.9 us
    ppermute x10, waiting for transfers between devices, swap(): return lax.ppermute(x, axis, [(i, i ^ mask) for i in range(count)])  12.6 us
    dot_general x6, matrix products, piece_weights(): lax.dot_general(rows, lib_ext, (((1,), (1,)), ((), ())), preferred_elemen...  8.58 us
    reduce_sum x1, other arithmetic, shards(): lib_sq = jnp.sum(jnp.square(library.astype(jnp.float32)), axis=1)  2.57 us
    reduce_sum x6, other arithmetic, piece_weights(): q_sq = jnp.sum(blockf * blockf, axis=1)  1.7 us
    concatenate x1, local copies, waits for them, and re-layouts, shards(): weight_b = jnp.concatenate([p[0] for p in parts], axis=0)  1.62 us
    dot_general x1, matrix products, shards(): numer = jnp.dot(weight_b, zvals, preferred_element_type=jnp.float32)  1.3 us
    reduce_sum x1, other arithmetic, shards(): jnp.sum(grouped * grouped, axis=0)  1.28 us
  transfers between devices with their start and end apart: 10, of which 6 were waited for; matrix products, arithmetic and copies ran while one was open for 23% of the time, Pallas kernels for 0%

profile of v9, /device:TPU:0, one launch (start us, length us, event | category | flops | bytes accessed | tf_op | source)
XLA Modules:
  0.0 48.9 jit_solution(7958076116936669269)
XLA Ops:
  0.0 0.0 copy-start.1
  0.0 0.0 copy-start
  0.0 1.3 %fusion.14 = (f32[8,256]{1,0:T(8,128)S(1)}, f32[8,256]{1,0:T(8,128)S(1)}) fusion(bf16[768,256]{1,0:T(8,128)(2,1)} %param.5), kind=kLoop, calls=%fused_computation.18 | loop fusion | flops 782336 | bytes 409600 | tf_op jit(solution)/shard_map/reduce_sum | solution.py:90
  1.4 0.8 %fusion.89 = bf16[1,16,2176]{2,1,0:T(8,128)(2,1)S(1)} fusion(bf16[16,128]{1,0:T(8,128)(2,1)S(1)} %fusion.99, bf16[16,2048]{1,0:T(8,128)(2,1)} %param.3), kind=kLoop, calls=%fused_computation.66 | loop fusion | flops 139264 | bytes 139264 | tf_op jit(solution)/shard_map/broadcast_in_dim | solution.py:61
  2.2 3.1 %collective-permute-start = (bf16[1,16,2176]{2,1,0:T(8,128)(2,1)S(1)}, bf16[1,16,2176]{2,1,0:T(8,128)(2,1)S(1)}, u32[]{:S(2)}, u32[]{:S(2)}) collective-permute-start(bf16[1,16,2176]{2,1,0:T(8,128)(2,1)S(1)} %fusion.89), channel_id=1, source_target_pairs={{0,4},{1,5},{2,6},{3,7},{4,0},{5,1},{6,2},{7,3},{8,12},{9,13},{10,... | collective-permute-start | bytes 208904 | tf_op jit(solution)/shard_map/ppermute | solution.py:37
  5.3 2.6 %collective-permute-start.1 = (bf16[1,16,2176]{2,1,0:T(8,128)(2,1)S(1)}, bf16[1,16,2176]{2,1,0:T(8,128)(2,1)S(1)}, u32[]{:S(2)}, u32[]{:S(2)}) collective-permute-start(bf16[1,16,2176]{2,1,0:T(8,128)(2,1)S(1)} %fusion.89), channel_id=1, source_target_pairs={{0,8},{1,9},{2,10},{3,11},{4,12},{5,13},{6,14},{7,15},{8,0},{9,1},... | collective-permute-start | bytes 208904 | tf_op jit(solution)/shard_map/ppermute | solution.py:37
  7.8 0.0 collective-permute-start.2
  7.8 0.8 %constant_dynamic-update-slice_fusion.14 = (bf16[16,16,2176]{2,1,0:T(8,128)(2,1)S(1)}, bf16[8,16,2176]{2,1,0:T(8,128)(2,1)S(1)}) fusion(bf16[16,128]{1,0:T(8,128)(2,1)S(1)} %fusion.99, bf16[16,2048]{1,0:T(8,128)(2,1)} %param.3), kind=kLoop, calls=%fused_computation.81 | loop fusion | flops 139262 | bytes 208896
  8.7 1.0 %multiply_reduce_fusion.6 = f32[16]{0:T(128)S(1)} fusion(bf16[16,2048]{1,0:T(8,128)(2,1)} %param.3), kind=kLoop, calls=%fused_computation.43 | loop fusion | flops 98288 | bytes 65600 | tf_op jit(solution)/shard_map/reduce_sum | solution.py:26
  9.7 2.6 %multiply_reduce_fusion = f32[768]{0:T(1024)S(1)} fusion(bf16[768,2048]{1,0:T(8,128)(2,1)} %param.4), kind=kLoop, calls=%fused_computation | loop fusion | flops 4717824 | bytes 3148800 | tf_op jit(solution)/shard_map/reduce_sum | solution.py:100
  12.2 0.0 copy-done.1
  12.3 0.0 copy-done
  12.3 1.1 %fusion.111 = (f32[16]{0:T(128)S(1)}, bf16[16,768]{1,0:T(8,128)(2,1)S(1)}) fusion(f32[768]{0:T(1024)S(1)} %multiply_reduce_fusion, f32[16]{0:T(128)S(1)} %multiply_reduce_fusion.6, bf16[768,2048]{1,0:T(8,128)(2,1)S(1)} %copy-done, bf16[16,128]{1,0:T(8,128)(2,1)S(1)} %fusion.99, bf16[16,2048]{1,0:T(8,128)(2,1)S(1)} %copy-done.1), kind=kOutput, calls=%fused_computation.119 | convolution fusion | flops 53702640 | bytes 3243136 | tf_op jit(solution)/shard_map/dot_general | solution.py:27
  13.3 0.0 collective-permute-done
  13.3 0.0 collective-permute-done.1
  13.4 0.7 %collective-permute-done.2 = bf16[1,16,2176]{2,1,0:T(8,128)(2,1)S(1)} collective-permute-done((bf16[1,16,2176]{2,1,0:T(8,128)(2,1)S(1)}, bf16[1,16,2176]{2,1,0:T(8,128)(2,1)S(1)}, u32[]{:S(2)}, u32[]{:S(2)}) %collective-permute-start.2) | collective-permute-done | bytes 69664 | tf_op jit(solution)/shard_map/ppermute | solution.py:37
  14.1 1.6 %collective-permute-start.3 = (bf16[4,16,2176]{2,1,0:T(8,128)(2,1)S(1)}, bf16[4,16,2176]{2,1,0:T(8,128)(2,1)S(1)}, u32[]{:S(2)}, u32[]{:S(2)}) collective-permute-start(bf16[4,16,2176]{2,1,0:T(8,128)(2,1)S(1)} %pad_maximum_fusion), channel_id=1, source_target_pairs={{0,2},{1,3},{2,0},{3,1},{4,6},{5,7},{6,4},{7,5},{8,10},{9,11},{10,... | collective-permute-start | bytes 835592 | tf_op jit(solution)/shard_map/ppermute | solution.py:37
  15.7 0.1 multiply_reduce_fusion.5
  15.8 0.1 multiply_reduce_fusion.4
  15.9 0.1 multiply_reduce_fusion.3
  16.1 1.1 %fusion.112 = (f32[16]{0:T(128)S(1)}, bf16[16,768]{1,0:T(8,128)(2,1)S(1)}) fusion(f32[768]{0:T(1024)S(1)} %multiply_reduce_fusion, f32[16]{0:T(128)S(1)} %multiply_reduce_fusion.5, bf16[768,2048]{1,0:T(8,128)(2,1)S(1)} %copy-done, bf16[1,16,2176]{2,1,0:T(8,128)(2,1)S(1)} %collective-permute-done), kind=kOutput, calls=%fused_computation.120 | convolution fusion | flops 53563376 | bytes 3243136 | tf_op jit(solution)/shard_map/dot_general | solution.py:27
  17.2 1.1 %fusion.113 = (f32[16]{0:T(128)S(1)}, bf16[16,768]{1,0:T(8,128)(2,1)S(1)}) fusion(f32[768]{0:T(1024)S(1)} %multiply_reduce_fusion, f32[16]{0:T(128)S(1)} %multiply_reduce_fusion.4, bf16[768,2048]{1,0:T(8,128)(2,1)S(1)} %copy-done, bf16[1,16,2176]{2,1,0:T(8,128)(2,1)S(1)} %collective-permute-done.1), kind=kOutput, calls=%fused_computation.121 | convolution fusion | flops 53563376 | bytes 3243136 | tf_op jit(solution)/shard_map/dot_general | solution.py:27
  18.3 1.1 %fusion.114 = (f32[16]{0:T(128)S(1)}, bf16[16,768]{1,0:T(8,128)(2,1)S(1)}) fusion(f32[768]{0:T(1024)S(1)} %multiply_reduce_fusion, f32[16]{0:T(128)S(1)} %multiply_reduce_fusion.3, bf16[768,2048]{1,0:T(8,128)(2,1)S(1)} %copy-done, bf16[1,16,2176]{2,1,0:T(8,128)(2,1)S(1)} %collective-permute-done.2), kind=kOutput, calls=%fused_computation.122 | convolution fusion | flops 53563376 | bytes 3243136 | tf_op jit(solution)/shard_map/dot_general | solution.py:27
  19.4 2.0 %collective-permute-done.3 = bf16[4,16,2176]{2,1,0:T(8,128)(2,1)S(1)} collective-permute-done((bf16[4,16,2176]{2,1,0:T(8,128)(2,1)S(1)}, bf16[4,16,2176]{2,1,0:T(8,128)(2,1)S(1)}, u32[]{:S(2)}, u32[]{:S(2)}) %collective-permute-start.3) | collective-permute-done | bytes 278560 | tf_op jit(solution)/shard_map/ppermute | solution.py:37
  21.4 0.1 collective-permute-start.4
  21.5 0.2 multiply_reduce_fusion.2
  21.6 1.8 %fusion.115 = (f32[64]{0:T(128)}, bf16[64,768]{1,0:T(8,128)(2,1)S(1)}) fusion(f32[768]{0:T(1024)S(1)} %multiply_reduce_fusion, f32[64]{0:T(128)S(1)} %multiply_reduce_fusion.2, bf16[64,2176]{1,0:T(8,128)(2,1)S(1)} %bitcast.69, bf16[768,2048]{1,0:T(8,128)(2,1)S(1)} %copy-done), kind=kOutput, calls=%fused_computation.123 | convolution fusion | flops 214253504 | bytes 3526144 | tf_op jit(solution)/shard_map/dot_general | solution.py:27
  23.4 0.0 copy-start.3
  23.4 0.0 collective-permute-done.4
  23.4 0.7 %copy-done.3 = bf16[256,768]{1,0:T(8,128)(2,1)} copy-done((bf16[256,768]{1,0:T(8,128)(2,1)}, bf16[256,768]{1,0:T(8,128)(2,1)S(1)}, u32[]{:S(2)}) %copy-start.3) | copy-done | bytes 393240
  24.2 0.1 constant_dynamic-update-slice_fusion.9
  24.3 0.6 %slice_multiply_fusion = (f32[256]{0:T(256)}, f32[256]{0:T(256)}) fusion(f32[512]{0:T(512)S(1)} %fusion.90), kind=kLoop, calls=%fused_computation.108 | loop fusion | flops 1280 | bytes 4096 | tf_op jit(solution)/shard_map/div | solution.py:109
  24.9 0.2 multiply_reduce_fusion.1
  25.1 0.0 copy-start.2
  25.1 2.5 %fusion.116 = (f32[128]{0:T(128)}, bf16[128,768]{1,0:T(8,128)(2,1)}) fusion(f32[768]{0:T(1024)S(1)} %multiply_reduce_fusion, f32[128]{0:T(128)S(1)} %multiply_reduce_fusion.1, bf16[128,2176]{1,0:T(8,128)(2,1)S(1)} %bitcast.71, bf16[768,2048]{1,0:T(8,128)(2,1)S(1)} %copy-done), kind=kOutput, calls=%fused_computation.124 | convolution fusion | flops 428507008 | bytes 3903488 | tf_op jit(solution)/shard_map/dot_general | solution.py:27
  27.6 0.7 %concatenate.35 = f32[256]{0:T(256)S(1)} concatenate(f32[16]{0:T(128)S(1)} %get-tuple-element.31, f32[16]{0:T(128)S(1)} %get-tuple-element.33, f32[16]{0:T(128)S(1)} %get-tuple-element.35, f32[16]{0:T(128)S(1)} %get-tuple-element.37, f32[64]{0:T(128)} %get-tuple-element.39, f32[128]{0:T(128)} %get-tuple-element.41), dimensions={0} | concatenate | bytes 2048 | tf_op jit(solution)/shard_map/concatenate | solution.py:114
  28.4 0.1 reshape.59
  28.5 1.6 %convert_dynamic-update-slice_fusion = bf16[256,768]{1,0:T(8,128)(2,1)} fusion(bf16[256,768]{1,0:T(8,128)(2,1)} %copy-done.3, bf16[128,768]{1,0:T(8,128)(2,1)} %get-tuple-element.42), kind=kLoop, calls=%fused_computation.38 | loop fusion | bytes 393216 | tf_op jit(solution)/shard_map/concatenate | solution.py:113
  30.1 0.0 copy-done.2
  30.2 1.3 %fusion.28 = f32[256,256]{1,0:T(8,128)S(1)} fusion(bf16[256,768]{1,0:T(8,128)(2,1)} %convert_dynamic-update-slice_fusion, bf16[768,256]{1,0:T(8,128)(2,1)S(1)} %copy-done.2, f32[256]{0:T(256)} %get-tuple-element.27, f32[256]{0:T(256)} %get-tuple-element.26), kind=kOutput, calls=%fused_computation.26 | convolution fusion | flops 101449728 | bytes 1050624 | tf_op jit(solution)/shard_map/dot_general | solution.py:115
  31.5 0.6 %collective-permute-start.5 = (f32[2,4,24,256]{3,2,1,0:T(8,128)S(1)}, f32[2,4,24,256]{3,2,1,0:T(8,128)S(1)}, u32[]{:S(2)}, u32[]{:S(2)}) collective-permute-start(f32[2,4,24,256]{3,2,1,0:T(8,128)S(1)} %bitcast.81), channel_id=1, source_target_pairs={{0,1},{1,0},{2,3},{3,2},{4,5},{5,4},{6,7},{7,6},{8,9},{9,8},{10,11... | collective-permute-start | bytes 589832 | tf_op jit(solution)/shard_map/ppermute | solution.py:37
  32.0 1.1 %collective-permute-done.5 = f32[2,4,24,256]{3,2,1,0:T(8,128)S(1)} collective-permute-done((f32[2,4,24,256]{3,2,1,0:T(8,128)S(1)}, f32[2,4,24,256]{3,2,1,0:T(8,128)S(1)}, u32[]{:S(2)}, u32[]{:S(2)}) %collective-permute-start.5) | collective-permute-done | bytes 196640 | tf_op jit(solution)/shard_map/ppermute | solution.py:37
  33.2 1.6 %collective-permute-start.6 = (f32[4,24,256]{2,1,0:T(8,128)S(1)}, f32[4,24,256]{2,1,0:T(8,128)S(1)}, u32[]{:S(2)}, u32[]{:S(2)}) collective-permute-start(f32[4,24,256]{2,1,0:T(8,128)S(1)} %slice_bitcast_fusion), channel_id=1, source_target_pairs={{0,2},{1,3},{2,0},{3,1},{4,6},{5,7},{6,4},{7,5},{8,10},{9,11},{10,... | collective-permute-start | bytes 294920 | tf_op jit(solution)/shard_map/ppermute | solution.py:37
  34.7 3.6 %collective-permute-done.6 = f32[4,24,256]{2,1,0:T(8,128)S(1)} collective-permute-done((f32[4,24,256]{2,1,0:T(8,128)S(1)}, f32[4,24,256]{2,1,0:T(8,128)S(1)}, u32[]{:S(2)}, u32[]{:S(2)}) %collective-permute-start.6) | collective-permute-done | bytes 98336 | tf_op jit(solution)/shard_map/ppermute | solution.py:37
  38.3 0.7 %collective-permute-start.7 = (f32[24,256]{1,0:T(8,128)S(1)}, f32[24,256]{1,0:T(8,128)S(1)}, u32[]{:S(2)}, u32[]{:S(2)}) collective-permute-start(f32[24,256]{1,0:T(8,128)S(1)} %get-tuple-element.15), channel_id=1, source_target_pairs={{0,4},{1,5},{2,6},{3,7},{4,0},{5,1},{6,2},{7,3},{8,12},{9,13},{10,... | collective-permute-start | bytes 73736 | tf_op jit(solution)/shard_map/ppermute | solution.py:37
  39.0 3.5 %collective-permute-start.8 = (f32[24,256]{1,0:T(8,128)S(1)}, f32[24,256]{1,0:T(8,128)S(1)}, u32[]{:S(2)}, u32[]{:S(2)}) collective-permute-start(f32[24,256]{1,0:T(8,128)S(1)} %get-tuple-element.17), channel_id=1, source_target_pairs={{0,8},{1,9},{2,10},{3,11},{4,12},{5,13},{6,14},{7,15},{8,0},{9,1},... | collective-permute-start | bytes 73736 | tf_op jit(solution)/shard_map/ppermute | solution.py:37
  42.5 0.3 collective-permute-start.9
  42.8 0.0 collective-permute-done.7
  42.8 1.6 %collective-permute-done.8 = f32[24,256]{1,0:T(8,128)S(1)} collective-permute-done((f32[24,256]{1,0:T(8,128)S(1)}, f32[24,256]{1,0:T(8,128)S(1)}, u32[]{:S(2)}, u32[]{:S(2)}) %collective-permute-start.8) | collective-permute-done | bytes 24608 | tf_op jit(solution)/shard_map/ppermute | solution.py:37
  44.4 3.7 %collective-permute-done.9 = f32[24,256]{1,0:T(8,128)S(1)} collective-permute-done((f32[24,256]{1,0:T(8,128)S(1)}, f32[24,256]{1,0:T(8,128)S(1)}, u32[]{:S(2)}, u32[]{:S(2)}) %collective-permute-start.9) | collective-permute-done | bytes 24608 | tf_op jit(solution)/shard_map/ppermute | solution.py:37
  48.2 0.7 %slice_divide_fusion = f32[16,256]{1,0:T(8,128)} fusion(f32[24,256]{1,0:T(8,128)S(1)} %fusion.93, f32[16]{0:T(128)S(1)} %slice.109), kind=kLoop, calls=%fused_computation.92 | loop fusion | flops 4096 | bytes 32832 | tf_op jit(solution)/shard_map/div | solution.py:125
  (28 shorter events, 0.5 us)
Async XLA Ops:
  0.0 12.2 %copy-start.1 = (bf16[16,2048]{1,0:T(8,128)(2,1)S(1)}, bf16[16,2048]{1,0:T(8,128)(2,1)}, u32[]{:S(2)}) copy-start(bf16[16,2048]{1,0:T(8,128)(2,1)} %param.3) | copy-start | bytes 196612
  0.0 12.3 %copy-start = (bf16[768,2048]{1,0:T(8,128)(2,1)S(1)}, bf16[768,2048]{1,0:T(8,128)(2,1)}, u32[]{:S(2)}) copy-start(bf16[768,2048]{1,0:T(8,128)(2,1)} %param.4) | copy-start | bytes 9437188
  2.2 11.1 %collective-permute-start = (bf16[1,16,2176]{2,1,0:T(8,128)(2,1)S(1)}, bf16[1,16,2176]{2,1,0:T(8,128)(2,1)S(1)}, u32[]{:S(2)}, u32[]{:S(2)}) collective-permute-start(bf16[1,16,2176]{2,1,0:T(8,128)(2,1)S(1)} %fusion.89), channel_id=1, source_target_pairs={{0,4},{1,5},{2,6},{3,7},{4,0},{5,1},{6,2},{7,3},{8,12},{9,13},{10,... | collective-permute-start | bytes 208904 | tf_op jit(solution)/shard_map/ppermute | solution.py:37
  5.3 8.1 %collective-permute-start.1 = (bf16[1,16,2176]{2,1,0:T(8,128)(2,1)S(1)}, bf16[1,16,2176]{2,1,0:T(8,128)(2,1)S(1)}, u32[]{:S(2)}, u32[]{:S(2)}) collective-permute-start(bf16[1,16,2176]{2,1,0:T(8,128)(2,1)S(1)} %fusion.89), channel_id=1, source_target_pairs={{0,8},{1,9},{2,10},{3,11},{4,12},{5,13},{6,14},{7,15},{8,0},{9,1},... | collective-permute-start | bytes 208904 | tf_op jit(solution)/shard_map/ppermute | solution.py:37
  7.8 6.2 %collective-permute-start.2 = (bf16[1,16,2176]{2,1,0:T(8,128)(2,1)S(1)}, bf16[1,16,2176]{2,1,0:T(8,128)(2,1)S(1)}, u32[]{:S(2)}, u32[]{:S(2)}) collective-permute-start(bf16[1,16,2176]{2,1,0:T(8,128)(2,1)S(1)} %fusion.89), channel_id=1, source_target_pairs={{0,12},{1,13},{2,14},{3,15},{4,8},{5,9},{6,10},{7,11},{8,4},{9,5},... | collective-permute-start | bytes 208904 | tf_op jit(solution)/shard_map/ppermute | solution.py:37
  14.1 7.2 %collective-permute-start.3 = (bf16[4,16,2176]{2,1,0:T(8,128)(2,1)S(1)}, bf16[4,16,2176]{2,1,0:T(8,128)(2,1)S(1)}, u32[]{:S(2)}, u32[]{:S(2)}) collective-permute-start(bf16[4,16,2176]{2,1,0:T(8,128)(2,1)S(1)} %pad_maximum_fusion), channel_id=1, source_target_pairs={{0,2},{1,3},{2,0},{3,1},{4,6},{5,7},{6,4},{7,5},{8,10},{9,11},{10,... | collective-permute-start | bytes 835592 | tf_op jit(solution)/shard_map/ppermute | solution.py:37
  21.4 2.1 %collective-permute-start.4 = (bf16[8,16,2176]{2,1,0:T(8,128)(2,1)S(1)}, bf16[8,16,2176]{2,1,0:T(8,128)(2,1)S(1)}, u32[]{:S(2)}, u32[]{:S(2)}) collective-permute-start(bf16[8,16,2176]{2,1,0:T(8,128)(2,1)S(1)} %get-tuple-element.14), channel_id=1, source_target_pairs={{0,1},{1,0},{2,3},{3,2},{4,5},{5,4},{6,7},{7,6},{8,9},{9,8},{10,11... | collective-permute-start | bytes 1671176 | tf_op jit(solution)/shard_map/ppermute | solution.py:37
  23.4 0.7 %copy-start.3 = (bf16[256,768]{1,0:T(8,128)(2,1)}, bf16[256,768]{1,0:T(8,128)(2,1)S(1)}, u32[]{:S(2)}) copy-start(bf16[256,768]{1,0:T(8,128)(2,1)S(1)} %convert_dynamic-update-slice_fusion.1) | copy-start | bytes 1179652
  25.1 5.0 %copy-start.2 = (bf16[768,256]{1,0:T(8,128)(2,1)S(1)}, bf16[768,256]{1,0:T(8,128)(2,1)}, u32[]{:S(2)}) copy-start(bf16[768,256]{1,0:T(8,128)(2,1)} %param.5) | copy-start | bytes 1179652
  31.5 1.6 %collective-permute-start.5 = (f32[2,4,24,256]{3,2,1,0:T(8,128)S(1)}, f32[2,4,24,256]{3,2,1,0:T(8,128)S(1)}, u32[]{:S(2)}, u32[]{:S(2)}) collective-permute-start(f32[2,4,24,256]{3,2,1,0:T(8,128)S(1)} %bitcast.81), channel_id=1, source_target_pairs={{0,1},{1,0},{2,3},{3,2},{4,5},{5,4},{6,7},{7,6},{8,9},{9,8},{10,11... | collective-permute-start | bytes 589832 | tf_op jit(solution)/shard_map/ppermute | solution.py:37
  33.2 5.1 %collective-permute-start.6 = (f32[4,24,256]{2,1,0:T(8,128)S(1)}, f32[4,24,256]{2,1,0:T(8,128)S(1)}, u32[]{:S(2)}, u32[]{:S(2)}) collective-permute-start(f32[4,24,256]{2,1,0:T(8,128)S(1)} %slice_bitcast_fusion), channel_id=1, source_target_pairs={{0,2},{1,3},{2,0},{3,1},{4,6},{5,7},{6,4},{7,5},{8,10},{9,11},{10,... | collective-permute-start | bytes 294920 | tf_op jit(solution)/shard_map/ppermute | solution.py:37
  38.3 4.5 %collective-permute-start.7 = (f32[24,256]{1,0:T(8,128)S(1)}, f32[24,256]{1,0:T(8,128)S(1)}, u32[]{:S(2)}, u32[]{:S(2)}) collective-permute-start(f32[24,256]{1,0:T(8,128)S(1)} %get-tuple-element.15), channel_id=1, source_target_pairs={{0,4},{1,5},{2,6},{3,7},{4,0},{5,1},{6,2},{7,3},{8,12},{9,13},{10,... | collective-permute-start | bytes 73736 | tf_op jit(solution)/shard_map/ppermute | solution.py:37
  39.0 5.4 %collective-permute-start.8 = (f32[24,256]{1,0:T(8,128)S(1)}, f32[24,256]{1,0:T(8,128)S(1)}, u32[]{:S(2)}, u32[]{:S(2)}) collective-permute-start(f32[24,256]{1,0:T(8,128)S(1)} %get-tuple-element.17), channel_id=1, source_target_pairs={{0,8},{1,9},{2,10},{3,11},{4,12},{5,13},{6,14},{7,15},{8,0},{9,1},... | collective-permute-start | bytes 73736 | tf_op jit(solution)/shard_map/ppermute | solution.py:37
  42.5 5.6 %collective-permute-start.9 = (f32[24,256]{1,0:T(8,128)S(1)}, f32[24,256]{1,0:T(8,128)S(1)}, u32[]{:S(2)}, u32[]{:S(2)}) collective-permute-start(f32[24,256]{1,0:T(8,128)S(1)} %get-tuple-element.16), channel_id=1, source_target_pairs={{0,12},{1,13},{2,14},{3,15},{4,8},{5,9},{6,10},{7,11},{8,4},{9,5},... | collective-permute-start | bytes 73736 | tf_op jit(solution)/shard_map/ppermute | solution.py:37

commit v10 on v8

--- a/solution.py
+++ b/solution.py
@@ -69,10 +69,10 @@
     return jnp.concatenate(pieces, axis=0), results
 
 
-def scatter_rounds(buf, axis, groups, fan=4):
-    rounds = []
-    for group in groups:
-        if rounds and sum(len(g) for g in rounds[-1]) + len(group) <= fan:
+def scatter_rounds(buf, axis, groups, fan=3):
+    rounds = [[groups[0]]]
+    for group in groups[1:]:
+        if len(rounds) > 1 and sum(len(g) for g in rounds[-1]) + len(group) <= fan:
             rounds[-1].append(group)
         else:
             rounds.append([group])

time: 53.2 us -> 44.3 us (0.83)
  starting transfers between devices: 28.7 us -> 18.7 us
  waiting for transfers between devices: 7.97 us -> 9.35 us
    ppermute x20 -> x13, starting transfers between devices: 28.7 us -> 18.7 us  [swap(): return lax.ppermute(x, axis, [(i, i ^ mask) for i in range(count)])]
    ppermute x20 -> x13, waiting for transfers between devices: 7.97 us -> 9.35 us  [swap(): return lax.ppermute(x, axis, [(i, i ^ mask) for i in range(count)])]
  transfers between devices with their start and end apart: 20 -> 13, of which waited for: 6 -> 7; matrix products, arithmetic and copies ran while one was open for 20% -> 24% of each run, Pallas kernels for 0% -> 0%
where the time goes in v10:
time: 44.3 us; the launch traced here: 44.1 us
  starting transfers between devices  18.7 us (42%)
  waiting for transfers between devices  9.35 us (21%)
  other arithmetic  8.13 us (18%)
  matrix products  7.13 us (16%)
  local copies, waits for them, and re-layouts  0.51 us (1%)
    ppermute x13, starting transfers between devices, swap(): return lax.ppermute(x, axis, [(i, i ^ mask) for i in range(count)])  18.7 us
    ppermute x13, waiting for transfers between devices, swap(): return lax.ppermute(x, axis, [(i, i ^ mask) for i in range(count)])  9.35 us
    dot_general x6, matrix products, piece_weights(): lax.dot_general(rows, lib_ext, (((1,), (1,)), ((), ())), preferred_elemen...  6.83 us
    reduce_sum x1, other arithmetic, shards(): lib_sq = jnp.sum(jnp.square(library.astype(jnp.float32)), axis=1)  2.57 us
    reduce_sum x6, other arithmetic, piece_weights(): q_sq = jnp.sum(blockf * blockf, axis=1)  1.7 us
    reduce_sum x1, other arithmetic, shards(): jnp.sum(values, axis=0)  1.29 us
  transfers between devices with their start and end apart: 13, of which 7 were waited for; matrix products, arithmetic and copies ran while one was open for 24% of the time, Pallas kernels for 0%

profile of v10, /device:TPU:0, one launch (start us, length us, event | category | flops | bytes accessed | tf_op | source)
XLA Modules:
  0.0 44.1 jit_solution(17548452365803011405)
XLA Ops:
  0.0 0.0 copy-start.1
  0.0 0.0 copy-start
  0.0 1.3 %convert_reduce_fusion = (f32[256]{0:T(256)S(1)}, f32[256]{0:T(256)S(1)}) fusion(bf16[768,256]{1,0:T(8,128)(2,1)} %param.5), kind=kLoop, calls=%fused_computation.15 | loop fusion | flops 785920 | bytes 395264 | tf_op jit(solution)/shard_map/reduce_sum | solution.py:97
  1.3 0.8 %fusion.86 = bf16[1,16,2176]{2,1,0:T(8,128)(2,1)S(1)} fusion(bf16[16,128]{1,0:T(8,128)(2,1)S(1)} %fusion.100, bf16[16,2048]{1,0:T(8,128)(2,1)} %param.3), kind=kLoop, calls=%fused_computation.62 | loop fusion | flops 139264 | bytes 139264 | tf_op jit(solution)/shard_map/broadcast_in_dim | solution.py:61
  2.2 3.1 %collective-permute-start = (bf16[1,16,2176]{2,1,0:T(8,128)(2,1)S(1)}, bf16[1,16,2176]{2,1,0:T(8,128)(2,1)S(1)}, u32[]{:S(2)}, u32[]{:S(2)}) collective-permute-start(bf16[1,16,2176]{2,1,0:T(8,128)(2,1)S(1)} %fusion.86), channel_id=1, source_target_pairs={{0,4},{1,5},{2,6},{3,7},{4,0},{5,1},{6,2},{7,3},{8,12},{9,13},{10,... | collective-permute-start | bytes 208904 | tf_op jit(solution)/shard_map/ppermute | solution.py:37
  5.2 2.6 %collective-permute-start.1 = (bf16[1,16,2176]{2,1,0:T(8,128)(2,1)S(1)}, bf16[1,16,2176]{2,1,0:T(8,128)(2,1)S(1)}, u32[]{:S(2)}, u32[]{:S(2)}) collective-permute-start(bf16[1,16,2176]{2,1,0:T(8,128)(2,1)S(1)} %fusion.86), channel_id=1, source_target_pairs={{0,8},{1,9},{2,10},{3,11},{4,12},{5,13},{6,14},{7,15},{8,0},{9,1},... | collective-permute-start | bytes 208904 | tf_op jit(solution)/shard_map/ppermute | solution.py:37
  7.8 0.0 collective-permute-start.2
  7.8 0.8 %constant_dynamic-update-slice_fusion.14 = (bf16[16,16,2176]{2,1,0:T(8,128)(2,1)S(1)}, bf16[8,16,2176]{2,1,0:T(8,128)(2,1)S(1)}) fusion(bf16[16,128]{1,0:T(8,128)(2,1)S(1)} %fusion.100, bf16[16,2048]{1,0:T(8,128)(2,1)} %param.3), kind=kLoop, calls=%fused_computation.77 | loop fusion | flops 139262 | bytes 208896
  8.7 1.0 %multiply_reduce_fusion.6 = f32[16]{0:T(128)S(1)} fusion(bf16[16,2048]{1,0:T(8,128)(2,1)} %param.3), kind=kLoop, calls=%fused_computation.42 | loop fusion | flops 98288 | bytes 65600 | tf_op jit(solution)/shard_map/reduce_sum | solution.py:26
  9.6 2.6 %multiply_reduce_fusion = f32[768]{0:T(1024)S(1)} fusion(bf16[768,2048]{1,0:T(8,128)(2,1)} %param.4), kind=kLoop, calls=%fused_computation | loop fusion | flops 4717824 | bytes 3148800 | tf_op jit(solution)/shard_map/reduce_sum | solution.py:105
  12.2 0.0 copy-done.1
  12.2 0.0 copy-done
  12.2 1.1 %fusion.112 = (f32[16]{0:T(128)S(1)}, bf16[16,768]{1,0:T(8,128)(2,1)S(1)}) fusion(f32[768]{0:T(1024)S(1)} %multiply_reduce_fusion, f32[16]{0:T(128)S(1)} %multiply_reduce_fusion.6, bf16[768,2048]{1,0:T(8,128)(2,1)S(1)} %copy-done, bf16[16,128]{1,0:T(8,128)(2,1)S(1)} %fusion.100, bf16[16,2048]{1,0:T(8,128)(2,1)S(1)} %copy-done.1), kind=kOutput, calls=%fused_computation.123 | convolution fusion | flops 53702640 | bytes 3243136 | tf_op jit(solution)/shard_map/dot_general | solution.py:27
  13.3 0.0 collective-permute-done
  13.3 0.0 collective-permute-done.1
  13.3 0.7 %collective-permute-done.2 = bf16[1,16,2176]{2,1,0:T(8,128)(2,1)S(1)} collective-permute-done((bf16[1,16,2176]{2,1,0:T(8,128)(2,1)S(1)}, bf16[1,16,2176]{2,1,0:T(8,128)(2,1)S(1)}, u32[]{:S(2)}, u32[]{:S(2)}) %collective-permute-start.2) | collective-permute-done | bytes 69664 | tf_op jit(solution)/shard_map/ppermute | solution.py:37
  14.1 1.6 %collective-permute-start.3 = (bf16[4,16,2176]{2,1,0:T(8,128)(2,1)S(1)}, bf16[4,16,2176]{2,1,0:T(8,128)(2,1)S(1)}, u32[]{:S(2)}, u32[]{:S(2)}) collective-permute-start(bf16[4,16,2176]{2,1,0:T(8,128)(2,1)S(1)} %pad_maximum_fusion), channel_id=1, source_target_pairs={{0,2},{1,3},{2,0},{3,1},{4,6},{5,7},{6,4},{7,5},{8,10},{9,11},{10,... | collective-permute-start | bytes 835592 | tf_op jit(solution)/shard_map/ppermute | solution.py:37
  15.7 0.1 multiply_reduce_fusion.5
  15.8 0.1 multiply_reduce_fusion.4
  15.9 0.1 multiply_reduce_fusion.3
  16.1 1.1 %fusion.113 = (f32[16]{0:T(128)S(1)}, bf16[16,768]{1,0:T(8,128)(2,1)S(1)}) fusion(f32[768]{0:T(1024)S(1)} %multiply_reduce_fusion, f32[16]{0:T(128)S(1)} %multiply_reduce_fusion.5, bf16[768,2048]{1,0:T(8,128)(2,1)S(1)} %copy-done, bf16[1,16,2176]{2,1,0:T(8,128)(2,1)S(1)} %collective-permute-done), kind=kOutput, calls=%fused_computation.124 | convolution fusion | flops 53563376 | bytes 3243136 | tf_op jit(solution)/shard_map/dot_general | solution.py:27
  17.1 1.1 %fusion.114 = (f32[16]{0:T(128)S(1)}, bf16[16,768]{1,0:T(8,128)(2,1)S(1)}) fusion(f32[768]{0:T(1024)S(1)} %multiply_reduce_fusion, f32[16]{0:T(128)S(1)} %multiply_reduce_fusion.4, bf16[768,2048]{1,0:T(8,128)(2,1)S(1)} %copy-done, bf16[1,16,2176]{2,1,0:T(8,128)(2,1)S(1)} %collective-permute-done.1), kind=kOutput, calls=%fused_computation.125 | convolution fusion | flops 53563376 | bytes 3243136 | tf_op jit(solution)/shard_map/dot_general | solution.py:27
  18.3 1.1 %fusion.115 = (f32[16]{0:T(128)S(1)}, bf16[16,768]{1,0:T(8,128)(2,1)S(1)}) fusion(f32[768]{0:T(1024)S(1)} %multiply_reduce_fusion, f32[16]{0:T(128)S(1)} %multiply_reduce_fusion.3, bf16[768,2048]{1,0:T(8,128)(2,1)S(1)} %copy-done, bf16[1,16,2176]{2,1,0:T(8,128)(2,1)S(1)} %collective-permute-done.2), kind=kOutput, calls=%fused_computation.126 | convolution fusion | flops 53563376 | bytes 3243136 | tf_op jit(solution)/shard_map/dot_general | solution.py:27
  19.3 2.0 %collective-permute-done.3 = bf16[4,16,2176]{2,1,0:T(8,128)(2,1)S(1)} collective-permute-done((bf16[4,16,2176]{2,1,0:T(8,128)(2,1)S(1)}, bf16[4,16,2176]{2,1,0:T(8,128)(2,1)S(1)}, u32[]{:S(2)}, u32[]{:S(2)}) %collective-permute-start.3) | collective-permute-done | bytes 278560 | tf_op jit(solution)/shard_map/ppermute | solution.py:37
  21.3 0.1 collective-permute-start.4
  21.4 0.2 multiply_reduce_fusion.2
  21.6 1.2 %fusion.116 = (f32[64]{0:T(128)S(1)}, bf16[64,768]{1,0:T(8,128)(2,1)S(1)}) fusion(f32[768]{0:T(1024)S(1)} %multiply_reduce_fusion, f32[64]{0:T(128)S(1)} %multiply_reduce_fusion.2, bf16[64,2176]{1,0:T(8,128)(2,1)S(1)} %bitcast.72, bf16[768,2048]{1,0:T(8,128)(2,1)S(1)} %copy-done), kind=kOutput, calls=%fused_computation.127 | convolution fusion | flops 214253504 | bytes 3526144 | tf_op jit(solution)/shard_map/dot_general | solution.py:27
  22.8 0.5 %collective-permute-done.4 = bf16[8,16,2176]{2,1,0:T(8,128)(2,1)S(1)} collective-permute-done((bf16[8,16,2176]{2,1,0:T(8,128)(2,1)S(1)}, bf16[8,16,2176]{2,1,0:T(8,128)(2,1)S(1)}, u32[]{:S(2)}, u32[]{:S(2)}) %collective-permute-start.4) | collective-permute-done | bytes 557088 | tf_op jit(solution)/shard_map/ppermute | solution.py:37
  23.4 0.1 constant_dynamic-update-slice_fusion.9
  23.5 0.2 multiply_reduce_fusion.1
  23.7 0.0 copy-start.2
  23.7 1.4 %fusion.117 = (f32[128]{0:T(128)S(1)}, bf16[128,768]{1,0:T(8,128)(2,1)S(1)}) fusion(f32[768]{0:T(1024)S(1)} %multiply_reduce_fusion, f32[128]{0:T(128)S(1)} %multiply_reduce_fusion.1, bf16[128,2176]{1,0:T(8,128)(2,1)S(1)} %bitcast.74, bf16[768,2048]{1,0:T(8,128)(2,1)S(1)} %copy-done), kind=kOutput, calls=%fused_computation.128 | convolution fusion | flops 428507008 | bytes 3903488 | tf_op jit(solution)/shard_map/dot_general | solution.py:27
  25.1 0.1 concatenate.35
  25.2 0.1 reshape.58
  25.4 0.0 copy-done.2
  25.4 0.3 fusion.26
  25.7 0.2 collective-permute-start.5
  25.9 1.3 %collective-permute-done.5 = f32[2,4,24,256]{3,2,1,0:T(8,128)S(1)} collective-permute-done((f32[2,4,24,256]{3,2,1,0:T(8,128)S(1)}, f32[2,4,24,256]{3,2,1,0:T(8,128)S(1)}, u32[]{:S(2)}, u32[]{:S(2)}) %collective-permute-start.5) | collective-permute-done | bytes 196640 | tf_op jit(solution)/shard_map/ppermute | solution.py:37
  27.3 1.6 %collective-permute-start.10 = (f32[24,256]{1,0:T(8,128)S(1)}, f32[24,256]{1,0:T(8,128)S(1)}, u32[]{:S(2)}, u32[]{:S(2)}) collective-permute-start(f32[24,256]{1,0:T(8,128)S(1)} %get-tuple-element.14), channel_id=1, source_target_pairs={{0,6},{1,7},{2,4},{3,5},{4,2},{5,3},{6,0},{7,1},{8,14},{9,15},{10,... | collective-permute-start | bytes 73736 | tf_op jit(solution)/shard_map/ppermute | solution.py:37
  28.9 3.4 %collective-permute-start.11 = (f32[24,256]{1,0:T(8,128)S(1)}, f32[24,256]{1,0:T(8,128)S(1)}, u32[]{:S(2)}, u32[]{:S(2)}) collective-permute-start(f32[24,256]{1,0:T(8,128)S(1)} %get-tuple-element.13), channel_id=1, source_target_pairs={{0,10},{1,11},{2,8},{3,9},{4,14},{5,15},{6,12},{7,13},{8,2},{9,3},... | collective-permute-start | bytes 73736 | tf_op jit(solution)/shard_map/ppermute | solution.py:37
  32.3 1.2 %collective-permute-start.12 = (f32[24,256]{1,0:T(8,128)S(1)}, f32[24,256]{1,0:T(8,128)S(1)}, u32[]{:S(2)}, u32[]{:S(2)}) collective-permute-start(f32[24,256]{1,0:T(8,128)S(1)} %get-tuple-element.12), channel_id=1, source_target_pairs={{0,14},{1,15},{2,12},{3,13},{4,10},{5,11},{6,8},{7,9},{8,6},{9,7},... | collective-permute-start | bytes 73736 | tf_op jit(solution)/shard_map/ppermute | solution.py:37
  33.6 0.0 collective-permute-start.6
  33.6 4.1 %collective-permute-start.7 = (f32[24,256]{1,0:T(8,128)S(1)}, f32[24,256]{1,0:T(8,128)S(1)}, u32[]{:S(2)}, u32[]{:S(2)}) collective-permute-start(f32[24,256]{1,0:T(8,128)S(1)} %get-tuple-element.17), channel_id=1, source_target_pairs={{0,8},{1,9},{2,10},{3,11},{4,12},{5,13},{6,14},{7,15},{8,0},{9,1},... | collective-permute-start | bytes 73736 | tf_op jit(solution)/shard_map/ppermute | solution.py:37
  37.7 0.0 collective-permute-done.10
  37.7 0.3 collective-permute-start.8
  38.0 0.0 collective-permute-done.11
  38.0 0.5 %collective-permute-start.9 = (f32[24,256]{1,0:T(8,128)S(1)}, f32[24,256]{1,0:T(8,128)S(1)}, u32[]{:S(2)}, u32[]{:S(2)}) collective-permute-start(f32[24,256]{1,0:T(8,128)S(1)} %get-tuple-element.15), channel_id=1, source_target_pairs={{0,2},{1,3},{2,0},{3,1},{4,6},{5,7},{6,4},{7,5},{8,10},{9,11},{10,... | collective-permute-start | bytes 73736 | tf_op jit(solution)/shard_map/ppermute | solution.py:37
  38.5 0.4 collective-permute-done.12
  38.9 0.0 collective-permute-done.6
  38.9 0.6 %collective-permute-done.7 = f32[24,256]{1,0:T(8,128)S(1)} collective-permute-done((f32[24,256]{1,0:T(8,128)S(1)}, f32[24,256]{1,0:T(8,128)S(1)}, u32[]{:S(2)}, u32[]{:S(2)}) %collective-permute-start.7) | collective-permute-done | bytes 24608 | tf_op jit(solution)/shard_map/ppermute | solution.py:37
  39.5 3.8 %collective-permute-done.8 = f32[24,256]{1,0:T(8,128)S(1)} collective-permute-done((f32[24,256]{1,0:T(8,128)S(1)}, f32[24,256]{1,0:T(8,128)S(1)}, u32[]{:S(2)}, u32[]{:S(2)}) %collective-permute-start.8) | collective-permute-done | bytes 24608 | tf_op jit(solution)/shard_map/ppermute | solution.py:37
  43.3 0.0 collective-permute-done.9
  43.4 0.7 %slice_divide_fusion = f32[16,256]{1,0:T(8,128)} fusion(f32[24,256]{1,0:T(8,128)S(1)} %fusion.94, f32[16]{0:T(128)S(1)} %slice.119), kind=kLoop, calls=%fused_computation.96 | loop fusion | flops 4096 | bytes 32832 | tf_op jit(solution)/shard_map/div | solution.py:130
  (26 shorter events, 0.5 us)
Async XLA Ops:
  0.0 12.2 %copy-start.1 = (bf16[16,2048]{1,0:T(8,128)(2,1)S(1)}, bf16[16,2048]{1,0:T(8,128)(2,1)}, u32[]{:S(2)}) copy-start(bf16[16,2048]{1,0:T(8,128)(2,1)} %param.3) | copy-start | bytes 196612
  0.0 12.2 %copy-start = (bf16[768,2048]{1,0:T(8,128)(2,1)S(1)}, bf16[768,2048]{1,0:T(8,128)(2,1)}, u32[]{:S(2)}) copy-start(bf16[768,2048]{1,0:T(8,128)(2,1)} %param.4) | copy-start | bytes 9437188
  2.2 11.1 %collective-permute-start = (bf16[1,16,2176]{2,1,0:T(8,128)(2,1)S(1)}, bf16[1,16,2176]{2,1,0:T(8,128)(2,1)S(1)}, u32[]{:S(2)}, u32[]{:S(2)}) collective-permute-start(bf16[1,16,2176]{2,1,0:T(8,128)(2,1)S(1)} %fusion.86), channel_id=1, source_target_pairs={{0,4},{1,5},{2,6},{3,7},{4,0},{5,1},{6,2},{7,3},{8,12},{9,13},{10,... | collective-permute-start | bytes 208904 | tf_op jit(solution)/shard_map/ppermute | solution.py:37
  5.2 8.1 %collective-permute-start.1 = (bf16[1,16,2176]{2,1,0:T(8,128)(2,1)S(1)}, bf16[1,16,2176]{2,1,0:T(8,128)(2,1)S(1)}, u32[]{:S(2)}, u32[]{:S(2)}) collective-permute-start(bf16[1,16,2176]{2,1,0:T(8,128)(2,1)S(1)} %fusion.86), channel_id=1, source_target_pairs={{0,8},{1,9},{2,10},{3,11},{4,12},{5,13},{6,14},{7,15},{8,0},{9,1},... | collective-permute-start | bytes 208904 | tf_op jit(solution)/shard_map/ppermute | solution.py:37
  7.8 6.2 %collective-permute-start.2 = (bf16[1,16,2176]{2,1,0:T(8,128)(2,1)S(1)}, bf16[1,16,2176]{2,1,0:T(8,128)(2,1)S(1)}, u32[]{:S(2)}, u32[]{:S(2)}) collective-permute-start(bf16[1,16,2176]{2,1,0:T(8,128)(2,1)S(1)} %fusion.86), channel_id=1, source_target_pairs={{0,12},{1,13},{2,14},{3,15},{4,8},{5,9},{6,10},{7,11},{8,4},{9,5},... | collective-permute-start | bytes 208904 | tf_op jit(solution)/shard_map/ppermute | solution.py:37
  14.1 7.2 %collective-permute-start.3 = (bf16[4,16,2176]{2,1,0:T(8,128)(2,1)S(1)}, bf16[4,16,2176]{2,1,0:T(8,128)(2,1)S(1)}, u32[]{:S(2)}, u32[]{:S(2)}) collective-permute-start(bf16[4,16,2176]{2,1,0:T(8,128)(2,1)S(1)} %pad_maximum_fusion), channel_id=1, source_target_pairs={{0,2},{1,3},{2,0},{3,1},{4,6},{5,7},{6,4},{7,5},{8,10},{9,11},{10,... | collective-permute-start | bytes 835592 | tf_op jit(solution)/shard_map/ppermute | solution.py:37
  21.3 2.0 %collective-permute-start.4 = (bf16[8,16,2176]{2,1,0:T(8,128)(2,1)S(1)}, bf16[8,16,2176]{2,1,0:T(8,128)(2,1)S(1)}, u32[]{:S(2)}, u32[]{:S(2)}) collective-permute-start(bf16[8,16,2176]{2,1,0:T(8,128)(2,1)S(1)} %get-tuple-element.10), channel_id=1, source_target_pairs={{0,1},{1,0},{2,3},{3,2},{4,5},{5,4},{6,7},{7,6},{8,9},{9,8},{10,11... | collective-permute-start | bytes 1671176 | tf_op jit(solution)/shard_map/ppermute | solution.py:37
  23.7 1.6 %copy-start.2 = (bf16[768,256]{1,0:T(8,128)(2,1)S(1)}, bf16[768,256]{1,0:T(8,128)(2,1)}, u32[]{:S(2)}) copy-start(bf16[768,256]{1,0:T(8,128)(2,1)} %param.5) | copy-start | bytes 1179652
  25.7 1.5 %collective-permute-start.5 = (f32[2,4,24,256]{3,2,1,0:T(8,128)S(1)}, f32[2,4,24,256]{3,2,1,0:T(8,128)S(1)}, u32[]{:S(2)}, u32[]{:S(2)}) collective-permute-start(f32[2,4,24,256]{3,2,1,0:T(8,128)S(1)} %bitcast.86), channel_id=1, source_target_pairs={{0,1},{1,0},{2,3},{3,2},{4,5},{5,4},{6,7},{7,6},{8,9},{9,8},{10,11... | collective-permute-start | bytes 589832 | tf_op jit(solution)/shard_map/ppermute | solution.py:37
  27.3 10.4 %collective-permute-start.10 = (f32[24,256]{1,0:T(8,128)S(1)}, f32[24,256]{1,0:T(8,128)S(1)}, u32[]{:S(2)}, u32[]{:S(2)}) collective-permute-start(f32[24,256]{1,0:T(8,128)S(1)} %get-tuple-element.14), channel_id=1, source_target_pairs={{0,6},{1,7},{2,4},{3,5},{4,2},{5,3},{6,0},{7,1},{8,14},{9,15},{10,... | collective-permute-start | bytes 73736 | tf_op jit(solution)/shard_map/ppermute | solution.py:37
  28.9 9.1 %collective-permute-start.11 = (f32[24,256]{1,0:T(8,128)S(1)}, f32[24,256]{1,0:T(8,128)S(1)}, u32[]{:S(2)}, u32[]{:S(2)}) collective-permute-start(f32[24,256]{1,0:T(8,128)S(1)} %get-tuple-element.13), channel_id=1, source_target_pairs={{0,10},{1,11},{2,8},{3,9},{4,14},{5,15},{6,12},{7,13},{8,2},{9,3},... | collective-permute-start | bytes 73736 | tf_op jit(solution)/shard_map/ppermute | solution.py:37
  32.3 6.5 %collective-permute-start.12 = (f32[24,256]{1,0:T(8,128)S(1)}, f32[24,256]{1,0:T(8,128)S(1)}, u32[]{:S(2)}, u32[]{:S(2)}) collective-permute-start(f32[24,256]{1,0:T(8,128)S(1)} %get-tuple-element.12), channel_id=1, source_target_pairs={{0,14},{1,15},{2,12},{3,13},{4,10},{5,11},{6,8},{7,9},{8,6},{9,7},... | collective-permute-start | bytes 73736 | tf_op jit(solution)/shard_map/ppermute | solution.py:37
  33.6 5.3 %collective-permute-start.6 = (f32[24,256]{1,0:T(8,128)S(1)}, f32[24,256]{1,0:T(8,128)S(1)}, u32[]{:S(2)}, u32[]{:S(2)}) collective-permute-start(f32[24,256]{1,0:T(8,128)S(1)} %get-tuple-element.11), channel_id=1, source_target_pairs={{0,4},{1,5},{2,6},{3,7},{4,0},{5,1},{6,2},{7,3},{8,12},{9,13},{10,... | collective-permute-start | bytes 73736 | tf_op jit(solution)/shard_map/ppermute | solution.py:37
  33.6 5.9 %collective-permute-start.7 = (f32[24,256]{1,0:T(8,128)S(1)}, f32[24,256]{1,0:T(8,128)S(1)}, u32[]{:S(2)}, u32[]{:S(2)}) collective-permute-start(f32[24,256]{1,0:T(8,128)S(1)} %get-tuple-element.17), channel_id=1, source_target_pairs={{0,8},{1,9},{2,10},{3,11},{4,12},{5,13},{6,14},{7,15},{8,0},{9,1},... | collective-permute-start | bytes 73736 | tf_op jit(solution)/shard_map/ppermute | solution.py:37
  37.7 5.6 %collective-permute-start.8 = (f32[24,256]{1,0:T(8,128)S(1)}, f32[24,256]{1,0:T(8,128)S(1)}, u32[]{:S(2)}, u32[]{:S(2)}) collective-permute-start(f32[24,256]{1,0:T(8,128)S(1)} %get-tuple-element.16), channel_id=1, source_target_pairs={{0,12},{1,13},{2,14},{3,15},{4,8},{5,9},{6,10},{7,11},{8,4},{9,5},... | collective-permute-start | bytes 73736 | tf_op jit(solution)/shard_map/ppermute | solution.py:37
  38.0 5.3 %collective-permute-start.9 = (f32[24,256]{1,0:T(8,128)S(1)}, f32[24,256]{1,0:T(8,128)S(1)}, u32[]{:S(2)}, u32[]{:S(2)}) collective-permute-start(f32[24,256]{1,0:T(8,128)S(1)} %get-tuple-element.15), channel_id=1, source_target_pairs={{0,2},{1,3},{2,0},{3,1},{4,6},{5,7},{6,4},{7,5},{8,10},{9,11},{10,... | collective-permute-start | bytes 73736 | tf_op jit(solution)/shard_map/ppermute | solution.py:37

commit v11 on v7

--- a/solution.py
+++ b/solution.py
@@ -59,13 +59,15 @@
 
 def gather_rounds(packet, axis, groups, work):
     pieces = [packet[None]]
-    results = [work(pieces[0])]
+    results = []
+    fresh = [packet[None]]
     for group in reversed(groups):
         buf = jnp.concatenate(pieces, axis=0) if len(pieces) > 1 else pieces[0]
-        for m in offsets(group)[1:]:
-            got = swap(buf, axis, m)
-            pieces.append(got)
-            results.append(work(got))
+        got = [swap(buf, axis, m) for m in offsets(group)[1:]]
+        pieces += got
+        fresh += got
+        results.append(work(jnp.concatenate(fresh, axis=0)))
+        fresh = []
     return jnp.concatenate(pieces, axis=0), results
 
 

time: 43 us -> 41.9 us (0.974)
  matrix products: 7.13 us -> 4.1 us
  waiting for transfers between devices: 13.2 us -> 16.1 us
  other arithmetic: 8.14 us -> 7.01 us
    dot_general x6 -> x3, matrix products: 6.83 us -> 3.8 us  [piece_weights(): lax.dot_general(rows, lib_ext, (((1,), (1,)), ((), ())), preferred_elemen...]
    ppermute x10, waiting for transfers between devices: 13.2 us -> 16.1 us  [swap(): return lax.ppermute(x, axis, [(i, i ^ mask) for i in range(count)])]
    reduce_sum x6 -> x3, other arithmetic: 1.7 us -> 0.5 us  [piece_weights(): q_sq = jnp.sum(blockf * blockf, axis=1)]
  transfers between devices with their start and end apart: 10 -> 10, of which waited for: 7 -> 7; matrix products, arithmetic and copies ran while one was open for 25% -> 15% of each run, Pallas kernels for 0% -> 0%
where the time goes in v11:
time: 41.9 us; the launch traced here: 41.7 us
  waiting for transfers between devices  16.1 us (38%)
  starting transfers between devices  13.9 us (33%)
  other arithmetic  7.01 us (17%)
  matrix products  4.1 us (10%)
    ppermute x10, waiting for transfers between devices, swap(): return lax.ppermute(x, axis, [(i, i ^ mask) for i in range(count)])  16.1 us
    ppermute x10, starting transfers between devices, swap(): return lax.ppermute(x, axis, [(i, i ^ mask) for i in range(count)])  13.9 us
    dot_general x3, matrix products, piece_weights(): lax.dot_general(rows, lib_ext, (((1,), (1,)), ((), ())), preferred_elemen...  3.8 us
    reduce_sum x1, other arithmetic, shards(): lib_sq = jnp.sum(jnp.square(library.astype(jnp.float32)), axis=1)  2.72 us
    reduce_sum x1, other arithmetic, shards(): jnp.sum(values, axis=0)  1.14 us
    unnamed x1, other arithmetic  0.85 us
    broadcast_in_dim x1, other arithmetic, gather_rounds(): fresh = [packet[None]]  0.85 us
  transfers between devices with their start and end apart: 10, of which 7 were waited for; matrix products, arithmetic and copies ran while one was open for 15% of the time, Pallas kernels for 0%

profile of v11, /device:TPU:0, one launch (start us, length us, event | category | flops | bytes accessed | tf_op | source)
XLA Modules:
  0.0 41.7 jit_solution(9678984782616261698)
XLA Ops:
  0.0 1.1 %convert_reduce_fusion = (f32[256]{0:T(256)S(1)}, f32[256]{0:T(256)S(1)}) fusion(bf16[768,256]{1,0:T(8,128)(2,1)} %param.5), kind=kLoop, calls=%fused_computation.9 | loop fusion | flops 785920 | bytes 395264 | tf_op jit(solution)/shard_map/reduce_sum | solution.py:90
  1.2 0.8 %maximum_bitcast_fusion = bf16[1,16,2176]{2,1,0:T(8,128)(2,1)S(1)} fusion(bf16[16,128]{1,0:T(8,128)(2,1)S(1)} %fusion.62, bf16[16,2048]{1,0:T(8,128)(2,1)} %param.3), kind=kLoop, calls=%fused_computation.45 | loop fusion | flops 139264 | bytes 139264 | tf_op jit(solution)/shard_map/broadcast_in_dim | solution.py:63
  2.0 3.1 %collective-permute-start = (bf16[1,16,2176]{2,1,0:T(8,128)(2,1)S(1)}, bf16[1,16,2176]{2,1,0:T(8,128)(2,1)S(1)}, u32[]{:S(2)}, u32[]{:S(2)}) collective-permute-start(bf16[1,16,2176]{2,1,0:T(8,128)(2,1)S(1)} %maximum_bitcast_fusion), channel_id=1, source_target_pairs={{0,4},{1,5},{2,6},{3,7},{4,0},{5,1},{6,2},{7,3},{8,12},{9,13},{10,... | collective-permute-start | bytes 208904 | tf_op jit(solution)/shard_map/ppermute | solution.py:37
  5.1 2.6 %collective-permute-start.1 = (bf16[1,16,2176]{2,1,0:T(8,128)(2,1)S(1)}, bf16[1,16,2176]{2,1,0:T(8,128)(2,1)S(1)}, u32[]{:S(2)}, u32[]{:S(2)}) collective-permute-start(bf16[1,16,2176]{2,1,0:T(8,128)(2,1)S(1)} %maximum_bitcast_fusion), channel_id=1, source_target_pairs={{0,8},{1,9},{2,10},{3,11},{4,12},{5,13},{6,14},{7,15},{8,0},{9,1},... | collective-permute-start | bytes 208904 | tf_op jit(solution)/shard_map/ppermute | solution.py:37
  7.7 0.0 collective-permute-start.2
  7.7 0.8 %constant_dynamic-update-slice_fusion.10 = (bf16[16,16,2176]{2,1,0:T(8,128)(2,1)S(1)}, bf16[8,16,2176]{2,1,0:T(8,128)(2,1)S(1)}) fusion(bf16[16,128]{1,0:T(8,128)(2,1)S(1)} %fusion.62, bf16[16,2048]{1,0:T(8,128)(2,1)} %param.3), kind=kLoop, calls=%fused_computation.67 | loop fusion | flops 139262 | bytes 208896
  8.5 0.0 copy-start
  8.5 2.7 %multiply_reduce_fusion = f32[768]{0:T(1024)S(1)} fusion(bf16[768,2048]{1,0:T(8,128)(2,1)} %param.4), kind=kLoop, calls=%fused_computation | loop fusion | flops 4717824 | bytes 3148800 | tf_op jit(solution)/shard_map/reduce_sum | solution.py:98
  11.3 0.0 collective-permute-done
  11.3 1.3 %collective-permute-done.1 = bf16[1,16,2176]{2,1,0:T(8,128)(2,1)S(1)} collective-permute-done((bf16[1,16,2176]{2,1,0:T(8,128)(2,1)S(1)}, bf16[1,16,2176]{2,1,0:T(8,128)(2,1)S(1)}, u32[]{:S(2)}, u32[]{:S(2)}) %collective-permute-start.1) | collective-permute-done | bytes 69664 | tf_op jit(solution)/shard_map/ppermute | solution.py:37
  12.6 1.3 %collective-permute-done.2 = bf16[1,16,2176]{2,1,0:T(8,128)(2,1)S(1)} collective-permute-done((bf16[1,16,2176]{2,1,0:T(8,128)(2,1)S(1)}, bf16[1,16,2176]{2,1,0:T(8,128)(2,1)S(1)}, u32[]{:S(2)}, u32[]{:S(2)}) %collective-permute-start.2) | collective-permute-done | bytes 69664 | tf_op jit(solution)/shard_map/ppermute | solution.py:37
  13.9 1.6 %collective-permute-start.3 = (bf16[4,16,2176]{2,1,0:T(8,128)(2,1)S(1)}, bf16[4,16,2176]{2,1,0:T(8,128)(2,1)S(1)}, u32[]{:S(2)}, u32[]{:S(2)}) collective-permute-start(bf16[4,16,2176]{2,1,0:T(8,128)(2,1)S(1)} %pad_maximum_fusion), channel_id=1, source_target_pairs={{0,2},{1,3},{2,0},{3,1},{4,6},{5,7},{6,4},{7,5},{8,10},{9,11},{10,... | collective-permute-start | bytes 835592 | tf_op jit(solution)/shard_map/ppermute | solution.py:37
  15.5 0.2 multiply_reduce_fusion.3
  15.7 4.9 %collective-permute-done.3 = bf16[4,16,2176]{2,1,0:T(8,128)(2,1)S(1)} collective-permute-done((bf16[4,16,2176]{2,1,0:T(8,128)(2,1)S(1)}, bf16[4,16,2176]{2,1,0:T(8,128)(2,1)S(1)}, u32[]{:S(2)}, u32[]{:S(2)}) %collective-permute-start.3) | collective-permute-done | bytes 278560 | tf_op jit(solution)/shard_map/ppermute | solution.py:37
  20.6 0.1 collective-permute-start.4
  20.7 0.0 copy-done
  20.7 1.2 %fusion.69 = (f32[64]{0:T(128)S(1)}, bf16[64,768]{1,0:T(8,128)(2,1)S(1)}) fusion(f32[768]{0:T(1024)S(1)} %multiply_reduce_fusion, f32[64]{0:T(128)S(1)} %multiply_reduce_fusion.3, bf16[64,2176]{1,0:T(8,128)(2,1)S(1)} %bitcast.49, bf16[768,2048]{1,0:T(8,128)(2,1)S(1)} %copy-done), kind=kOutput, calls=%fused_computation.91 | convolution fusion | flops 214253504 | bytes 3526144 | tf_op jit(solution)/shard_map/dot_general | solution.py:27
  21.9 0.2 multiply_reduce_fusion.2
  22.1 1.2 %fusion.70 = (f32[64]{0:T(128)S(1)}, bf16[64,768]{1,0:T(8,128)(2,1)S(1)}) fusion(f32[768]{0:T(1024)S(1)} %multiply_reduce_fusion, f32[64]{0:T(128)S(1)} %multiply_reduce_fusion.2, bf16[64,2176]{1,0:T(8,128)(2,1)S(1)} %bitcast.47, bf16[768,2048]{1,0:T(8,128)(2,1)S(1)} %copy-done), kind=kOutput, calls=%fused_computation.92 | convolution fusion | flops 214253504 | bytes 3526144 | tf_op jit(solution)/shard_map/dot_general | solution.py:27
  23.3 0.0 collective-permute-done.4
  23.3 0.1 constant_dynamic-update-slice_fusion.5
  23.5 0.2 multiply_reduce_fusion.1
  23.7 0.0 copy-start.1
  23.7 1.4 %fusion.68 = (f32[128]{0:T(128)S(1)}, bf16[128,768]{1,0:T(8,128)(2,1)S(1)}) fusion(f32[768]{0:T(1024)S(1)} %multiply_reduce_fusion, f32[128]{0:T(128)S(1)} %multiply_reduce_fusion.1, bf16[128,2176]{1,0:T(8,128)(2,1)S(1)} %bitcast.51, bf16[768,2048]{1,0:T(8,128)(2,1)S(1)} %copy-done), kind=kOutput, calls=%fused_computation.90 | convolution fusion | flops 428507008 | bytes 3903488 | tf_op jit(solution)/shard_map/dot_general | solution.py:27
  25.1 0.1 pad_maximum_fusion.3
  25.1 0.1 reshape.44
  25.3 0.0 copy-done.1
  25.3 0.3 fusion.20
  25.6 0.6 %collective-permute-start.5 = (f32[2,4,24,256]{3,2,1,0:T(8,128)S(1)}, f32[2,4,24,256]{3,2,1,0:T(8,128)S(1)}, u32[]{:S(2)}, u32[]{:S(2)}) collective-permute-start(f32[2,4,24,256]{3,2,1,0:T(8,128)S(1)} %bitcast.58), channel_id=1, source_target_pairs={{0,1},{1,0},{2,3},{3,2},{4,5},{5,4},{6,7},{7,6},{8,9},{9,8},{10,11... | collective-permute-start | bytes 589832 | tf_op jit(solution)/shard_map/ppermute | solution.py:37
  26.2 1.1 %collective-permute-done.5 = f32[2,4,24,256]{3,2,1,0:T(8,128)S(1)} collective-permute-done((f32[2,4,24,256]{3,2,1,0:T(8,128)S(1)}, f32[2,4,24,256]{3,2,1,0:T(8,128)S(1)}, u32[]{:S(2)}, u32[]{:S(2)}) %collective-permute-start.5) | collective-permute-done | bytes 196640 | tf_op jit(solution)/shard_map/ppermute | solution.py:37
  27.3 1.6 %collective-permute-start.6 = (f32[4,24,256]{2,1,0:T(8,128)S(1)}, f32[4,24,256]{2,1,0:T(8,128)S(1)}, u32[]{:S(2)}, u32[]{:S(2)}) collective-permute-start(f32[4,24,256]{2,1,0:T(8,128)S(1)} %slice_bitcast_fusion), channel_id=1, source_target_pairs={{0,2},{1,3},{2,0},{3,1},{4,6},{5,7},{6,4},{7,5},{8,10},{9,11},{10,... | collective-permute-start | bytes 294920 | tf_op jit(solution)/shard_map/ppermute | solution.py:37
  28.9 3.6 %collective-permute-done.6 = f32[4,24,256]{2,1,0:T(8,128)S(1)} collective-permute-done((f32[4,24,256]{2,1,0:T(8,128)S(1)}, f32[4,24,256]{2,1,0:T(8,128)S(1)}, u32[]{:S(2)}, u32[]{:S(2)}) %collective-permute-start.6) | collective-permute-done | bytes 98336 | tf_op jit(solution)/shard_map/ppermute | solution.py:37
  32.5 1.1 %collective-permute-start.7 = (f32[24,256]{1,0:T(8,128)S(1)}, f32[24,256]{1,0:T(8,128)S(1)}, u32[]{:S(2)}, u32[]{:S(2)}) collective-permute-start(f32[24,256]{1,0:T(8,128)S(1)} %get-tuple-element.17), channel_id=1, source_target_pairs={{0,4},{1,5},{2,6},{3,7},{4,0},{5,1},{6,2},{7,3},{8,12},{9,13},{10,... | collective-permute-start | bytes 73736 | tf_op jit(solution)/shard_map/ppermute | solution.py:37
  33.6 1.7 %collective-permute-start.8 = (f32[24,256]{1,0:T(8,128)S(1)}, f32[24,256]{1,0:T(8,128)S(1)}, u32[]{:S(2)}, u32[]{:S(2)}) collective-permute-start(f32[24,256]{1,0:T(8,128)S(1)} %get-tuple-element.19), channel_id=1, source_target_pairs={{0,8},{1,9},{2,10},{3,11},{4,12},{5,13},{6,14},{7,15},{8,0},{9,1},... | collective-permute-start | bytes 73736 | tf_op jit(solution)/shard_map/ppermute | solution.py:37
  35.3 1.6 %collective-permute-start.9 = (f32[24,256]{1,0:T(8,128)S(1)}, f32[24,256]{1,0:T(8,128)S(1)}, u32[]{:S(2)}, u32[]{:S(2)}) collective-permute-start(f32[24,256]{1,0:T(8,128)S(1)} %get-tuple-element.18), channel_id=1, source_target_pairs={{0,12},{1,13},{2,14},{3,15},{4,8},{5,9},{6,10},{7,11},{8,4},{9,5},... | collective-permute-start | bytes 73736 | tf_op jit(solution)/shard_map/ppermute | solution.py:37
  36.9 0.0 collective-permute-done.7
  36.9 1.6 %collective-permute-done.8 = f32[24,256]{1,0:T(8,128)S(1)} collective-permute-done((f32[24,256]{1,0:T(8,128)S(1)}, f32[24,256]{1,0:T(8,128)S(1)}, u32[]{:S(2)}, u32[]{:S(2)}) %collective-permute-start.8) | collective-permute-done | bytes 24608 | tf_op jit(solution)/shard_map/ppermute | solution.py:37
  38.6 2.4 %collective-permute-done.9 = f32[24,256]{1,0:T(8,128)S(1)} collective-permute-done((f32[24,256]{1,0:T(8,128)S(1)}, f32[24,256]{1,0:T(8,128)S(1)}, u32[]{:S(2)}, u32[]{:S(2)}) %collective-permute-start.9) | collective-permute-done | bytes 24608 | tf_op jit(solution)/shard_map/ppermute | solution.py:37
  41.0 0.7 %slice_divide_fusion = f32[16,256]{1,0:T(8,128)} fusion(f32[24,256]{1,0:T(8,128)S(1)} %fusion.56, f32[16]{0:T(128)S(1)} %slice.99), kind=kLoop, calls=%fused_computation.68 | loop fusion | flops 4096 | bytes 32832 | tf_op jit(solution)/shard_map/div | solution.py:123
  (22 shorter events, 0.4 us)
Async XLA Ops:
  2.0 9.2 %collective-permute-start = (bf16[1,16,2176]{2,1,0:T(8,128)(2,1)S(1)}, bf16[1,16,2176]{2,1,0:T(8,128)(2,1)S(1)}, u32[]{:S(2)}, u32[]{:S(2)}) collective-permute-start(bf16[1,16,2176]{2,1,0:T(8,128)(2,1)S(1)} %maximum_bitcast_fusion), channel_id=1, source_target_pairs={{0,4},{1,5},{2,6},{3,7},{4,0},{5,1},{6,2},{7,3},{8,12},{9,13},{10,... | collective-permute-start | bytes 208904 | tf_op jit(solution)/shard_map/ppermute | solution.py:37
  5.1 7.5 %collective-permute-start.1 = (bf16[1,16,2176]{2,1,0:T(8,128)(2,1)S(1)}, bf16[1,16,2176]{2,1,0:T(8,128)(2,1)S(1)}, u32[]{:S(2)}, u32[]{:S(2)}) collective-permute-start(bf16[1,16,2176]{2,1,0:T(8,128)(2,1)S(1)} %maximum_bitcast_fusion), channel_id=1, source_target_pairs={{0,8},{1,9},{2,10},{3,11},{4,12},{5,13},{6,14},{7,15},{8,0},{9,1},... | collective-permute-start | bytes 208904 | tf_op jit(solution)/shard_map/ppermute | solution.py:37
  7.7 6.2 %collective-permute-start.2 = (bf16[1,16,2176]{2,1,0:T(8,128)(2,1)S(1)}, bf16[1,16,2176]{2,1,0:T(8,128)(2,1)S(1)}, u32[]{:S(2)}, u32[]{:S(2)}) collective-permute-start(bf16[1,16,2176]{2,1,0:T(8,128)(2,1)S(1)} %maximum_bitcast_fusion), channel_id=1, source_target_pairs={{0,12},{1,13},{2,14},{3,15},{4,8},{5,9},{6,10},{7,11},{8,4},{9,5},... | collective-permute-start | bytes 208904 | tf_op jit(solution)/shard_map/ppermute | solution.py:37
  8.5 12.2 %copy-start = (bf16[768,2048]{1,0:T(8,128)(2,1)S(1)}, bf16[768,2048]{1,0:T(8,128)(2,1)}, u32[]{:S(2)}) copy-start(bf16[768,2048]{1,0:T(8,128)(2,1)} %param.4) | copy-start | bytes 9437188
  13.9 6.7 %collective-permute-start.3 = (bf16[4,16,2176]{2,1,0:T(8,128)(2,1)S(1)}, bf16[4,16,2176]{2,1,0:T(8,128)(2,1)S(1)}, u32[]{:S(2)}, u32[]{:S(2)}) collective-permute-start(bf16[4,16,2176]{2,1,0:T(8,128)(2,1)S(1)} %pad_maximum_fusion), channel_id=1, source_target_pairs={{0,2},{1,3},{2,0},{3,1},{4,6},{5,7},{6,4},{7,5},{8,10},{9,11},{10,... | collective-permute-start | bytes 835592 | tf_op jit(solution)/shard_map/ppermute | solution.py:37
  20.6 2.7 %collective-permute-start.4 = (bf16[8,16,2176]{2,1,0:T(8,128)(2,1)S(1)}, bf16[8,16,2176]{2,1,0:T(8,128)(2,1)S(1)}, u32[]{:S(2)}, u32[]{:S(2)}) collective-permute-start(bf16[8,16,2176]{2,1,0:T(8,128)(2,1)S(1)} %get-tuple-element.12), channel_id=1, source_target_pairs={{0,1},{1,0},{2,3},{3,2},{4,5},{5,4},{6,7},{7,6},{8,9},{9,8},{10,11... | collective-permute-start | bytes 1671176 | tf_op jit(solution)/shard_map/ppermute | solution.py:37
  23.7 1.6 %copy-start.1 = (bf16[768,256]{1,0:T(8,128)(2,1)S(1)}, bf16[768,256]{1,0:T(8,128)(2,1)}, u32[]{:S(2)}) copy-start(bf16[768,256]{1,0:T(8,128)(2,1)} %param.5) | copy-start | bytes 1179652
  25.6 1.6 %collective-permute-start.5 = (f32[2,4,24,256]{3,2,1,0:T(8,128)S(1)}, f32[2,4,24,256]{3,2,1,0:T(8,128)S(1)}, u32[]{:S(2)}, u32[]{:S(2)}) collective-permute-start(f32[2,4,24,256]{3,2,1,0:T(8,128)S(1)} %bitcast.58), channel_id=1, source_target_pairs={{0,1},{1,0},{2,3},{3,2},{4,5},{5,4},{6,7},{7,6},{8,9},{9,8},{10,11... | collective-permute-start | bytes 589832 | tf_op jit(solution)/shard_map/ppermute | solution.py:37
  27.3 5.1 %collective-permute-start.6 = (f32[4,24,256]{2,1,0:T(8,128)S(1)}, f32[4,24,256]{2,1,0:T(8,128)S(1)}, u32[]{:S(2)}, u32[]{:S(2)}) collective-permute-start(f32[4,24,256]{2,1,0:T(8,128)S(1)} %slice_bitcast_fusion), channel_id=1, source_target_pairs={{0,2},{1,3},{2,0},{3,1},{4,6},{5,7},{6,4},{7,5},{8,10},{9,11},{10,... | collective-permute-start | bytes 294920 | tf_op jit(solution)/shard_map/ppermute | solution.py:37
  32.5 4.5 %collective-permute-start.7 = (f32[24,256]{1,0:T(8,128)S(1)}, f32[24,256]{1,0:T(8,128)S(1)}, u32[]{:S(2)}, u32[]{:S(2)}) collective-permute-start(f32[24,256]{1,0:T(8,128)S(1)} %get-tuple-element.17), channel_id=1, source_target_pairs={{0,4},{1,5},{2,6},{3,7},{4,0},{5,1},{6,2},{7,3},{8,12},{9,13},{10,... | collective-permute-start | bytes 73736 | tf_op jit(solution)/shard_map/ppermute | solution.py:37
  33.6 5.0 %collective-permute-start.8 = (f32[24,256]{1,0:T(8,128)S(1)}, f32[24,256]{1,0:T(8,128)S(1)}, u32[]{:S(2)}, u32[]{:S(2)}) collective-permute-start(f32[24,256]{1,0:T(8,128)S(1)} %get-tuple-element.19), channel_id=1, source_target_pairs={{0,8},{1,9},{2,10},{3,11},{4,12},{5,13},{6,14},{7,15},{8,0},{9,1},... | collective-permute-start | bytes 73736 | tf_op jit(solution)/shard_map/ppermute | solution.py:37
  35.3 5.6 %collective-permute-start.9 = (f32[24,256]{1,0:T(8,128)S(1)}, f32[24,256]{1,0:T(8,128)S(1)}, u32[]{:S(2)}, u32[]{:S(2)}) collective-permute-start(f32[24,256]{1,0:T(8,128)S(1)} %get-tuple-element.18), channel_id=1, source_target_pairs={{0,12},{1,13},{2,14},{3,15},{4,8},{5,9},{6,10},{7,11},{8,4},{9,5},... | collective-permute-start | bytes 73736 | tf_op jit(solution)/shard_map/ppermute | solution.py:37

commit v12 on v11

--- a/solution.py
+++ b/solution.py
@@ -64,6 +64,8 @@
     for group in reversed(groups):
         buf = jnp.concatenate(pieces, axis=0) if len(pieces) > 1 else pieces[0]
         got = [swap(buf, axis, m) for m in offsets(group)[1:]]
+        if results:
+            got, results[-1] = lax.optimization_barrier((got, results[-1]))
         pieces += got
         fresh += got
         results.append(work(jnp.concatenate(fresh, axis=0)))

time: 41.9 us -> 40.9 us (0.976)
  waiting for transfers between devices: 16.1 us -> 15.4 us
    ppermute x10, waiting for transfers between devices: 16.1 us -> 15.4 us  [swap(): return lax.ppermute(x, axis, [(i, i ^ mask) for i in range(count)])]
  transfers between devices with their start and end apart: 10 -> 10, of which waited for: 7 -> 8; matrix products, arithmetic and copies ran while one was open for 15% -> 16% of each run, Pallas kernels for 0% -> 0%
where the time goes in v12:
time: 40.9 us; the launch traced here: 40.6 us
  waiting for transfers between devices  15.4 us (38%)
  starting transfers between devices  13.5 us (33%)
  other arithmetic  7.01 us (17%)
  matrix products  4.09 us (10%)
    ppermute x10, waiting for transfers between devices, swap(): return lax.ppermute(x, axis, [(i, i ^ mask) for i in range(count)])  15.4 us
    ppermute x10, starting transfers between devices, swap(): return lax.ppermute(x, axis, [(i, i ^ mask) for i in range(count)])  13.5 us
    dot_general x3, matrix products, piece_weights(): lax.dot_general(rows, lib_ext, (((1,), (1,)), ((), ())), preferred_elemen...  3.79 us
    reduce_sum x1, other arithmetic, shards(): lib_sq = jnp.sum(jnp.square(library.astype(jnp.float32)), axis=1)  2.72 us
    reduce_sum x1, other arithmetic, shards(): jnp.sum(values, axis=0)  1.14 us
    unnamed x1, other arithmetic  0.85 us
    broadcast_in_dim x1, other arithmetic, gather_rounds(): pieces = [packet[None]]  0.85 us
  transfers between devices with their start and end apart: 10, of which 8 were waited for; matrix products, arithmetic and copies ran while one was open for 16% of the time, Pallas kernels for 0%

profile of v12, /device:TPU:0, one launch (start us, length us, event | category | flops | bytes accessed | tf_op | source)
XLA Modules:
  0.0 40.6 jit_solution(9303253823762789734)
XLA Ops:
  0.0 1.1 %convert_reduce_fusion = (f32[256]{0:T(256)S(1)}, f32[256]{0:T(256)S(1)}) fusion(bf16[768,256]{1,0:T(8,128)(2,1)} %param.5), kind=kLoop, calls=%fused_computation.9 | loop fusion | flops 785920 | bytes 395264 | tf_op jit(solution)/shard_map/reduce_sum | solution.py:92
  1.2 0.8 %maximum_bitcast_fusion = bf16[1,16,2176]{2,1,0:T(8,128)(2,1)S(1)} fusion(bf16[16,128]{1,0:T(8,128)(2,1)S(1)} %fusion.62, bf16[16,2048]{1,0:T(8,128)(2,1)} %param.3), kind=kLoop, calls=%fused_computation.45 | loop fusion | flops 139264 | bytes 139264 | tf_op jit(solution)/shard_map/broadcast_in_dim | solution.py:61
  2.0 3.1 %collective-permute-start = (bf16[1,16,2176]{2,1,0:T(8,128)(2,1)S(1)}, bf16[1,16,2176]{2,1,0:T(8,128)(2,1)S(1)}, u32[]{:S(2)}, u32[]{:S(2)}) collective-permute-start(bf16[1,16,2176]{2,1,0:T(8,128)(2,1)S(1)} %maximum_bitcast_fusion), channel_id=1, source_target_pairs={{0,4},{1,5},{2,6},{3,7},{4,0},{5,1},{6,2},{7,3},{8,12},{9,13},{10,... | collective-permute-start | bytes 208904 | tf_op jit(solution)/shard_map/ppermute | solution.py:37
  5.1 2.6 %collective-permute-start.1 = (bf16[1,16,2176]{2,1,0:T(8,128)(2,1)S(1)}, bf16[1,16,2176]{2,1,0:T(8,128)(2,1)S(1)}, u32[]{:S(2)}, u32[]{:S(2)}) collective-permute-start(bf16[1,16,2176]{2,1,0:T(8,128)(2,1)S(1)} %maximum_bitcast_fusion), channel_id=1, source_target_pairs={{0,8},{1,9},{2,10},{3,11},{4,12},{5,13},{6,14},{7,15},{8,0},{9,1},... | collective-permute-start | bytes 208904 | tf_op jit(solution)/shard_map/ppermute | solution.py:37
  7.7 0.0 collective-permute-start.2
  7.7 0.8 %constant_dynamic-update-slice_fusion.10 = (bf16[16,16,2176]{2,1,0:T(8,128)(2,1)S(1)}, bf16[8,16,2176]{2,1,0:T(8,128)(2,1)S(1)}) fusion(bf16[16,128]{1,0:T(8,128)(2,1)S(1)} %fusion.62, bf16[16,2048]{1,0:T(8,128)(2,1)} %param.3), kind=kLoop, calls=%fused_computation.67 | loop fusion | flops 139262 | bytes 208896
  8.5 0.0 copy-start
  8.5 2.7 %multiply_reduce_fusion = f32[768]{0:T(1024)S(1)} fusion(bf16[768,2048]{1,0:T(8,128)(2,1)} %param.4), kind=kLoop, calls=%fused_computation | loop fusion | flops 4717824 | bytes 3148800 | tf_op jit(solution)/shard_map/reduce_sum | solution.py:100
  11.3 0.0 collective-permute-done
  11.3 1.3 %collective-permute-done.1 = bf16[1,16,2176]{2,1,0:T(8,128)(2,1)S(1)} collective-permute-done((bf16[1,16,2176]{2,1,0:T(8,128)(2,1)S(1)}, bf16[1,16,2176]{2,1,0:T(8,128)(2,1)S(1)}, u32[]{:S(2)}, u32[]{:S(2)}) %collective-permute-start.1) | collective-permute-done | bytes 69664 | tf_op jit(solution)/shard_map/ppermute | solution.py:37
  12.6 1.3 %collective-permute-done.2 = bf16[1,16,2176]{2,1,0:T(8,128)(2,1)S(1)} collective-permute-done((bf16[1,16,2176]{2,1,0:T(8,128)(2,1)S(1)}, bf16[1,16,2176]{2,1,0:T(8,128)(2,1)S(1)}, u32[]{:S(2)}, u32[]{:S(2)}) %collective-permute-start.2) | collective-permute-done | bytes 69664 | tf_op jit(solution)/shard_map/ppermute | solution.py:37
  13.9 1.6 %collective-permute-start.3 = (bf16[4,16,2176]{2,1,0:T(8,128)(2,1)S(1)}, bf16[4,16,2176]{2,1,0:T(8,128)(2,1)S(1)}, u32[]{:S(2)}, u32[]{:S(2)}) collective-permute-start(bf16[4,16,2176]{2,1,0:T(8,128)(2,1)S(1)} %pad_maximum_fusion), channel_id=1, source_target_pairs={{0,2},{1,3},{2,0},{3,1},{4,6},{5,7},{6,4},{7,5},{8,10},{9,11},{10,... | collective-permute-start | bytes 835592 | tf_op jit(solution)/shard_map/ppermute | solution.py:37
  15.6 0.2 multiply_reduce_fusion.3
  15.7 0.0 copy-done
  15.7 1.2 %fusion.70 = (f32[64]{0:T(128)S(1)}, bf16[64,768]{1,0:T(8,128)(2,1)S(1)}) fusion(f32[768]{0:T(1024)S(1)} %multiply_reduce_fusion, f32[64]{0:T(128)S(1)} %multiply_reduce_fusion.3, bf16[64,2176]{1,0:T(8,128)(2,1)S(1)} %bitcast.49, bf16[768,2048]{1,0:T(8,128)(2,1)S(1)} %copy-done), kind=kOutput, calls=%fused_computation.92 | convolution fusion | flops 214253504 | bytes 3526144 | tf_op jit(solution)/shard_map/dot_general | solution.py:27
  16.9 3.6 %collective-permute-done.3 = bf16[4,16,2176]{2,1,0:T(8,128)(2,1)S(1)} collective-permute-done((bf16[4,16,2176]{2,1,0:T(8,128)(2,1)S(1)}, bf16[4,16,2176]{2,1,0:T(8,128)(2,1)S(1)}, u32[]{:S(2)}, u32[]{:S(2)}) %collective-permute-start.3) | collective-permute-done | bytes 278560 | tf_op jit(solution)/shard_map/ppermute | solution.py:37
  20.6 0.1 collective-permute-start.4
  20.7 0.2 multiply_reduce_fusion.2
  20.9 1.2 %fusion.69 = (f32[64]{0:T(128)S(1)}, bf16[64,768]{1,0:T(8,128)(2,1)S(1)}) fusion(f32[768]{0:T(1024)S(1)} %multiply_reduce_fusion, f32[64]{0:T(128)S(1)} %multiply_reduce_fusion.2, bf16[64,2176]{1,0:T(8,128)(2,1)S(1)} %bitcast.47, bf16[768,2048]{1,0:T(8,128)(2,1)S(1)} %copy-done), kind=kOutput, calls=%fused_computation.91 | convolution fusion | flops 214253504 | bytes 3526144 | tf_op jit(solution)/shard_map/dot_general | solution.py:27
  22.1 0.6 %collective-permute-done.4 = bf16[8,16,2176]{2,1,0:T(8,128)(2,1)S(1)} collective-permute-done((bf16[8,16,2176]{2,1,0:T(8,128)(2,1)S(1)}, bf16[8,16,2176]{2,1,0:T(8,128)(2,1)S(1)}, u32[]{:S(2)}, u32[]{:S(2)}) %collective-permute-start.4) | collective-permute-done | bytes 557088 | tf_op jit(solution)/shard_map/ppermute | solution.py:37
  22.6 0.1 constant_dynamic-update-slice_fusion.5
  22.8 0.2 multiply_reduce_fusion.1
  23.0 0.0 copy-start.1
  23.0 1.4 %fusion.68 = (f32[128]{0:T(128)S(1)}, bf16[128,768]{1,0:T(8,128)(2,1)S(1)}) fusion(f32[768]{0:T(1024)S(1)} %multiply_reduce_fusion, f32[128]{0:T(128)S(1)} %multiply_reduce_fusion.1, bf16[128,2176]{1,0:T(8,128)(2,1)S(1)} %bitcast.51, bf16[768,2048]{1,0:T(8,128)(2,1)S(1)} %copy-done), kind=kOutput, calls=%fused_computation.90 | convolution fusion | flops 428507008 | bytes 3903488 | tf_op jit(solution)/shard_map/dot_general | solution.py:27
  24.4 0.1 pad_maximum_fusion.3
  24.4 0.1 reshape.44
  24.6 0.0 copy-done.1
  24.6 0.3 fusion.20
  25.0 0.2 collective-permute-start.5
  25.2 1.3 %collective-permute-done.5 = f32[2,4,24,256]{3,2,1,0:T(8,128)S(1)} collective-permute-done((f32[2,4,24,256]{3,2,1,0:T(8,128)S(1)}, f32[2,4,24,256]{3,2,1,0:T(8,128)S(1)}, u32[]{:S(2)}, u32[]{:S(2)}) %collective-permute-start.5) | collective-permute-done | bytes 196640 | tf_op jit(solution)/shard_map/ppermute | solution.py:37
  26.5 1.6 %collective-permute-start.6 = (f32[4,24,256]{2,1,0:T(8,128)S(1)}, f32[4,24,256]{2,1,0:T(8,128)S(1)}, u32[]{:S(2)}, u32[]{:S(2)}) collective-permute-start(f32[4,24,256]{2,1,0:T(8,128)S(1)} %slice_bitcast_fusion), channel_id=1, source_target_pairs={{0,2},{1,3},{2,0},{3,1},{4,6},{5,7},{6,4},{7,5},{8,10},{9,11},{10,... | collective-permute-start | bytes 294920 | tf_op jit(solution)/shard_map/ppermute | solution.py:37
  28.1 3.3 %collective-permute-done.6 = f32[4,24,256]{2,1,0:T(8,128)S(1)} collective-permute-done((f32[4,24,256]{2,1,0:T(8,128)S(1)}, f32[4,24,256]{2,1,0:T(8,128)S(1)}, u32[]{:S(2)}, u32[]{:S(2)}) %collective-permute-start.6) | collective-permute-done | bytes 98336 | tf_op jit(solution)/shard_map/ppermute | solution.py:37
  31.4 1.1 %collective-permute-start.7 = (f32[24,256]{1,0:T(8,128)S(1)}, f32[24,256]{1,0:T(8,128)S(1)}, u32[]{:S(2)}, u32[]{:S(2)}) collective-permute-start(f32[24,256]{1,0:T(8,128)S(1)} %get-tuple-element.29), channel_id=1, source_target_pairs={{0,4},{1,5},{2,6},{3,7},{4,0},{5,1},{6,2},{7,3},{8,12},{9,13},{10,... | collective-permute-start | bytes 73736 | tf_op jit(solution)/shard_map/ppermute | solution.py:37
  32.5 1.7 %collective-permute-start.8 = (f32[24,256]{1,0:T(8,128)S(1)}, f32[24,256]{1,0:T(8,128)S(1)}, u32[]{:S(2)}, u32[]{:S(2)}) collective-permute-start(f32[24,256]{1,0:T(8,128)S(1)} %get-tuple-element.31), channel_id=1, source_target_pairs={{0,8},{1,9},{2,10},{3,11},{4,12},{5,13},{6,14},{7,15},{8,0},{9,1},... | collective-permute-start | bytes 73736 | tf_op jit(solution)/shard_map/ppermute | solution.py:37
  34.3 1.6 %collective-permute-start.9 = (f32[24,256]{1,0:T(8,128)S(1)}, f32[24,256]{1,0:T(8,128)S(1)}, u32[]{:S(2)}, u32[]{:S(2)}) collective-permute-start(f32[24,256]{1,0:T(8,128)S(1)} %get-tuple-element.30), channel_id=1, source_target_pairs={{0,12},{1,13},{2,14},{3,15},{4,8},{5,9},{6,10},{7,11},{8,4},{9,5},... | collective-permute-start | bytes 73736 | tf_op jit(solution)/shard_map/ppermute | solution.py:37
  35.9 0.0 collective-permute-done.7
  35.9 1.4 %collective-permute-done.8 = f32[24,256]{1,0:T(8,128)S(1)} collective-permute-done((f32[24,256]{1,0:T(8,128)S(1)}, f32[24,256]{1,0:T(8,128)S(1)}, u32[]{:S(2)}, u32[]{:S(2)}) %collective-permute-start.8) | collective-permute-done | bytes 24608 | tf_op jit(solution)/shard_map/ppermute | solution.py:37
  37.3 2.6 %collective-permute-done.9 = f32[24,256]{1,0:T(8,128)S(1)} collective-permute-done((f32[24,256]{1,0:T(8,128)S(1)}, f32[24,256]{1,0:T(8,128)S(1)}, u32[]{:S(2)}, u32[]{:S(2)}) %collective-permute-start.9) | collective-permute-done | bytes 24608 | tf_op jit(solution)/shard_map/ppermute | solution.py:37
  40.0 0.7 %slice_divide_fusion = f32[16,256]{1,0:T(8,128)} fusion(f32[24,256]{1,0:T(8,128)S(1)} %fusion.56, f32[16]{0:T(128)S(1)} %slice.99), kind=kLoop, calls=%fused_computation.68 | loop fusion | flops 4096 | bytes 32832 | tf_op jit(solution)/shard_map/div | solution.py:125
  (22 shorter events, 0.4 us)
Async XLA Ops:
  2.0 9.2 %collective-permute-start = (bf16[1,16,2176]{2,1,0:T(8,128)(2,1)S(1)}, bf16[1,16,2176]{2,1,0:T(8,128)(2,1)S(1)}, u32[]{:S(2)}, u32[]{:S(2)}) collective-permute-start(bf16[1,16,2176]{2,1,0:T(8,128)(2,1)S(1)} %maximum_bitcast_fusion), channel_id=1, source_target_pairs={{0,4},{1,5},{2,6},{3,7},{4,0},{5,1},{6,2},{7,3},{8,12},{9,13},{10,... | collective-permute-start | bytes 208904 | tf_op jit(solution)/shard_map/ppermute | solution.py:37
  5.1 7.5 %collective-permute-start.1 = (bf16[1,16,2176]{2,1,0:T(8,128)(2,1)S(1)}, bf16[1,16,2176]{2,1,0:T(8,128)(2,1)S(1)}, u32[]{:S(2)}, u32[]{:S(2)}) collective-permute-start(bf16[1,16,2176]{2,1,0:T(8,128)(2,1)S(1)} %maximum_bitcast_fusion), channel_id=1, source_target_pairs={{0,8},{1,9},{2,10},{3,11},{4,12},{5,13},{6,14},{7,15},{8,0},{9,1},... | collective-permute-start | bytes 208904 | tf_op jit(solution)/shard_map/ppermute | solution.py:37
  7.7 6.2 %collective-permute-start.2 = (bf16[1,16,2176]{2,1,0:T(8,128)(2,1)S(1)}, bf16[1,16,2176]{2,1,0:T(8,128)(2,1)S(1)}, u32[]{:S(2)}, u32[]{:S(2)}) collective-permute-start(bf16[1,16,2176]{2,1,0:T(8,128)(2,1)S(1)} %maximum_bitcast_fusion), channel_id=1, source_target_pairs={{0,12},{1,13},{2,14},{3,15},{4,8},{5,9},{6,10},{7,11},{8,4},{9,5},... | collective-permute-start | bytes 208904 | tf_op jit(solution)/shard_map/ppermute | solution.py:37
  8.5 7.2 %copy-start = (bf16[768,2048]{1,0:T(8,128)(2,1)S(1)}, bf16[768,2048]{1,0:T(8,128)(2,1)}, u32[]{:S(2)}) copy-start(bf16[768,2048]{1,0:T(8,128)(2,1)} %param.4) | copy-start | bytes 9437188
  13.9 6.7 %collective-permute-start.3 = (bf16[4,16,2176]{2,1,0:T(8,128)(2,1)S(1)}, bf16[4,16,2176]{2,1,0:T(8,128)(2,1)S(1)}, u32[]{:S(2)}, u32[]{:S(2)}) collective-permute-start(bf16[4,16,2176]{2,1,0:T(8,128)(2,1)S(1)} %pad_maximum_fusion), channel_id=1, source_target_pairs={{0,2},{1,3},{2,0},{3,1},{4,6},{5,7},{6,4},{7,5},{8,10},{9,11},{10,... | collective-permute-start | bytes 835592 | tf_op jit(solution)/shard_map/ppermute | solution.py:37
  20.6 2.0 %collective-permute-start.4 = (bf16[8,16,2176]{2,1,0:T(8,128)(2,1)S(1)}, bf16[8,16,2176]{2,1,0:T(8,128)(2,1)S(1)}, u32[]{:S(2)}, u32[]{:S(2)}) collective-permute-start(bf16[8,16,2176]{2,1,0:T(8,128)(2,1)S(1)} %get-tuple-element.24), channel_id=1, source_target_pairs={{0,1},{1,0},{2,3},{3,2},{4,5},{5,4},{6,7},{7,6},{8,9},{9,8},{10,11... | collective-permute-start | bytes 1671176 | tf_op jit(solution)/shard_map/ppermute | solution.py:37
  23.0 1.6 %copy-start.1 = (bf16[768,256]{1,0:T(8,128)(2,1)S(1)}, bf16[768,256]{1,0:T(8,128)(2,1)}, u32[]{:S(2)}) copy-start(bf16[768,256]{1,0:T(8,128)(2,1)} %param.5) | copy-start | bytes 1179652
  25.0 1.5 %collective-permute-start.5 = (f32[2,4,24,256]{3,2,1,0:T(8,128)S(1)}, f32[2,4,24,256]{3,2,1,0:T(8,128)S(1)}, u32[]{:S(2)}, u32[]{:S(2)}) collective-permute-start(f32[2,4,24,256]{3,2,1,0:T(8,128)S(1)} %bitcast.58), channel_id=1, source_target_pairs={{0,1},{1,0},{2,3},{3,2},{4,5},{5,4},{6,7},{7,6},{8,9},{9,8},{10,11... | collective-permute-start | bytes 589832 | tf_op jit(solution)/shard_map/ppermute | solution.py:37
  26.5 4.9 %collective-permute-start.6 = (f32[4,24,256]{2,1,0:T(8,128)S(1)}, f32[4,24,256]{2,1,0:T(8,128)S(1)}, u32[]{:S(2)}, u32[]{:S(2)}) collective-permute-start(f32[4,24,256]{2,1,0:T(8,128)S(1)} %slice_bitcast_fusion), channel_id=1, source_target_pairs={{0,2},{1,3},{2,0},{3,1},{4,6},{5,7},{6,4},{7,5},{8,10},{9,11},{10,... | collective-permute-start | bytes 294920 | tf_op jit(solution)/shard_map/ppermute | solution.py:37
  31.4 4.5 %collective-permute-start.7 = (f32[24,256]{1,0:T(8,128)S(1)}, f32[24,256]{1,0:T(8,128)S(1)}, u32[]{:S(2)}, u32[]{:S(2)}) collective-permute-start(f32[24,256]{1,0:T(8,128)S(1)} %get-tuple-element.29), channel_id=1, source_target_pairs={{0,4},{1,5},{2,6},{3,7},{4,0},{5,1},{6,2},{7,3},{8,12},{9,13},{10,... | collective-permute-start | bytes 73736 | tf_op jit(solution)/shard_map/ppermute | solution.py:37
  32.5 4.8 %collective-permute-start.8 = (f32[24,256]{1,0:T(8,128)S(1)}, f32[24,256]{1,0:T(8,128)S(1)}, u32[]{:S(2)}, u32[]{:S(2)}) collective-permute-start(f32[24,256]{1,0:T(8,128)S(1)} %get-tuple-element.31), channel_id=1, source_target_pairs={{0,8},{1,9},{2,10},{3,11},{4,12},{5,13},{6,14},{7,15},{8,0},{9,1},... | collective-permute-start | bytes 73736 | tf_op jit(solution)/shard_map/ppermute | solution.py:37
  34.3 5.6 %collective-permute-start.9 = (f32[24,256]{1,0:T(8,128)S(1)}, f32[24,256]{1,0:T(8,128)S(1)}, u32[]{:S(2)}, u32[]{:S(2)}) collective-permute-start(f32[24,256]{1,0:T(8,128)S(1)} %get-tuple-element.30), channel_id=1, source_target_pairs={{0,12},{1,13},{2,14},{3,15},{4,8},{5,9},{6,10},{7,11},{8,4},{9,5},... | collective-permute-start | bytes 73736 | tf_op jit(solution)/shard_map/ppermute | solution.py:37

commit v13 on v11

--- a/solution.py
+++ b/solution.py
@@ -20,13 +20,20 @@
     return (parts[..., :n] + parts[..., n:2 * n]) + parts[..., 2 * n:3 * n]
 
 
-def piece_weights(piece, lib_ext, lib_sq, feat):
-    rows = piece.reshape(-1, piece.shape[-1])
-    blockf = rows[:, :feat].astype(jnp.float32)
-    q_sq = jnp.sum(blockf * blockf, axis=1)
-    inner = lax.dot_general(
-        rows, lib_ext, (((1,), (1,)), ((), ())), preferred_element_type=jnp.float32
-    )
+def piece_weights(pieces, libs, lib_sq, feat):
+    inner, q_sq, start = None, None, 0
+    for piece, lib in zip(pieces, libs):
+        rows = piece.reshape(-1, piece.shape[-1])
+        used = max(0, min(feat - start, rows.shape[1]))
+        if used:
+            part = rows[:, :used].astype(jnp.float32)
+            part = jnp.sum(part * part, axis=1)
+            q_sq = part if q_sq is None else q_sq + part
+        part = lax.dot_general(
+            rows, lib, (((1,), (1,)), ((), ())), preferred_element_type=jnp.float32
+        )
+        inner = part if inner is None else inner + part
+        start += rows.shape[1]
     tanimoto = inner / (q_sq[:, None] + lib_sq[None, :] - inner)
     weight = jnp.exp((tanimoto - 1.0) / TAU)
     return weight.astype(jnp.bfloat16), jnp.sum(weight, axis=1)
@@ -57,18 +64,25 @@
     return masks
 
 
-def gather_rounds(packet, axis, groups, work):
-    pieces = [packet[None]]
+def gather_rounds(packets, axis, groups, work):
+    rounds = list(reversed(groups))
+    held = [[p[None]] for p in packets]
+    brought = [[[p[None]] for p in packets]] + [[[] for _ in packets] for _ in rounds[1:]]
     results = []
-    fresh = [packet[None]]
-    for group in reversed(groups):
-        buf = jnp.concatenate(pieces, axis=0) if len(pieces) > 1 else pieces[0]
-        got = [swap(buf, axis, m) for m in offsets(group)[1:]]
-        pieces += got
-        fresh += got
-        results.append(work(jnp.concatenate(fresh, axis=0)))
-        fresh = []
-    return jnp.concatenate(pieces, axis=0), results
+    for stage in range(len(rounds) + len(packets) - 1):
+        for s in range(len(packets)):
+            r = stage - s
+            if 0 <= r < len(rounds):
+                buf = jnp.concatenate(held[s], axis=0) if len(held[s]) > 1 else held[s][0]
+                if s:
+                    buf, _ = lax.optimization_barrier((buf, brought[r][s - 1]))
+                got = [swap(buf, axis, m) for m in offsets(rounds[r])[1:]]
+                held[s] += got
+                brought[r][s] += got
+        r = stage - len(packets) + 1
+        if r >= 0:
+            results.append(work([jnp.concatenate(b, axis=0) for b in brought[r]]))
+    return [jnp.concatenate(h, axis=0) for h in held], results
 
 
 def scatter_rounds(buf, axis, groups):
@@ -96,10 +110,15 @@
     packet = jnp.concatenate([queries, coded], axis=1)
     lib_ext = jnp.pad(library, ((0, 0), (0, lanes)))
     lib_sq = jnp.sum(jnp.square(library.astype(jnp.float32)), axis=1)
-    got, parts = gather_rounds(
-        packet, "blk", groups, lambda piece: piece_weights(piece, lib_ext, lib_sq, feat)
+    cut = (feat // 2) // 128 * 128
+    packets = [packet[:, :cut], packet[:, cut:]]
+    libs = [lib_ext[:, :cut], lib_ext[:, cut:]]
+    helds, parts = gather_rounds(
+        packets, "blk", groups, lambda pieces: piece_weights(pieces, libs, lib_sq, feat)
     )
-    stats = join3(got[:, :, feat:].reshape(nblk, q_dev * lanes), 2 * width)
+    got = helds[-1]
+    stat_lo = feat - cut
+    stats = join3(got[:, :, stat_lo:].reshape(nblk, q_dev * lanes), 2 * width)
     stats = jnp.sum(stats, axis=0)
 
     col_sum, col_sq = stats[:width], stats[width:]

time: 41.9 us -> 60.2 us (1.44)
  local copies, waits for them, and re-layouts: 0.39 us -> 9.65 us
  starting transfers between devices: 13.9 us -> 20 us
  matrix products: 4.1 us -> 9.61 us
  waiting for transfers between devices: 16.1 us -> 11 us
  other arithmetic: 7.01 us -> 9.19 us
    unnamed x12 -> x17, local copies, waits for them, and re-layouts: 0.21 us -> 6.79 us
    ppermute x10 -> x15, starting transfers between devices: 13.9 us -> 20 us  [swap(): return lax.ppermute(x, axis, [(i, i ^ mask) for i in range(count)])]
    ppermute x10 -> x15, waiting for transfers between devices: 16.1 us -> 11 us  [swap(): return lax.ppermute(x, axis, [(i, i ^ mask) for i in range(count)])]
    dot_general x3 -> x6, matrix products: 3.8 us -> 8.21 us  [piece_weights(): lax.dot_general(rows, lib, (((1,), (1,)), ((), ())), preferred_element_ty...]
    reduce_sum x3 -> x6, other arithmetic: 0.5 us -> 3.16 us  [piece_weights(): part = jnp.sum(part * part, axis=1)]
    concatenate x1 -> x2, local copies, waits for them, and re-layouts: 0.06 us -> 1.59 us  [the longest x1 1.56 us: gather_rounds(): buf = jnp.concatenate(held[s], axis=0) if len(held[s]) > 1 else held[s][0]]
    dot_general x1, matrix products: 0.3 us -> 1.4 us  [shards(): numer = jnp.dot(weight_b, zvals, preferred_element_type=jnp.float32)]
    broadcast_in_dim x0 -> x1, local copies, waits for them, and re-layouts: none -> 0.91 us  [gather_rounds(): p[None]]
  transfers between devices with their start and end apart: 10 -> 15, of which waited for: 7 -> 6; matrix products, arithmetic and copies ran while one was open for 15% -> 37% of each run, Pallas kernels for 0% -> 0%
where the time goes in v13:
time: 60.2 us; the launch traced here: 59.6 us
  starting transfers between devices  20 us (33%)
  waiting for transfers between devices  11 us (18%)
  local copies, waits for them, and re-layouts  9.65 us (16%)
  matrix products  9.61 us (16%)
  other arithmetic  9.19 us (15%)
    ppermute x15, starting transfers between devices, swap(): return lax.ppermute(x, axis, [(i, i ^ mask) for i in range(count)])  20 us
    ppermute x15, waiting for transfers between devices, swap(): return lax.ppermute(x, axis, [(i, i ^ mask) for i in range(count)])  11 us
    dot_general x6, matrix products, piece_weights(): lax.dot_general(rows, lib, (((1,), (1,)), ((), ())), preferred_element_ty...  8.21 us
    unnamed x17, local copies, waits for them, and re-layouts  6.79 us
    reduce_sum x6, other arithmetic, piece_weights(): part = jnp.sum(part * part, axis=1)  3.16 us
    reduce_sum x1, other arithmetic, shards(): lib_sq = jnp.sum(jnp.square(library.astype(jnp.float32)), axis=1)  2.57 us
    concatenate x1, local copies, waits for them, and re-layouts, gather_rounds(): buf = jnp.concatenate(held[s], axis=0) if len(held[s]) > 1 else held[s][0]  1.56 us
    dot_general x1, matrix products, shards(): numer = jnp.dot(weight_b, zvals, preferred_element_type=jnp.float32)  1.4 us
  transfers between devices with their start and end apart: 15, of which 6 were waited for; matrix products, arithmetic and copies ran while one was open for 37% of the time, Pallas kernels for 0%

profile of v13, /device:TPU:0, one launch (start us, length us, event | category | flops | bytes accessed | tf_op | source)
XLA Modules:
  0.0 59.6 jit_solution(15416543758369612279)
XLA Ops:
  0.0 0.9 %slice_bitcast_fusion.2 = bf16[1,16,1024]{2,1,0:T(8,128)(2,1)S(1)} fusion(bf16[16,2048]{1,0:T(8,128)(2,1)} %param.3), kind=kLoop, calls=%fused_computation.77 | loop fusion | bytes 65536 | tf_op jit(solution)/shard_map/broadcast_in_dim | solution.py:70
  0.9 3.1 %collective-permute-start = (bf16[1,16,1024]{2,1,0:T(8,128)(2,1)S(1)}, bf16[1,16,1024]{2,1,0:T(8,128)(2,1)S(1)}, u32[]{:S(2)}, u32[]{:S(2)}) collective-permute-start(bf16[1,16,1024]{2,1,0:T(8,128)(2,1)S(1)} %slice_bitcast_fusion.2), channel_id=1, source_target_pairs={{0,4},{1,5},{2,6},{3,7},{4,0},{5,1},{6,2},{7,3},{8,12},{9,13},{10,... | collective-permute-start | bytes 98312 | tf_op jit(solution)/shard_map/ppermute | solution.py:44
  4.0 2.6 %collective-permute-start.1 = (bf16[1,16,1024]{2,1,0:T(8,128)(2,1)S(1)}, bf16[1,16,1024]{2,1,0:T(8,128)(2,1)S(1)}, u32[]{:S(2)}, u32[]{:S(2)}) collective-permute-start(bf16[1,16,1024]{2,1,0:T(8,128)(2,1)S(1)} %slice_bitcast_fusion.2), channel_id=1, source_target_pairs={{0,8},{1,9},{2,10},{3,11},{4,12},{5,13},{6,14},{7,15},{8,0},{9,1},... | collective-permute-start | bytes 98312 | tf_op jit(solution)/shard_map/ppermute | solution.py:44
  6.6 0.0 collective-permute-start.2
  6.6 1.4 %constant_dynamic-update-slice_fusion.4 = bf16[8,16,1024]{2,1,0:T(8,128)(2,1)} fusion(bf16[16,2048]{1,0:T(8,128)(2,1)} %param.3), kind=kLoop, calls=%fused_computation.62 | loop fusion | bytes 65536
  7.9 1.1 %convert_reduce_fusion = (f32[256]{0:T(256)S(1)}, f32[256]{0:T(256)S(1)}) fusion(bf16[768,256]{1,0:T(8,128)(2,1)} %param.5), kind=kLoop, calls=%fused_computation.10 | loop fusion | flops 785920 | bytes 395264 | tf_op jit(solution)/shard_map/reduce_sum | solution.py:104
  9.1 1.4 %constant_dynamic-update-slice_fusion.15 = (bf16[16,16,1152]{2,1,0:T(8,128)(2,1)}, bf16[1,16,1152]{2,1,0:T(8,128)(2,1)S(1)}) fusion(bf16[16,128]{1,0:T(8,128)(2,1)S(1)} %fusion.71, bf16[16,2048]{1,0:T(8,128)(2,1)} %param.3), kind=kLoop, calls=%fused_computation.73 | loop fusion | flops 73727 | bytes 143360
  10.5 2.6 %multiply_reduce_fusion = f32[768]{0:T(1024)S(1)} fusion(bf16[768,2048]{1,0:T(8,128)(2,1)} %param.4), kind=kLoop, calls=%fused_computation | loop fusion | flops 4717824 | bytes 3148800 | tf_op jit(solution)/shard_map/reduce_sum | solution.py:112
  13.0 0.6 %constant_dynamic-update-slice_fusion.9 = bf16[8,16,1152]{2,1,0:T(8,128)(2,1)} fusion(bf16[1,16,1152]{2,1,0:T(8,128)(2,1)S(1)} %get-tuple-element.8), kind=kLoop, calls=%fused_computation.67 | loop fusion | bytes 73728
  13.6 0.0 collective-permute-done
  13.7 0.0 collective-permute-done.1
  13.7 0.0 collective-permute-done.2
  13.7 1.0 %collective-permute-start.3 = (bf16[1,16,1152]{2,1,0:T(8,128)(2,1)S(1)}, bf16[1,16,1152]{2,1,0:T(8,128)(2,1)S(1)}, u32[]{:S(2)}, u32[]{:S(2)}) collective-permute-start(bf16[1,16,1152]{2,1,0:T(8,128)(2,1)S(1)} %get-tuple-element.8), channel_id=1, source_target_pairs={{0,4},{1,5},{2,6},{3,7},{4,0},{5,1},{6,2},{7,3},{8,12},{9,13},{10,... | collective-permute-start | bytes 110600 | tf_op jit(solution)/shard_map/ppermute | solution.py:44
  14.6 3.5 %collective-permute-start.4 = (bf16[1,16,1152]{2,1,0:T(8,128)(2,1)S(1)}, bf16[1,16,1152]{2,1,0:T(8,128)(2,1)S(1)}, u32[]{:S(2)}, u32[]{:S(2)}) collective-permute-start(bf16[1,16,1152]{2,1,0:T(8,128)(2,1)S(1)} %get-tuple-element.8), channel_id=1, source_target_pairs={{0,8},{1,9},{2,10},{3,11},{4,12},{5,13},{6,14},{7,15},{8,0},{9,1},... | collective-permute-start | bytes 110600 | tf_op jit(solution)/shard_map/ppermute | solution.py:44
  18.1 0.0 collective-permute-start.5
  18.1 0.7 %multiply_reduce_fusion.6 = (f32[4,16]{1,0:T(4,128)S(1)}, bf16[4,16,1024]{2,1,0:T(8,128)(2,1)}) fusion(bf16[1,16,1024]{2,1,0:T(8,128)(2,1)S(1)} %collective-permute-done.2, bf16[1,16,1024]{2,1,0:T(8,128)(2,1)S(1)} %collective-permute-done.1, bf16[1,16,1024]{2,1,0:T(8,128)(2,1)S(1)} %collective-permute-done, bf16[1,16,1024]{2,1,0:T(8,128)(2,1)S(1)} %slice_bitcast_fusion.2), kind=kLoop, calls=%fused_computation.46 | loop fusion | flops 393152 | bytes 262400 | tf_op jit(solution)/shard_map/reduce_sum | solution.py:30
  18.8 1.7 %collective-permute-start.6 = (bf16[4,16,1024]{2,1,0:T(8,128)(2,1)}, bf16[4,16,1024]{2,1,0:T(8,128)(2,1)}, u32[]{:S(2)}, u32[]{:S(2)}) collective-permute-start(bf16[4,16,1024]{2,1,0:T(8,128)(2,1)} %get-tuple-element.16), channel_id=1, source_target_pairs={{0,2},{1,3},{2,0},{3,1},{4,6},{5,7},{6,4},{7,5},{8,10},{9,11},{10,... | collective-permute-start | bytes 393224 | tf_op jit(solution)/shard_map/ppermute | solution.py:44
  20.5 0.6 %constant_dynamic-update-slice_fusion.3 = bf16[8,16,1024]{2,1,0:T(8,128)(2,1)} fusion(bf16[8,16,1024]{2,1,0:T(8,128)(2,1)} %constant_dynamic-update-slice_fusion.4, bf16[1,16,1024]{2,1,0:T(8,128)(2,1)S(1)} %collective-permute-done), kind=kLoop, calls=%fused_computation.61 | loop fusion | bytes 65536
  21.1 0.6 %constant_dynamic-update-slice_fusion.2 = bf16[8,16,1024]{2,1,0:T(8,128)(2,1)} fusion(bf16[8,16,1024]{2,1,0:T(8,128)(2,1)} %constant_dynamic-update-slice_fusion.3, bf16[1,16,1024]{2,1,0:T(8,128)(2,1)S(1)} %collective-permute-done.1), kind=kLoop, calls=%fused_computation.60 | loop fusion | bytes 65536
  21.7 0.6 %constant_dynamic-update-slice_fusion.1 = bf16[8,16,1024]{2,1,0:T(8,128)(2,1)} fusion(bf16[8,16,1024]{2,1,0:T(8,128)(2,1)} %constant_dynamic-update-slice_fusion.2, bf16[1,16,1024]{2,1,0:T(8,128)(2,1)S(1)} %collective-permute-done.2), kind=kLoop, calls=%fused_computation.59 | loop fusion | bytes 65536
  22.3 0.1 reduce_sum.126
  22.4 0.0 collective-permute-done.3
  22.4 0.0 collective-permute-done.4
  22.4 1.4 %collective-permute-done.5 = bf16[1,16,1152]{2,1,0:T(8,128)(2,1)S(1)} collective-permute-done((bf16[1,16,1152]{2,1,0:T(8,128)(2,1)S(1)}, bf16[1,16,1152]{2,1,0:T(8,128)(2,1)S(1)}, u32[]{:S(2)}, u32[]{:S(2)}) %collective-permute-start.5) | collective-permute-done | bytes 36896 | tf_op jit(solution)/shard_map/ppermute | solution.py:44
  23.9 0.1 multiply_reduce_fusion.5
  24.0 0.6 %fusion.27 = f32[64,768]{1,0:T(8,128)S(1)} fusion(bf16[64,1152]{1,0:T(8,128)(2,1)S(1)} %bitcast.58, bf16[768,2048]{1,0:T(8,128)(2,1)S(1)} %copy-done), kind=kOutput, calls=%fused_computation.22 | convolution fusion | flops 113246208 | bytes 3489792 | tf_op jit(solution)/shard_map/dot_general | solution.py:32
  24.7 2.3 %fusion.79 = (f32[64]{0:T(128)S(1)}, bf16[64,768]{1,0:T(8,128)(2,1)}) fusion(f32[768]{0:T(1024)S(1)} %multiply_reduce_fusion, f32[64]{0:T(128)S(1)} %add.104, f32[64,768]{1,0:T(8,128)S(1)} %fusion.27, bf16[64,1024]{1,0:T(8,128)(2,1)} %bitcast.1, bf16[768,2048]{1,0:T(8,128)(2,1)S(1)} %copy-done), kind=kOutput, calls=%fused_computation.108 | convolution fusion | flops 101056448 | bytes 2003712 | tf_op jit(solution)/shard_map/dot_general | solution.py:32
  26.9 0.6 %constant_dynamic-update-slice_fusion.14 = (bf16[16,16,1152]{2,1,0:T(8,128)(2,1)}, bf16[8,16,1152]{2,1,0:T(8,128)(2,1)}) fusion(bf16[16,16,1152]{2,1,0:T(8,128)(2,1)} %get-tuple-element.13, bf16[1,16,1152]{2,1,0:T(8,128)(2,1)S(1)} %collective-permute-done.3, bf16[8,16,1152]{2,1,0:T(8,128)(2,1)} %constant_dynamic-update-slice_fusion.9), kind=kLoop, calls=%fused_computation.72 | loop fusion | bytes 110592
  27.6 0.6 %constant_dynamic-update-slice_fusion.13 = (bf16[16,16,1152]{2,1,0:T(8,128)(2,1)}, bf16[8,16,1152]{2,1,0:T(8,128)(2,1)}) fusion(bf16[16,16,1152]{2,1,0:T(8,128)(2,1)} %get-tuple-element.34, bf16[1,16,1152]{2,1,0:T(8,128)(2,1)S(1)} %collective-permute-done.4, bf16[8,16,1152]{2,1,0:T(8,128)(2,1)} %get-tuple-element.35), kind=kLoop, calls=%fused_computation.71 | loop fusion | bytes 110592
  28.2 0.7 %constant_dynamic-update-slice_fusion.12 = (bf16[16,16,1152]{2,1,0:T(8,128)(2,1)}, bf16[8,16,1152]{2,1,0:T(8,128)(2,1)}) fusion(bf16[16,16,1152]{2,1,0:T(8,128)(2,1)} %get-tuple-element.32, bf16[1,16,1152]{2,1,0:T(8,128)(2,1)S(1)} %collective-permute-done.5, bf16[8,16,1152]{2,1,0:T(8,128)(2,1)} %get-tuple-element.33), kind=kLoop, calls=%fused_computation.70 | loop fusion | bytes 110592
  28.9 0.0 collective-permute-done.6
  28.9 1.5 %collective-permute-start.7 = (bf16[4,16,1152]{2,1,0:T(8,128)(2,1)S(1)}, bf16[4,16,1152]{2,1,0:T(8,128)(2,1)S(1)}, u32[]{:S(2)}, u32[]{:S(2)}) collective-permute-start(bf16[4,16,1152]{2,1,0:T(8,128)(2,1)S(1)} %pad_maximum_fusion.1), channel_id=1, source_target_pairs={{0,2},{1,3},{2,0},{3,1},{4,6},{5,7},{6,4},{7,5},{8,10},{9,11},{10,... | collective-permute-start | bytes 442376 | tf_op jit(solution)/shard_map/ppermute | solution.py:44
  30.4 1.6 %constant_dynamic-update-slice_fusion = bf16[8,16,1024]{2,1,0:T(8,128)(2,1)} fusion(bf16[8,16,1024]{2,1,0:T(8,128)(2,1)} %constant_dynamic-update-slice_fusion.1, bf16[4,16,1024]{2,1,0:T(8,128)(2,1)} %collective-permute-done.6), kind=kLoop, calls=%fused_computation.58 | loop fusion | bytes 262144 | tf_op jit(solution)/shard_map/concatenate | solution.py:76
  32.0 0.0 collective-permute-start.8
  32.0 1.0 %multiply_reduce_fusion.4 = f32[4,16]{1,0:T(4,128)S(1)} fusion(bf16[4,16,1024]{2,1,0:T(8,128)(2,1)} %collective-permute-done.6), kind=kLoop, calls=%fused_computation.44 | loop fusion | flops 196544 | bytes 131328 | tf_op jit(solution)/shard_map/reduce_sum | solution.py:30
  33.0 0.1 reduce_sum.130
  33.1 1.0 %collective-permute-done.7 = bf16[4,16,1152]{2,1,0:T(8,128)(2,1)S(1)} collective-permute-done((bf16[4,16,1152]{2,1,0:T(8,128)(2,1)S(1)}, bf16[4,16,1152]{2,1,0:T(8,128)(2,1)S(1)}, u32[]{:S(2)}, u32[]{:S(2)}) %collective-permute-start.7) | collective-permute-done | bytes 147488 | tf_op jit(solution)/shard_map/ppermute | solution.py:44
  34.0 0.6 %fusion.26 = f32[64,768]{1,0:T(8,128)S(1)} fusion(bf16[64,1152]{1,0:T(8,128)(2,1)S(1)} %bitcast.55, bf16[768,2048]{1,0:T(8,128)(2,1)S(1)} %copy-done), kind=kOutput, calls=%fused_computation.21 | convolution fusion | flops 113246208 | bytes 3489792 | tf_op jit(solution)/shard_map/dot_general | solution.py:32
  34.6 0.1 multiply_reduce_fusion.3
  34.8 0.7 %constant_dynamic-update-slice_fusion.11 = (bf16[16,16,1152]{2,1,0:T(8,128)(2,1)}, bf16[8,16,1152]{2,1,0:T(8,128)(2,1)}) fusion(bf16[16,16,1152]{2,1,0:T(8,128)(2,1)} %get-tuple-element.30, bf16[4,16,1152]{2,1,0:T(8,128)(2,1)S(1)} %collective-permute-done.7, bf16[8,16,1152]{2,1,0:T(8,128)(2,1)} %get-tuple-element.31), kind=kLoop, calls=%fused_computation.69 | loop fusion | bytes 442368
  35.5 0.0 collective-permute-done.8
  35.5 0.0 collective-permute-start.9
  35.5 2.3 %fusion.80 = (f32[64]{0:T(128)S(1)}, bf16[64,768]{1,0:T(8,128)(2,1)}) fusion(f32[768]{0:T(1024)S(1)} %multiply_reduce_fusion, f32[64]{0:T(128)S(1)} %add.109, f32[64,768]{1,0:T(8,128)S(1)} %fusion.26, bf16[64,1024]{1,0:T(8,128)(2,1)} %bitcast.5, bf16[768,2048]{1,0:T(8,128)(2,1)S(1)} %copy-done), kind=kOutput, calls=%fused_computation.109 | convolution fusion | flops 101056448 | bytes 2003712 | tf_op jit(solution)/shard_map/dot_general | solution.py:32
  37.8 1.1 %multiply_reduce_fusion.2 = f32[8,16]{1,0:T(8,128)S(1)} fusion(bf16[8,16,1024]{2,1,0:T(8,128)(2,1)} %collective-permute-done.8), kind=kLoop, calls=%fused_computation.24 | loop fusion | flops 393088 | bytes 262656 | tf_op jit(solution)/shard_map/reduce_sum | solution.py:30
  38.9 0.1 reduce_sum.133
  39.0 0.0 collective-permute-done.9
  39.0 0.7 %fusion.25 = f32[128,768]{1,0:T(8,128)S(1)} fusion(bf16[128,1152]{1,0:T(8,128)(2,1)S(1)} %bitcast.53, bf16[768,2048]{1,0:T(8,128)(2,1)S(1)} %copy-done), kind=kOutput, calls=%fused_computation.20 | convolution fusion | flops 226492416 | bytes 3833856 | tf_op jit(solution)/shard_map/dot_general | solution.py:32
  39.7 0.1 multiply_reduce_fusion.1
  39.8 0.2 copy-done.1
  40.2 1.7 %fusion.78 = (f32[128]{0:T(128)S(1)}, bf16[128,768]{1,0:T(8,128)(2,1)S(1)}) fusion(f32[768]{0:T(1024)S(1)} %multiply_reduce_fusion, f32[128]{0:T(128)S(1)} %add.113, f32[128,768]{1,0:T(8,128)S(1)} %fusion.25, bf16[128,1024]{1,0:T(8,128)(2,1)} %bitcast.7, bf16[768,2048]{1,0:T(8,128)(2,1)S(1)} %copy-done), kind=kOutput, calls=%fused_computation.107 | convolution fusion | flops 202112896 | bytes 2429952 | tf_op jit(solution)/shard_map/dot_general | solution.py:32
  41.9 0.1 pad_maximum_fusion.5
  42.0 0.1 reshape.80
  42.2 1.4 %fusion.28 = f32[256,256]{1,0:T(8,128)S(1)} fusion(bf16[768,256]{1,0:T(8,128)(2,1)} %param.5, bf16[128,768]{1,0:T(8,128)(2,1)S(1)} %get-tuple-element.20, bf16[64,768]{1,0:T(8,128)(2,1)} %get-tuple-element.24, bf16[64,768]{1,0:T(8,128)(2,1)} %get-tuple-element.22, f32[256]{0:T(256)S(1)} %get-tuple-element.37, f32[256]{0:T(256)S(1)} %get-tuple-element.36), kind=kOutput, calls=%fused_computation.25 | convolution fusion | flops 102629376 | bytes 1050624 | tf_op jit(solution)/shard_map/dot_general | solution.py:132
  43.6 0.6 collective-permute-start.10
  44.2 1.1 %collective-permute-done.10 = f32[2,4,24,256]{3,2,1,0:T(8,128)S(1)} collective-permute-done((f32[2,4,24,256]{3,2,1,0:T(8,128)S(1)}, f32[2,4,24,256]{3,2,1,0:T(8,128)S(1)}, u32[]{:S(2)}, u32[]{:S(2)}) %collective-permute-start.10) | collective-permute-done | bytes 196640 | tf_op jit(solution)/shard_map/ppermute | solution.py:44
  45.3 1.6 %collective-permute-start.11 = (f32[4,24,256]{2,1,0:T(8,128)S(1)}, f32[4,24,256]{2,1,0:T(8,128)S(1)}, u32[]{:S(2)}, u32[]{:S(2)}) collective-permute-start(f32[4,24,256]{2,1,0:T(8,128)S(1)} %slice_bitcast_fusion), channel_id=1, source_target_pairs={{0,2},{1,3},{2,0},{3,1},{4,6},{5,7},{6,4},{7,5},{8,10},{9,11},{10,... | collective-permute-start | bytes 294920 | tf_op jit(solution)/shard_map/ppermute | solution.py:44
  46.9 3.6 %collective-permute-done.11 = f32[4,24,256]{2,1,0:T(8,128)S(1)} collective-permute-done((f32[4,24,256]{2,1,0:T(8,128)S(1)}, f32[4,24,256]{2,1,0:T(8,128)S(1)}, u32[]{:S(2)}, u32[]{:S(2)}) %collective-permute-start.11) | collective-permute-done | bytes 98336 | tf_op jit(solution)/shard_map/ppermute | solution.py:44
  50.5 0.1 collective-permute-start.12
  50.6 2.7 %collective-permute-start.13 = (f32[24,256]{1,0:T(8,128)S(1)}, f32[24,256]{1,0:T(8,128)S(1)}, u32[]{:S(2)}, u32[]{:S(2)}) collective-permute-start(f32[24,256]{1,0:T(8,128)S(1)} %get-tuple-element.29), channel_id=1, source_target_pairs={{0,8},{1,9},{2,10},{3,11},{4,12},{5,13},{6,14},{7,15},{8,0},{9,1},... | collective-permute-start | bytes 73736 | tf_op jit(solution)/shard_map/ppermute | solution.py:44
  53.3 1.6 %collective-permute-start.14 = (f32[24,256]{1,0:T(8,128)S(1)}, f32[24,256]{1,0:T(8,128)S(1)}, u32[]{:S(2)}, u32[]{:S(2)}) collective-permute-start(f32[24,256]{1,0:T(8,128)S(1)} %get-tuple-element.28), channel_id=1, source_target_pairs={{0,12},{1,13},{2,14},{3,15},{4,8},{5,9},{6,10},{7,11},{8,4},{9,5},... | collective-permute-start | bytes 73736 | tf_op jit(solution)/shard_map/ppermute | solution.py:44
  54.9 0.0 collective-permute-done.12
  54.9 0.5 collective-permute-done.13
  55.4 3.5 %collective-permute-done.14 = f32[24,256]{1,0:T(8,128)S(1)} collective-permute-done((f32[24,256]{1,0:T(8,128)S(1)}, f32[24,256]{1,0:T(8,128)S(1)}, u32[]{:S(2)}, u32[]{:S(2)}) %collective-permute-start.14) | collective-permute-done | bytes 24608 | tf_op jit(solution)/shard_map/ppermute | solution.py:44
  59.0 0.7 %slice_divide_fusion = f32[16,256]{1,0:T(8,128)} fusion(f32[24,256]{1,0:T(8,128)S(1)} %fusion.65, f32[16]{0:T(128)S(1)} %slice.116), kind=kLoop, calls=%fused_computation.85 | loop fusion | flops 4096 | bytes 32832 | tf_op jit(solution)/shard_map/div | solution.py:142
  (25 shorter events, 0.4 us)
Async XLA Ops:
  0.0 24.0 %copy-start = (bf16[768,2048]{1,0:T(8,128)(2,1)S(1)}, bf16[768,2048]{1,0:T(8,128)(2,1)}, u32[]{:S(2)}) copy-start(bf16[768,2048]{1,0:T(8,128)(2,1)} %param.4) | copy-start | bytes 9437188
  0.9 12.7 %collective-permute-start = (bf16[1,16,1024]{2,1,0:T(8,128)(2,1)S(1)}, bf16[1,16,1024]{2,1,0:T(8,128)(2,1)S(1)}, u32[]{:S(2)}, u32[]{:S(2)}) collective-permute-start(bf16[1,16,1024]{2,1,0:T(8,128)(2,1)S(1)} %slice_bitcast_fusion.2), channel_id=1, source_target_pairs={{0,4},{1,5},{2,6},{3,7},{4,0},{5,1},{6,2},{7,3},{8,12},{9,13},{10,... | collective-permute-start | bytes 98312 | tf_op jit(solution)/shard_map/ppermute | solution.py:44
  4.0 9.7 %collective-permute-start.1 = (bf16[1,16,1024]{2,1,0:T(8,128)(2,1)S(1)}, bf16[1,16,1024]{2,1,0:T(8,128)(2,1)S(1)}, u32[]{:S(2)}, u32[]{:S(2)}) collective-permute-start(bf16[1,16,1024]{2,1,0:T(8,128)(2,1)S(1)} %slice_bitcast_fusion.2), channel_id=1, source_target_pairs={{0,8},{1,9},{2,10},{3,11},{4,12},{5,13},{6,14},{7,15},{8,0},{9,1},... | collective-permute-start | bytes 98312 | tf_op jit(solution)/shard_map/ppermute | solution.py:44
  6.6 7.1 %collective-permute-start.2 = (bf16[1,16,1024]{2,1,0:T(8,128)(2,1)S(1)}, bf16[1,16,1024]{2,1,0:T(8,128)(2,1)S(1)}, u32[]{:S(2)}, u32[]{:S(2)}) collective-permute-start(bf16[1,16,1024]{2,1,0:T(8,128)(2,1)S(1)} %slice_bitcast_fusion.2), channel_id=1, source_target_pairs={{0,12},{1,13},{2,14},{3,15},{4,8},{5,9},{6,10},{7,11},{8,4},{9,5},... | collective-permute-start | bytes 98312 | tf_op jit(solution)/shard_map/ppermute | solution.py:44
  13.7 8.8 %collective-permute-start.3 = (bf16[1,16,1152]{2,1,0:T(8,128)(2,1)S(1)}, bf16[1,16,1152]{2,1,0:T(8,128)(2,1)S(1)}, u32[]{:S(2)}, u32[]{:S(2)}) collective-permute-start(bf16[1,16,1152]{2,1,0:T(8,128)(2,1)S(1)} %get-tuple-element.8), channel_id=1, source_target_pairs={{0,4},{1,5},{2,6},{3,7},{4,0},{5,1},{6,2},{7,3},{8,12},{9,13},{10,... | collective-permute-start | bytes 110600 | tf_op jit(solution)/shard_map/ppermute | solution.py:44
  14.6 7.8 %collective-permute-start.4 = (bf16[1,16,1152]{2,1,0:T(8,128)(2,1)S(1)}, bf16[1,16,1152]{2,1,0:T(8,128)(2,1)S(1)}, u32[]{:S(2)}, u32[]{:S(2)}) collective-permute-start(bf16[1,16,1152]{2,1,0:T(8,128)(2,1)S(1)} %get-tuple-element.8), channel_id=1, source_target_pairs={{0,8},{1,9},{2,10},{3,11},{4,12},{5,13},{6,14},{7,15},{8,0},{9,1},... | collective-permute-start | bytes 110600 | tf_op jit(solution)/shard_map/ppermute | solution.py:44
  18.1 5.8 %collective-permute-start.5 = (bf16[1,16,1152]{2,1,0:T(8,128)(2,1)S(1)}, bf16[1,16,1152]{2,1,0:T(8,128)(2,1)S(1)}, u32[]{:S(2)}, u32[]{:S(2)}) collective-permute-start(bf16[1,16,1152]{2,1,0:T(8,128)(2,1)S(1)} %get-tuple-element.8), channel_id=1, source_target_pairs={{0,12},{1,13},{2,14},{3,15},{4,8},{5,9},{6,10},{7,11},{8,4},{9,5},... | collective-permute-start | bytes 110600 | tf_op jit(solution)/shard_map/ppermute | solution.py:44
  18.8 10.1 %collective-permute-start.6 = (bf16[4,16,1024]{2,1,0:T(8,128)(2,1)}, bf16[4,16,1024]{2,1,0:T(8,128)(2,1)}, u32[]{:S(2)}, u32[]{:S(2)}) collective-permute-start(bf16[4,16,1024]{2,1,0:T(8,128)(2,1)} %get-tuple-element.16), channel_id=1, source_target_pairs={{0,2},{1,3},{2,0},{3,1},{4,6},{5,7},{6,4},{7,5},{8,10},{9,11},{10,... | collective-permute-start | bytes 393224 | tf_op jit(solution)/shard_map/ppermute | solution.py:44
  28.9 5.1 %collective-permute-start.7 = (bf16[4,16,1152]{2,1,0:T(8,128)(2,1)S(1)}, bf16[4,16,1152]{2,1,0:T(8,128)(2,1)S(1)}, u32[]{:S(2)}, u32[]{:S(2)}) collective-permute-start(bf16[4,16,1152]{2,1,0:T(8,128)(2,1)S(1)} %pad_maximum_fusion.1), channel_id=1, source_target_pairs={{0,2},{1,3},{2,0},{3,1},{4,6},{5,7},{6,4},{7,5},{8,10},{9,11},{10,... | collective-permute-start | bytes 442376 | tf_op jit(solution)/shard_map/ppermute | solution.py:44
  32.0 3.5 %collective-permute-start.8 = (bf16[8,16,1024]{2,1,0:T(8,128)(2,1)}, bf16[8,16,1024]{2,1,0:T(8,128)(2,1)}, u32[]{:S(2)}, u32[]{:S(2)}) collective-permute-start(bf16[8,16,1024]{2,1,0:T(8,128)(2,1)} %constant_dynamic-update-slice_fusion), channel_id=1, source_target_pairs={{0,1},{1,0},{2,3},{3,2},{4,5},{5,4},{6,7},{7,6},{8,9},{9,8},{10,11... | collective-permute-start | bytes 786440 | tf_op jit(solution)/shard_map/ppermute | solution.py:44
  35.5 3.5 %collective-permute-start.9 = (bf16[8,16,1152]{2,1,0:T(8,128)(2,1)}, bf16[8,16,1152]{2,1,0:T(8,128)(2,1)S(1)}, u32[]{:S(2)}, u32[]{:S(2)}) collective-permute-start(bf16[8,16,1152]{2,1,0:T(8,128)(2,1)} %get-tuple-element.10), channel_id=1, source_target_pairs={{0,1},{1,0},{2,3},{3,2},{4,5},{5,4},{6,7},{7,6},{8,9},{9,8},{10,11... | collective-permute-start | bytes 884744 | tf_op jit(solution)/shard_map/ppermute | solution.py:44
  39.0 1.1 %copy-start.1 = (bf16[16,16,1152]{2,1,0:T(8,128)(2,1)S(1)}, bf16[16,16,1152]{2,1,0:T(8,128)(2,1)}, u32[]{:S(2)}) copy-start(bf16[16,16,1152]{2,1,0:T(8,128)(2,1)} %get-tuple-element.25) | copy-start | bytes 1769476
  43.6 1.6 %collective-permute-start.10 = (f32[2,4,24,256]{3,2,1,0:T(8,128)S(1)}, f32[2,4,24,256]{3,2,1,0:T(8,128)S(1)}, u32[]{:S(2)}, u32[]{:S(2)}) collective-permute-start(f32[2,4,24,256]{3,2,1,0:T(8,128)S(1)} %bitcast.65), channel_id=1, source_target_pairs={{0,1},{1,0},{2,3},{3,2},{4,5},{5,4},{6,7},{7,6},{8,9},{9,8},{10,11... | collective-permute-start | bytes 589832 | tf_op jit(solution)/shard_map/ppermute | solution.py:44
  45.3 5.1 %collective-permute-start.11 = (f32[4,24,256]{2,1,0:T(8,128)S(1)}, f32[4,24,256]{2,1,0:T(8,128)S(1)}, u32[]{:S(2)}, u32[]{:S(2)}) collective-permute-start(f32[4,24,256]{2,1,0:T(8,128)S(1)} %slice_bitcast_fusion), channel_id=1, source_target_pairs={{0,2},{1,3},{2,0},{3,1},{4,6},{5,7},{6,4},{7,5},{8,10},{9,11},{10,... | collective-permute-start | bytes 294920 | tf_op jit(solution)/shard_map/ppermute | solution.py:44
  50.5 4.5 %collective-permute-start.12 = (f32[24,256]{1,0:T(8,128)S(1)}, f32[24,256]{1,0:T(8,128)S(1)}, u32[]{:S(2)}, u32[]{:S(2)}) collective-permute-start(f32[24,256]{1,0:T(8,128)S(1)} %get-tuple-element.27), channel_id=1, source_target_pairs={{0,4},{1,5},{2,6},{3,7},{4,0},{5,1},{6,2},{7,3},{8,12},{9,13},{10,... | collective-permute-start | bytes 73736 | tf_op jit(solution)/shard_map/ppermute | solution.py:44
  50.6 4.9 %collective-permute-start.13 = (f32[24,256]{1,0:T(8,128)S(1)}, f32[24,256]{1,0:T(8,128)S(1)}, u32[]{:S(2)}, u32[]{:S(2)}) collective-permute-start(f32[24,256]{1,0:T(8,128)S(1)} %get-tuple-element.29), channel_id=1, source_target_pairs={{0,8},{1,9},{2,10},{3,11},{4,12},{5,13},{6,14},{7,15},{8,0},{9,1},... | collective-permute-start | bytes 73736 | tf_op jit(solution)/shard_map/ppermute | solution.py:44
  53.3 5.6 %collective-permute-start.14 = (f32[24,256]{1,0:T(8,128)S(1)}, f32[24,256]{1,0:T(8,128)S(1)}, u32[]{:S(2)}, u32[]{:S(2)}) collective-permute-start(f32[24,256]{1,0:T(8,128)S(1)} %get-tuple-element.28), channel_id=1, source_target_pairs={{0,12},{1,13},{2,14},{3,15},{4,8},{5,9},{6,10},{7,11},{8,4},{9,5},... | collective-permute-start | bytes 73736 | tf_op jit(solution)/shard_map/ppermute | solution.py:44

commit v14 on v12

--- a/solution.py
+++ b/solution.py
@@ -113,16 +113,11 @@
     weight_b = jnp.concatenate([p[0] for p in parts], axis=0)
     denom = jnp.concatenate([p[1] for p in parts], axis=0)
     numer = jnp.dot(weight_b, zvals, preferred_element_type=jnp.float32)
-    den_rows = -(-q_dev // width)
-    den_rows += -(q_dev + den_rows) % 8
-    den = jnp.pad(denom.reshape(nblk, q_dev), ((0, 0), (0, den_rows * width - q_dev)))
-    den = den.reshape(nblk, den_rows, width)
-    sums = jnp.concatenate([numer.reshape(nblk, q_dev, width), den], axis=1)
+    den = jnp.broadcast_to(denom[:, None], (denom.shape[0], 128))
+    sums = jnp.concatenate([numer, den], axis=1).reshape(nblk, q_dev, width + 128)
     sums = sums.reshape(tuple(len(offsets(g)) for g in groups) + sums.shape[1:])
     mine = scatter_rounds(sums, "blk", groups)
-    own_num = mine[:q_dev]
-    own_den = mine[q_dev:].reshape(den_rows * width)[:q_dev]
-    return own_num / own_den[:, None]
+    return mine[:, :width] / mine[:, width:width + 1]
 
 
 def solution(mesh):

time: 40.9 us -> 41 us (level)
  no operation moved by 1% of the time
where the time goes in v14:
time: 41 us; the launch traced here: 40.7 us
  waiting for transfers between devices  15.3 us (37%)
  starting transfers between devices  13.5 us (33%)
  other arithmetic  7.01 us (17%)
  matrix products  4.12 us (10%)
  local copies, waits for them, and re-layouts  0.6 us (1%)
    ppermute x10, waiting for transfers between devices, swap(): return lax.ppermute(x, axis, [(i, i ^ mask) for i in range(count)])  15.3 us
    ppermute x10, starting transfers between devices, swap(): return lax.ppermute(x, axis, [(i, i ^ mask) for i in range(count)])  13.5 us
    dot_general x3, matrix products, piece_weights(): lax.dot_general(rows, lib_ext, (((1,), (1,)), ((), ())), preferred_elemen...  3.79 us
    reduce_sum x1, other arithmetic, shards(): lib_sq = jnp.sum(jnp.square(library.astype(jnp.float32)), axis=1)  2.72 us
    reduce_sum x1, other arithmetic, shards(): jnp.sum(values, axis=0)  1.14 us
    unnamed x1, other arithmetic  0.85 us
    broadcast_in_dim x1, other arithmetic, gather_rounds(): pieces = [packet[None]]  0.85 us
  transfers between devices with their start and end apart: 10, of which 8 were waited for; matrix products, arithmetic and copies ran while one was open for 16% of the time, Pallas kernels for 0%

profile of v14, /device:TPU:0, one launch (start us, length us, event | category | flops | bytes accessed | tf_op | source)
XLA Modules:
  0.0 40.7 jit_solution(12299862026625367887)
XLA Ops:
  0.0 1.1 %convert_reduce_fusion = (f32[256]{0:T(256)S(1)}, f32[256]{0:T(256)S(1)}) fusion(bf16[768,256]{1,0:T(8,128)(2,1)} %param.5), kind=kLoop, calls=%fused_computation.9 | loop fusion | flops 785920 | bytes 395264 | tf_op jit(solution)/shard_map/reduce_sum | solution.py:92
  1.2 0.8 %maximum_bitcast_fusion = bf16[1,16,2176]{2,1,0:T(8,128)(2,1)S(1)} fusion(bf16[16,128]{1,0:T(8,128)(2,1)S(1)} %fusion.62, bf16[16,2048]{1,0:T(8,128)(2,1)} %param.3), kind=kLoop, calls=%fused_computation.45 | loop fusion | flops 139264 | bytes 139264 | tf_op jit(solution)/shard_map/broadcast_in_dim | solution.py:61
  2.0 3.1 %collective-permute-start = (bf16[1,16,2176]{2,1,0:T(8,128)(2,1)S(1)}, bf16[1,16,2176]{2,1,0:T(8,128)(2,1)S(1)}, u32[]{:S(2)}, u32[]{:S(2)}) collective-permute-start(bf16[1,16,2176]{2,1,0:T(8,128)(2,1)S(1)} %maximum_bitcast_fusion), channel_id=1, source_target_pairs={{0,4},{1,5},{2,6},{3,7},{4,0},{5,1},{6,2},{7,3},{8,12},{9,13},{10,... | collective-permute-start | bytes 208904 | tf_op jit(solution)/shard_map/ppermute | solution.py:37
  5.1 2.6 %collective-permute-start.1 = (bf16[1,16,2176]{2,1,0:T(8,128)(2,1)S(1)}, bf16[1,16,2176]{2,1,0:T(8,128)(2,1)S(1)}, u32[]{:S(2)}, u32[]{:S(2)}) collective-permute-start(bf16[1,16,2176]{2,1,0:T(8,128)(2,1)S(1)} %maximum_bitcast_fusion), channel_id=1, source_target_pairs={{0,8},{1,9},{2,10},{3,11},{4,12},{5,13},{6,14},{7,15},{8,0},{9,1},... | collective-permute-start | bytes 208904 | tf_op jit(solution)/shard_map/ppermute | solution.py:37
  7.7 0.0 collective-permute-start.2
  7.7 0.8 %constant_dynamic-update-slice_fusion.10 = (bf16[16,16,2176]{2,1,0:T(8,128)(2,1)S(1)}, bf16[8,16,2176]{2,1,0:T(8,128)(2,1)S(1)}) fusion(bf16[16,128]{1,0:T(8,128)(2,1)S(1)} %fusion.62, bf16[16,2048]{1,0:T(8,128)(2,1)} %param.3), kind=kLoop, calls=%fused_computation.67 | loop fusion | flops 139262 | bytes 208896
  8.5 0.0 copy-start
  8.5 2.7 %multiply_reduce_fusion = f32[768]{0:T(1024)S(1)} fusion(bf16[768,2048]{1,0:T(8,128)(2,1)} %param.4), kind=kLoop, calls=%fused_computation | loop fusion | flops 4717824 | bytes 3148800 | tf_op jit(solution)/shard_map/reduce_sum | solution.py:100
  11.3 0.0 collective-permute-done
  11.3 1.3 %collective-permute-done.1 = bf16[1,16,2176]{2,1,0:T(8,128)(2,1)S(1)} collective-permute-done((bf16[1,16,2176]{2,1,0:T(8,128)(2,1)S(1)}, bf16[1,16,2176]{2,1,0:T(8,128)(2,1)S(1)}, u32[]{:S(2)}, u32[]{:S(2)}) %collective-permute-start.1) | collective-permute-done | bytes 69664 | tf_op jit(solution)/shard_map/ppermute | solution.py:37
  12.6 1.3 %collective-permute-done.2 = bf16[1,16,2176]{2,1,0:T(8,128)(2,1)S(1)} collective-permute-done((bf16[1,16,2176]{2,1,0:T(8,128)(2,1)S(1)}, bf16[1,16,2176]{2,1,0:T(8,128)(2,1)S(1)}, u32[]{:S(2)}, u32[]{:S(2)}) %collective-permute-start.2) | collective-permute-done | bytes 69664 | tf_op jit(solution)/shard_map/ppermute | solution.py:37
  13.9 1.6 %collective-permute-start.3 = (bf16[4,16,2176]{2,1,0:T(8,128)(2,1)S(1)}, bf16[4,16,2176]{2,1,0:T(8,128)(2,1)S(1)}, u32[]{:S(2)}, u32[]{:S(2)}) collective-permute-start(bf16[4,16,2176]{2,1,0:T(8,128)(2,1)S(1)} %pad_maximum_fusion), channel_id=1, source_target_pairs={{0,2},{1,3},{2,0},{3,1},{4,6},{5,7},{6,4},{7,5},{8,10},{9,11},{10,... | collective-permute-start | bytes 835592 | tf_op jit(solution)/shard_map/ppermute | solution.py:37
  15.6 0.2 multiply_reduce_fusion.3
  15.7 0.0 copy-done
  15.7 1.2 %fusion.70 = (f32[64]{0:T(128)S(1)}, bf16[64,768]{1,0:T(8,128)(2,1)S(1)}) fusion(f32[768]{0:T(1024)S(1)} %multiply_reduce_fusion, f32[64]{0:T(128)S(1)} %multiply_reduce_fusion.3, bf16[64,2176]{1,0:T(8,128)(2,1)S(1)} %bitcast.43, bf16[768,2048]{1,0:T(8,128)(2,1)S(1)} %copy-done), kind=kOutput, calls=%fused_computation.92 | convolution fusion | flops 214253504 | bytes 3526144 | tf_op jit(solution)/shard_map/dot_general | solution.py:27
  16.9 3.6 %collective-permute-done.3 = bf16[4,16,2176]{2,1,0:T(8,128)(2,1)S(1)} collective-permute-done((bf16[4,16,2176]{2,1,0:T(8,128)(2,1)S(1)}, bf16[4,16,2176]{2,1,0:T(8,128)(2,1)S(1)}, u32[]{:S(2)}, u32[]{:S(2)}) %collective-permute-start.3) | collective-permute-done | bytes 278560 | tf_op jit(solution)/shard_map/ppermute | solution.py:37
  20.6 0.1 collective-permute-start.4
  20.7 0.2 multiply_reduce_fusion.2
  20.9 1.2 %fusion.69 = (f32[64]{0:T(128)S(1)}, bf16[64,768]{1,0:T(8,128)(2,1)S(1)}) fusion(f32[768]{0:T(1024)S(1)} %multiply_reduce_fusion, f32[64]{0:T(128)S(1)} %multiply_reduce_fusion.2, bf16[64,2176]{1,0:T(8,128)(2,1)S(1)} %bitcast.41, bf16[768,2048]{1,0:T(8,128)(2,1)S(1)} %copy-done), kind=kOutput, calls=%fused_computation.91 | convolution fusion | flops 214253504 | bytes 3526144 | tf_op jit(solution)/shard_map/dot_general | solution.py:27
  22.1 0.6 %collective-permute-done.4 = bf16[8,16,2176]{2,1,0:T(8,128)(2,1)S(1)} collective-permute-done((bf16[8,16,2176]{2,1,0:T(8,128)(2,1)S(1)}, bf16[8,16,2176]{2,1,0:T(8,128)(2,1)S(1)}, u32[]{:S(2)}, u32[]{:S(2)}) %collective-permute-start.4) | collective-permute-done | bytes 557088 | tf_op jit(solution)/shard_map/ppermute | solution.py:37
  22.6 0.1 constant_dynamic-update-slice_fusion.5
  22.8 0.2 multiply_reduce_fusion.1
  23.0 0.0 copy-start.1
  23.0 1.4 %fusion.68 = (f32[128]{0:T(128)S(1)}, bf16[128,768]{1,0:T(8,128)(2,1)S(1)}) fusion(f32[768]{0:T(1024)S(1)} %multiply_reduce_fusion, f32[128]{0:T(128)S(1)} %multiply_reduce_fusion.1, bf16[128,2176]{1,0:T(8,128)(2,1)S(1)} %bitcast.45, bf16[768,2048]{1,0:T(8,128)(2,1)S(1)} %copy-done), kind=kOutput, calls=%fused_computation.90 | convolution fusion | flops 428507008 | bytes 3903488 | tf_op jit(solution)/shard_map/dot_general | solution.py:27
  24.4 0.1 pad_maximum_fusion.3
  24.4 0.0 copy-done.1
  24.4 0.3 fusion.20
  24.8 0.1 copy.7
  25.0 0.2 collective-permute-start.5
  25.2 0.1 copy.6
  25.3 1.2 %collective-permute-done.5 = f32[2,4,16,384]{3,2,1,0:T(8,128)S(1)} collective-permute-done((f32[2,4,16,384]{3,2,1,0:T(8,128)S(1)}, f32[2,4,16,384]{3,2,1,0:T(8,128)S(1)}, u32[]{:S(2)}, u32[]{:S(2)}) %collective-permute-start.5) | collective-permute-done | bytes 196640 | tf_op jit(solution)/shard_map/ppermute | solution.py:37
  26.5 1.6 %collective-permute-start.6 = (f32[4,16,384]{2,1,0:T(8,128)S(1)}, f32[4,16,384]{2,1,0:T(8,128)S(1)}, u32[]{:S(2)}, u32[]{:S(2)}) collective-permute-start(f32[4,16,384]{2,1,0:T(8,128)S(1)} %slice_bitcast_fusion), channel_id=1, source_target_pairs={{0,2},{1,3},{2,0},{3,1},{4,6},{5,7},{6,4},{7,5},{8,10},{9,11},{10,... | collective-permute-start | bytes 294920 | tf_op jit(solution)/shard_map/ppermute | solution.py:37
  28.1 3.3 %collective-permute-done.6 = f32[4,16,384]{2,1,0:T(8,128)S(1)} collective-permute-done((f32[4,16,384]{2,1,0:T(8,128)S(1)}, f32[4,16,384]{2,1,0:T(8,128)S(1)}, u32[]{:S(2)}, u32[]{:S(2)}) %collective-permute-start.6) | collective-permute-done | bytes 98336 | tf_op jit(solution)/shard_map/ppermute | solution.py:37
  31.5 1.1 %collective-permute-start.7 = (f32[16,384]{1,0:T(8,128)S(1)}, f32[16,384]{1,0:T(8,128)S(1)}, u32[]{:S(2)}, u32[]{:S(2)}) collective-permute-start(f32[16,384]{1,0:T(8,128)S(1)} %get-tuple-element.29), channel_id=1, source_target_pairs={{0,4},{1,5},{2,6},{3,7},{4,0},{5,1},{6,2},{7,3},{8,12},{9,13},{10,... | collective-permute-start | bytes 73736 | tf_op jit(solution)/shard_map/ppermute | solution.py:37
  32.6 1.7 %collective-permute-start.8 = (f32[16,384]{1,0:T(8,128)S(1)}, f32[16,384]{1,0:T(8,128)S(1)}, u32[]{:S(2)}, u32[]{:S(2)}) collective-permute-start(f32[16,384]{1,0:T(8,128)S(1)} %get-tuple-element.31), channel_id=1, source_target_pairs={{0,8},{1,9},{2,10},{3,11},{4,12},{5,13},{6,14},{7,15},{8,0},{9,1},... | collective-permute-start | bytes 73736 | tf_op jit(solution)/shard_map/ppermute | solution.py:37
  34.3 1.6 %collective-permute-start.9 = (f32[16,384]{1,0:T(8,128)S(1)}, f32[16,384]{1,0:T(8,128)S(1)}, u32[]{:S(2)}, u32[]{:S(2)}) collective-permute-start(f32[16,384]{1,0:T(8,128)S(1)} %get-tuple-element.30), channel_id=1, source_target_pairs={{0,12},{1,13},{2,14},{3,15},{4,8},{5,9},{6,10},{7,11},{8,4},{9,5},... | collective-permute-start | bytes 73736 | tf_op jit(solution)/shard_map/ppermute | solution.py:37
  35.9 0.0 collective-permute-done.7
  35.9 1.4 %collective-permute-done.8 = f32[16,384]{1,0:T(8,128)S(1)} collective-permute-done((f32[16,384]{1,0:T(8,128)S(1)}, f32[16,384]{1,0:T(8,128)S(1)}, u32[]{:S(2)}, u32[]{:S(2)}) %collective-permute-start.8) | collective-permute-done | bytes 24608 | tf_op jit(solution)/shard_map/ppermute | solution.py:37
  37.3 2.6 %collective-permute-done.9 = f32[16,384]{1,0:T(8,128)S(1)} collective-permute-done((f32[16,384]{1,0:T(8,128)S(1)}, f32[16,384]{1,0:T(8,128)S(1)}, u32[]{:S(2)}, u32[]{:S(2)}) %collective-permute-start.9) | collective-permute-done | bytes 24608 | tf_op jit(solution)/shard_map/ppermute | solution.py:37
  39.9 0.1 slice_reduce_fusion
  40.0 0.7 %slice_divide_fusion = f32[16,256]{1,0:T(8,128)} fusion(f32[16,384]{1,0:T(8,128)S(1)} %fusion.56, f32[16]{0:T(128)S(1)} %slice_reduce_fusion), kind=kLoop, calls=%fused_computation.68 | loop fusion | flops 4096 | bytes 32832 | tf_op jit(solution)/shard_map/div | solution.py:120
  (18 shorter events, 0.4 us)
Async XLA Ops:
  2.0 9.2 %collective-permute-start = (bf16[1,16,2176]{2,1,0:T(8,128)(2,1)S(1)}, bf16[1,16,2176]{2,1,0:T(8,128)(2,1)S(1)}, u32[]{:S(2)}, u32[]{:S(2)}) collective-permute-start(bf16[1,16,2176]{2,1,0:T(8,128)(2,1)S(1)} %maximum_bitcast_fusion), channel_id=1, source_target_pairs={{0,4},{1,5},{2,6},{3,7},{4,0},{5,1},{6,2},{7,3},{8,12},{9,13},{10,... | collective-permute-start | bytes 208904 | tf_op jit(solution)/shard_map/ppermute | solution.py:37
  5.1 7.5 %collective-permute-start.1 = (bf16[1,16,2176]{2,1,0:T(8,128)(2,1)S(1)}, bf16[1,16,2176]{2,1,0:T(8,128)(2,1)S(1)}, u32[]{:S(2)}, u32[]{:S(2)}) collective-permute-start(bf16[1,16,2176]{2,1,0:T(8,128)(2,1)S(1)} %maximum_bitcast_fusion), channel_id=1, source_target_pairs={{0,8},{1,9},{2,10},{3,11},{4,12},{5,13},{6,14},{7,15},{8,0},{9,1},... | collective-permute-start | bytes 208904 | tf_op jit(solution)/shard_map/ppermute | solution.py:37
  7.7 6.2 %collective-permute-start.2 = (bf16[1,16,2176]{2,1,0:T(8,128)(2,1)S(1)}, bf16[1,16,2176]{2,1,0:T(8,128)(2,1)S(1)}, u32[]{:S(2)}, u32[]{:S(2)}) collective-permute-start(bf16[1,16,2176]{2,1,0:T(8,128)(2,1)S(1)} %maximum_bitcast_fusion), channel_id=1, source_target_pairs={{0,12},{1,13},{2,14},{3,15},{4,8},{5,9},{6,10},{7,11},{8,4},{9,5},... | collective-permute-start | bytes 208904 | tf_op jit(solution)/shard_map/ppermute | solution.py:37
  8.5 7.2 %copy-start = (bf16[768,2048]{1,0:T(8,128)(2,1)S(1)}, bf16[768,2048]{1,0:T(8,128)(2,1)}, u32[]{:S(2)}) copy-start(bf16[768,2048]{1,0:T(8,128)(2,1)} %param.4) | copy-start | bytes 9437188
  13.9 6.7 %collective-permute-start.3 = (bf16[4,16,2176]{2,1,0:T(8,128)(2,1)S(1)}, bf16[4,16,2176]{2,1,0:T(8,128)(2,1)S(1)}, u32[]{:S(2)}, u32[]{:S(2)}) collective-permute-start(bf16[4,16,2176]{2,1,0:T(8,128)(2,1)S(1)} %pad_maximum_fusion), channel_id=1, source_target_pairs={{0,2},{1,3},{2,0},{3,1},{4,6},{5,7},{6,4},{7,5},{8,10},{9,11},{10,... | collective-permute-start | bytes 835592 | tf_op jit(solution)/shard_map/ppermute | solution.py:37
  20.6 2.0 %collective-permute-start.4 = (bf16[8,16,2176]{2,1,0:T(8,128)(2,1)S(1)}, bf16[8,16,2176]{2,1,0:T(8,128)(2,1)S(1)}, u32[]{:S(2)}, u32[]{:S(2)}) collective-permute-start(bf16[8,16,2176]{2,1,0:T(8,128)(2,1)S(1)} %get-tuple-element.24), channel_id=1, source_target_pairs={{0,1},{1,0},{2,3},{3,2},{4,5},{5,4},{6,7},{7,6},{8,9},{9,8},{10,11... | collective-permute-start | bytes 1671176 | tf_op jit(solution)/shard_map/ppermute | solution.py:37
  23.0 1.4 %copy-start.1 = (bf16[768,256]{1,0:T(8,128)(2,1)S(1)}, bf16[768,256]{1,0:T(8,128)(2,1)}, u32[]{:S(2)}) copy-start(bf16[768,256]{1,0:T(8,128)(2,1)} %param.5) | copy-start | bytes 1179652
  25.0 1.5 %collective-permute-start.5 = (f32[2,4,16,384]{3,2,1,0:T(8,128)S(1)}, f32[2,4,16,384]{3,2,1,0:T(8,128)S(1)}, u32[]{:S(2)}, u32[]{:S(2)}) collective-permute-start(f32[2,4,16,384]{3,2,1,0:T(8,128)S(1)} %bitcast.49), channel_id=1, source_target_pairs={{0,1},{1,0},{2,3},{3,2},{4,5},{5,4},{6,7},{7,6},{8,9},{9,8},{10,11... | collective-permute-start | bytes 589832 | tf_op jit(solution)/shard_map/ppermute | solution.py:37
  26.5 4.9 %collective-permute-start.6 = (f32[4,16,384]{2,1,0:T(8,128)S(1)}, f32[4,16,384]{2,1,0:T(8,128)S(1)}, u32[]{:S(2)}, u32[]{:S(2)}) collective-permute-start(f32[4,16,384]{2,1,0:T(8,128)S(1)} %slice_bitcast_fusion), channel_id=1, source_target_pairs={{0,2},{1,3},{2,0},{3,1},{4,6},{5,7},{6,4},{7,5},{8,10},{9,11},{10,... | collective-permute-start | bytes 294920 | tf_op jit(solution)/shard_map/ppermute | solution.py:37
  31.5 4.5 %collective-permute-start.7 = (f32[16,384]{1,0:T(8,128)S(1)}, f32[16,384]{1,0:T(8,128)S(1)}, u32[]{:S(2)}, u32[]{:S(2)}) collective-permute-start(f32[16,384]{1,0:T(8,128)S(1)} %get-tuple-element.29), channel_id=1, source_target_pairs={{0,4},{1,5},{2,6},{3,7},{4,0},{5,1},{6,2},{7,3},{8,12},{9,13},{10,... | collective-permute-start | bytes 73736 | tf_op jit(solution)/shard_map/ppermute | solution.py:37
  32.6 4.8 %collective-permute-start.8 = (f32[16,384]{1,0:T(8,128)S(1)}, f32[16,384]{1,0:T(8,128)S(1)}, u32[]{:S(2)}, u32[]{:S(2)}) collective-permute-start(f32[16,384]{1,0:T(8,128)S(1)} %get-tuple-element.31), channel_id=1, source_target_pairs={{0,8},{1,9},{2,10},{3,11},{4,12},{5,13},{6,14},{7,15},{8,0},{9,1},... | collective-permute-start | bytes 73736 | tf_op jit(solution)/shard_map/ppermute | solution.py:37
  34.3 5.6 %collective-permute-start.9 = (f32[16,384]{1,0:T(8,128)S(1)}, f32[16,384]{1,0:T(8,128)S(1)}, u32[]{:S(2)}, u32[]{:S(2)}) collective-permute-start(f32[16,384]{1,0:T(8,128)S(1)} %get-tuple-element.30), channel_id=1, source_target_pairs={{0,12},{1,13},{2,14},{3,15},{4,8},{5,9},{6,10},{7,11},{8,4},{9,5},... | collective-permute-start | bytes 73736 | tf_op jit(solution)/shard_map/ppermute | solution.py:37

commit v15 on v14

--- a/solution.py
+++ b/solution.py
@@ -58,12 +58,23 @@
 
 
 def gather_rounds(packet, axis, groups, work):
+    rounds = list(reversed(groups))
     pieces = [packet[None]]
     results = []
     fresh = [packet[None]]
-    for group in reversed(groups):
+    early = []
+    for r, group in enumerate(rounds):
         buf = jnp.concatenate(pieces, axis=0) if len(pieces) > 1 else pieces[0]
-        got = [swap(buf, axis, m) for m in offsets(group)[1:]]
+        if r == 1:
+            got = [
+                [head, swap(buf[1:], axis, m)]
+                for head, m in zip(early, offsets(group)[1:])
+            ]
+            got = [g for pair in got for g in pair]
+        else:
+            got = [swap(buf, axis, m) for m in offsets(group)[1:]]
+        if r == 0 and len(rounds) > 1:
+            early = [swap(packet[None], axis, m) for m in offsets(rounds[1])[1:]]
         if results:
             got, results[-1] = lax.optimization_barrier((got, results[-1]))
         pieces += got

time: 41 us -> 40.1 us (0.978)
  waiting for transfers between devices: 15.3 us -> 11.8 us
  starting transfers between devices: 13.5 us -> 15.3 us
  local copies, waits for them, and re-layouts: 0.6 us -> 1.36 us
    ppermute x10 -> x11, waiting for transfers between devices: 15.3 us -> 11.8 us  [swap(): return lax.ppermute(x, axis, [(i, i ^ mask) for i in range(count)])]
    ppermute x10 -> x11, starting transfers between devices: 13.5 us -> 15.3 us  [swap(): return lax.ppermute(x, axis, [(i, i ^ mask) for i in range(count)])]
    unnamed x9 -> x10, local copies, waits for them, and re-layouts: 0.16 us -> 0.91 us
  transfers between devices with their start and end apart: 10 -> 11, of which waited for: 8 -> 7; matrix products, arithmetic and copies ran while one was open for 16% -> 17% of each run, Pallas kernels for 0% -> 0%
where the time goes in v15:
time: 40.1 us; the launch traced here: 39.8 us
  starting transfers between devices  15.3 us (38%)
  waiting for transfers between devices  11.8 us (29%)
  other arithmetic  7.07 us (18%)
  matrix products  4.12 us (10%)
  local copies, waits for them, and re-layouts  1.36 us (3%)
    ppermute x11, starting transfers between devices, swap(): return lax.ppermute(x, axis, [(i, i ^ mask) for i in range(count)])  15.3 us
    ppermute x11, waiting for transfers between devices, swap(): return lax.ppermute(x, axis, [(i, i ^ mask) for i in range(count)])  11.8 us
    dot_general x3, matrix products, piece_weights(): lax.dot_general(rows, lib_ext, (((1,), (1,)), ((), ())), preferred_elemen...  3.79 us
    reduce_sum x1, other arithmetic, shards(): lib_sq = jnp.sum(jnp.square(library.astype(jnp.float32)), axis=1)  2.72 us
    reduce_sum x1, other arithmetic, shards(): jnp.sum(values, axis=0)  1.14 us
    unnamed x10, local copies, waits for them, and re-layouts  0.91 us
    unnamed x1, other arithmetic  0.85 us
    broadcast_in_dim x1, other arithmetic, gather_rounds(): early = [swap(packet[None], axis, m) for m in offsets(rounds[1])[1:]]  0.85 us
  transfers between devices with their start and end apart: 11, of which 7 were waited for; matrix products, arithmetic and copies ran while one was open for 17% of the time, Pallas kernels for 0%

profile of v15, /device:TPU:0, one launch (start us, length us, event | category | flops | bytes accessed | tf_op | source)
XLA Modules:
  0.0 39.8 jit_solution(12641501369992738292)
XLA Ops:
  0.0 1.1 %convert_reduce_fusion = (f32[256]{0:T(256)S(1)}, f32[256]{0:T(256)S(1)}) fusion(bf16[768,256]{1,0:T(8,128)(2,1)} %param.5), kind=kLoop, calls=%fused_computation.9 | loop fusion | flops 785920 | bytes 395264 | tf_op jit(solution)/shard_map/reduce_sum | solution.py:103
  1.2 0.8 %maximum_bitcast_fusion = bf16[1,16,2176]{2,1,0:T(8,128)(2,1)S(1)} fusion(bf16[16,128]{1,0:T(8,128)(2,1)S(1)} %fusion.62, bf16[16,2048]{1,0:T(8,128)(2,1)} %param.3), kind=kLoop, calls=%fused_computation.47 | loop fusion | flops 139264 | bytes 139264 | tf_op jit(solution)/shard_map/broadcast_in_dim | solution.py:77
  2.0 3.1 %collective-permute-start.1 = (bf16[1,16,2176]{2,1,0:T(8,128)(2,1)S(1)}, bf16[1,16,2176]{2,1,0:T(8,128)(2,1)S(1)}, u32[]{:S(2)}, u32[]{:S(2)}) collective-permute-start(bf16[1,16,2176]{2,1,0:T(8,128)(2,1)S(1)} %maximum_bitcast_fusion), channel_id=1, source_target_pairs={{0,4},{1,5},{2,6},{3,7},{4,0},{5,1},{6,2},{7,3},{8,12},{9,13},{10,... | collective-permute-start | bytes 208904 | tf_op jit(solution)/shard_map/ppermute | solution.py:37
  5.1 2.6 %collective-permute-start.2 = (bf16[1,16,2176]{2,1,0:T(8,128)(2,1)S(1)}, bf16[1,16,2176]{2,1,0:T(8,128)(2,1)S(1)}, u32[]{:S(2)}, u32[]{:S(2)}) collective-permute-start(bf16[1,16,2176]{2,1,0:T(8,128)(2,1)S(1)} %maximum_bitcast_fusion), channel_id=1, source_target_pairs={{0,8},{1,9},{2,10},{3,11},{4,12},{5,13},{6,14},{7,15},{8,0},{9,1},... | collective-permute-start | bytes 208904 | tf_op jit(solution)/shard_map/ppermute | solution.py:37
  7.7 0.0 collective-permute-start.3
  7.7 1.7 %collective-permute-start = (bf16[1,16,2176]{2,1,0:T(8,128)(2,1)S(1)}, bf16[1,16,2176]{2,1,0:T(8,128)(2,1)S(1)}, u32[]{:S(2)}, u32[]{:S(2)}) collective-permute-start(bf16[1,16,2176]{2,1,0:T(8,128)(2,1)S(1)} %maximum_bitcast_fusion), channel_id=1, source_target_pairs={{0,2},{1,3},{2,0},{3,1},{4,6},{5,7},{6,4},{7,5},{8,10},{9,11},{10,... | collective-permute-start | bytes 208904 | tf_op jit(solution)/shard_map/ppermute | solution.py:37
  9.4 0.8 %constant_dynamic-update-slice_fusion.12 = (bf16[16,16,2176]{2,1,0:T(8,128)(2,1)S(1)}, bf16[8,16,2176]{2,1,0:T(8,128)(2,1)S(1)}) fusion(bf16[16,128]{1,0:T(8,128)(2,1)S(1)} %fusion.62, bf16[16,2048]{1,0:T(8,128)(2,1)} %param.3), kind=kLoop, calls=%fused_computation.64 | loop fusion | flops 139262 | bytes 208896
  10.3 0.0 copy-start
  10.3 2.7 %multiply_reduce_fusion = f32[768]{0:T(1024)S(1)} fusion(bf16[768,2048]{1,0:T(8,128)(2,1)} %param.4), kind=kLoop, calls=%fused_computation | loop fusion | flops 4717824 | bytes 3148800 | tf_op jit(solution)/shard_map/reduce_sum | solution.py:111
  13.0 0.0 collective-permute-done.1
  13.0 0.0 collective-permute-done.2
  13.0 0.9 %collective-permute-done.3 = bf16[1,16,2176]{2,1,0:T(8,128)(2,1)S(1)} collective-permute-done((bf16[1,16,2176]{2,1,0:T(8,128)(2,1)S(1)}, bf16[1,16,2176]{2,1,0:T(8,128)(2,1)S(1)}, u32[]{:S(2)}, u32[]{:S(2)}) %collective-permute-start.3) | collective-permute-done | bytes 69664 | tf_op jit(solution)/shard_map/ppermute | solution.py:37
  13.9 1.6 %collective-permute-start.4 = (bf16[3,16,2176]{2,1,0:T(8,128)(2,1)S(1)}, bf16[3,16,2176]{2,1,0:T(8,128)(2,1)S(1)}, u32[]{:S(2)}, u32[]{:S(2)}) collective-permute-start(bf16[3,16,2176]{2,1,0:T(8,128)(2,1)S(1)} %pad_maximum_fusion.2), channel_id=1, source_target_pairs={{0,2},{1,3},{2,0},{3,1},{4,6},{5,7},{6,4},{7,5},{8,10},{9,11},{10,... | collective-permute-start | bytes 626696 | tf_op jit(solution)/shard_map/ppermute | solution.py:37
  15.5 0.2 multiply_reduce_fusion.3
  15.8 0.0 copy-done
  15.8 1.2 %fusion.70 = (f32[64]{0:T(128)S(1)}, bf16[64,768]{1,0:T(8,128)(2,1)S(1)}) fusion(f32[768]{0:T(1024)S(1)} %multiply_reduce_fusion, f32[64]{0:T(128)S(1)} %multiply_reduce_fusion.3, bf16[64,2176]{1,0:T(8,128)(2,1)S(1)} %bitcast.41, bf16[768,2048]{1,0:T(8,128)(2,1)S(1)} %copy-done), kind=kOutput, calls=%fused_computation.96 | convolution fusion | flops 214253504 | bytes 3526144 | tf_op jit(solution)/shard_map/dot_general | solution.py:27
  17.0 0.0 collective-permute-done
  17.0 2.8 %collective-permute-done.4 = bf16[3,16,2176]{2,1,0:T(8,128)(2,1)S(1)} collective-permute-done((bf16[3,16,2176]{2,1,0:T(8,128)(2,1)S(1)}, bf16[3,16,2176]{2,1,0:T(8,128)(2,1)S(1)}, u32[]{:S(2)}, u32[]{:S(2)}) %collective-permute-start.4) | collective-permute-done | bytes 208928 | tf_op jit(solution)/shard_map/ppermute | solution.py:37
  19.8 0.1 collective-permute-start.5
  20.0 0.2 multiply_reduce_fusion.2
  20.1 1.2 %fusion.69 = (f32[64]{0:T(128)S(1)}, bf16[64,768]{1,0:T(8,128)(2,1)S(1)}) fusion(f32[768]{0:T(1024)S(1)} %multiply_reduce_fusion, f32[64]{0:T(128)S(1)} %multiply_reduce_fusion.2, bf16[64,2176]{1,0:T(8,128)(2,1)S(1)} %bitcast.43, bf16[768,2048]{1,0:T(8,128)(2,1)S(1)} %copy-done), kind=kOutput, calls=%fused_computation.95 | convolution fusion | flops 214253504 | bytes 3526144 | tf_op jit(solution)/shard_map/dot_general | solution.py:27
  21.3 0.5 %collective-permute-done.5 = bf16[8,16,2176]{2,1,0:T(8,128)(2,1)S(1)} collective-permute-done((bf16[8,16,2176]{2,1,0:T(8,128)(2,1)S(1)}, bf16[8,16,2176]{2,1,0:T(8,128)(2,1)S(1)}, u32[]{:S(2)}, u32[]{:S(2)}) %collective-permute-start.5) | collective-permute-done | bytes 557088 | tf_op jit(solution)/shard_map/ppermute | solution.py:37
  21.9 0.2 multiply_reduce_fusion.1
  22.0 1.4 %fusion.68 = (f32[128]{0:T(128)S(1)}, bf16[128,768]{1,0:T(8,128)(2,1)S(1)}) fusion(f32[768]{0:T(1024)S(1)} %multiply_reduce_fusion, f32[128]{0:T(128)S(1)} %multiply_reduce_fusion.1, bf16[128,2176]{1,0:T(8,128)(2,1)S(1)} %bitcast.45, bf16[768,2048]{1,0:T(8,128)(2,1)S(1)} %copy-done), kind=kOutput, calls=%fused_computation.94 | convolution fusion | flops 428507008 | bytes 3903488 | tf_op jit(solution)/shard_map/dot_general | solution.py:27
  23.4 0.0 copy-start.1
  23.4 0.1 constant_dynamic-update-slice_fusion.6
  23.6 0.1 pad_maximum_fusion.5
  23.7 0.7 %copy-done.1 = bf16[768,256]{1,0:T(8,128)(2,1)S(1)} copy-done((bf16[768,256]{1,0:T(8,128)(2,1)S(1)}, bf16[768,256]{1,0:T(8,128)(2,1)}, u32[]{:S(2)}) %copy-start.1) | copy-done | bytes 393240
  24.4 0.3 fusion.20
  24.8 0.1 copy.7
  24.9 0.2 collective-permute-start.6
  25.1 0.1 copy.6
  25.3 1.2 %collective-permute-done.6 = f32[2,4,16,384]{3,2,1,0:T(8,128)S(1)} collective-permute-done((f32[2,4,16,384]{3,2,1,0:T(8,128)S(1)}, f32[2,4,16,384]{3,2,1,0:T(8,128)S(1)}, u32[]{:S(2)}, u32[]{:S(2)}) %collective-permute-start.6) | collective-permute-done | bytes 196640 | tf_op jit(solution)/shard_map/ppermute | solution.py:37
  26.5 1.6 %collective-permute-start.7 = (f32[4,16,384]{2,1,0:T(8,128)S(1)}, f32[4,16,384]{2,1,0:T(8,128)S(1)}, u32[]{:S(2)}, u32[]{:S(2)}) collective-permute-start(f32[4,16,384]{2,1,0:T(8,128)S(1)} %slice_bitcast_fusion), channel_id=1, source_target_pairs={{0,2},{1,3},{2,0},{3,1},{4,6},{5,7},{6,4},{7,5},{8,10},{9,11},{10,... | collective-permute-start | bytes 294920 | tf_op jit(solution)/shard_map/ppermute | solution.py:37
  28.1 3.3 %collective-permute-done.7 = f32[4,16,384]{2,1,0:T(8,128)S(1)} collective-permute-done((f32[4,16,384]{2,1,0:T(8,128)S(1)}, f32[4,16,384]{2,1,0:T(8,128)S(1)}, u32[]{:S(2)}, u32[]{:S(2)}) %collective-permute-start.7) | collective-permute-done | bytes 98336 | tf_op jit(solution)/shard_map/ppermute | solution.py:37
  31.4 2.8 %collective-permute-start.10 = (f32[16,384]{1,0:T(8,128)S(1)}, f32[16,384]{1,0:T(8,128)S(1)}, u32[]{:S(2)}, u32[]{:S(2)}) collective-permute-start(f32[16,384]{1,0:T(8,128)S(1)} %get-tuple-element.32), channel_id=1, source_target_pairs={{0,12},{1,13},{2,14},{3,15},{4,8},{5,9},{6,10},{7,11},{8,4},{9,5},... | collective-permute-start | bytes 73736 | tf_op jit(solution)/shard_map/ppermute | solution.py:37
  34.2 0.0 collective-permute-start.9
  34.2 1.6 %collective-permute-start.8 = (f32[16,384]{1,0:T(8,128)S(1)}, f32[16,384]{1,0:T(8,128)S(1)}, u32[]{:S(2)}, u32[]{:S(2)}) collective-permute-start(f32[16,384]{1,0:T(8,128)S(1)} %get-tuple-element.31), channel_id=1, source_target_pairs={{0,4},{1,5},{2,6},{3,7},{4,0},{5,1},{6,2},{7,3},{8,12},{9,13},{10,... | collective-permute-start | bytes 73736 | tf_op jit(solution)/shard_map/ppermute | solution.py:37
  35.9 1.3 %collective-permute-done.10 = f32[16,384]{1,0:T(8,128)S(1)} collective-permute-done((f32[16,384]{1,0:T(8,128)S(1)}, f32[16,384]{1,0:T(8,128)S(1)}, u32[]{:S(2)}, u32[]{:S(2)}) %collective-permute-start.10) | collective-permute-done | bytes 24608 | tf_op jit(solution)/shard_map/ppermute | solution.py:37
  37.2 1.8 %collective-permute-done.9 = f32[16,384]{1,0:T(8,128)S(1)} collective-permute-done((f32[16,384]{1,0:T(8,128)S(1)}, f32[16,384]{1,0:T(8,128)S(1)}, u32[]{:S(2)}, u32[]{:S(2)}) %collective-permute-start.9) | collective-permute-done | bytes 24608 | tf_op jit(solution)/shard_map/ppermute | solution.py:37
  39.0 0.0 collective-permute-done.8
  39.0 0.1 slice_reduce_fusion
  39.1 0.7 %slice_divide_fusion = f32[16,256]{1,0:T(8,128)} fusion(f32[16,384]{1,0:T(8,128)S(1)} %fusion.56, f32[16]{0:T(128)S(1)} %slice_reduce_fusion), kind=kLoop, calls=%fused_computation.72 | loop fusion | flops 4096 | bytes 32832 | tf_op jit(solution)/shard_map/div | solution.py:131
  (21 shorter events, 0.4 us)
Async XLA Ops:
  2.0 11.0 %collective-permute-start.1 = (bf16[1,16,2176]{2,1,0:T(8,128)(2,1)S(1)}, bf16[1,16,2176]{2,1,0:T(8,128)(2,1)S(1)}, u32[]{:S(2)}, u32[]{:S(2)}) collective-permute-start(bf16[1,16,2176]{2,1,0:T(8,128)(2,1)S(1)} %maximum_bitcast_fusion), channel_id=1, source_target_pairs={{0,4},{1,5},{2,6},{3,7},{4,0},{5,1},{6,2},{7,3},{8,12},{9,13},{10,... | collective-permute-start | bytes 208904 | tf_op jit(solution)/shard_map/ppermute | solution.py:37
  5.1 7.9 %collective-permute-start.2 = (bf16[1,16,2176]{2,1,0:T(8,128)(2,1)S(1)}, bf16[1,16,2176]{2,1,0:T(8,128)(2,1)S(1)}, u32[]{:S(2)}, u32[]{:S(2)}) collective-permute-start(bf16[1,16,2176]{2,1,0:T(8,128)(2,1)S(1)} %maximum_bitcast_fusion), channel_id=1, source_target_pairs={{0,8},{1,9},{2,10},{3,11},{4,12},{5,13},{6,14},{7,15},{8,0},{9,1},... | collective-permute-start | bytes 208904 | tf_op jit(solution)/shard_map/ppermute | solution.py:37
  7.7 6.2 %collective-permute-start.3 = (bf16[1,16,2176]{2,1,0:T(8,128)(2,1)S(1)}, bf16[1,16,2176]{2,1,0:T(8,128)(2,1)S(1)}, u32[]{:S(2)}, u32[]{:S(2)}) collective-permute-start(bf16[1,16,2176]{2,1,0:T(8,128)(2,1)S(1)} %maximum_bitcast_fusion), channel_id=1, source_target_pairs={{0,12},{1,13},{2,14},{3,15},{4,8},{5,9},{6,10},{7,11},{8,4},{9,5},... | collective-permute-start | bytes 208904 | tf_op jit(solution)/shard_map/ppermute | solution.py:37
  7.7 9.3 %collective-permute-start = (bf16[1,16,2176]{2,1,0:T(8,128)(2,1)S(1)}, bf16[1,16,2176]{2,1,0:T(8,128)(2,1)S(1)}, u32[]{:S(2)}, u32[]{:S(2)}) collective-permute-start(bf16[1,16,2176]{2,1,0:T(8,128)(2,1)S(1)} %maximum_bitcast_fusion), channel_id=1, source_target_pairs={{0,2},{1,3},{2,0},{3,1},{4,6},{5,7},{6,4},{7,5},{8,10},{9,11},{10,... | collective-permute-start | bytes 208904 | tf_op jit(solution)/shard_map/ppermute | solution.py:37
  10.3 5.5 %copy-start = (bf16[768,2048]{1,0:T(8,128)(2,1)S(1)}, bf16[768,2048]{1,0:T(8,128)(2,1)}, u32[]{:S(2)}) copy-start(bf16[768,2048]{1,0:T(8,128)(2,1)} %param.4) | copy-start | bytes 9437188
  13.9 5.9 %collective-permute-start.4 = (bf16[3,16,2176]{2,1,0:T(8,128)(2,1)S(1)}, bf16[3,16,2176]{2,1,0:T(8,128)(2,1)S(1)}, u32[]{:S(2)}, u32[]{:S(2)}) collective-permute-start(bf16[3,16,2176]{2,1,0:T(8,128)(2,1)S(1)} %pad_maximum_fusion.2), channel_id=1, source_target_pairs={{0,2},{1,3},{2,0},{3,1},{4,6},{5,7},{6,4},{7,5},{8,10},{9,11},{10,... | collective-permute-start | bytes 626696 | tf_op jit(solution)/shard_map/ppermute | solution.py:37
  19.8 2.0 %collective-permute-start.5 = (bf16[8,16,2176]{2,1,0:T(8,128)(2,1)S(1)}, bf16[8,16,2176]{2,1,0:T(8,128)(2,1)S(1)}, u32[]{:S(2)}, u32[]{:S(2)}) collective-permute-start(bf16[8,16,2176]{2,1,0:T(8,128)(2,1)S(1)} %get-tuple-element.26), channel_id=1, source_target_pairs={{0,1},{1,0},{2,3},{3,2},{4,5},{5,4},{6,7},{7,6},{8,9},{9,8},{10,11... | collective-permute-start | bytes 1671176 | tf_op jit(solution)/shard_map/ppermute | solution.py:37
  23.4 1.0 %copy-start.1 = (bf16[768,256]{1,0:T(8,128)(2,1)S(1)}, bf16[768,256]{1,0:T(8,128)(2,1)}, u32[]{:S(2)}) copy-start(bf16[768,256]{1,0:T(8,128)(2,1)} %param.5) | copy-start | bytes 1179652
  24.9 1.5 %collective-permute-start.6 = (f32[2,4,16,384]{3,2,1,0:T(8,128)S(1)}, f32[2,4,16,384]{3,2,1,0:T(8,128)S(1)}, u32[]{:S(2)}, u32[]{:S(2)}) collective-permute-start(f32[2,4,16,384]{3,2,1,0:T(8,128)S(1)} %bitcast.49), channel_id=1, source_target_pairs={{0,1},{1,0},{2,3},{3,2},{4,5},{5,4},{6,7},{7,6},{8,9},{9,8},{10,11... | collective-permute-start | bytes 589832 | tf_op jit(solution)/shard_map/ppermute | solution.py:37
  26.5 4.9 %collective-permute-start.7 = (f32[4,16,384]{2,1,0:T(8,128)S(1)}, f32[4,16,384]{2,1,0:T(8,128)S(1)}, u32[]{:S(2)}, u32[]{:S(2)}) collective-permute-start(f32[4,16,384]{2,1,0:T(8,128)S(1)} %slice_bitcast_fusion), channel_id=1, source_target_pairs={{0,2},{1,3},{2,0},{3,1},{4,6},{5,7},{6,4},{7,5},{8,10},{9,11},{10,... | collective-permute-start | bytes 294920 | tf_op jit(solution)/shard_map/ppermute | solution.py:37
  31.4 5.8 %collective-permute-start.10 = (f32[16,384]{1,0:T(8,128)S(1)}, f32[16,384]{1,0:T(8,128)S(1)}, u32[]{:S(2)}, u32[]{:S(2)}) collective-permute-start(f32[16,384]{1,0:T(8,128)S(1)} %get-tuple-element.32), channel_id=1, source_target_pairs={{0,12},{1,13},{2,14},{3,15},{4,8},{5,9},{6,10},{7,11},{8,4},{9,5},... | collective-permute-start | bytes 73736 | tf_op jit(solution)/shard_map/ppermute | solution.py:37
  34.2 4.7 %collective-permute-start.9 = (f32[16,384]{1,0:T(8,128)S(1)}, f32[16,384]{1,0:T(8,128)S(1)}, u32[]{:S(2)}, u32[]{:S(2)}) collective-permute-start(f32[16,384]{1,0:T(8,128)S(1)} %get-tuple-element.33), channel_id=1, source_target_pairs={{0,8},{1,9},{2,10},{3,11},{4,12},{5,13},{6,14},{7,15},{8,0},{9,1},... | collective-permute-start | bytes 73736 | tf_op jit(solution)/shard_map/ppermute | solution.py:37
  34.2 4.7 %collective-permute-start.8 = (f32[16,384]{1,0:T(8,128)S(1)}, f32[16,384]{1,0:T(8,128)S(1)}, u32[]{:S(2)}, u32[]{:S(2)}) collective-permute-start(f32[16,384]{1,0:T(8,128)S(1)} %get-tuple-element.31), channel_id=1, source_target_pairs={{0,4},{1,5},{2,6},{3,7},{4,0},{5,1},{6,2},{7,3},{8,12},{9,13},{10,... | collective-permute-start | bytes 73736 | tf_op jit(solution)/shard_map/ppermute | solution.py:37

commit v16 on v14

--- a/solution.py
+++ b/solution.py
@@ -57,20 +57,34 @@
     return masks
 
 
+def cat(parts):
+    return jnp.concatenate(parts, axis=0) if len(parts) > 1 else parts[0]
+
+
 def gather_rounds(packet, axis, groups, work):
+    rounds = list(reversed(groups))
     pieces = [packet[None]]
     results = []
     fresh = [packet[None]]
-    for group in reversed(groups):
-        buf = jnp.concatenate(pieces, axis=0) if len(pieces) > 1 else pieces[0]
-        got = [swap(buf, axis, m) for m in offsets(group)[1:]]
+    early, mark = None, 0
+    for r, group in enumerate(rounds):
+        masks = offsets(group)[1:]
+        if early is None:
+            got = [[swap(cat(pieces), axis, m)] for m in masks]
+        else:
+            rest = cat(pieces[mark:])
+            got = [[head, swap(rest, axis, m)] for head, m in zip(early, masks)]
+        if r + 1 < len(rounds):
+            early = [swap(cat(pieces), axis, m) for m in offsets(rounds[r + 1])[1:]]
+            mark = len(pieces)
         if results:
             got, results[-1] = lax.optimization_barrier((got, results[-1]))
+        got = [piece for pair in got for piece in pair]
         pieces += got
         fresh += got
-        results.append(work(jnp.concatenate(fresh, axis=0)))
+        results.append(work(cat(fresh)))
         fresh = []
-    return jnp.concatenate(pieces, axis=0), results
+    return cat(pieces), results
 
 
 def scatter_rounds(buf, axis, groups):

time: 41 us -> 39.4 us (0.961)
  waiting for transfers between devices: 15.3 us -> 12.3 us
  starting transfers between devices: 13.5 us -> 14.9 us
    ppermute x10 -> x12, waiting for transfers between devices: 15.3 us -> 12.3 us  [swap(): return lax.ppermute(x, axis, [(i, i ^ mask) for i in range(count)])]
    ppermute x10 -> x12, starting transfers between devices: 13.5 us -> 14.9 us  [swap(): return lax.ppermute(x, axis, [(i, i ^ mask) for i in range(count)])]
  transfers between devices with their start and end apart: 10 -> 12, of which waited for: 8 -> 7; matrix products, arithmetic and copies ran while one was open for 16% -> 17% of each run, Pallas kernels for 0% -> 0%
where the time goes in v16:
time: 39.4 us; the launch traced here: 39.2 us
  starting transfers between devices  14.9 us (38%)
  waiting for transfers between devices  12.3 us (31%)
  other arithmetic  7.1 us (18%)
  matrix products  4.13 us (10%)
  local copies, waits for them, and re-layouts  0.59 us (1%)
    ppermute x12, starting transfers between devices, swap(): return lax.ppermute(x, axis, [(i, i ^ mask) for i in range(count)])  14.9 us
    ppermute x12, waiting for transfers between devices, swap(): return lax.ppermute(x, axis, [(i, i ^ mask) for i in range(count)])  12.3 us
    dot_general x3, matrix products, piece_weights(): lax.dot_general(rows, lib_ext, (((1,), (1,)), ((), ())), preferred_elemen...  3.79 us
    reduce_sum x1, other arithmetic, shards(): lib_sq = jnp.sum(jnp.square(library.astype(jnp.float32)), axis=1)  2.72 us
    reduce_sum x1, other arithmetic, shards(): jnp.sum(values, axis=0)  1.14 us
    broadcast_in_dim x1, other arithmetic, gather_rounds(): pieces = [packet[None]]  0.85 us
    unnamed x1, other arithmetic  0.84 us
  transfers between devices with their start and end apart: 12, of which 7 were waited for; matrix products, arithmetic and copies ran while one was open for 17% of the time, Pallas kernels for 0%

profile of v16, /device:TPU:0, one launch (start us, length us, event | category | flops | bytes accessed | tf_op | source)
XLA Modules:
  0.0 39.2 jit_solution(6347446725590209326)
XLA Ops:
  0.0 1.1 %convert_reduce_fusion = (f32[256]{0:T(256)S(1)}, f32[256]{0:T(256)S(1)}) fusion(bf16[768,256]{1,0:T(8,128)(2,1)} %param.5), kind=kLoop, calls=%fused_computation.9 | loop fusion | flops 785920 | bytes 395264 | tf_op jit(solution)/shard_map/reduce_sum | solution.py:106
  1.2 0.8 %maximum_bitcast_fusion = bf16[1,16,2176]{2,1,0:T(8,128)(2,1)S(1)} fusion(bf16[16,128]{1,0:T(8,128)(2,1)S(1)} %fusion.62, bf16[16,2048]{1,0:T(8,128)(2,1)} %param.3), kind=kLoop, calls=%fused_computation.47 | loop fusion | flops 139264 | bytes 139264 | tf_op jit(solution)/shard_map/broadcast_in_dim | solution.py:66
  2.0 5.1 %collective-permute-start.3 = (bf16[1,16,2176]{2,1,0:T(8,128)(2,1)S(1)}, bf16[1,16,2176]{2,1,0:T(8,128)(2,1)S(1)}, u32[]{:S(2)}, u32[]{:S(2)}) collective-permute-start(bf16[1,16,2176]{2,1,0:T(8,128)(2,1)S(1)} %maximum_bitcast_fusion), channel_id=1, source_target_pairs={{0,12},{1,13},{2,14},{3,15},{4,8},{5,9},{6,10},{7,11},{8,4},{9,5},... | collective-permute-start | bytes 208904 | tf_op jit(solution)/shard_map/ppermute | solution.py:37
  7.1 0.0 collective-permute-start.2
  7.1 0.6 %collective-permute-start.1 = (bf16[1,16,2176]{2,1,0:T(8,128)(2,1)S(1)}, bf16[1,16,2176]{2,1,0:T(8,128)(2,1)S(1)}, u32[]{:S(2)}, u32[]{:S(2)}) collective-permute-start(bf16[1,16,2176]{2,1,0:T(8,128)(2,1)S(1)} %maximum_bitcast_fusion), channel_id=1, source_target_pairs={{0,4},{1,5},{2,6},{3,7},{4,0},{5,1},{6,2},{7,3},{8,12},{9,13},{10,... | collective-permute-start | bytes 208904 | tf_op jit(solution)/shard_map/ppermute | solution.py:37
  7.7 1.7 %collective-permute-start = (bf16[1,16,2176]{2,1,0:T(8,128)(2,1)S(1)}, bf16[1,16,2176]{2,1,0:T(8,128)(2,1)S(1)}, u32[]{:S(2)}, u32[]{:S(2)}) collective-permute-start(bf16[1,16,2176]{2,1,0:T(8,128)(2,1)S(1)} %maximum_bitcast_fusion), channel_id=1, source_target_pairs={{0,2},{1,3},{2,0},{3,1},{4,6},{5,7},{6,4},{7,5},{8,10},{9,11},{10,... | collective-permute-start | bytes 208904 | tf_op jit(solution)/shard_map/ppermute | solution.py:37
  9.4 0.8 %constant_dynamic-update-slice_fusion.9 = bf16[16,16,2176]{2,1,0:T(8,128)(2,1)S(1)} fusion(bf16[16,128]{1,0:T(8,128)(2,1)S(1)} %fusion.62, bf16[16,2048]{1,0:T(8,128)(2,1)} %param.3), kind=kLoop, calls=%fused_computation.68 | loop fusion | flops 139263 | bytes 139264
  10.3 0.0 copy-start
  10.3 2.7 %multiply_reduce_fusion = f32[768]{0:T(1024)S(1)} fusion(bf16[768,2048]{1,0:T(8,128)(2,1)} %param.4), kind=kLoop, calls=%fused_computation | loop fusion | flops 4717824 | bytes 3148800 | tf_op jit(solution)/shard_map/reduce_sum | solution.py:114
  13.0 0.0 collective-permute-done.3
  13.0 0.0 collective-permute-done.2
  13.0 0.0 collective-permute-done.1
  13.0 1.6 %collective-permute-start.4 = (bf16[3,16,2176]{2,1,0:T(8,128)(2,1)S(1)}, bf16[3,16,2176]{2,1,0:T(8,128)(2,1)S(1)}, u32[]{:S(2)}, u32[]{:S(2)}) collective-permute-start(bf16[3,16,2176]{2,1,0:T(8,128)(2,1)S(1)} %pad_maximum_fusion.2), channel_id=1, source_target_pairs={{0,2},{1,3},{2,0},{3,1},{4,6},{5,7},{6,4},{7,5},{8,10},{9,11},{10,... | collective-permute-start | bytes 626696 | tf_op jit(solution)/shard_map/ppermute | solution.py:37
  14.7 0.1 collective-permute-start.5
  14.8 0.2 multiply_reduce_fusion.3
  15.0 0.0 copy-done
  15.0 1.2 %fusion.70 = (f32[64]{0:T(128)S(1)}, bf16[64,768]{1,0:T(8,128)(2,1)S(1)}) fusion(f32[768]{0:T(1024)S(1)} %multiply_reduce_fusion, f32[64]{0:T(128)S(1)} %multiply_reduce_fusion.3, bf16[64,2176]{1,0:T(8,128)(2,1)S(1)} %bitcast.39, bf16[768,2048]{1,0:T(8,128)(2,1)S(1)} %copy-done), kind=kOutput, calls=%fused_computation.93 | convolution fusion | flops 214253504 | bytes 3526144 | tf_op jit(solution)/shard_map/dot_general | solution.py:27
  16.2 0.0 collective-permute-done
  16.2 3.5 %collective-permute-done.4 = bf16[3,16,2176]{2,1,0:T(8,128)(2,1)S(1)} collective-permute-done((bf16[3,16,2176]{2,1,0:T(8,128)(2,1)S(1)}, bf16[3,16,2176]{2,1,0:T(8,128)(2,1)S(1)}, u32[]{:S(2)}, u32[]{:S(2)}) %collective-permute-start.4) | collective-permute-done | bytes 208928 | tf_op jit(solution)/shard_map/ppermute | solution.py:37
  19.7 0.1 collective-permute-start.6
  19.8 0.2 multiply_reduce_fusion.2
  20.0 1.2 %fusion.69 = (f32[64]{0:T(128)S(1)}, bf16[64,768]{1,0:T(8,128)(2,1)S(1)}) fusion(f32[768]{0:T(1024)S(1)} %multiply_reduce_fusion, f32[64]{0:T(128)S(1)} %multiply_reduce_fusion.2, bf16[64,2176]{1,0:T(8,128)(2,1)S(1)} %bitcast.43, bf16[768,2048]{1,0:T(8,128)(2,1)S(1)} %copy-done), kind=kOutput, calls=%fused_computation.92 | convolution fusion | flops 214253504 | bytes 3526144 | tf_op jit(solution)/shard_map/dot_general | solution.py:27
  21.2 0.0 collective-permute-done.5
  21.2 0.2 collective-permute-done.6
  21.4 0.1 pad_maximum_fusion
  21.6 0.2 multiply_reduce_fusion.1
  21.8 0.0 copy-start.1
  21.8 1.4 %fusion.68 = (f32[128]{0:T(128)S(1)}, bf16[128,768]{1,0:T(8,128)(2,1)S(1)}) fusion(f32[768]{0:T(1024)S(1)} %multiply_reduce_fusion, f32[128]{0:T(128)S(1)} %multiply_reduce_fusion.1, bf16[128,2176]{1,0:T(8,128)(2,1)S(1)} %bitcast.41, bf16[768,2048]{1,0:T(8,128)(2,1)S(1)} %copy-done), kind=kOutput, calls=%fused_computation.91 | convolution fusion | flops 428507008 | bytes 3903488 | tf_op jit(solution)/shard_map/dot_general | solution.py:27
  23.1 0.1 pad_maximum_fusion.5
  23.2 0.0 copy-done.1
  23.2 0.3 fusion.20
  23.6 0.1 copy.7
  23.8 0.4 %collective-permute-start.7 = (f32[2,4,16,384]{3,2,1,0:T(8,128)S(1)}, f32[2,4,16,384]{3,2,1,0:T(8,128)S(1)}, u32[]{:S(2)}, u32[]{:S(2)}) collective-permute-start(f32[2,4,16,384]{3,2,1,0:T(8,128)S(1)} %bitcast.47), channel_id=1, source_target_pairs={{0,1},{1,0},{2,3},{3,2},{4,5},{5,4},{6,7},{7,6},{8,9},{9,8},{10,11... | collective-permute-start | bytes 589832 | tf_op jit(solution)/shard_map/ppermute | solution.py:37
  24.2 0.1 copy.6
  24.3 1.0 %collective-permute-done.7 = f32[2,4,16,384]{3,2,1,0:T(8,128)S(1)} collective-permute-done((f32[2,4,16,384]{3,2,1,0:T(8,128)S(1)}, f32[2,4,16,384]{3,2,1,0:T(8,128)S(1)}, u32[]{:S(2)}, u32[]{:S(2)}) %collective-permute-start.7) | collective-permute-done | bytes 196640 | tf_op jit(solution)/shard_map/ppermute | solution.py:37
  25.3 1.8 %collective-permute-start.8 = (f32[4,16,384]{2,1,0:T(8,128)S(1)}, f32[4,16,384]{2,1,0:T(8,128)S(1)}, u32[]{:S(2)}, u32[]{:S(2)}) collective-permute-start(f32[4,16,384]{2,1,0:T(8,128)S(1)} %slice_bitcast_fusion), channel_id=1, source_target_pairs={{0,2},{1,3},{2,0},{3,1},{4,6},{5,7},{6,4},{7,5},{8,10},{9,11},{10,... | collective-permute-start | bytes 294920 | tf_op jit(solution)/shard_map/ppermute | solution.py:37
  27.1 3.3 %collective-permute-done.8 = f32[4,16,384]{2,1,0:T(8,128)S(1)} collective-permute-done((f32[4,16,384]{2,1,0:T(8,128)S(1)}, f32[4,16,384]{2,1,0:T(8,128)S(1)}, u32[]{:S(2)}, u32[]{:S(2)}) %collective-permute-start.8) | collective-permute-done | bytes 98336 | tf_op jit(solution)/shard_map/ppermute | solution.py:37
  30.5 0.8 %collective-permute-start.9 = (f32[16,384]{1,0:T(8,128)S(1)}, f32[16,384]{1,0:T(8,128)S(1)}, u32[]{:S(2)}, u32[]{:S(2)}) collective-permute-start(f32[16,384]{1,0:T(8,128)S(1)} %get-tuple-element.33), channel_id=1, source_target_pairs={{0,4},{1,5},{2,6},{3,7},{4,0},{5,1},{6,2},{7,3},{8,12},{9,13},{10,... | collective-permute-start | bytes 73736 | tf_op jit(solution)/shard_map/ppermute | solution.py:37
  31.3 2.4 %collective-permute-start.11 = (f32[16,384]{1,0:T(8,128)S(1)}, f32[16,384]{1,0:T(8,128)S(1)}, u32[]{:S(2)}, u32[]{:S(2)}) collective-permute-start(f32[16,384]{1,0:T(8,128)S(1)} %get-tuple-element.34), channel_id=1, source_target_pairs={{0,12},{1,13},{2,14},{3,15},{4,8},{5,9},{6,10},{7,11},{8,4},{9,5},... | collective-permute-start | bytes 73736 | tf_op jit(solution)/shard_map/ppermute | solution.py:37
  33.6 0.4 collective-permute-start.10
  34.0 0.3 collective-permute-done.9
  34.3 2.6 %collective-permute-done.11 = f32[16,384]{1,0:T(8,128)S(1)} collective-permute-done((f32[16,384]{1,0:T(8,128)S(1)}, f32[16,384]{1,0:T(8,128)S(1)}, u32[]{:S(2)}, u32[]{:S(2)}) %collective-permute-start.11) | collective-permute-done | bytes 24608 | tf_op jit(solution)/shard_map/ppermute | solution.py:37
  36.9 1.4 %collective-permute-done.10 = f32[16,384]{1,0:T(8,128)S(1)} collective-permute-done((f32[16,384]{1,0:T(8,128)S(1)}, f32[16,384]{1,0:T(8,128)S(1)}, u32[]{:S(2)}, u32[]{:S(2)}) %collective-permute-start.10) | collective-permute-done | bytes 24608 | tf_op jit(solution)/shard_map/ppermute | solution.py:37
  38.4 0.1 slice_reduce_fusion
  38.5 0.7 %slice_divide_fusion = f32[16,256]{1,0:T(8,128)} fusion(f32[16,384]{1,0:T(8,128)S(1)} %fusion.56, f32[16]{0:T(128)S(1)} %slice_reduce_fusion), kind=kLoop, calls=%fused_computation.69 | loop fusion | flops 4096 | bytes 32832 | tf_op jit(solution)/shard_map/div | solution.py:134
  (22 shorter events, 0.4 us)
Async XLA Ops:
  2.0 11.0 %collective-permute-start.3 = (bf16[1,16,2176]{2,1,0:T(8,128)(2,1)S(1)}, bf16[1,16,2176]{2,1,0:T(8,128)(2,1)S(1)}, u32[]{:S(2)}, u32[]{:S(2)}) collective-permute-start(bf16[1,16,2176]{2,1,0:T(8,128)(2,1)S(1)} %maximum_bitcast_fusion), channel_id=1, source_target_pairs={{0,12},{1,13},{2,14},{3,15},{4,8},{5,9},{6,10},{7,11},{8,4},{9,5},... | collective-permute-start | bytes 208904 | tf_op jit(solution)/shard_map/ppermute | solution.py:37
  7.1 5.9 %collective-permute-start.2 = (bf16[1,16,2176]{2,1,0:T(8,128)(2,1)S(1)}, bf16[1,16,2176]{2,1,0:T(8,128)(2,1)S(1)}, u32[]{:S(2)}, u32[]{:S(2)}) collective-permute-start(bf16[1,16,2176]{2,1,0:T(8,128)(2,1)S(1)} %maximum_bitcast_fusion), channel_id=1, source_target_pairs={{0,8},{1,9},{2,10},{3,11},{4,12},{5,13},{6,14},{7,15},{8,0},{9,1},... | collective-permute-start | bytes 208904 | tf_op jit(solution)/shard_map/ppermute | solution.py:37
  7.1 5.9 %collective-permute-start.1 = (bf16[1,16,2176]{2,1,0:T(8,128)(2,1)S(1)}, bf16[1,16,2176]{2,1,0:T(8,128)(2,1)S(1)}, u32[]{:S(2)}, u32[]{:S(2)}) collective-permute-start(bf16[1,16,2176]{2,1,0:T(8,128)(2,1)S(1)} %maximum_bitcast_fusion), channel_id=1, source_target_pairs={{0,4},{1,5},{2,6},{3,7},{4,0},{5,1},{6,2},{7,3},{8,12},{9,13},{10,... | collective-permute-start | bytes 208904 | tf_op jit(solution)/shard_map/ppermute | solution.py:37
  7.7 8.5 %collective-permute-start = (bf16[1,16,2176]{2,1,0:T(8,128)(2,1)S(1)}, bf16[1,16,2176]{2,1,0:T(8,128)(2,1)S(1)}, u32[]{:S(2)}, u32[]{:S(2)}) collective-permute-start(bf16[1,16,2176]{2,1,0:T(8,128)(2,1)S(1)} %maximum_bitcast_fusion), channel_id=1, source_target_pairs={{0,2},{1,3},{2,0},{3,1},{4,6},{5,7},{6,4},{7,5},{8,10},{9,11},{10,... | collective-permute-start | bytes 208904 | tf_op jit(solution)/shard_map/ppermute | solution.py:37
  10.3 4.7 %copy-start = (bf16[768,2048]{1,0:T(8,128)(2,1)S(1)}, bf16[768,2048]{1,0:T(8,128)(2,1)}, u32[]{:S(2)}) copy-start(bf16[768,2048]{1,0:T(8,128)(2,1)} %param.4) | copy-start | bytes 9437188
  13.0 6.6 %collective-permute-start.4 = (bf16[3,16,2176]{2,1,0:T(8,128)(2,1)S(1)}, bf16[3,16,2176]{2,1,0:T(8,128)(2,1)S(1)}, u32[]{:S(2)}, u32[]{:S(2)}) collective-permute-start(bf16[3,16,2176]{2,1,0:T(8,128)(2,1)S(1)} %pad_maximum_fusion.2), channel_id=1, source_target_pairs={{0,2},{1,3},{2,0},{3,1},{4,6},{5,7},{6,4},{7,5},{8,10},{9,11},{10,... | collective-permute-start | bytes 626696 | tf_op jit(solution)/shard_map/ppermute | solution.py:37
  14.7 6.5 %collective-permute-start.5 = (bf16[4,16,2176]{2,1,0:T(8,128)(2,1)S(1)}, bf16[4,16,2176]{2,1,0:T(8,128)(2,1)S(1)}, u32[]{:S(2)}, u32[]{:S(2)}) collective-permute-start(bf16[4,16,2176]{2,1,0:T(8,128)(2,1)S(1)} %pad_maximum_fusion.1), channel_id=1, source_target_pairs={{0,1},{1,0},{2,3},{3,2},{4,5},{5,4},{6,7},{7,6},{8,9},{9,8},{10,11... | collective-permute-start | bytes 835592 | tf_op jit(solution)/shard_map/ppermute | solution.py:37
  19.7 1.6 %collective-permute-start.6 = (bf16[4,16,2176]{2,1,0:T(8,128)(2,1)S(1)}, bf16[4,16,2176]{2,1,0:T(8,128)(2,1)S(1)}, u32[]{:S(2)}, u32[]{:S(2)}) collective-permute-start(bf16[4,16,2176]{2,1,0:T(8,128)(2,1)S(1)} %get-tuple-element.28), channel_id=1, source_target_pairs={{0,1},{1,0},{2,3},{3,2},{4,5},{5,4},{6,7},{7,6},{8,9},{9,8},{10,11... | collective-permute-start | bytes 835592 | tf_op jit(solution)/shard_map/ppermute | solution.py:37
  21.8 1.4 %copy-start.1 = (bf16[768,256]{1,0:T(8,128)(2,1)S(1)}, bf16[768,256]{1,0:T(8,128)(2,1)}, u32[]{:S(2)}) copy-start(bf16[768,256]{1,0:T(8,128)(2,1)} %param.5) | copy-start | bytes 1179652
  23.8 1.5 %collective-permute-start.7 = (f32[2,4,16,384]{3,2,1,0:T(8,128)S(1)}, f32[2,4,16,384]{3,2,1,0:T(8,128)S(1)}, u32[]{:S(2)}, u32[]{:S(2)}) collective-permute-start(f32[2,4,16,384]{3,2,1,0:T(8,128)S(1)} %bitcast.47), channel_id=1, source_target_pairs={{0,1},{1,0},{2,3},{3,2},{4,5},{5,4},{6,7},{7,6},{8,9},{9,8},{10,11... | collective-permute-start | bytes 589832 | tf_op jit(solution)/shard_map/ppermute | solution.py:37
  25.3 5.1 %collective-permute-start.8 = (f32[4,16,384]{2,1,0:T(8,128)S(1)}, f32[4,16,384]{2,1,0:T(8,128)S(1)}, u32[]{:S(2)}, u32[]{:S(2)}) collective-permute-start(f32[4,16,384]{2,1,0:T(8,128)S(1)} %slice_bitcast_fusion), channel_id=1, source_target_pairs={{0,2},{1,3},{2,0},{3,1},{4,6},{5,7},{6,4},{7,5},{8,10},{9,11},{10,... | collective-permute-start | bytes 294920 | tf_op jit(solution)/shard_map/ppermute | solution.py:37
  30.5 3.9 %collective-permute-start.9 = (f32[16,384]{1,0:T(8,128)S(1)}, f32[16,384]{1,0:T(8,128)S(1)}, u32[]{:S(2)}, u32[]{:S(2)}) collective-permute-start(f32[16,384]{1,0:T(8,128)S(1)} %get-tuple-element.33), channel_id=1, source_target_pairs={{0,4},{1,5},{2,6},{3,7},{4,0},{5,1},{6,2},{7,3},{8,12},{9,13},{10,... | collective-permute-start | bytes 73736 | tf_op jit(solution)/shard_map/ppermute | solution.py:37
  31.3 5.7 %collective-permute-start.11 = (f32[16,384]{1,0:T(8,128)S(1)}, f32[16,384]{1,0:T(8,128)S(1)}, u32[]{:S(2)}, u32[]{:S(2)}) collective-permute-start(f32[16,384]{1,0:T(8,128)S(1)} %get-tuple-element.34), channel_id=1, source_target_pairs={{0,12},{1,13},{2,14},{3,15},{4,8},{5,9},{6,10},{7,11},{8,4},{9,5},... | collective-permute-start | bytes 73736 | tf_op jit(solution)/shard_map/ppermute | solution.py:37
  33.6 4.7 %collective-permute-start.10 = (f32[16,384]{1,0:T(8,128)S(1)}, f32[16,384]{1,0:T(8,128)S(1)}, u32[]{:S(2)}, u32[]{:S(2)}) collective-permute-start(f32[16,384]{1,0:T(8,128)S(1)} %get-tuple-element.35), channel_id=1, source_target_pairs={{0,8},{1,9},{2,10},{3,11},{4,12},{5,13},{6,14},{7,15},{8,0},{9,1},... | collective-permute-start | bytes 73736 | tf_op jit(solution)/shard_map/ppermute | solution.py:37

commit v17 on v16

--- a/solution.py
+++ b/solution.py
@@ -25,11 +25,11 @@
     blockf = rows[:, :feat].astype(jnp.float32)
     q_sq = jnp.sum(blockf * blockf, axis=1)
     inner = lax.dot_general(
-        rows, lib_ext, (((1,), (1,)), ((), ())), preferred_element_type=jnp.float32
+        lib_ext, rows, (((1,), (1,)), ((), ())), preferred_element_type=jnp.float32
     )
-    tanimoto = inner / (q_sq[:, None] + lib_sq[None, :] - inner)
+    tanimoto = inner / (q_sq[None, :] + lib_sq[:, None] - inner)
     weight = jnp.exp((tanimoto - 1.0) / TAU)
-    return weight.astype(jnp.bfloat16), jnp.sum(weight, axis=1)
+    return weight.astype(jnp.bfloat16), jnp.sum(weight, axis=0)
 
 
 def swap(x, axis, mask):
@@ -124,9 +124,11 @@
     spread = col_sq / total - mean * mean
     zvals = ((values - mean) * lax.rsqrt(spread + EPS)).astype(jnp.bfloat16)
 
-    weight_b = jnp.concatenate([p[0] for p in parts], axis=0)
+    weight_b = jnp.concatenate([p[0] for p in parts], axis=1)
     denom = jnp.concatenate([p[1] for p in parts], axis=0)
-    numer = jnp.dot(weight_b, zvals, preferred_element_type=jnp.float32)
+    numer = lax.dot_general(
+        weight_b, zvals, (((0,), (0,)), ((), ())), preferred_element_type=jnp.float32
+    )
     den = jnp.broadcast_to(denom[:, None], (denom.shape[0], 128))
     sums = jnp.concatenate([numer, den], axis=1).reshape(nblk, q_dev, width + 128)
     sums = sums.reshape(tuple(len(offsets(g)) for g in groups) + sums.shape[1:])

time: 39.4 us -> 55 us (1.40)
  matrix products: 4.13 us -> 9.44 us
  local copies, waits for them, and re-layouts: 0.59 us -> 5.69 us
  other arithmetic: 7.1 us -> 11.3 us
  waiting for transfers between devices: 12.3 us -> 13.1 us
    dot_general x4, matrix products: 4.13 us -> 9.44 us  [the longest x3 7.94 us: piece_weights(): lax.dot_general(lib_ext, rows, (((1,), (1,)), ((), ())), preferred_elemen...]
    unnamed x11 -> x15, local copies, waits for them, and re-layouts: 0.17 us -> 2.44 us
    reduce_sum x3, other arithmetic: 0.5 us -> 2.39 us  [piece_weights(): q_sq = jnp.sum(blockf * blockf, axis=1)]
    optimization_barrier x0 -> x2, local copies, waits for them, and re-layouts: none -> 1.87 us  [gather_rounds(): got, results[-1] = lax.optimization_barrier((got, results[-1]))]
    concatenate x3, other arithmetic: 0.14 us -> 1.8 us  [cat(): return jnp.concatenate(parts, axis=0) if len(parts) > 1 else parts[0]]
    concatenate x1, local copies, waits for them, and re-layouts: 0.03 us -> 0.98 us  [cat(): return jnp.concatenate(parts, axis=0) if len(parts) > 1 else parts[0]]
    ppermute x12, waiting for transfers between devices: 12.3 us -> 13.1 us  [swap(): return lax.ppermute(x, axis, [(i, i ^ mask) for i in range(count)])]
    concatenate x1, other arithmetic: 0.08 us -> 0.77 us  [shards(): denom = jnp.concatenate([p[1] for p in parts], axis=0)]
  transfers between devices with their start and end apart: 12 -> 12, of which waited for: 7 -> 6; matrix products, arithmetic and copies ran while one was open for 17% -> 27% of each run, Pallas kernels for 0% -> 0%
where the time goes in v17:
time: 55 us; the launch traced here: 54.5 us
  starting transfers between devices  14.7 us (27%)
  waiting for transfers between devices  13.1 us (24%)
  other arithmetic  11.3 us (21%)
  matrix products  9.44 us (17%)
  local copies, waits for them, and re-layouts  5.69 us (10%)
    ppermute x12, starting transfers between devices, swap(): return lax.ppermute(x, axis, [(i, i ^ mask) for i in range(count)])  14.7 us
    ppermute x12, waiting for transfers between devices, swap(): return lax.ppermute(x, axis, [(i, i ^ mask) for i in range(count)])  13.1 us
    dot_general x3, matrix products, piece_weights(): lax.dot_general(lib_ext, rows, (((1,), (1,)), ((), ())), preferred_elemen...  7.94 us
    reduce_sum x1, other arithmetic, shards(): lib_sq = jnp.sum(jnp.square(library.astype(jnp.float32)), axis=1)  2.72 us
    unnamed x15, local copies, waits for them, and re-layouts  2.44 us
    reduce_sum x3, other arithmetic, piece_weights(): q_sq = jnp.sum(blockf * blockf, axis=1)  2.39 us
    optimization_barrier x2, local copies, waits for them, and re-layouts, gather_rounds(): got, results[-1] = lax.optimization_barrier((got, results[-1]))  1.87 us
    concatenate x3, other arithmetic, cat(): return jnp.concatenate(parts, axis=0) if len(parts) > 1 else parts[0]  1.8 us
  transfers between devices with their start and end apart: 12, of which 6 were waited for; matrix products, arithmetic and copies ran while one was open for 27% of the time, Pallas kernels for 0%

profile of v17, /device:TPU:0, one launch (start us, length us, event | category | flops | bytes accessed | tf_op | source)
XLA Modules:
  0.0 54.5 jit_solution(15152614641049841530)
XLA Ops:
  0.0 1.1 %convert_reduce_fusion = (f32[256]{0:T(256)S(1)}, f32[256]{0:T(256)S(1)}) fusion(bf16[768,256]{1,0:T(8,128)(2,1)} %param.5), kind=kLoop, calls=%fused_computation.9 | loop fusion | flops 785920 | bytes 395264 | tf_op jit(solution)/shard_map/reduce_sum | solution.py:106
  1.2 0.8 %maximum_bitcast_fusion = bf16[1,16,2176]{2,1,0:T(8,128)(2,1)S(1)} fusion(bf16[16,128]{1,0:T(8,128)(2,1)S(1)} %fusion.62, bf16[16,2048]{1,0:T(8,128)(2,1)} %param.3), kind=kLoop, calls=%fused_computation.47 | loop fusion | flops 139264 | bytes 139264 | tf_op jit(solution)/shard_map/broadcast_in_dim | solution.py:66
  2.0 3.1 %collective-permute-start.1 = (bf16[1,16,2176]{2,1,0:T(8,128)(2,1)S(1)}, bf16[1,16,2176]{2,1,0:T(8,128)(2,1)S(1)}, u32[]{:S(2)}, u32[]{:S(2)}) collective-permute-start(bf16[1,16,2176]{2,1,0:T(8,128)(2,1)S(1)} %maximum_bitcast_fusion), channel_id=1, source_target_pairs={{0,4},{1,5},{2,6},{3,7},{4,0},{5,1},{6,2},{7,3},{8,12},{9,13},{10,... | collective-permute-start | bytes 208904 | tf_op jit(solution)/shard_map/ppermute | solution.py:37
  5.1 2.6 %collective-permute-start.2 = (bf16[1,16,2176]{2,1,0:T(8,128)(2,1)S(1)}, bf16[1,16,2176]{2,1,0:T(8,128)(2,1)S(1)}, u32[]{:S(2)}, u32[]{:S(2)}) collective-permute-start(bf16[1,16,2176]{2,1,0:T(8,128)(2,1)S(1)} %maximum_bitcast_fusion), channel_id=1, source_target_pairs={{0,8},{1,9},{2,10},{3,11},{4,12},{5,13},{6,14},{7,15},{8,0},{9,1},... | collective-permute-start | bytes 208904 | tf_op jit(solution)/shard_map/ppermute | solution.py:37
  7.7 0.0 collective-permute-start.3
  7.7 1.7 %collective-permute-start = (bf16[1,16,2176]{2,1,0:T(8,128)(2,1)S(1)}, bf16[1,16,2176]{2,1,0:T(8,128)(2,1)S(1)}, u32[]{:S(2)}, u32[]{:S(2)}) collective-permute-start(bf16[1,16,2176]{2,1,0:T(8,128)(2,1)S(1)} %maximum_bitcast_fusion), channel_id=1, source_target_pairs={{0,2},{1,3},{2,0},{3,1},{4,6},{5,7},{6,4},{7,5},{8,10},{9,11},{10,... | collective-permute-start | bytes 208904 | tf_op jit(solution)/shard_map/ppermute | solution.py:37
  9.4 0.8 %constant_dynamic-update-slice_fusion.9 = bf16[16,16,2176]{2,1,0:T(8,128)(2,1)S(1)} fusion(bf16[16,128]{1,0:T(8,128)(2,1)S(1)} %fusion.62, bf16[16,2048]{1,0:T(8,128)(2,1)} %param.3), kind=kLoop, calls=%fused_computation.68 | loop fusion | flops 139263 | bytes 139264
  10.3 0.0 copy-start
  10.3 2.7 %multiply_reduce_fusion = f32[768]{0:T(1024)S(1)} fusion(bf16[768,2048]{1,0:T(8,128)(2,1)} %param.4), kind=kLoop, calls=%fused_computation | loop fusion | flops 4717824 | bytes 3148800 | tf_op jit(solution)/shard_map/reduce_sum | solution.py:114
  13.0 0.0 collective-permute-done.1
  13.0 0.0 collective-permute-done.2
  13.0 0.9 %collective-permute-done.3 = bf16[1,16,2176]{2,1,0:T(8,128)(2,1)S(1)} collective-permute-done((bf16[1,16,2176]{2,1,0:T(8,128)(2,1)S(1)}, bf16[1,16,2176]{2,1,0:T(8,128)(2,1)S(1)}, u32[]{:S(2)}, u32[]{:S(2)}) %collective-permute-start.3) | collective-permute-done | bytes 69664 | tf_op jit(solution)/shard_map/ppermute | solution.py:37
  13.9 0.7 %pad_maximum_fusion.1 = bf16[4,16,2176]{2,1,0:T(8,128)(2,1)} fusion(bf16[1,16,2176]{2,1,0:T(8,128)(2,1)S(1)} %collective-permute-done.3, bf16[1,16,2176]{2,1,0:T(8,128)(2,1)S(1)} %collective-permute-done.2, bf16[1,16,2176]{2,1,0:T(8,128)(2,1)S(1)} %collective-permute-done.1, bf16[1,16,2176]{2,1,0:T(8,128)(2,1)S(1)} %maximum_bitcast_fusion), kind=kLoop, calls=%fused_computation.39 | loop fusion | flops 417792 | bytes 557056 | tf_op jit(solution)/shard_map/concatenate | solution.py:61
  14.6 0.0 collective-permute-start.5
  14.6 1.1 %multiply_reduce_fusion.3 = f32[64]{0:T(128)S(1)} fusion(bf16[64,2176]{1,0:T(8,128)(2,1)} %bitcast.2), kind=kLoop, calls=%fused_computation.20 | loop fusion | flops 393152 | bytes 262400 | tf_op jit(solution)/shard_map/reduce_sum | solution.py:26
  15.8 1.6 %collective-permute-start.4 = (bf16[3,16,2176]{2,1,0:T(8,128)(2,1)S(1)}, bf16[3,16,2176]{2,1,0:T(8,128)(2,1)S(1)}, u32[]{:S(2)}, u32[]{:S(2)}) collective-permute-start(bf16[3,16,2176]{2,1,0:T(8,128)(2,1)S(1)} %pad_maximum_fusion.2), channel_id=1, source_target_pairs={{0,2},{1,3},{2,0},{3,1},{4,6},{5,7},{6,4},{7,5},{8,10},{9,11},{10,... | collective-permute-start | bytes 626696 | tf_op jit(solution)/shard_map/ppermute | solution.py:37
  17.4 0.0 copy-done
  17.4 2.2 %fusion.70 = (f32[64]{0:T(128)S(1)}, bf16[768,64]{0,1:T(8,128)(2,1)S(1)}) fusion(f32[768]{0:T(1024)S(1)} %multiply_reduce_fusion, f32[64]{0:T(128)S(1)} %multiply_reduce_fusion.3, bf16[64,2176]{1,0:T(8,128)(2,1)} %bitcast.2, bf16[768,2048]{1,0:T(8,128)(2,1)S(1)} %copy-done), kind=kOutput, calls=%fused_computation.93 | convolution fusion | flops 214253504 | bytes 3526144 | tf_op jit(solution)/shard_map/dot_general | solution.py:27
  19.6 0.0 collective-permute-done
  19.6 3.8 %collective-permute-done.4 = bf16[3,16,2176]{2,1,0:T(8,128)(2,1)S(1)} collective-permute-done((bf16[3,16,2176]{2,1,0:T(8,128)(2,1)S(1)}, bf16[3,16,2176]{2,1,0:T(8,128)(2,1)S(1)}, u32[]{:S(2)}, u32[]{:S(2)}) %collective-permute-start.4) | collective-permute-done | bytes 208928 | tf_op jit(solution)/shard_map/ppermute | solution.py:37
  23.4 0.6 %constant_dynamic-update-slice_fusion.5 = (bf16[16,16,2176]{2,1,0:T(8,128)(2,1)S(1)}, bf16[4,16,2176]{2,1,0:T(8,128)(2,1)}) fusion(bf16[16,16,2176]{2,1,0:T(8,128)(2,1)S(1)} %constant_dynamic-update-slice_fusion.6, bf16[1,16,2176]{2,1,0:T(8,128)(2,1)S(1)} %collective-permute-done), kind=kLoop, calls=%fused_computation.64 | loop fusion | bytes 208896
  24.1 0.7 %constant_dynamic-update-slice_fusion.4 = (bf16[16,16,2176]{2,1,0:T(8,128)(2,1)S(1)}, bf16[4,16,2176]{2,1,0:T(8,128)(2,1)}) fusion(bf16[16,16,2176]{2,1,0:T(8,128)(2,1)S(1)} %get-tuple-element.36, bf16[3,16,2176]{2,1,0:T(8,128)(2,1)S(1)} %collective-permute-done.4, bf16[4,16,2176]{2,1,0:T(8,128)(2,1)} %get-tuple-element.37), kind=kLoop, calls=%fused_computation.63 | loop fusion | bytes 626688
  24.8 0.0 copy-start.2
  24.8 1.0 %copy-done.2 = bf16[16,16,2176]{2,1,0:T(8,128)(2,1)} copy-done((bf16[16,16,2176]{2,1,0:T(8,128)(2,1)}, bf16[16,16,2176]{2,1,0:T(8,128)(2,1)S(1)}, u32[]{:S(2)}) %copy-start.2) | copy-done | bytes 1114136
  25.7 0.0 collective-permute-start.6
  25.7 1.1 %multiply_reduce_fusion.2 = f32[64]{0:T(128)S(1)} fusion(bf16[64,2176]{1,0:T(8,128)(2,1)} %bitcast.3), kind=kLoop, calls=%fused_computation.19 | loop fusion | flops 393152 | bytes 262400 | tf_op jit(solution)/shard_map/reduce_sum | solution.py:26
  26.9 0.8 %copy.8 = bf16[768,64]{1,0:T(8,128)(2,1)} copy(bf16[768,64]{0,1:T(8,128)(2,1)S(1)} %get-tuple-element.13) | data formatting | bytes 196608 | tf_op jit(solution)/shard_map/optimization_barrier | solution.py:81
  27.7 0.0 copy-start.3
  27.7 3.5 %fusion.69 = (f32[64]{0:T(128)}, bf16[768,64]{0,1:T(8,128)(2,1)}) fusion(f32[768]{0:T(1024)S(1)} %multiply_reduce_fusion, f32[64]{0:T(128)S(1)} %multiply_reduce_fusion.2, bf16[64,2176]{1,0:T(8,128)(2,1)} %bitcast.3, bf16[768,2048]{1,0:T(8,128)(2,1)S(1)} %copy-done), kind=kOutput, calls=%fused_computation.92 | convolution fusion | flops 214253504 | bytes 3526144 | tf_op jit(solution)/shard_map/dot_general | solution.py:27
  31.2 0.0 collective-permute-done.5
  31.2 0.0 collective-permute-done.6
  31.2 0.0 copy-done.3
  31.2 1.0 %pad_maximum_fusion = bf16[8,16,2176]{2,1,0:T(8,128)(2,1)S(1)} fusion(bf16[4,16,2176]{2,1,0:T(8,128)(2,1)} %collective-permute-done.6, bf16[4,16,2176]{2,1,0:T(8,128)(2,1)S(1)} %collective-permute-done.5), kind=kLoop, calls=%fused_computation.18 | loop fusion | flops 278528 | bytes 1114112 | tf_op jit(solution)/shard_map/concatenate | solution.py:61
  32.2 1.0 %constant_dynamic-update-slice_fusion.2 = bf16[16,16,2176]{2,1,0:T(8,128)(2,1)S(1)} fusion(bf16[16,16,2176]{2,1,0:T(8,128)(2,1)S(1)} %constant_dynamic-update-slice_fusion.3, bf16[4,16,2176]{2,1,0:T(8,128)(2,1)} %collective-permute-done.6), kind=kLoop, calls=%fused_computation.61 | loop fusion | bytes 557056 | tf_op jit(solution)/shard_map/concatenate | solution.py:61
  33.3 0.2 multiply_reduce_fusion.1
  33.5 0.0 copy-start.1
  33.5 2.3 %fusion.68 = (f32[128]{0:T(128)}, bf16[768,128]{1,0:T(8,128)(2,1)}) fusion(f32[768]{0:T(1024)S(1)} %multiply_reduce_fusion, f32[128]{0:T(128)S(1)} %multiply_reduce_fusion.1, bf16[128,2176]{1,0:T(8,128)(2,1)S(1)} %bitcast.39, bf16[768,2048]{1,0:T(8,128)(2,1)S(1)} %copy-done), kind=kOutput, calls=%fused_computation.91 | convolution fusion | flops 428507008 | bytes 3903488 | tf_op jit(solution)/shard_map/dot_general | solution.py:27
  35.8 1.1 %copy.9 = bf16[768,64]{1,0:T(8,128)(2,1)S(1)} copy(bf16[768,64]{0,1:T(8,128)(2,1)} %get-tuple-element.16) | data formatting | bytes 196608 | tf_op jit(solution)/shard_map/optimization_barrier | solution.py:81
  36.8 0.8 %pad_maximum_fusion.5 = f32[256]{0:T(256)S(1)} fusion(f32[128]{0:T(128)} %get-tuple-element.25, f32[64]{0:T(128)} %get-tuple-element.20, f32[64]{0:T(128)S(1)} %get-tuple-element.19), kind=kLoop, calls=%fused_computation.84 | loop fusion | flops 512 | bytes 2048 | tf_op jit(solution)/shard_map/concatenate | solution.py:128
  37.6 0.0 copy-done.1
  37.6 1.5 %fusion.20 = f32[256,256]{0,1:T(8,128)S(1)} fusion(bf16[768,256]{1,0:T(8,128)(2,1)S(1)} %copy-done.1, bf16[768,128]{1,0:T(8,128)(2,1)} %get-tuple-element.26, bf16[768,64]{1,0:T(8,128)(2,1)S(1)} %copy.9, bf16[768,64]{1,0:T(8,128)(2,1)} %copy.8, f32[256]{0:T(256)S(1)} %get-tuple-element.39, f32[256]{0:T(256)S(1)} %get-tuple-element.38), kind=kOutput, calls=%fused_computation.21 | convolution fusion | flops 102629376 | bytes 1050624 | tf_op jit(solution)/shard_map/dot_general | solution.py:129
  39.2 0.1 copy.11
  39.3 0.6 %collective-permute-start.7 = (f32[2,4,16,384]{3,2,1,0:T(8,128)S(1)}, f32[2,4,16,384]{3,2,1,0:T(8,128)S(1)}, u32[]{:S(2)}, u32[]{:S(2)}) collective-permute-start(f32[2,4,16,384]{3,2,1,0:T(8,128)S(1)} %bitcast.43), channel_id=1, source_target_pairs={{0,1},{1,0},{2,3},{3,2},{4,5},{5,4},{6,7},{7,6},{8,9},{9,8},{10,11... | collective-permute-start | bytes 589832 | tf_op jit(solution)/shard_map/ppermute | solution.py:37
  39.9 0.1 copy.10
  40.0 0.9 %collective-permute-done.7 = f32[2,4,16,384]{3,2,1,0:T(8,128)S(1)} collective-permute-done((f32[2,4,16,384]{3,2,1,0:T(8,128)S(1)}, f32[2,4,16,384]{3,2,1,0:T(8,128)S(1)}, u32[]{:S(2)}, u32[]{:S(2)}) %collective-permute-start.7) | collective-permute-done | bytes 196640 | tf_op jit(solution)/shard_map/ppermute | solution.py:37
  41.0 1.6 %collective-permute-start.8 = (f32[4,16,384]{2,1,0:T(8,128)S(1)}, f32[4,16,384]{2,1,0:T(8,128)S(1)}, u32[]{:S(2)}, u32[]{:S(2)}) collective-permute-start(f32[4,16,384]{2,1,0:T(8,128)S(1)} %slice_bitcast_fusion), channel_id=1, source_target_pairs={{0,2},{1,3},{2,0},{3,1},{4,6},{5,7},{6,4},{7,5},{8,10},{9,11},{10,... | collective-permute-start | bytes 294920 | tf_op jit(solution)/shard_map/ppermute | solution.py:37
  42.6 3.5 %collective-permute-done.8 = f32[4,16,384]{2,1,0:T(8,128)S(1)} collective-permute-done((f32[4,16,384]{2,1,0:T(8,128)S(1)}, f32[4,16,384]{2,1,0:T(8,128)S(1)}, u32[]{:S(2)}, u32[]{:S(2)}) %collective-permute-start.8) | collective-permute-done | bytes 98336 | tf_op jit(solution)/shard_map/ppermute | solution.py:37
  46.2 1.9 %collective-permute-start.10 = (f32[16,384]{1,0:T(8,128)S(1)}, f32[16,384]{1,0:T(8,128)S(1)}, u32[]{:S(2)}, u32[]{:S(2)}) collective-permute-start(f32[16,384]{1,0:T(8,128)S(1)} %get-tuple-element.35), channel_id=1, source_target_pairs={{0,8},{1,9},{2,10},{3,11},{4,12},{5,13},{6,14},{7,15},{8,0},{9,1},... | collective-permute-start | bytes 73736 | tf_op jit(solution)/shard_map/ppermute | solution.py:37
  48.0 1.3 %collective-permute-start.11 = (f32[16,384]{1,0:T(8,128)S(1)}, f32[16,384]{1,0:T(8,128)S(1)}, u32[]{:S(2)}, u32[]{:S(2)}) collective-permute-start(f32[16,384]{1,0:T(8,128)S(1)} %get-tuple-element.34), channel_id=1, source_target_pairs={{0,12},{1,13},{2,14},{3,15},{4,8},{5,9},{6,10},{7,11},{8,4},{9,5},... | collective-permute-start | bytes 73736 | tf_op jit(solution)/shard_map/ppermute | solution.py:37
  49.4 0.3 collective-permute-start.9
  49.7 1.7 %collective-permute-done.10 = f32[16,384]{1,0:T(8,128)S(1)} collective-permute-done((f32[16,384]{1,0:T(8,128)S(1)}, f32[16,384]{1,0:T(8,128)S(1)}, u32[]{:S(2)}, u32[]{:S(2)}) %collective-permute-start.10) | collective-permute-done | bytes 24608 | tf_op jit(solution)/shard_map/ppermute | solution.py:37
  51.4 2.3 %collective-permute-done.11 = f32[16,384]{1,0:T(8,128)S(1)} collective-permute-done((f32[16,384]{1,0:T(8,128)S(1)}, f32[16,384]{1,0:T(8,128)S(1)}, u32[]{:S(2)}, u32[]{:S(2)}) %collective-permute-start.11) | collective-permute-done | bytes 24608 | tf_op jit(solution)/shard_map/ppermute | solution.py:37
  53.7 0.0 collective-permute-done.9
  53.7 0.1 slice_reduce_fusion
  53.8 0.7 %slice_divide_fusion = f32[16,256]{1,0:T(8,128)} fusion(f32[16,384]{1,0:T(8,128)S(1)} %fusion.56, f32[16]{0:T(128)S(1)} %slice_reduce_fusion), kind=kLoop, calls=%fused_computation.69 | loop fusion | flops 4096 | bytes 32832 | tf_op jit(solution)/shard_map/div | solution.py:136
  (18 shorter events, 0.3 us)
Async XLA Ops:
  2.0 11.0 %collective-permute-start.1 = (bf16[1,16,2176]{2,1,0:T(8,128)(2,1)S(1)}, bf16[1,16,2176]{2,1,0:T(8,128)(2,1)S(1)}, u32[]{:S(2)}, u32[]{:S(2)}) collective-permute-start(bf16[1,16,2176]{2,1,0:T(8,128)(2,1)S(1)} %maximum_bitcast_fusion), channel_id=1, source_target_pairs={{0,4},{1,5},{2,6},{3,7},{4,0},{5,1},{6,2},{7,3},{8,12},{9,13},{10,... | collective-permute-start | bytes 208904 | tf_op jit(solution)/shard_map/ppermute | solution.py:37
  5.1 7.9 %collective-permute-start.2 = (bf16[1,16,2176]{2,1,0:T(8,128)(2,1)S(1)}, bf16[1,16,2176]{2,1,0:T(8,128)(2,1)S(1)}, u32[]{:S(2)}, u32[]{:S(2)}) collective-permute-start(bf16[1,16,2176]{2,1,0:T(8,128)(2,1)S(1)} %maximum_bitcast_fusion), channel_id=1, source_target_pairs={{0,8},{1,9},{2,10},{3,11},{4,12},{5,13},{6,14},{7,15},{8,0},{9,1},... | collective-permute-start | bytes 208904 | tf_op jit(solution)/shard_map/ppermute | solution.py:37
  7.7 6.2 %collective-permute-start.3 = (bf16[1,16,2176]{2,1,0:T(8,128)(2,1)S(1)}, bf16[1,16,2176]{2,1,0:T(8,128)(2,1)S(1)}, u32[]{:S(2)}, u32[]{:S(2)}) collective-permute-start(bf16[1,16,2176]{2,1,0:T(8,128)(2,1)S(1)} %maximum_bitcast_fusion), channel_id=1, source_target_pairs={{0,12},{1,13},{2,14},{3,15},{4,8},{5,9},{6,10},{7,11},{8,4},{9,5},... | collective-permute-start | bytes 208904 | tf_op jit(solution)/shard_map/ppermute | solution.py:37
  7.7 11.9 %collective-permute-start = (bf16[1,16,2176]{2,1,0:T(8,128)(2,1)S(1)}, bf16[1,16,2176]{2,1,0:T(8,128)(2,1)S(1)}, u32[]{:S(2)}, u32[]{:S(2)}) collective-permute-start(bf16[1,16,2176]{2,1,0:T(8,128)(2,1)S(1)} %maximum_bitcast_fusion), channel_id=1, source_target_pairs={{0,2},{1,3},{2,0},{3,1},{4,6},{5,7},{6,4},{7,5},{8,10},{9,11},{10,... | collective-permute-start | bytes 208904 | tf_op jit(solution)/shard_map/ppermute | solution.py:37
  10.3 7.1 %copy-start = (bf16[768,2048]{1,0:T(8,128)(2,1)S(1)}, bf16[768,2048]{1,0:T(8,128)(2,1)}, u32[]{:S(2)}) copy-start(bf16[768,2048]{1,0:T(8,128)(2,1)} %param.4) | copy-start | bytes 9437188
  14.6 16.6 %collective-permute-start.5 = (bf16[4,16,2176]{2,1,0:T(8,128)(2,1)}, bf16[4,16,2176]{2,1,0:T(8,128)(2,1)S(1)}, u32[]{:S(2)}, u32[]{:S(2)}) collective-permute-start(bf16[4,16,2176]{2,1,0:T(8,128)(2,1)} %pad_maximum_fusion.1), channel_id=1, source_target_pairs={{0,1},{1,0},{2,3},{3,2},{4,5},{5,4},{6,7},{7,6},{8,9},{9,8},{10,11... | collective-permute-start | bytes 835592 | tf_op jit(solution)/shard_map/ppermute | solution.py:37
  15.8 7.6 %collective-permute-start.4 = (bf16[3,16,2176]{2,1,0:T(8,128)(2,1)S(1)}, bf16[3,16,2176]{2,1,0:T(8,128)(2,1)S(1)}, u32[]{:S(2)}, u32[]{:S(2)}) collective-permute-start(bf16[3,16,2176]{2,1,0:T(8,128)(2,1)S(1)} %pad_maximum_fusion.2), channel_id=1, source_target_pairs={{0,2},{1,3},{2,0},{3,1},{4,6},{5,7},{6,4},{7,5},{8,10},{9,11},{10,... | collective-permute-start | bytes 626696 | tf_op jit(solution)/shard_map/ppermute | solution.py:37
  24.8 1.0 %copy-start.2 = (bf16[16,16,2176]{2,1,0:T(8,128)(2,1)}, bf16[16,16,2176]{2,1,0:T(8,128)(2,1)S(1)}, u32[]{:S(2)}) copy-start(bf16[16,16,2176]{2,1,0:T(8,128)(2,1)S(1)} %get-tuple-element.27) | copy-start | bytes 3342340
  25.7 5.4 %collective-permute-start.6 = (bf16[4,16,2176]{2,1,0:T(8,128)(2,1)}, bf16[4,16,2176]{2,1,0:T(8,128)(2,1)}, u32[]{:S(2)}, u32[]{:S(2)}) collective-permute-start(bf16[4,16,2176]{2,1,0:T(8,128)(2,1)} %get-tuple-element.28), channel_id=1, source_target_pairs={{0,1},{1,0},{2,3},{3,2},{4,5},{5,4},{6,7},{7,6},{8,9},{9,8},{10,11... | collective-permute-start | bytes 835592 | tf_op jit(solution)/shard_map/ppermute | solution.py:37
  27.7 3.5 %copy-start.3 = (bf16[16,16,2176]{2,1,0:T(8,128)(2,1)S(1)}, bf16[16,16,2176]{2,1,0:T(8,128)(2,1)}, u32[]{:S(2)}) copy-start(bf16[16,16,2176]{2,1,0:T(8,128)(2,1)} %copy-done.2) | copy-start | bytes 3342340
  33.5 4.1 %copy-start.1 = (bf16[768,256]{1,0:T(8,128)(2,1)S(1)}, bf16[768,256]{1,0:T(8,128)(2,1)}, u32[]{:S(2)}) copy-start(bf16[768,256]{1,0:T(8,128)(2,1)} %param.5) | copy-start | bytes 1179652
  39.3 1.6 %collective-permute-start.7 = (f32[2,4,16,384]{3,2,1,0:T(8,128)S(1)}, f32[2,4,16,384]{3,2,1,0:T(8,128)S(1)}, u32[]{:S(2)}, u32[]{:S(2)}) collective-permute-start(f32[2,4,16,384]{3,2,1,0:T(8,128)S(1)} %bitcast.43), channel_id=1, source_target_pairs={{0,1},{1,0},{2,3},{3,2},{4,5},{5,4},{6,7},{7,6},{8,9},{9,8},{10,11... | collective-permute-start | bytes 589832 | tf_op jit(solution)/shard_map/ppermute | solution.py:37
  41.0 5.1 %collective-permute-start.8 = (f32[4,16,384]{2,1,0:T(8,128)S(1)}, f32[4,16,384]{2,1,0:T(8,128)S(1)}, u32[]{:S(2)}, u32[]{:S(2)}) collective-permute-start(f32[4,16,384]{2,1,0:T(8,128)S(1)} %slice_bitcast_fusion), channel_id=1, source_target_pairs={{0,2},{1,3},{2,0},{3,1},{4,6},{5,7},{6,4},{7,5},{8,10},{9,11},{10,... | collective-permute-start | bytes 294920 | tf_op jit(solution)/shard_map/ppermute | solution.py:37
  46.2 5.2 %collective-permute-start.10 = (f32[16,384]{1,0:T(8,128)S(1)}, f32[16,384]{1,0:T(8,128)S(1)}, u32[]{:S(2)}, u32[]{:S(2)}) collective-permute-start(f32[16,384]{1,0:T(8,128)S(1)} %get-tuple-element.35), channel_id=1, source_target_pairs={{0,8},{1,9},{2,10},{3,11},{4,12},{5,13},{6,14},{7,15},{8,0},{9,1},... | collective-permute-start | bytes 73736 | tf_op jit(solution)/shard_map/ppermute | solution.py:37
  48.0 5.6 %collective-permute-start.11 = (f32[16,384]{1,0:T(8,128)S(1)}, f32[16,384]{1,0:T(8,128)S(1)}, u32[]{:S(2)}, u32[]{:S(2)}) collective-permute-start(f32[16,384]{1,0:T(8,128)S(1)} %get-tuple-element.34), channel_id=1, source_target_pairs={{0,12},{1,13},{2,14},{3,15},{4,8},{5,9},{6,10},{7,11},{8,4},{9,5},... | collective-permute-start | bytes 73736 | tf_op jit(solution)/shard_map/ppermute | solution.py:37
  49.4 4.3 %collective-permute-start.9 = (f32[16,384]{1,0:T(8,128)S(1)}, f32[16,384]{1,0:T(8,128)S(1)}, u32[]{:S(2)}, u32[]{:S(2)}) collective-permute-start(f32[16,384]{1,0:T(8,128)S(1)} %get-tuple-element.33), channel_id=1, source_target_pairs={{0,4},{1,5},{2,6},{3,7},{4,0},{5,1},{6,2},{7,3},{8,12},{9,13},{10,... | collective-permute-start | bytes 73736 | tf_op jit(solution)/shard_map/ppermute | solution.py:37

commit v18 on v16

--- a/solution.py
+++ b/solution.py
@@ -20,16 +20,20 @@
     return (parts[..., :n] + parts[..., n:2 * n]) + parts[..., 2 * n:3 * n]
 
 
-def piece_weights(piece, lib_ext, lib_sq, feat):
+def piece_weights(piece, libs, lib_sqs, feat):
     rows = piece.reshape(-1, piece.shape[-1])
     blockf = rows[:, :feat].astype(jnp.float32)
     q_sq = jnp.sum(blockf * blockf, axis=1)
-    inner = lax.dot_general(
-        rows, lib_ext, (((1,), (1,)), ((), ())), preferred_element_type=jnp.float32
-    )
-    tanimoto = inner / (q_sq[:, None] + lib_sq[None, :] - inner)
-    weight = jnp.exp((tanimoto - 1.0) / TAU)
-    return weight.astype(jnp.bfloat16), jnp.sum(weight, axis=1)
+    out, denom = [], 0.0
+    for lib_ext, lib_sq in zip(libs, lib_sqs):
+        inner = lax.dot_general(
+            rows, lib_ext, (((1,), (1,)), ((), ())), preferred_element_type=jnp.float32
+        )
+        tanimoto = inner / (q_sq[:, None] + lib_sq[None, :] - inner)
+        weight = jnp.exp((tanimoto - 1.0) / TAU)
+        out.append(weight.astype(jnp.bfloat16))
+        denom = denom + jnp.sum(weight, axis=1)
+    return out, denom
 
 
 def swap(x, axis, mask):
@@ -100,35 +104,43 @@
 def shards(queries, library, assays):
     nblk = lax.axis_size("blk")
     groups = digit_groups(nblk)
+    core, groups = groups[0][0], groups[1:]
+    lineage = nblk // 2
     q_dev, feat = queries.shape
     width = assays.shape[1]
     values = assays.astype(jnp.float32)
     partial = jnp.concatenate([jnp.sum(values, axis=0), jnp.sum(values * values, axis=0)])
+
+    partial = partial + swap(partial, "blk", core)
+    pair_lib = swap(library, "blk", core)
+    pair_values = swap(assays, "blk", core).astype(jnp.float32)
 
     coded = split3(partial)
     lanes = -(-coded.shape[0] // q_dev)
     lanes += -lanes % 128
     coded = jnp.pad(coded, (0, q_dev * lanes - coded.shape[0])).reshape(q_dev, lanes)
     packet = jnp.concatenate([queries, coded], axis=1)
-    lib_ext = jnp.pad(library, ((0, 0), (0, lanes)))
-    lib_sq = jnp.sum(jnp.square(library.astype(jnp.float32)), axis=1)
+    libs = [jnp.pad(lib, ((0, 0), (0, lanes))) for lib in (library, pair_lib)]
+    lib_sqs = [jnp.sum(jnp.square(lib.astype(jnp.float32)), axis=1) for lib in (library, pair_lib)]
     got, parts = gather_rounds(
-        packet, "blk", groups, lambda piece: piece_weights(piece, lib_ext, lib_sq, feat)
+        packet, "blk", groups, lambda piece: piece_weights(piece, libs, lib_sqs, feat)
     )
-    stats = join3(got[:, :, feat:].reshape(nblk, q_dev * lanes), 2 * width)
+    stats = join3(got[:, :, feat:].reshape(lineage, q_dev * lanes), 2 * width)
     stats = jnp.sum(stats, axis=0)
 
     col_sum, col_sq = stats[:width], stats[width:]
     total = library.shape[0] * nblk
     mean = col_sum / total
     spread = col_sq / total - mean * mean
-    zvals = ((values - mean) * lax.rsqrt(spread + EPS)).astype(jnp.bfloat16)
-
-    weight_b = jnp.concatenate([p[0] for p in parts], axis=0)
+    scale = lax.rsqrt(spread + EPS)
+    numer = 0.0
+    for k, vals in enumerate((values, pair_values)):
+        zvals = ((vals - mean) * scale).astype(jnp.bfloat16)
+        weight_b = jnp.concatenate([p[0][k] for p in parts], axis=0)
+        numer = numer + jnp.dot(weight_b, zvals, preferred_element_type=jnp.float32)
     denom = jnp.concatenate([p[1] for p in parts], axis=0)
-    numer = jnp.dot(weight_b, zvals, preferred_element_type=jnp.float32)
     den = jnp.broadcast_to(denom[:, None], (denom.shape[0], 128))
-    sums = jnp.concatenate([numer, den], axis=1).reshape(nblk, q_dev, width + 128)
+    sums = jnp.concatenate([numer, den], axis=1).reshape(lineage, q_dev, width + 128)
     sums = sums.reshape(tuple(len(offsets(g)) for g in groups) + sums.shape[1:])
     mine = scatter_rounds(sums, "blk", groups)
     return mine[:, :width] / mine[:, width:width + 1]

time: 39.4 us -> 39.4 us (level)
  other arithmetic: 7.1 us -> 5.72 us
  matrix products: 4.13 us -> 5.35 us
  starting transfers between devices: 14.9 us -> 15.7 us
    dot_general x3 -> x4, matrix products: 3.79 us -> 4.87 us  [piece_weights(): lax.dot_general(rows, lib_ext, (((1,), (1,)), ((), ())), preferred_elemen...]
    broadcast_in_dim x1, other arithmetic: 0.85 us -> 0.01 us  [gather_rounds(): pieces = [packet[None]]]
    unnamed x1 -> x2, other arithmetic: 0.84 us -> 0.01 us
    ppermute x12, starting transfers between devices: 14.9 us -> 15.7 us  [swap(): return lax.ppermute(x, axis, [(i, i ^ mask) for i in range(count)])]
    reduce_sum x1 -> x2, other arithmetic: 2.72 us -> 3.25 us  [shards(): jnp.sum(jnp.square(lib.astype(jnp.float32)), axis=1)]
  transfers between devices with their start and end apart: 12 -> 12, of which waited for: 7 -> 6; matrix products, arithmetic and copies ran while one was open for 17% -> 26% of each run, Pallas kernels for 0% -> 0%
where the time goes in v18:
time: 39.4 us; the launch traced here: 39.3 us
  starting transfers between devices  15.7 us (40%)
  waiting for transfers between devices  12 us (30%)
  other arithmetic  5.72 us (15%)
  matrix products  5.35 us (14%)
    ppermute x12, starting transfers between devices, swap(): return lax.ppermute(x, axis, [(i, i ^ mask) for i in range(count)])  15.7 us
    ppermute x12, waiting for transfers between devices, swap(): return lax.ppermute(x, axis, [(i, i ^ mask) for i in range(count)])  12 us
    dot_general x4, matrix products, piece_weights(): lax.dot_general(rows, lib_ext, (((1,), (1,)), ((), ())), preferred_elemen...  4.87 us
    reduce_sum x2, other arithmetic, shards(): jnp.sum(jnp.square(lib.astype(jnp.float32)), axis=1)  3.25 us
    reduce_sum x1, other arithmetic, shards(): jnp.sum(values, axis=0)  1.15 us
  transfers between devices with their start and end apart: 12, of which 6 were waited for; matrix products, arithmetic and copies ran while one was open for 26% of the time, Pallas kernels for 0%

profile of v18, /device:TPU:0, one launch (start us, length us, event | category | flops | bytes accessed | tf_op | source)
XLA Modules:
  0.0 39.3 jit_solution(10922075262320634676)
XLA Ops:
  0.0 0.0 copy-start
  0.0 0.0 copy-start.2
  0.0 0.5 %collective-permute-start.7 = (bf16[768,256]{1,0:T(8,128)(2,1)}, bf16[768,256]{1,0:T(8,128)(2,1)S(1)}, u32[]{:S(2)}, u32[]{:S(2)}) collective-permute-start(bf16[768,256]{1,0:T(8,128)(2,1)} %param.5), channel_id=1, source_target_pairs={{0,1},{1,0},{2,3},{3,2},{4,5},{5,4},{6,7},{7,6},{8,9},{9,8},{10,11... | collective-permute-start | bytes 1179656 | tf_op jit(solution)/shard_map/ppermute | solution.py:41
  0.5 1.2 %convert_reduce_fusion = (f32[256]{0:T(256)S(1)}, f32[256]{0:T(256)S(1)}) fusion(bf16[768,256]{1,0:T(8,128)(2,1)} %param.5), kind=kLoop, calls=%fused_computation.12 | loop fusion | flops 785920 | bytes 395264 | tf_op jit(solution)/shard_map/reduce_sum | solution.py:112
  1.7 0.2 collective-permute-start
  1.9 0.3 collective-permute-start.6
  2.2 2.6 %multiply_reduce_fusion.1 = f32[768]{0:T(1024)S(1)} fusion(bf16[768,2048]{1,0:T(8,128)(2,1)} %param.4), kind=kLoop, calls=%fused_computation.1 | loop fusion | flops 4717824 | bytes 3148800 | tf_op jit(solution)/shard_map/reduce_sum | solution.py:124
  4.8 0.0 collective-permute-done
  4.9 0.0 copy-done.2
  4.9 4.8 %collective-permute-start.4 = (bf16[1,16,2176]{2,1,0:T(8,128)(2,1)S(1)}, bf16[1,16,2176]{2,1,0:T(8,128)(2,1)S(1)}, u32[]{:S(2)}, u32[]{:S(2)}) collective-permute-start(bf16[1,16,2176]{2,1,0:T(8,128)(2,1)S(1)} %maximum_bitcast_fusion), channel_id=1, source_target_pairs={{0,12},{1,13},{2,14},{3,15},{4,8},{5,9},{6,10},{7,11},{8,4},{9,5},... | collective-permute-start | bytes 208904 | tf_op jit(solution)/shard_map/ppermute | solution.py:41
  9.7 0.0 collective-permute-start.3
  9.7 0.6 %collective-permute-start.2 = (bf16[1,16,2176]{2,1,0:T(8,128)(2,1)S(1)}, bf16[1,16,2176]{2,1,0:T(8,128)(2,1)S(1)}, u32[]{:S(2)}, u32[]{:S(2)}) collective-permute-start(bf16[1,16,2176]{2,1,0:T(8,128)(2,1)S(1)} %maximum_bitcast_fusion), channel_id=1, source_target_pairs={{0,4},{1,5},{2,6},{3,7},{4,0},{5,1},{6,2},{7,3},{8,12},{9,13},{10,... | collective-permute-start | bytes 208904 | tf_op jit(solution)/shard_map/ppermute | solution.py:41
  10.3 2.4 %collective-permute-done.4 = bf16[1,16,2176]{2,1,0:T(8,128)(2,1)S(1)} collective-permute-done((bf16[1,16,2176]{2,1,0:T(8,128)(2,1)S(1)}, bf16[1,16,2176]{2,1,0:T(8,128)(2,1)S(1)}, u32[]{:S(2)}, u32[]{:S(2)}) %collective-permute-start.4) | collective-permute-done | bytes 69664 | tf_op jit(solution)/shard_map/ppermute | solution.py:41
  12.8 1.5 %collective-permute-start.1 = (bf16[1,16,2176]{2,1,0:T(8,128)(2,1)S(1)}, bf16[1,16,2176]{2,1,0:T(8,128)(2,1)S(1)}, u32[]{:S(2)}, u32[]{:S(2)}) collective-permute-start(bf16[1,16,2176]{2,1,0:T(8,128)(2,1)S(1)} %maximum_bitcast_fusion), channel_id=1, source_target_pairs={{0,2},{1,3},{2,0},{3,1},{4,6},{5,7},{6,4},{7,5},{8,10},{9,11},{10,... | collective-permute-start | bytes 208904 | tf_op jit(solution)/shard_map/ppermute | solution.py:41
  14.3 1.8 %collective-permute-done.3 = bf16[1,16,2176]{2,1,0:T(8,128)(2,1)S(1)} collective-permute-done((bf16[1,16,2176]{2,1,0:T(8,128)(2,1)S(1)}, bf16[1,16,2176]{2,1,0:T(8,128)(2,1)S(1)}, u32[]{:S(2)}, u32[]{:S(2)}) %collective-permute-start.3) | collective-permute-done | bytes 69664 | tf_op jit(solution)/shard_map/ppermute | solution.py:41
  16.1 0.0 collective-permute-done.2
  16.1 1.6 %collective-permute-start.5 = (bf16[3,16,2176]{2,1,0:T(8,128)(2,1)S(1)}, bf16[3,16,2176]{2,1,0:T(8,128)(2,1)S(1)}, u32[]{:S(2)}, u32[]{:S(2)}) collective-permute-start(bf16[3,16,2176]{2,1,0:T(8,128)(2,1)S(1)} %pad_maximum_fusion.2), channel_id=1, source_target_pairs={{0,2},{1,3},{2,0},{3,1},{4,6},{5,7},{6,4},{7,5},{8,10},{9,11},{10,... | collective-permute-start | bytes 626696 | tf_op jit(solution)/shard_map/ppermute | solution.py:41
  17.8 0.2 multiply_reduce_fusion.3
  17.9 0.0 copy-done
  17.9 1.2 %fusion.88 = (f32[64]{0:T(128)S(1)}, bf16[64,768]{1,0:T(8,128)(2,1)S(1)}) fusion(f32[768]{0:T(1024)S(1)} %multiply_reduce_fusion.1, f32[64]{0:T(128)S(1)} %multiply_reduce_fusion.3, bf16[64,2176]{1,0:T(8,128)(2,1)S(1)} %bitcast.37, bf16[768,2048]{1,0:T(8,128)(2,1)S(1)} %copy-done), kind=kOutput, calls=%fused_computation.100 | convolution fusion | flops 214253504 | bytes 3526144 | tf_op jit(solution)/shard_map/dot_general | solution.py:29
  19.2 0.0 collective-permute-done.6
  19.2 0.7 %multiply_reduce_fusion = f32[768]{0:T(1024)S(1)} fusion(bf16[768,2048]{1,0:T(8,128)(2,1)S(1)} %collective-permute-done.6), kind=kLoop, calls=%fused_computation | loop fusion | flops 4717824 | bytes 3148800 | tf_op jit(solution)/shard_map/reduce_sum | solution.py:124
  19.9 1.2 %fusion.87 = (f32[64]{0:T(128)S(1)}, bf16[64,768]{1,0:T(8,128)(2,1)S(1)}) fusion(f32[768]{0:T(1024)S(1)} %multiply_reduce_fusion, f32[64]{0:T(128)S(1)} %multiply_reduce_fusion.3, bf16[64,2176]{1,0:T(8,128)(2,1)S(1)} %bitcast.38, bf16[768,2048]{1,0:T(8,128)(2,1)S(1)} %collective-permute-done.6), kind=kOutput, calls=%fused_computation.99 | convolution fusion | flops 214253504 | bytes 3526144 | tf_op jit(solution)/shard_map/dot_general | solution.py:29
  21.1 0.0 collective-permute-done.1
  21.1 1.7 %collective-permute-done.5 = bf16[3,16,2176]{2,1,0:T(8,128)(2,1)S(1)} collective-permute-done((bf16[3,16,2176]{2,1,0:T(8,128)(2,1)S(1)}, bf16[3,16,2176]{2,1,0:T(8,128)(2,1)S(1)}, u32[]{:S(2)}, u32[]{:S(2)}) %collective-permute-start.5) | collective-permute-done | bytes 208928 | tf_op jit(solution)/shard_map/ppermute | solution.py:41
  22.9 0.2 multiply_reduce_fusion.2
  23.0 0.0 copy-start.1
  23.0 1.2 %fusion.86 = (f32[64]{0:T(128)S(1)}, bf16[64,768]{1,0:T(8,128)(2,1)S(1)}) fusion(f32[768]{0:T(1024)S(1)} %multiply_reduce_fusion.1, f32[64]{0:T(128)S(1)} %multiply_reduce_fusion.2, bf16[64,2176]{1,0:T(8,128)(2,1)S(1)} %bitcast.34, bf16[768,2048]{1,0:T(8,128)(2,1)S(1)} %copy-done), kind=kOutput, calls=%fused_computation.98 | convolution fusion | flops 214253504 | bytes 3526144 | tf_op jit(solution)/shard_map/dot_general | solution.py:29
  24.4 1.2 %fusion.85 = (f32[64]{0:T(128)S(1)}, bf16[64,768]{1,0:T(8,128)(2,1)S(1)}) fusion(f32[768]{0:T(1024)S(1)} %multiply_reduce_fusion, f32[64]{0:T(128)S(1)} %multiply_reduce_fusion.2, bf16[64,2176]{1,0:T(8,128)(2,1)S(1)} %bitcast.35, bf16[768,2048]{1,0:T(8,128)(2,1)S(1)} %collective-permute-done.6), kind=kOutput, calls=%fused_computation.97 | convolution fusion | flops 214253504 | bytes 3526144 | tf_op jit(solution)/shard_map/dot_general | solution.py:29
  25.6 0.1 pad_maximum_fusion.5
  25.7 0.0 copy-done.1
  25.7 0.2 fusion.11
  25.9 0.0 collective-permute-done.7
  26.0 0.2 convolution_add_fusion
  26.2 0.1 broadcast_in_dim.5
  26.3 1.6 %collective-permute-start.8 = (f32[4,16,384]{2,1,0:T(8,128)S(1)}, f32[4,16,384]{2,1,0:T(8,128)S(1)}, u32[]{:S(2)}, u32[]{:S(2)}) collective-permute-start(f32[4,16,384]{2,1,0:T(8,128)S(1)} %bitcast.41), channel_id=1, source_target_pairs={{0,2},{1,3},{2,0},{3,1},{4,6},{5,7},{6,4},{7,5},{8,10},{9,11},{10,... | collective-permute-start | bytes 294920 | tf_op jit(solution)/shard_map/ppermute | solution.py:41
  27.9 3.1 %collective-permute-done.8 = f32[4,16,384]{2,1,0:T(8,128)S(1)} collective-permute-done((f32[4,16,384]{2,1,0:T(8,128)S(1)}, f32[4,16,384]{2,1,0:T(8,128)S(1)}, u32[]{:S(2)}, u32[]{:S(2)}) %collective-permute-start.8) | collective-permute-done | bytes 98336 | tf_op jit(solution)/shard_map/ppermute | solution.py:41
  31.0 2.7 %collective-permute-start.11 = (f32[16,384]{1,0:T(8,128)S(1)}, f32[16,384]{1,0:T(8,128)S(1)}, u32[]{:S(2)}, u32[]{:S(2)}) collective-permute-start(f32[16,384]{1,0:T(8,128)S(1)} %get-tuple-element.28), channel_id=1, source_target_pairs={{0,12},{1,13},{2,14},{3,15},{4,8},{5,9},{6,10},{7,11},{8,4},{9,5},... | collective-permute-start | bytes 73736 | tf_op jit(solution)/shard_map/ppermute | solution.py:41
  33.7 0.5 %collective-permute-start.10 = (f32[16,384]{1,0:T(8,128)S(1)}, f32[16,384]{1,0:T(8,128)S(1)}, u32[]{:S(2)}, u32[]{:S(2)}) collective-permute-start(f32[16,384]{1,0:T(8,128)S(1)} %get-tuple-element.29), channel_id=1, source_target_pairs={{0,8},{1,9},{2,10},{3,11},{4,12},{5,13},{6,14},{7,15},{8,0},{9,1},... | collective-permute-start | bytes 73736 | tf_op jit(solution)/shard_map/ppermute | solution.py:41
  34.2 1.3 %collective-permute-start.9 = (f32[16,384]{1,0:T(8,128)S(1)}, f32[16,384]{1,0:T(8,128)S(1)}, u32[]{:S(2)}, u32[]{:S(2)}) collective-permute-start(f32[16,384]{1,0:T(8,128)S(1)} %get-tuple-element.27), channel_id=1, source_target_pairs={{0,4},{1,5},{2,6},{3,7},{4,0},{5,1},{6,2},{7,3},{8,12},{9,13},{10,... | collective-permute-start | bytes 73736 | tf_op jit(solution)/shard_map/ppermute | solution.py:41
  35.5 1.2 %collective-permute-done.11 = f32[16,384]{1,0:T(8,128)S(1)} collective-permute-done((f32[16,384]{1,0:T(8,128)S(1)}, f32[16,384]{1,0:T(8,128)S(1)}, u32[]{:S(2)}, u32[]{:S(2)}) %collective-permute-start.11) | collective-permute-done | bytes 24608 | tf_op jit(solution)/shard_map/ppermute | solution.py:41
  36.7 1.7 %collective-permute-done.10 = f32[16,384]{1,0:T(8,128)S(1)} collective-permute-done((f32[16,384]{1,0:T(8,128)S(1)}, f32[16,384]{1,0:T(8,128)S(1)}, u32[]{:S(2)}, u32[]{:S(2)}) %collective-permute-start.10) | collective-permute-done | bytes 24608 | tf_op jit(solution)/shard_map/ppermute | solution.py:41
  38.4 0.0 collective-permute-done.9
  38.5 0.1 slice_reduce_fusion
  38.6 0.7 %slice_divide_fusion = f32[16,256]{1,0:T(8,128)} fusion(f32[16,384]{1,0:T(8,128)S(1)} %fusion.70, f32[16]{0:T(128)S(1)} %slice_reduce_fusion), kind=kLoop, calls=%fused_computation.64 | loop fusion | flops 4096 | bytes 32832 | tf_op jit(solution)/shard_map/div | solution.py:146
  (23 shorter events, 0.4 us)
Async XLA Ops:
  0.0 17.9 %copy-start = (bf16[768,2048]{1,0:T(8,128)(2,1)S(1)}, bf16[768,2048]{1,0:T(8,128)(2,1)}, u32[]{:S(2)}) copy-start(bf16[768,2048]{1,0:T(8,128)(2,1)} %param.4) | copy-start | bytes 9437188
  0.0 4.9 %copy-start.2 = (bf16[16,2048]{1,0:T(8,128)(2,1)S(1)}, bf16[16,2048]{1,0:T(8,128)(2,1)}, u32[]{:S(2)}) copy-start(bf16[16,2048]{1,0:T(8,128)(2,1)} %param.3) | copy-start | bytes 196612
  0.0 25.9 %collective-permute-start.7 = (bf16[768,256]{1,0:T(8,128)(2,1)}, bf16[768,256]{1,0:T(8,128)(2,1)S(1)}, u32[]{:S(2)}, u32[]{:S(2)}) collective-permute-start(bf16[768,256]{1,0:T(8,128)(2,1)} %param.5), channel_id=1, source_target_pairs={{0,1},{1,0},{2,3},{3,2},{4,5},{5,4},{6,7},{7,6},{8,9},{9,8},{10,11... | collective-permute-start | bytes 1179656 | tf_op jit(solution)/shard_map/ppermute | solution.py:41
  1.7 3.1 %collective-permute-start = (f32[512]{0:T(512)S(1)}, f32[512]{0:T(512)S(1)}, u32[]{:S(2)}, u32[]{:S(2)}) collective-permute-start(f32[512]{0:T(512)S(1)} %pad_maximum_fusion.4), channel_id=1, source_target_pairs={{0,1},{1,0},{2,3},{3,2},{4,5},{5,4},{6,7},{7,6},{8,9},{9,8},{10,11... | collective-permute-start | bytes 6152 | tf_op jit(solution)/shard_map/ppermute | solution.py:41
  1.9 17.3 %collective-permute-start.6 = (bf16[768,2048]{1,0:T(8,128)(2,1)}, bf16[768,2048]{1,0:T(8,128)(2,1)S(1)}, u32[]{:S(2)}, u32[]{:S(2)}) collective-permute-start(bf16[768,2048]{1,0:T(8,128)(2,1)} %param.4), channel_id=1, source_target_pairs={{0,1},{1,0},{2,3},{3,2},{4,5},{5,4},{6,7},{7,6},{8,9},{9,8},{10,11... | collective-permute-start | bytes 9437192 | tf_op jit(solution)/shard_map/ppermute | solution.py:41
  4.9 7.9 %collective-permute-start.4 = (bf16[1,16,2176]{2,1,0:T(8,128)(2,1)S(1)}, bf16[1,16,2176]{2,1,0:T(8,128)(2,1)S(1)}, u32[]{:S(2)}, u32[]{:S(2)}) collective-permute-start(bf16[1,16,2176]{2,1,0:T(8,128)(2,1)S(1)} %maximum_bitcast_fusion), channel_id=1, source_target_pairs={{0,12},{1,13},{2,14},{3,15},{4,8},{5,9},{6,10},{7,11},{8,4},{9,5},... | collective-permute-start | bytes 208904 | tf_op jit(solution)/shard_map/ppermute | solution.py:41
  9.7 6.4 %collective-permute-start.3 = (bf16[1,16,2176]{2,1,0:T(8,128)(2,1)S(1)}, bf16[1,16,2176]{2,1,0:T(8,128)(2,1)S(1)}, u32[]{:S(2)}, u32[]{:S(2)}) collective-permute-start(bf16[1,16,2176]{2,1,0:T(8,128)(2,1)S(1)} %maximum_bitcast_fusion), channel_id=1, source_target_pairs={{0,8},{1,9},{2,10},{3,11},{4,12},{5,13},{6,14},{7,15},{8,0},{9,1},... | collective-permute-start | bytes 208904 | tf_op jit(solution)/shard_map/ppermute | solution.py:41
  9.7 6.4 %collective-permute-start.2 = (bf16[1,16,2176]{2,1,0:T(8,128)(2,1)S(1)}, bf16[1,16,2176]{2,1,0:T(8,128)(2,1)S(1)}, u32[]{:S(2)}, u32[]{:S(2)}) collective-permute-start(bf16[1,16,2176]{2,1,0:T(8,128)(2,1)S(1)} %maximum_bitcast_fusion), channel_id=1, source_target_pairs={{0,4},{1,5},{2,6},{3,7},{4,0},{5,1},{6,2},{7,3},{8,12},{9,13},{10,... | collective-permute-start | bytes 208904 | tf_op jit(solution)/shard_map/ppermute | solution.py:41
  12.8 8.4 %collective-permute-start.1 = (bf16[1,16,2176]{2,1,0:T(8,128)(2,1)S(1)}, bf16[1,16,2176]{2,1,0:T(8,128)(2,1)S(1)}, u32[]{:S(2)}, u32[]{:S(2)}) collective-permute-start(bf16[1,16,2176]{2,1,0:T(8,128)(2,1)S(1)} %maximum_bitcast_fusion), channel_id=1, source_target_pairs={{0,2},{1,3},{2,0},{3,1},{4,6},{5,7},{6,4},{7,5},{8,10},{9,11},{10,... | collective-permute-start | bytes 208904 | tf_op jit(solution)/shard_map/ppermute | solution.py:41
  16.1 6.7 %collective-permute-start.5 = (bf16[3,16,2176]{2,1,0:T(8,128)(2,1)S(1)}, bf16[3,16,2176]{2,1,0:T(8,128)(2,1)S(1)}, u32[]{:S(2)}, u32[]{:S(2)}) collective-permute-start(bf16[3,16,2176]{2,1,0:T(8,128)(2,1)S(1)} %pad_maximum_fusion.2), channel_id=1, source_target_pairs={{0,2},{1,3},{2,0},{3,1},{4,6},{5,7},{6,4},{7,5},{8,10},{9,11},{10,... | collective-permute-start | bytes 626696 | tf_op jit(solution)/shard_map/ppermute | solution.py:41
  23.0 2.7 %copy-start.1 = (bf16[768,256]{1,0:T(8,128)(2,1)S(1)}, bf16[768,256]{1,0:T(8,128)(2,1)}, u32[]{:S(2)}) copy-start(bf16[768,256]{1,0:T(8,128)(2,1)} %param.5) | copy-start | bytes 1179652
  26.3 4.7 %collective-permute-start.8 = (f32[4,16,384]{2,1,0:T(8,128)S(1)}, f32[4,16,384]{2,1,0:T(8,128)S(1)}, u32[]{:S(2)}, u32[]{:S(2)}) collective-permute-start(f32[4,16,384]{2,1,0:T(8,128)S(1)} %bitcast.41), channel_id=1, source_target_pairs={{0,2},{1,3},{2,0},{3,1},{4,6},{5,7},{6,4},{7,5},{8,10},{9,11},{10,... | collective-permute-start | bytes 294920 | tf_op jit(solution)/shard_map/ppermute | solution.py:41
  31.0 5.7 %collective-permute-start.11 = (f32[16,384]{1,0:T(8,128)S(1)}, f32[16,384]{1,0:T(8,128)S(1)}, u32[]{:S(2)}, u32[]{:S(2)}) collective-permute-start(f32[16,384]{1,0:T(8,128)S(1)} %get-tuple-element.28), channel_id=1, source_target_pairs={{0,12},{1,13},{2,14},{3,15},{4,8},{5,9},{6,10},{7,11},{8,4},{9,5},... | collective-permute-start | bytes 73736 | tf_op jit(solution)/shard_map/ppermute | solution.py:41
  33.7 4.7 %collective-permute-start.10 = (f32[16,384]{1,0:T(8,128)S(1)}, f32[16,384]{1,0:T(8,128)S(1)}, u32[]{:S(2)}, u32[]{:S(2)}) collective-permute-start(f32[16,384]{1,0:T(8,128)S(1)} %get-tuple-element.29), channel_id=1, source_target_pairs={{0,8},{1,9},{2,10},{3,11},{4,12},{5,13},{6,14},{7,15},{8,0},{9,1},... | collective-permute-start | bytes 73736 | tf_op jit(solution)/shard_map/ppermute | solution.py:41
  34.2 4.2 %collective-permute-start.9 = (f32[16,384]{1,0:T(8,128)S(1)}, f32[16,384]{1,0:T(8,128)S(1)}, u32[]{:S(2)}, u32[]{:S(2)}) collective-permute-start(f32[16,384]{1,0:T(8,128)S(1)} %get-tuple-element.27), channel_id=1, source_target_pairs={{0,4},{1,5},{2,6},{3,7},{4,0},{5,1},{6,2},{7,3},{8,12},{9,13},{10,... | collective-permute-start | bytes 73736 | tf_op jit(solution)/shard_map/ppermute | solution.py:41

commit v19 on v18

--- a/solution.py
+++ b/solution.py
@@ -120,8 +120,9 @@
     lanes += -lanes % 128
     coded = jnp.pad(coded, (0, q_dev * lanes - coded.shape[0])).reshape(q_dev, lanes)
     packet = jnp.concatenate([queries, coded], axis=1)
-    libs = [jnp.pad(lib, ((0, 0), (0, lanes))) for lib in (library, pair_lib)]
-    lib_sqs = [jnp.sum(jnp.square(lib.astype(jnp.float32)), axis=1) for lib in (library, pair_lib)]
+    chip_lib = jnp.concatenate([library, pair_lib], axis=0)
+    libs = [jnp.pad(chip_lib, ((0, 0), (0, lanes)))]
+    lib_sqs = [jnp.sum(jnp.square(chip_lib.astype(jnp.float32)), axis=1)]
     got, parts = gather_rounds(
         packet, "blk", groups, lambda piece: piece_weights(piece, libs, lib_sqs, feat)
     )
@@ -133,11 +134,10 @@
     mean = col_sum / total
     spread = col_sq / total - mean * mean
     scale = lax.rsqrt(spread + EPS)
-    numer = 0.0
-    for k, vals in enumerate((values, pair_values)):
-        zvals = ((vals - mean) * scale).astype(jnp.bfloat16)
-        weight_b = jnp.concatenate([p[0][k] for p in parts], axis=0)
-        numer = numer + jnp.dot(weight_b, zvals, preferred_element_type=jnp.float32)
+    chip_values = jnp.concatenate([values, pair_values], axis=0)
+    zvals = ((chip_values - mean) * scale).astype(jnp.bfloat16)
+    weight_b = jnp.concatenate([p[0][0] for p in parts], axis=0)
+    numer = jnp.dot(weight_b, zvals, preferred_element_type=jnp.float32)
     denom = jnp.concatenate([p[1] for p in parts], axis=0)
     den = jnp.broadcast_to(denom[:, None], (denom.shape[0], 128))
     sums = jnp.concatenate([numer, den], axis=1).reshape(lineage, q_dev, width + 128)

time: 39.4 us -> 40.8 us (1.036)
  local copies, waits for them, and re-layouts: 0.31 us -> 2.95 us
  other arithmetic: 5.72 us -> 3.85 us
  waiting for transfers between devices: 12 us -> 13.2 us
  matrix products: 5.35 us -> 4.6 us
    unnamed x11 -> x10, local copies, waits for them, and re-layouts: 0.09 us -> 2.35 us
    reduce_sum x2 -> x1, other arithmetic: 3.25 us -> 1.29 us  [shards(): lib_sqs = [jnp.sum(jnp.square(chip_lib.astype(jnp.float32)), axis=1)]]
    ppermute x12, waiting for transfers between devices: 12 us -> 13.2 us  [swap(): return lax.ppermute(x, axis, [(i, i ^ mask) for i in range(count)])]
    dot_general x4 -> x2, matrix products: 4.87 us -> 4.28 us  [piece_weights(): lax.dot_general(rows, lib_ext, (((1,), (1,)), ((), ())), preferred_elemen...]
  transfers between devices with their start and end apart: 12 -> 12, of which waited for: 6 -> 7; matrix products, arithmetic and copies ran while one was open for 26% -> 19% of each run, Pallas kernels for 0% -> 0%
where the time goes in v19:
time: 40.8 us; the launch traced here: 40.6 us
  starting transfers between devices  15.9 us (39%)
  waiting for transfers between devices  13.2 us (32%)
  matrix products  4.6 us (11%)
  other arithmetic  3.85 us (9%)
  local copies, waits for them, and re-layouts  2.95 us (7%)
    ppermute x12, starting transfers between devices, swap(): return lax.ppermute(x, axis, [(i, i ^ mask) for i in range(count)])  15.9 us
    ppermute x12, waiting for transfers between devices, swap(): return lax.ppermute(x, axis, [(i, i ^ mask) for i in range(count)])  13.2 us
    dot_general x2, matrix products, piece_weights(): lax.dot_general(rows, lib_ext, (((1,), (1,)), ((), ())), preferred_elemen...  4.28 us
    unnamed x10, local copies, waits for them, and re-layouts  2.35 us
    reduce_sum x1, other arithmetic, shards(): lib_sqs = [jnp.sum(jnp.square(chip_lib.astype(jnp.float32)), axis=1)]  1.29 us
    reduce_sum x1, other arithmetic, shards(): jnp.sum(values, axis=0)  1.14 us
  transfers between devices with their start and end apart: 12, of which 7 were waited for; matrix products, arithmetic and copies ran while one was open for 19% of the time, Pallas kernels for 0%

profile of v19, /device:TPU:0, one launch (start us, length us, event | category | flops | bytes accessed | tf_op | source)
XLA Modules:
  0.0 40.6 jit_solution(12803044961406434046)
XLA Ops:
  0.0 0.0 copy-start
  0.0 0.0 copy-start.1
  0.0 0.5 %collective-permute-start.6 = (bf16[768,2048]{1,0:T(8,128)(2,1)}, bf16[768,2048]{1,0:T(8,128)(2,1)S(1)}, u32[]{:S(2)}, u32[]{:S(2)}) collective-permute-start(bf16[768,2048]{1,0:T(8,128)(2,1)} %param.4), channel_id=1, source_target_pairs={{0,1},{1,0},{2,3},{3,2},{4,5},{5,4},{6,7},{7,6},{8,9},{9,8},{10,11... | collective-permute-start | bytes 9437192 | tf_op jit(solution)/shard_map/ppermute | solution.py:41
  0.5 0.1 collective-permute-start.7
  0.6 1.1 %convert_reduce_fusion = (f32[256]{0:T(256)S(1)}, f32[256]{0:T(256)S(1)}) fusion(bf16[768,256]{1,0:T(8,128)(2,1)} %param.5), kind=kLoop, calls=%fused_computation.23 | loop fusion | flops 785920 | bytes 395264 | tf_op jit(solution)/shard_map/reduce_sum | solution.py:112
  1.7 0.5 %collective-permute-start = (f32[512]{0:T(512)S(1)}, f32[512]{0:T(512)S(1)}, u32[]{:S(2)}, u32[]{:S(2)}) collective-permute-start(f32[512]{0:T(512)S(1)} %pad_maximum_fusion.4), channel_id=1, source_target_pairs={{0,1},{1,0},{2,3},{3,2},{4,5},{5,4},{6,7},{7,6},{8,9},{9,8},{10,11... | collective-permute-start | bytes 6152 | tf_op jit(solution)/shard_map/ppermute | solution.py:41
  2.2 2.3 %constant_dynamic-update-slice_fusion.1 = bf16[1536,2048]{1,0:T(8,128)(2,1)S(1)} fusion(bf16[768,2048]{1,0:T(8,128)(2,1)} %param.4), kind=kLoop, calls=%fused_computation.42 | loop fusion | bytes 6291456
  4.5 0.0 copy-done
  4.5 0.1 convert_element_type.35
  4.6 2.0 %collective-permute-done = f32[512]{0:T(512)S(1)} collective-permute-done((f32[512]{0:T(512)S(1)}, f32[512]{0:T(512)S(1)}, u32[]{:S(2)}, u32[]{:S(2)}) %collective-permute-start) | collective-permute-done | bytes 2080 | tf_op jit(solution)/shard_map/ppermute | solution.py:41
  6.6 0.0 copy-done.1
  6.6 5.0 %collective-permute-start.4 = (bf16[1,16,2176]{2,1,0:T(8,128)(2,1)S(1)}, bf16[1,16,2176]{2,1,0:T(8,128)(2,1)S(1)}, u32[]{:S(2)}, u32[]{:S(2)}) collective-permute-start(bf16[1,16,2176]{2,1,0:T(8,128)(2,1)S(1)} %maximum_bitcast_fusion), channel_id=1, source_target_pairs={{0,12},{1,13},{2,14},{3,15},{4,8},{5,9},{6,10},{7,11},{8,4},{9,5},... | collective-permute-start | bytes 208904 | tf_op jit(solution)/shard_map/ppermute | solution.py:41
  11.6 0.0 collective-permute-start.3
  11.6 0.6 %collective-permute-start.2 = (bf16[1,16,2176]{2,1,0:T(8,128)(2,1)S(1)}, bf16[1,16,2176]{2,1,0:T(8,128)(2,1)S(1)}, u32[]{:S(2)}, u32[]{:S(2)}) collective-permute-start(bf16[1,16,2176]{2,1,0:T(8,128)(2,1)S(1)} %maximum_bitcast_fusion), channel_id=1, source_target_pairs={{0,4},{1,5},{2,6},{3,7},{4,0},{5,1},{6,2},{7,3},{8,12},{9,13},{10,... | collective-permute-start | bytes 208904 | tf_op jit(solution)/shard_map/ppermute | solution.py:41
  12.3 2.1 %collective-permute-done.4 = bf16[1,16,2176]{2,1,0:T(8,128)(2,1)S(1)} collective-permute-done((bf16[1,16,2176]{2,1,0:T(8,128)(2,1)S(1)}, bf16[1,16,2176]{2,1,0:T(8,128)(2,1)S(1)}, u32[]{:S(2)}, u32[]{:S(2)}) %collective-permute-start.4) | collective-permute-done | bytes 69664 | tf_op jit(solution)/shard_map/ppermute | solution.py:41
  14.4 1.5 %collective-permute-start.1 = (bf16[1,16,2176]{2,1,0:T(8,128)(2,1)S(1)}, bf16[1,16,2176]{2,1,0:T(8,128)(2,1)S(1)}, u32[]{:S(2)}, u32[]{:S(2)}) collective-permute-start(bf16[1,16,2176]{2,1,0:T(8,128)(2,1)S(1)} %maximum_bitcast_fusion), channel_id=1, source_target_pairs={{0,2},{1,3},{2,0},{3,1},{4,6},{5,7},{6,4},{7,5},{8,10},{9,11},{10,... | collective-permute-start | bytes 208904 | tf_op jit(solution)/shard_map/ppermute | solution.py:41
  15.9 1.9 %collective-permute-done.3 = bf16[1,16,2176]{2,1,0:T(8,128)(2,1)S(1)} collective-permute-done((bf16[1,16,2176]{2,1,0:T(8,128)(2,1)S(1)}, bf16[1,16,2176]{2,1,0:T(8,128)(2,1)S(1)}, u32[]{:S(2)}, u32[]{:S(2)}) %collective-permute-start.3) | collective-permute-done | bytes 69664 | tf_op jit(solution)/shard_map/ppermute | solution.py:41
  17.8 0.0 collective-permute-done.2
  17.9 1.6 %collective-permute-start.5 = (bf16[3,16,2176]{2,1,0:T(8,128)(2,1)S(1)}, bf16[3,16,2176]{2,1,0:T(8,128)(2,1)S(1)}, u32[]{:S(2)}, u32[]{:S(2)}) collective-permute-start(bf16[3,16,2176]{2,1,0:T(8,128)(2,1)S(1)} %pad_maximum_fusion.2), channel_id=1, source_target_pairs={{0,2},{1,3},{2,0},{3,1},{4,6},{5,7},{6,4},{7,5},{8,10},{9,11},{10,... | collective-permute-start | bytes 626696 | tf_op jit(solution)/shard_map/ppermute | solution.py:41
  19.5 0.2 multiply_reduce_fusion.3
  19.7 0.0 collective-permute-done.7
  19.7 0.1 convert_element_type.41
  19.8 0.0 collective-permute-done.6
  19.8 0.4 constant_dynamic-update-slice_fusion
  20.2 1.3 %multiply_reduce_fusion = f32[1536]{0:T(1024)S(1)} fusion(bf16[1536,2048]{1,0:T(8,128)(2,1)S(1)} %constant_dynamic-update-slice_fusion), kind=kLoop, calls=%fused_computation | loop fusion | flops 9435648 | bytes 6297600 | tf_op jit(solution)/shard_map/reduce_sum | solution.py:125
  21.5 2.1 %fusion.50 = (f32[64]{0:T(128)S(1)}, bf16[64,1536]{1,0:T(8,128)(2,1)S(1)}) fusion(f32[1536]{0:T(1024)S(1)} %multiply_reduce_fusion, f32[64]{0:T(128)S(1)} %multiply_reduce_fusion.3, bf16[64,2176]{1,0:T(8,128)(2,1)S(1)} %bitcast.32, bf16[1536,2048]{1,0:T(8,128)(2,1)S(1)} %constant_dynamic-update-slice_fusion), kind=kOutput, calls=%fused_computation.75 | convolution fusion | flops 428507072 | bytes 6773248 | tf_op jit(solution)/shard_map/dot_general | solution.py:29
  23.6 0.0 collective-permute-done.1
  23.6 0.9 %collective-permute-done.5 = bf16[3,16,2176]{2,1,0:T(8,128)(2,1)S(1)} collective-permute-done((bf16[3,16,2176]{2,1,0:T(8,128)(2,1)S(1)}, bf16[3,16,2176]{2,1,0:T(8,128)(2,1)S(1)}, u32[]{:S(2)}, u32[]{:S(2)}) %collective-permute-start.5) | collective-permute-done | bytes 208928 | tf_op jit(solution)/shard_map/ppermute | solution.py:41
  24.5 0.2 multiply_reduce_fusion.2
  24.7 2.1 %fusion.49 = (f32[64]{0:T(128)S(1)}, bf16[64,1536]{1,0:T(8,128)(2,1)S(1)}) fusion(f32[1536]{0:T(1024)S(1)} %multiply_reduce_fusion, f32[64]{0:T(128)S(1)} %multiply_reduce_fusion.2, bf16[64,2176]{1,0:T(8,128)(2,1)S(1)} %bitcast.34, bf16[1536,2048]{1,0:T(8,128)(2,1)S(1)} %constant_dynamic-update-slice_fusion), kind=kOutput, calls=%fused_computation.74 | convolution fusion | flops 428507072 | bytes 6773248 | tf_op jit(solution)/shard_map/dot_general | solution.py:29
  27.0 0.1 pad_maximum_fusion.5
  27.1 0.3 fusion.6
  27.4 0.1 broadcast_in_dim.5
  27.5 1.6 %collective-permute-start.8 = (f32[4,16,384]{2,1,0:T(8,128)S(1)}, f32[4,16,384]{2,1,0:T(8,128)S(1)}, u32[]{:S(2)}, u32[]{:S(2)}) collective-permute-start(f32[4,16,384]{2,1,0:T(8,128)S(1)} %bitcast.37), channel_id=1, source_target_pairs={{0,2},{1,3},{2,0},{3,1},{4,6},{5,7},{6,4},{7,5},{8,10},{9,11},{10,... | collective-permute-start | bytes 294920 | tf_op jit(solution)/shard_map/ppermute | solution.py:41
  29.1 3.1 %collective-permute-done.8 = f32[4,16,384]{2,1,0:T(8,128)S(1)} collective-permute-done((f32[4,16,384]{2,1,0:T(8,128)S(1)}, f32[4,16,384]{2,1,0:T(8,128)S(1)}, u32[]{:S(2)}, u32[]{:S(2)}) %collective-permute-start.8) | collective-permute-done | bytes 98336 | tf_op jit(solution)/shard_map/ppermute | solution.py:41
  32.2 2.9 %collective-permute-start.11 = (f32[16,384]{1,0:T(8,128)S(1)}, f32[16,384]{1,0:T(8,128)S(1)}, u32[]{:S(2)}, u32[]{:S(2)}) collective-permute-start(f32[16,384]{1,0:T(8,128)S(1)} %get-tuple-element.22), channel_id=1, source_target_pairs={{0,12},{1,13},{2,14},{3,15},{4,8},{5,9},{6,10},{7,11},{8,4},{9,5},... | collective-permute-start | bytes 73736 | tf_op jit(solution)/shard_map/ppermute | solution.py:41
  35.1 0.0 collective-permute-start.10
  35.1 1.6 %collective-permute-start.9 = (f32[16,384]{1,0:T(8,128)S(1)}, f32[16,384]{1,0:T(8,128)S(1)}, u32[]{:S(2)}, u32[]{:S(2)}) collective-permute-start(f32[16,384]{1,0:T(8,128)S(1)} %get-tuple-element.21), channel_id=1, source_target_pairs={{0,4},{1,5},{2,6},{3,7},{4,0},{5,1},{6,2},{7,3},{8,12},{9,13},{10,... | collective-permute-start | bytes 73736 | tf_op jit(solution)/shard_map/ppermute | solution.py:41
  36.7 1.2 %collective-permute-done.11 = f32[16,384]{1,0:T(8,128)S(1)} collective-permute-done((f32[16,384]{1,0:T(8,128)S(1)}, f32[16,384]{1,0:T(8,128)S(1)}, u32[]{:S(2)}, u32[]{:S(2)}) %collective-permute-start.11) | collective-permute-done | bytes 24608 | tf_op jit(solution)/shard_map/ppermute | solution.py:41
  37.9 1.9 %collective-permute-done.10 = f32[16,384]{1,0:T(8,128)S(1)} collective-permute-done((f32[16,384]{1,0:T(8,128)S(1)}, f32[16,384]{1,0:T(8,128)S(1)}, u32[]{:S(2)}, u32[]{:S(2)}) %collective-permute-start.10) | collective-permute-done | bytes 24608 | tf_op jit(solution)/shard_map/ppermute | solution.py:41
  39.8 0.0 collective-permute-done.9
  39.8 0.1 slice_reduce_fusion
  39.9 0.7 %slice_divide_fusion = f32[16,256]{1,0:T(8,128)} fusion(f32[16,384]{1,0:T(8,128)S(1)} %fusion.36, f32[16]{0:T(128)S(1)} %slice_reduce_fusion), kind=kLoop, calls=%fused_computation.49 | loop fusion | flops 4096 | bytes 32832 | tf_op jit(solution)/shard_map/div | solution.py:146
  (21 shorter events, 0.3 us)
Async XLA Ops:
  0.0 4.5 %copy-start = (bf16[768,256]{1,0:T(8,128)(2,1)S(1)}, bf16[768,256]{1,0:T(8,128)(2,1)}, u32[]{:S(2)}) copy-start(bf16[768,256]{1,0:T(8,128)(2,1)} %param.5) | copy-start | bytes 1179652
  0.0 6.6 %copy-start.1 = (bf16[16,2048]{1,0:T(8,128)(2,1)S(1)}, bf16[16,2048]{1,0:T(8,128)(2,1)}, u32[]{:S(2)}) copy-start(bf16[16,2048]{1,0:T(8,128)(2,1)} %param.3) | copy-start | bytes 196612
  0.0 19.8 %collective-permute-start.6 = (bf16[768,2048]{1,0:T(8,128)(2,1)}, bf16[768,2048]{1,0:T(8,128)(2,1)S(1)}, u32[]{:S(2)}, u32[]{:S(2)}) collective-permute-start(bf16[768,2048]{1,0:T(8,128)(2,1)} %param.4), channel_id=1, source_target_pairs={{0,1},{1,0},{2,3},{3,2},{4,5},{5,4},{6,7},{7,6},{8,9},{9,8},{10,11... | collective-permute-start | bytes 9437192 | tf_op jit(solution)/shard_map/ppermute | solution.py:41
  0.5 19.2 %collective-permute-start.7 = (bf16[768,256]{1,0:T(8,128)(2,1)}, bf16[768,256]{1,0:T(8,128)(2,1)S(1)}, u32[]{:S(2)}, u32[]{:S(2)}) collective-permute-start(bf16[768,256]{1,0:T(8,128)(2,1)} %param.5), channel_id=1, source_target_pairs={{0,1},{1,0},{2,3},{3,2},{4,5},{5,4},{6,7},{7,6},{8,9},{9,8},{10,11... | collective-permute-start | bytes 1179656 | tf_op jit(solution)/shard_map/ppermute | solution.py:41
  1.7 4.8 %collective-permute-start = (f32[512]{0:T(512)S(1)}, f32[512]{0:T(512)S(1)}, u32[]{:S(2)}, u32[]{:S(2)}) collective-permute-start(f32[512]{0:T(512)S(1)} %pad_maximum_fusion.4), channel_id=1, source_target_pairs={{0,1},{1,0},{2,3},{3,2},{4,5},{5,4},{6,7},{7,6},{8,9},{9,8},{10,11... | collective-permute-start | bytes 6152 | tf_op jit(solution)/shard_map/ppermute | solution.py:41
  6.6 7.8 %collective-permute-start.4 = (bf16[1,16,2176]{2,1,0:T(8,128)(2,1)S(1)}, bf16[1,16,2176]{2,1,0:T(8,128)(2,1)S(1)}, u32[]{:S(2)}, u32[]{:S(2)}) collective-permute-start(bf16[1,16,2176]{2,1,0:T(8,128)(2,1)S(1)} %maximum_bitcast_fusion), channel_id=1, source_target_pairs={{0,12},{1,13},{2,14},{3,15},{4,8},{5,9},{6,10},{7,11},{8,4},{9,5},... | collective-permute-start | bytes 208904 | tf_op jit(solution)/shard_map/ppermute | solution.py:41
  11.6 6.2 %collective-permute-start.3 = (bf16[1,16,2176]{2,1,0:T(8,128)(2,1)S(1)}, bf16[1,16,2176]{2,1,0:T(8,128)(2,1)S(1)}, u32[]{:S(2)}, u32[]{:S(2)}) collective-permute-start(bf16[1,16,2176]{2,1,0:T(8,128)(2,1)S(1)} %maximum_bitcast_fusion), channel_id=1, source_target_pairs={{0,8},{1,9},{2,10},{3,11},{4,12},{5,13},{6,14},{7,15},{8,0},{9,1},... | collective-permute-start | bytes 208904 | tf_op jit(solution)/shard_map/ppermute | solution.py:41
  11.6 6.2 %collective-permute-start.2 = (bf16[1,16,2176]{2,1,0:T(8,128)(2,1)S(1)}, bf16[1,16,2176]{2,1,0:T(8,128)(2,1)S(1)}, u32[]{:S(2)}, u32[]{:S(2)}) collective-permute-start(bf16[1,16,2176]{2,1,0:T(8,128)(2,1)S(1)} %maximum_bitcast_fusion), channel_id=1, source_target_pairs={{0,4},{1,5},{2,6},{3,7},{4,0},{5,1},{6,2},{7,3},{8,12},{9,13},{10,... | collective-permute-start | bytes 208904 | tf_op jit(solution)/shard_map/ppermute | solution.py:41
  14.4 9.2 %collective-permute-start.1 = (bf16[1,16,2176]{2,1,0:T(8,128)(2,1)S(1)}, bf16[1,16,2176]{2,1,0:T(8,128)(2,1)S(1)}, u32[]{:S(2)}, u32[]{:S(2)}) collective-permute-start(bf16[1,16,2176]{2,1,0:T(8,128)(2,1)S(1)} %maximum_bitcast_fusion), channel_id=1, source_target_pairs={{0,2},{1,3},{2,0},{3,1},{4,6},{5,7},{6,4},{7,5},{8,10},{9,11},{10,... | collective-permute-start | bytes 208904 | tf_op jit(solution)/shard_map/ppermute | solution.py:41
  17.9 6.6 %collective-permute-start.5 = (bf16[3,16,2176]{2,1,0:T(8,128)(2,1)S(1)}, bf16[3,16,2176]{2,1,0:T(8,128)(2,1)S(1)}, u32[]{:S(2)}, u32[]{:S(2)}) collective-permute-start(bf16[3,16,2176]{2,1,0:T(8,128)(2,1)S(1)} %pad_maximum_fusion.2), channel_id=1, source_target_pairs={{0,2},{1,3},{2,0},{3,1},{4,6},{5,7},{6,4},{7,5},{8,10},{9,11},{10,... | collective-permute-start | bytes 626696 | tf_op jit(solution)/shard_map/ppermute | solution.py:41
  27.5 4.7 %collective-permute-start.8 = (f32[4,16,384]{2,1,0:T(8,128)S(1)}, f32[4,16,384]{2,1,0:T(8,128)S(1)}, u32[]{:S(2)}, u32[]{:S(2)}) collective-permute-start(f32[4,16,384]{2,1,0:T(8,128)S(1)} %bitcast.37), channel_id=1, source_target_pairs={{0,2},{1,3},{2,0},{3,1},{4,6},{5,7},{6,4},{7,5},{8,10},{9,11},{10,... | collective-permute-start | bytes 294920 | tf_op jit(solution)/shard_map/ppermute | solution.py:41
  32.2 5.7 %collective-permute-start.11 = (f32[16,384]{1,0:T(8,128)S(1)}, f32[16,384]{1,0:T(8,128)S(1)}, u32[]{:S(2)}, u32[]{:S(2)}) collective-permute-start(f32[16,384]{1,0:T(8,128)S(1)} %get-tuple-element.22), channel_id=1, source_target_pairs={{0,12},{1,13},{2,14},{3,15},{4,8},{5,9},{6,10},{7,11},{8,4},{9,5},... | collective-permute-start | bytes 73736 | tf_op jit(solution)/shard_map/ppermute | solution.py:41
  35.1 4.7 %collective-permute-start.10 = (f32[16,384]{1,0:T(8,128)S(1)}, f32[16,384]{1,0:T(8,128)S(1)}, u32[]{:S(2)}, u32[]{:S(2)}) collective-permute-start(f32[16,384]{1,0:T(8,128)S(1)} %get-tuple-element.23), channel_id=1, source_target_pairs={{0,8},{1,9},{2,10},{3,11},{4,12},{5,13},{6,14},{7,15},{8,0},{9,1},... | collective-permute-start | bytes 73736 | tf_op jit(solution)/shard_map/ppermute | solution.py:41
  35.1 4.7 %collective-permute-start.9 = (f32[16,384]{1,0:T(8,128)S(1)}, f32[16,384]{1,0:T(8,128)S(1)}, u32[]{:S(2)}, u32[]{:S(2)}) collective-permute-start(f32[16,384]{1,0:T(8,128)S(1)} %get-tuple-element.21), channel_id=1, source_target_pairs={{0,4},{1,5},{2,6},{3,7},{4,0},{5,1},{6,2},{7,3},{8,12},{9,13},{10,... | collective-permute-start | bytes 73736 | tf_op jit(solution)/shard_map/ppermute | solution.py:41

commit v20 on v18

--- a/solution.py
+++ b/solution.py
@@ -111,7 +111,6 @@
     values = assays.astype(jnp.float32)
     partial = jnp.concatenate([jnp.sum(values, axis=0), jnp.sum(values * values, axis=0)])
 
-    partial = partial + swap(partial, "blk", core)
     pair_lib = swap(library, "blk", core)
     pair_values = swap(assays, "blk", core).astype(jnp.float32)
 
@@ -127,6 +126,7 @@
     )
     stats = join3(got[:, :, feat:].reshape(lineage, q_dev * lanes), 2 * width)
     stats = jnp.sum(stats, axis=0)
+    stats = stats + swap(stats, "blk", core)
 
     col_sum, col_sq = stats[:width], stats[width:]
     total = library.shape[0] * nblk

time: 39.4 us -> 39.1 us (level)
  starting transfers between devices: 15.7 us -> 13.3 us
  other arithmetic: 5.72 us -> 7.39 us
    ppermute x12, starting transfers between devices: 15.7 us -> 13.3 us  [swap(): return lax.ppermute(x, axis, [(i, i ^ mask) for i in range(count)])]
    broadcast_in_dim x1, other arithmetic: 0.01 us -> 0.85 us  [gather_rounds(): pieces = [packet[None]]]
    unnamed x2, other arithmetic: 0.01 us -> 0.85 us
  transfers between devices with their start and end apart: 12 -> 12, of which waited for: 6 -> 5; matrix products, arithmetic and copies ran while one was open for 26% -> 31% of each run, Pallas kernels for 0% -> 0%
where the time goes in v20:
time: 39.1 us; the launch traced here: 38.8 us
  starting transfers between devices  13.3 us (34%)
  waiting for transfers between devices  12.3 us (31%)
  other arithmetic  7.39 us (19%)
  matrix products  5.37 us (14%)
    ppermute x12, starting transfers between devices, swap(): return lax.ppermute(x, axis, [(i, i ^ mask) for i in range(count)])  13.3 us
    ppermute x12, waiting for transfers between devices, swap(): return lax.ppermute(x, axis, [(i, i ^ mask) for i in range(count)])  12.3 us
    dot_general x4, matrix products, piece_weights(): lax.dot_general(rows, lib_ext, (((1,), (1,)), ((), ())), preferred_elemen...  4.87 us
    reduce_sum x2, other arithmetic, shards(): jnp.sum(jnp.square(lib.astype(jnp.float32)), axis=1)  3.25 us
    reduce_sum x1, other arithmetic, shards(): jnp.sum(values, axis=0)  1.14 us
    unnamed x2, other arithmetic  0.85 us
    broadcast_in_dim x1, other arithmetic, gather_rounds(): pieces = [packet[None]]  0.85 us
  transfers between devices with their start and end apart: 12, of which 5 were waited for; matrix products, arithmetic and copies ran while one was open for 31% of the time, Pallas kernels for 0%

profile of v20, /device:TPU:0, one launch (start us, length us, event | category | flops | bytes accessed | tf_op | source)
XLA Modules:
  0.0 38.8 jit_solution(15896970702275668578)
XLA Ops:
  0.0 0.0 copy-start
  0.0 0.0 copy-start.1
  0.0 0.5 %collective-permute-start.5 = (bf16[768,2048]{1,0:T(8,128)(2,1)}, bf16[768,2048]{1,0:T(8,128)(2,1)S(1)}, u32[]{:S(2)}, u32[]{:S(2)}) collective-permute-start(bf16[768,2048]{1,0:T(8,128)(2,1)} %param.4), channel_id=1, source_target_pairs={{0,1},{1,0},{2,3},{3,2},{4,5},{5,4},{6,7},{7,6},{8,9},{9,8},{10,11... | collective-permute-start | bytes 9437192 | tf_op jit(solution)/shard_map/ppermute | solution.py:41
  0.5 1.1 %convert_reduce_fusion = (f32[256]{0:T(256)S(1)}, f32[256]{0:T(256)S(1)}) fusion(bf16[768,256]{1,0:T(8,128)(2,1)} %param.5), kind=kLoop, calls=%fused_computation.12 | loop fusion | flops 785920 | bytes 395264 | tf_op jit(solution)/shard_map/reduce_sum | solution.py:112
  1.7 0.8 %maximum_bitcast_fusion = bf16[1,16,2176]{2,1,0:T(8,128)(2,1)S(1)} fusion(bf16[16,128]{1,0:T(8,128)(2,1)S(1)} %fusion.77, bf16[16,2048]{1,0:T(8,128)(2,1)} %param.3), kind=kLoop, calls=%fused_computation.54 | loop fusion | flops 139264 | bytes 139264 | tf_op jit(solution)/shard_map/broadcast_in_dim | solution.py:70
  2.5 2.7 %collective-permute-start = (bf16[1,16,2176]{2,1,0:T(8,128)(2,1)S(1)}, bf16[1,16,2176]{2,1,0:T(8,128)(2,1)S(1)}, u32[]{:S(2)}, u32[]{:S(2)}) collective-permute-start(bf16[1,16,2176]{2,1,0:T(8,128)(2,1)S(1)} %maximum_bitcast_fusion), channel_id=1, source_target_pairs={{0,2},{1,3},{2,0},{3,1},{4,6},{5,7},{6,4},{7,5},{8,10},{9,11},{10,... | collective-permute-start | bytes 208904 | tf_op jit(solution)/shard_map/ppermute | solution.py:41
  5.2 3.6 %collective-permute-start.3 = (bf16[1,16,2176]{2,1,0:T(8,128)(2,1)S(1)}, bf16[1,16,2176]{2,1,0:T(8,128)(2,1)S(1)}, u32[]{:S(2)}, u32[]{:S(2)}) collective-permute-start(bf16[1,16,2176]{2,1,0:T(8,128)(2,1)S(1)} %maximum_bitcast_fusion), channel_id=1, source_target_pairs={{0,12},{1,13},{2,14},{3,15},{4,8},{5,9},{6,10},{7,11},{8,4},{9,5},... | collective-permute-start | bytes 208904 | tf_op jit(solution)/shard_map/ppermute | solution.py:41
  8.8 0.0 collective-permute-start.2
  8.8 0.8 %collective-permute-start.1 = (bf16[1,16,2176]{2,1,0:T(8,128)(2,1)S(1)}, bf16[1,16,2176]{2,1,0:T(8,128)(2,1)S(1)}, u32[]{:S(2)}, u32[]{:S(2)}) collective-permute-start(bf16[1,16,2176]{2,1,0:T(8,128)(2,1)S(1)} %maximum_bitcast_fusion), channel_id=1, source_target_pairs={{0,4},{1,5},{2,6},{3,7},{4,0},{5,1},{6,2},{7,3},{8,12},{9,13},{10,... | collective-permute-start | bytes 208904 | tf_op jit(solution)/shard_map/ppermute | solution.py:41
  9.6 0.8 %constant_dynamic-update-slice_fusion.5 = bf16[8,16,2176]{2,1,0:T(8,128)(2,1)S(1)} fusion(bf16[16,128]{1,0:T(8,128)(2,1)S(1)} %fusion.77, bf16[16,2048]{1,0:T(8,128)(2,1)} %param.3), kind=kLoop, calls=%fused_computation.73 | loop fusion | flops 139263 | bytes 139264
  10.4 2.6 %multiply_reduce_fusion.1 = f32[768]{0:T(1024)S(1)} fusion(bf16[768,2048]{1,0:T(8,128)(2,1)} %param.4), kind=kLoop, calls=%fused_computation.1 | loop fusion | flops 4717824 | bytes 3148800 | tf_op jit(solution)/shard_map/reduce_sum | solution.py:123
  13.0 0.0 collective-permute-done.3
  13.0 0.0 copy-done.1
  13.0 0.1 collective-permute-start.7
  13.1 1.9 %collective-permute-done.2 = bf16[1,16,2176]{2,1,0:T(8,128)(2,1)S(1)} collective-permute-done((bf16[1,16,2176]{2,1,0:T(8,128)(2,1)S(1)}, bf16[1,16,2176]{2,1,0:T(8,128)(2,1)S(1)}, u32[]{:S(2)}, u32[]{:S(2)}) %collective-permute-start.2) | collective-permute-done | bytes 69664 | tf_op jit(solution)/shard_map/ppermute | solution.py:41
  15.0 0.0 collective-permute-done.1
  15.0 0.6 %collective-permute-start.4 = (bf16[3,16,2176]{2,1,0:T(8,128)(2,1)S(1)}, bf16[3,16,2176]{2,1,0:T(8,128)(2,1)S(1)}, u32[]{:S(2)}, u32[]{:S(2)}) collective-permute-start(bf16[3,16,2176]{2,1,0:T(8,128)(2,1)S(1)} %pad_maximum_fusion.2), channel_id=1, source_target_pairs={{0,2},{1,3},{2,0},{3,1},{4,6},{5,7},{6,4},{7,5},{8,10},{9,11},{10,... | collective-permute-start | bytes 626696 | tf_op jit(solution)/shard_map/ppermute | solution.py:41
  15.6 0.2 multiply_reduce_fusion.3
  15.8 0.0 copy-done
  15.8 1.2 %fusion.88 = (f32[64]{0:T(128)S(1)}, bf16[64,768]{1,0:T(8,128)(2,1)S(1)}) fusion(f32[768]{0:T(1024)S(1)} %multiply_reduce_fusion.1, f32[64]{0:T(128)S(1)} %multiply_reduce_fusion.3, bf16[64,2176]{1,0:T(8,128)(2,1)S(1)} %bitcast.37, bf16[768,2048]{1,0:T(8,128)(2,1)S(1)} %copy-done), kind=kOutput, calls=%fused_computation.100 | convolution fusion | flops 214253504 | bytes 3526144 | tf_op jit(solution)/shard_map/dot_general | solution.py:29
  17.1 0.0 collective-permute-done.5
  17.1 0.7 %multiply_reduce_fusion = f32[768]{0:T(1024)S(1)} fusion(bf16[768,2048]{1,0:T(8,128)(2,1)S(1)} %collective-permute-done.5), kind=kLoop, calls=%fused_computation | loop fusion | flops 4717824 | bytes 3148800 | tf_op jit(solution)/shard_map/reduce_sum | solution.py:123
  17.8 1.2 %fusion.87 = (f32[64]{0:T(128)S(1)}, bf16[64,768]{1,0:T(8,128)(2,1)S(1)}) fusion(f32[768]{0:T(1024)S(1)} %multiply_reduce_fusion, f32[64]{0:T(128)S(1)} %multiply_reduce_fusion.3, bf16[64,2176]{1,0:T(8,128)(2,1)S(1)} %bitcast.38, bf16[768,2048]{1,0:T(8,128)(2,1)S(1)} %collective-permute-done.5), kind=kOutput, calls=%fused_computation.99 | convolution fusion | flops 214253504 | bytes 3526144 | tf_op jit(solution)/shard_map/dot_general | solution.py:29
  19.0 0.0 collective-permute-done
  19.0 2.7 %collective-permute-done.4 = bf16[3,16,2176]{2,1,0:T(8,128)(2,1)S(1)} collective-permute-done((bf16[3,16,2176]{2,1,0:T(8,128)(2,1)S(1)}, bf16[3,16,2176]{2,1,0:T(8,128)(2,1)S(1)}, u32[]{:S(2)}, u32[]{:S(2)}) %collective-permute-start.4) | collective-permute-done | bytes 208928 | tf_op jit(solution)/shard_map/ppermute | solution.py:41
  21.7 0.2 multiply_reduce_fusion.2
  21.8 1.2 %fusion.86 = (f32[64]{0:T(128)S(1)}, bf16[64,768]{1,0:T(8,128)(2,1)S(1)}) fusion(f32[768]{0:T(1024)S(1)} %multiply_reduce_fusion.1, f32[64]{0:T(128)S(1)} %multiply_reduce_fusion.2, bf16[64,2176]{1,0:T(8,128)(2,1)S(1)} %bitcast.34, bf16[768,2048]{1,0:T(8,128)(2,1)S(1)} %copy-done), kind=kOutput, calls=%fused_computation.98 | convolution fusion | flops 214253504 | bytes 3526144 | tf_op jit(solution)/shard_map/dot_general | solution.py:29
  23.2 0.1 collective-permute-start.6
  23.3 1.2 %fusion.85 = (f32[64]{0:T(128)S(1)}, bf16[64,768]{1,0:T(8,128)(2,1)S(1)}) fusion(f32[768]{0:T(1024)S(1)} %multiply_reduce_fusion, f32[64]{0:T(128)S(1)} %multiply_reduce_fusion.2, bf16[64,2176]{1,0:T(8,128)(2,1)S(1)} %bitcast.35, bf16[768,2048]{1,0:T(8,128)(2,1)S(1)} %collective-permute-done.5), kind=kOutput, calls=%fused_computation.97 | convolution fusion | flops 214253504 | bytes 3526144 | tf_op jit(solution)/shard_map/dot_general | solution.py:29
  24.5 0.1 pad_maximum_fusion.5
  24.6 0.0 collective-permute-done.6
  24.6 0.3 fusion.11
  24.8 0.0 collective-permute-done.7
  24.9 0.2 convolution_add_fusion
  25.1 0.1 broadcast_in_dim.5
  25.2 0.6 %collective-permute-start.8 = (f32[4,16,384]{2,1,0:T(8,128)S(1)}, f32[4,16,384]{2,1,0:T(8,128)S(1)}, u32[]{:S(2)}, u32[]{:S(2)}) collective-permute-start(f32[4,16,384]{2,1,0:T(8,128)S(1)} %bitcast.41), channel_id=1, source_target_pairs={{0,2},{1,3},{2,0},{3,1},{4,6},{5,7},{6,4},{7,5},{8,10},{9,11},{10,... | collective-permute-start | bytes 294920 | tf_op jit(solution)/shard_map/ppermute | solution.py:41
  25.8 4.7 %collective-permute-done.8 = f32[4,16,384]{2,1,0:T(8,128)S(1)} collective-permute-done((f32[4,16,384]{2,1,0:T(8,128)S(1)}, f32[4,16,384]{2,1,0:T(8,128)S(1)}, u32[]{:S(2)}, u32[]{:S(2)}) %collective-permute-start.8) | collective-permute-done | bytes 98336 | tf_op jit(solution)/shard_map/ppermute | solution.py:41
  30.5 2.8 %collective-permute-start.11 = (f32[16,384]{1,0:T(8,128)S(1)}, f32[16,384]{1,0:T(8,128)S(1)}, u32[]{:S(2)}, u32[]{:S(2)}) collective-permute-start(f32[16,384]{1,0:T(8,128)S(1)} %get-tuple-element.28), channel_id=1, source_target_pairs={{0,12},{1,13},{2,14},{3,15},{4,8},{5,9},{6,10},{7,11},{8,4},{9,5},... | collective-permute-start | bytes 73736 | tf_op jit(solution)/shard_map/ppermute | solution.py:41
  33.3 0.0 collective-permute-start.10
  33.3 1.7 %collective-permute-start.9 = (f32[16,384]{1,0:T(8,128)S(1)}, f32[16,384]{1,0:T(8,128)S(1)}, u32[]{:S(2)}, u32[]{:S(2)}) collective-permute-start(f32[16,384]{1,0:T(8,128)S(1)} %get-tuple-element.27), channel_id=1, source_target_pairs={{0,4},{1,5},{2,6},{3,7},{4,0},{5,1},{6,2},{7,3},{8,12},{9,13},{10,... | collective-permute-start | bytes 73736 | tf_op jit(solution)/shard_map/ppermute | solution.py:41
  35.0 1.2 %collective-permute-done.11 = f32[16,384]{1,0:T(8,128)S(1)} collective-permute-done((f32[16,384]{1,0:T(8,128)S(1)}, f32[16,384]{1,0:T(8,128)S(1)}, u32[]{:S(2)}, u32[]{:S(2)}) %collective-permute-start.11) | collective-permute-done | bytes 24608 | tf_op jit(solution)/shard_map/ppermute | solution.py:41
  36.2 1.8 %collective-permute-done.10 = f32[16,384]{1,0:T(8,128)S(1)} collective-permute-done((f32[16,384]{1,0:T(8,128)S(1)}, f32[16,384]{1,0:T(8,128)S(1)}, u32[]{:S(2)}, u32[]{:S(2)}) %collective-permute-start.10) | collective-permute-done | bytes 24608 | tf_op jit(solution)/shard_map/ppermute | solution.py:41
  38.0 0.0 collective-permute-done.9
  38.0 0.1 slice_reduce_fusion
  38.2 0.7 %slice_divide_fusion = f32[16,256]{1,0:T(8,128)} fusion(f32[16,384]{1,0:T(8,128)S(1)} %fusion.70, f32[16]{0:T(128)S(1)} %slice_reduce_fusion), kind=kLoop, calls=%fused_computation.64 | loop fusion | flops 4096 | bytes 32832 | tf_op jit(solution)/shard_map/div | solution.py:146
  (21 shorter events, 0.3 us)
Async XLA Ops:
  0.0 15.8 %copy-start = (bf16[768,2048]{1,0:T(8,128)(2,1)S(1)}, bf16[768,2048]{1,0:T(8,128)(2,1)}, u32[]{:S(2)}) copy-start(bf16[768,2048]{1,0:T(8,128)(2,1)} %param.4) | copy-start | bytes 9437188
  0.0 13.0 %copy-start.1 = (bf16[768,256]{1,0:T(8,128)(2,1)S(1)}, bf16[768,256]{1,0:T(8,128)(2,1)}, u32[]{:S(2)}) copy-start(bf16[768,256]{1,0:T(8,128)(2,1)} %param.5) | copy-start | bytes 1179652
  0.0 17.1 %collective-permute-start.5 = (bf16[768,2048]{1,0:T(8,128)(2,1)}, bf16[768,2048]{1,0:T(8,128)(2,1)S(1)}, u32[]{:S(2)}, u32[]{:S(2)}) collective-permute-start(bf16[768,2048]{1,0:T(8,128)(2,1)} %param.4), channel_id=1, source_target_pairs={{0,1},{1,0},{2,3},{3,2},{4,5},{5,4},{6,7},{7,6},{8,9},{9,8},{10,11... | collective-permute-start | bytes 9437192 | tf_op jit(solution)/shard_map/ppermute | solution.py:41
  2.5 16.5 %collective-permute-start = (bf16[1,16,2176]{2,1,0:T(8,128)(2,1)S(1)}, bf16[1,16,2176]{2,1,0:T(8,128)(2,1)S(1)}, u32[]{:S(2)}, u32[]{:S(2)}) collective-permute-start(bf16[1,16,2176]{2,1,0:T(8,128)(2,1)S(1)} %maximum_bitcast_fusion), channel_id=1, source_target_pairs={{0,2},{1,3},{2,0},{3,1},{4,6},{5,7},{6,4},{7,5},{8,10},{9,11},{10,... | collective-permute-start | bytes 208904 | tf_op jit(solution)/shard_map/ppermute | solution.py:41
  5.2 7.8 %collective-permute-start.3 = (bf16[1,16,2176]{2,1,0:T(8,128)(2,1)S(1)}, bf16[1,16,2176]{2,1,0:T(8,128)(2,1)S(1)}, u32[]{:S(2)}, u32[]{:S(2)}) collective-permute-start(bf16[1,16,2176]{2,1,0:T(8,128)(2,1)S(1)} %maximum_bitcast_fusion), channel_id=1, source_target_pairs={{0,12},{1,13},{2,14},{3,15},{4,8},{5,9},{6,10},{7,11},{8,4},{9,5},... | collective-permute-start | bytes 208904 | tf_op jit(solution)/shard_map/ppermute | solution.py:41
  8.8 6.2 %collective-permute-start.2 = (bf16[1,16,2176]{2,1,0:T(8,128)(2,1)S(1)}, bf16[1,16,2176]{2,1,0:T(8,128)(2,1)S(1)}, u32[]{:S(2)}, u32[]{:S(2)}) collective-permute-start(bf16[1,16,2176]{2,1,0:T(8,128)(2,1)S(1)} %maximum_bitcast_fusion), channel_id=1, source_target_pairs={{0,8},{1,9},{2,10},{3,11},{4,12},{5,13},{6,14},{7,15},{8,0},{9,1},... | collective-permute-start | bytes 208904 | tf_op jit(solution)/shard_map/ppermute | solution.py:41
  8.8 6.2 %collective-permute-start.1 = (bf16[1,16,2176]{2,1,0:T(8,128)(2,1)S(1)}, bf16[1,16,2176]{2,1,0:T(8,128)(2,1)S(1)}, u32[]{:S(2)}, u32[]{:S(2)}) collective-permute-start(bf16[1,16,2176]{2,1,0:T(8,128)(2,1)S(1)} %maximum_bitcast_fusion), channel_id=1, source_target_pairs={{0,4},{1,5},{2,6},{3,7},{4,0},{5,1},{6,2},{7,3},{8,12},{9,13},{10,... | collective-permute-start | bytes 208904 | tf_op jit(solution)/shard_map/ppermute | solution.py:41
  13.0 11.8 %collective-permute-start.7 = (bf16[768,256]{1,0:T(8,128)(2,1)S(1)}, bf16[768,256]{1,0:T(8,128)(2,1)S(1)}, u32[]{:S(2)}, u32[]{:S(2)}) collective-permute-start(bf16[768,256]{1,0:T(8,128)(2,1)S(1)} %copy-done.1), channel_id=1, source_target_pairs={{0,1},{1,0},{2,3},{3,2},{4,5},{5,4},{6,7},{7,6},{8,9},{9,8},{10,11... | collective-permute-start | bytes 1179656 | tf_op jit(solution)/shard_map/ppermute | solution.py:41
  15.0 6.6 %collective-permute-start.4 = (bf16[3,16,2176]{2,1,0:T(8,128)(2,1)S(1)}, bf16[3,16,2176]{2,1,0:T(8,128)(2,1)S(1)}, u32[]{:S(2)}, u32[]{:S(2)}) collective-permute-start(bf16[3,16,2176]{2,1,0:T(8,128)(2,1)S(1)} %pad_maximum_fusion.2), channel_id=1, source_target_pairs={{0,2},{1,3},{2,0},{3,1},{4,6},{5,7},{6,4},{7,5},{8,10},{9,11},{10,... | collective-permute-start | bytes 626696 | tf_op jit(solution)/shard_map/ppermute | solution.py:41
  23.2 1.4 %collective-permute-start.6 = (f32[512]{0:T(512)S(1)}, f32[512]{0:T(512)S(1)}, u32[]{:S(2)}, u32[]{:S(2)}) collective-permute-start(f32[512]{0:T(512)S(1)} %fusion.71), channel_id=1, source_target_pairs={{0,1},{1,0},{2,3},{3,2},{4,5},{5,4},{6,7},{7,6},{8,9},{9,8},{10,11... | collective-permute-start | bytes 6152 | tf_op jit(solution)/shard_map/ppermute | solution.py:41
  25.2 5.3 %collective-permute-start.8 = (f32[4,16,384]{2,1,0:T(8,128)S(1)}, f32[4,16,384]{2,1,0:T(8,128)S(1)}, u32[]{:S(2)}, u32[]{:S(2)}) collective-permute-start(f32[4,16,384]{2,1,0:T(8,128)S(1)} %bitcast.41), channel_id=1, source_target_pairs={{0,2},{1,3},{2,0},{3,1},{4,6},{5,7},{6,4},{7,5},{8,10},{9,11},{10,... | collective-permute-start | bytes 294920 | tf_op jit(solution)/shard_map/ppermute | solution.py:41
  30.5 5.7 %collective-permute-start.11 = (f32[16,384]{1,0:T(8,128)S(1)}, f32[16,384]{1,0:T(8,128)S(1)}, u32[]{:S(2)}, u32[]{:S(2)}) collective-permute-start(f32[16,384]{1,0:T(8,128)S(1)} %get-tuple-element.28), channel_id=1, source_target_pairs={{0,12},{1,13},{2,14},{3,15},{4,8},{5,9},{6,10},{7,11},{8,4},{9,5},... | collective-permute-start | bytes 73736 | tf_op jit(solution)/shard_map/ppermute | solution.py:41
  33.3 4.7 %collective-permute-start.10 = (f32[16,384]{1,0:T(8,128)S(1)}, f32[16,384]{1,0:T(8,128)S(1)}, u32[]{:S(2)}, u32[]{:S(2)}) collective-permute-start(f32[16,384]{1,0:T(8,128)S(1)} %get-tuple-element.29), channel_id=1, source_target_pairs={{0,8},{1,9},{2,10},{3,11},{4,12},{5,13},{6,14},{7,15},{8,0},{9,1},... | collective-permute-start | bytes 73736 | tf_op jit(solution)/shard_map/ppermute | solution.py:41
  33.3 4.7 %collective-permute-start.9 = (f32[16,384]{1,0:T(8,128)S(1)}, f32[16,384]{1,0:T(8,128)S(1)}, u32[]{:S(2)}, u32[]{:S(2)}) collective-permute-start(f32[16,384]{1,0:T(8,128)S(1)} %get-tuple-element.27), channel_id=1, source_target_pairs={{0,4},{1,5},{2,6},{3,7},{4,0},{5,1},{6,2},{7,3},{8,12},{9,13},{10,... | collective-permute-start | bytes 73736 | tf_op jit(solution)/shard_map/ppermute | solution.py:41

commit v21 on v20

--- a/solution.py
+++ b/solution.py
@@ -142,7 +142,9 @@
     den = jnp.broadcast_to(denom[:, None], (denom.shape[0], 128))
     sums = jnp.concatenate([numer, den], axis=1).reshape(lineage, q_dev, width + 128)
     sums = sums.reshape(tuple(len(offsets(g)) for g in groups) + sums.shape[1:])
-    mine = scatter_rounds(sums, "blk", groups)
+    order = list(range(1, len(groups))) + [0]
+    sums = jnp.transpose(sums, order + list(range(len(groups), sums.ndim)))
+    mine = scatter_rounds(sums, "blk", [groups[k] for k in order])
     return mine[:, :width] / mine[:, width:width + 1]
 
 

time: 39.1 us -> 38.4 us (0.982)
  waiting for transfers between devices: 12.3 us -> 11.6 us
    ppermute x12, waiting for transfers between devices: 12.3 us -> 11.6 us  [swap(): return lax.ppermute(x, axis, [(i, i ^ mask) for i in range(count)])]
where the time goes in v21:
time: 38.4 us; the launch traced here: 38.1 us
  starting transfers between devices  13.3 us (35%)
  waiting for transfers between devices  11.6 us (30%)
  other arithmetic  7.39 us (19%)
  matrix products  5.37 us (14%)
    ppermute x12, starting transfers between devices, swap(): return lax.ppermute(x, axis, [(i, i ^ mask) for i in range(count)])  13.3 us
    ppermute x12, waiting for transfers between devices, swap(): return lax.ppermute(x, axis, [(i, i ^ mask) for i in range(count)])  11.6 us
    dot_general x4, matrix products, piece_weights(): lax.dot_general(rows, lib_ext, (((1,), (1,)), ((), ())), preferred_elemen...  4.87 us
    reduce_sum x2, other arithmetic, shards(): jnp.sum(jnp.square(lib.astype(jnp.float32)), axis=1)  3.25 us
    reduce_sum x1, other arithmetic, shards(): jnp.sum(values, axis=0)  1.14 us
    unnamed x2, other arithmetic  0.85 us
    broadcast_in_dim x1, other arithmetic, gather_rounds(): pieces = [packet[None]]  0.85 us
  transfers between devices with their start and end apart: 12, of which 5 were waited for; matrix products, arithmetic and copies ran while one was open for 31% of the time, Pallas kernels for 0%

profile of v21, /device:TPU:0, one launch (start us, length us, event | category | flops | bytes accessed | tf_op | source)
XLA Modules:
  0.0 38.1 jit_solution(1543150455150692718)
XLA Ops:
  0.0 0.0 copy-start
  0.0 0.0 copy-start.1
  0.0 0.5 %collective-permute-start.5 = (bf16[768,2048]{1,0:T(8,128)(2,1)}, bf16[768,2048]{1,0:T(8,128)(2,1)S(1)}, u32[]{:S(2)}, u32[]{:S(2)}) collective-permute-start(bf16[768,2048]{1,0:T(8,128)(2,1)} %param.4), channel_id=1, source_target_pairs={{0,1},{1,0},{2,3},{3,2},{4,5},{5,4},{6,7},{7,6},{8,9},{9,8},{10,11... | collective-permute-start | bytes 9437192 | tf_op jit(solution)/shard_map/ppermute | solution.py:41
  0.5 1.1 %convert_reduce_fusion = (f32[256]{0:T(256)S(1)}, f32[256]{0:T(256)S(1)}) fusion(bf16[768,256]{1,0:T(8,128)(2,1)} %param.5), kind=kLoop, calls=%fused_computation.12 | loop fusion | flops 785920 | bytes 395264 | tf_op jit(solution)/shard_map/reduce_sum | solution.py:112
  1.7 0.8 %maximum_bitcast_fusion = bf16[1,16,2176]{2,1,0:T(8,128)(2,1)S(1)} fusion(bf16[16,128]{1,0:T(8,128)(2,1)S(1)} %fusion.77, bf16[16,2048]{1,0:T(8,128)(2,1)} %param.3), kind=kLoop, calls=%fused_computation.52 | loop fusion | flops 139264 | bytes 139264 | tf_op jit(solution)/shard_map/broadcast_in_dim | solution.py:70
  2.5 2.7 %collective-permute-start = (bf16[1,16,2176]{2,1,0:T(8,128)(2,1)S(1)}, bf16[1,16,2176]{2,1,0:T(8,128)(2,1)S(1)}, u32[]{:S(2)}, u32[]{:S(2)}) collective-permute-start(bf16[1,16,2176]{2,1,0:T(8,128)(2,1)S(1)} %maximum_bitcast_fusion), channel_id=1, source_target_pairs={{0,2},{1,3},{2,0},{3,1},{4,6},{5,7},{6,4},{7,5},{8,10},{9,11},{10,... | collective-permute-start | bytes 208904 | tf_op jit(solution)/shard_map/ppermute | solution.py:41
  5.2 3.6 %collective-permute-start.3 = (bf16[1,16,2176]{2,1,0:T(8,128)(2,1)S(1)}, bf16[1,16,2176]{2,1,0:T(8,128)(2,1)S(1)}, u32[]{:S(2)}, u32[]{:S(2)}) collective-permute-start(bf16[1,16,2176]{2,1,0:T(8,128)(2,1)S(1)} %maximum_bitcast_fusion), channel_id=1, source_target_pairs={{0,12},{1,13},{2,14},{3,15},{4,8},{5,9},{6,10},{7,11},{8,4},{9,5},... | collective-permute-start | bytes 208904 | tf_op jit(solution)/shard_map/ppermute | solution.py:41
  8.8 0.0 collective-permute-start.2
  8.8 0.8 %collective-permute-start.1 = (bf16[1,16,2176]{2,1,0:T(8,128)(2,1)S(1)}, bf16[1,16,2176]{2,1,0:T(8,128)(2,1)S(1)}, u32[]{:S(2)}, u32[]{:S(2)}) collective-permute-start(bf16[1,16,2176]{2,1,0:T(8,128)(2,1)S(1)} %maximum_bitcast_fusion), channel_id=1, source_target_pairs={{0,4},{1,5},{2,6},{3,7},{4,0},{5,1},{6,2},{7,3},{8,12},{9,13},{10,... | collective-permute-start | bytes 208904 | tf_op jit(solution)/shard_map/ppermute | solution.py:41
  9.6 0.8 %constant_dynamic-update-slice_fusion.5 = bf16[8,16,2176]{2,1,0:T(8,128)(2,1)S(1)} fusion(bf16[16,128]{1,0:T(8,128)(2,1)S(1)} %fusion.77, bf16[16,2048]{1,0:T(8,128)(2,1)} %param.3), kind=kLoop, calls=%fused_computation.74 | loop fusion | flops 139263 | bytes 139264
  10.4 2.6 %multiply_reduce_fusion.1 = f32[768]{0:T(1024)S(1)} fusion(bf16[768,2048]{1,0:T(8,128)(2,1)} %param.4), kind=kLoop, calls=%fused_computation.1 | loop fusion | flops 4717824 | bytes 3148800 | tf_op jit(solution)/shard_map/reduce_sum | solution.py:123
  13.0 0.0 collective-permute-done.3
  13.0 0.0 copy-done.1
  13.0 0.1 collective-permute-start.7
  13.1 1.9 %collective-permute-done.2 = bf16[1,16,2176]{2,1,0:T(8,128)(2,1)S(1)} collective-permute-done((bf16[1,16,2176]{2,1,0:T(8,128)(2,1)S(1)}, bf16[1,16,2176]{2,1,0:T(8,128)(2,1)S(1)}, u32[]{:S(2)}, u32[]{:S(2)}) %collective-permute-start.2) | collective-permute-done | bytes 69664 | tf_op jit(solution)/shard_map/ppermute | solution.py:41
  15.0 0.0 collective-permute-done.1
  15.0 0.6 %collective-permute-start.4 = (bf16[3,16,2176]{2,1,0:T(8,128)(2,1)S(1)}, bf16[3,16,2176]{2,1,0:T(8,128)(2,1)S(1)}, u32[]{:S(2)}, u32[]{:S(2)}) collective-permute-start(bf16[3,16,2176]{2,1,0:T(8,128)(2,1)S(1)} %pad_maximum_fusion.2), channel_id=1, source_target_pairs={{0,2},{1,3},{2,0},{3,1},{4,6},{5,7},{6,4},{7,5},{8,10},{9,11},{10,... | collective-permute-start | bytes 626696 | tf_op jit(solution)/shard_map/ppermute | solution.py:41
  15.6 0.2 multiply_reduce_fusion.3
  15.8 0.0 copy-done
  15.8 1.2 %fusion.88 = (f32[64]{0:T(128)S(1)}, bf16[64,768]{1,0:T(8,128)(2,1)S(1)}) fusion(f32[768]{0:T(1024)S(1)} %multiply_reduce_fusion.1, f32[64]{0:T(128)S(1)} %multiply_reduce_fusion.3, bf16[64,2176]{1,0:T(8,128)(2,1)S(1)} %bitcast.45, bf16[768,2048]{1,0:T(8,128)(2,1)S(1)} %copy-done), kind=kOutput, calls=%fused_computation.101 | convolution fusion | flops 214253504 | bytes 3526144 | tf_op jit(solution)/shard_map/dot_general | solution.py:29
  17.1 0.0 collective-permute-done.5
  17.1 0.7 %multiply_reduce_fusion = f32[768]{0:T(1024)S(1)} fusion(bf16[768,2048]{1,0:T(8,128)(2,1)S(1)} %collective-permute-done.5), kind=kLoop, calls=%fused_computation | loop fusion | flops 4717824 | bytes 3148800 | tf_op jit(solution)/shard_map/reduce_sum | solution.py:123
  17.8 1.2 %fusion.87 = (f32[64]{0:T(128)S(1)}, bf16[64,768]{1,0:T(8,128)(2,1)S(1)}) fusion(f32[768]{0:T(1024)S(1)} %multiply_reduce_fusion, f32[64]{0:T(128)S(1)} %multiply_reduce_fusion.3, bf16[64,2176]{1,0:T(8,128)(2,1)S(1)} %bitcast.46, bf16[768,2048]{1,0:T(8,128)(2,1)S(1)} %collective-permute-done.5), kind=kOutput, calls=%fused_computation.100 | convolution fusion | flops 214253504 | bytes 3526144 | tf_op jit(solution)/shard_map/dot_general | solution.py:29
  19.0 0.0 collective-permute-done
  19.0 2.7 %collective-permute-done.4 = bf16[3,16,2176]{2,1,0:T(8,128)(2,1)S(1)} collective-permute-done((bf16[3,16,2176]{2,1,0:T(8,128)(2,1)S(1)}, bf16[3,16,2176]{2,1,0:T(8,128)(2,1)S(1)}, u32[]{:S(2)}, u32[]{:S(2)}) %collective-permute-start.4) | collective-permute-done | bytes 208928 | tf_op jit(solution)/shard_map/ppermute | solution.py:41
  21.7 0.2 multiply_reduce_fusion.2
  21.8 1.2 %fusion.86 = (bf16[64,768]{1,0:T(8,128)(2,1)S(1)}, f32[64]{0:T(128)S(1)}) fusion(f32[768]{0:T(1024)S(1)} %multiply_reduce_fusion.1, f32[64]{0:T(128)S(1)} %multiply_reduce_fusion.2, bf16[64,2176]{1,0:T(8,128)(2,1)S(1)} %bitcast.42, bf16[768,2048]{1,0:T(8,128)(2,1)S(1)} %copy-done), kind=kOutput, calls=%fused_computation.99 | convolution fusion | flops 214253504 | bytes 3526144 | tf_op jit(solution)/shard_map/dot_general | solution.py:29
  23.2 0.1 collective-permute-start.6
  23.3 1.2 %fusion.85 = (bf16[64,768]{1,0:T(8,128)(2,1)S(1)}, f32[64]{0:T(128)S(1)}) fusion(f32[768]{0:T(1024)S(1)} %multiply_reduce_fusion, f32[64]{0:T(128)S(1)} %multiply_reduce_fusion.2, bf16[64,2176]{1,0:T(8,128)(2,1)S(1)} %bitcast.43, bf16[768,2048]{1,0:T(8,128)(2,1)S(1)} %collective-permute-done.5), kind=kOutput, calls=%fused_computation.98 | convolution fusion | flops 214253504 | bytes 3526144 | tf_op jit(solution)/shard_map/dot_general | solution.py:29
  24.5 0.1 pad_maximum_fusion.5
  24.6 0.0 collective-permute-done.6
  24.6 0.3 fusion.11
  24.8 0.0 collective-permute-done.7
  24.9 0.2 convolution_add_fusion
  25.1 0.1 broadcast_in_dim.5
  25.3 2.8 %collective-permute-start.10 = (f32[2,16,384]{2,1,0:T(8,128)S(1)}, f32[2,16,384]{2,1,0:T(8,128)S(1)}, u32[]{:S(2)}, u32[]{:S(2)}) collective-permute-start(f32[2,16,384]{2,1,0:T(8,128)S(1)} %get-tuple-element.18), channel_id=1, source_target_pairs={{0,12},{1,13},{2,14},{3,15},{4,8},{5,9},{6,10},{7,11},{8,4},{9,5},... | collective-permute-start | bytes 147464 | tf_op jit(solution)/shard_map/ppermute | solution.py:41
  28.0 0.0 collective-permute-start.9
  28.0 1.7 %collective-permute-start.8 = (f32[2,16,384]{2,1,0:T(8,128)S(1)}, f32[2,16,384]{2,1,0:T(8,128)S(1)}, u32[]{:S(2)}, u32[]{:S(2)}) collective-permute-start(f32[2,16,384]{2,1,0:T(8,128)S(1)} %get-tuple-element.17), channel_id=1, source_target_pairs={{0,4},{1,5},{2,6},{3,7},{4,0},{5,1},{6,2},{7,3},{8,12},{9,13},{10,... | collective-permute-start | bytes 147464 | tf_op jit(solution)/shard_map/ppermute | solution.py:41
  29.7 2.0 %collective-permute-done.10 = f32[2,16,384]{2,1,0:T(8,128)S(1)} collective-permute-done((f32[2,16,384]{2,1,0:T(8,128)S(1)}, f32[2,16,384]{2,1,0:T(8,128)S(1)}, u32[]{:S(2)}, u32[]{:S(2)}) %collective-permute-start.10) | collective-permute-done | bytes 49184 | tf_op jit(solution)/shard_map/ppermute | solution.py:41
  31.7 1.7 %collective-permute-done.9 = f32[2,16,384]{2,1,0:T(8,128)S(1)} collective-permute-done((f32[2,16,384]{2,1,0:T(8,128)S(1)}, f32[2,16,384]{2,1,0:T(8,128)S(1)}, u32[]{:S(2)}, u32[]{:S(2)}) %collective-permute-start.9) | collective-permute-done | bytes 49184 | tf_op jit(solution)/shard_map/ppermute | solution.py:41
  33.4 0.0 collective-permute-done.8
  33.4 0.6 %collective-permute-start.11 = (f32[16,384]{1,0:T(8,128)S(1)}, f32[16,384]{1,0:T(8,128)S(1)}, u32[]{:S(2)}, u32[]{:S(2)}) collective-permute-start(f32[16,384]{1,0:T(8,128)S(1)} %slice_bitcast_fusion.4), channel_id=1, source_target_pairs={{0,2},{1,3},{2,0},{3,1},{4,6},{5,7},{6,4},{7,5},{8,10},{9,11},{10,... | collective-permute-start | bytes 73736 | tf_op jit(solution)/shard_map/ppermute | solution.py:41
  34.0 3.3 %collective-permute-done.11 = f32[16,384]{1,0:T(8,128)S(1)} collective-permute-done((f32[16,384]{1,0:T(8,128)S(1)}, f32[16,384]{1,0:T(8,128)S(1)}, u32[]{:S(2)}, u32[]{:S(2)}) %collective-permute-start.11) | collective-permute-done | bytes 24608 | tf_op jit(solution)/shard_map/ppermute | solution.py:41
  37.3 0.1 slice_reduce_fusion
  37.5 0.7 %slice_divide_fusion = f32[16,256]{1,0:T(8,128)} fusion(f32[16,384]{1,0:T(8,128)S(1)} %fusion.70, f32[16]{0:T(128)S(1)} %slice_reduce_fusion), kind=kLoop, calls=%fused_computation.65 | loop fusion | flops 4096 | bytes 32832 | tf_op jit(solution)/shard_map/div | solution.py:148
  (23 shorter events, 0.4 us)
Async XLA Ops:
  0.0 15.8 %copy-start = (bf16[768,2048]{1,0:T(8,128)(2,1)S(1)}, bf16[768,2048]{1,0:T(8,128)(2,1)}, u32[]{:S(2)}) copy-start(bf16[768,2048]{1,0:T(8,128)(2,1)} %param.4) | copy-start | bytes 9437188
  0.0 13.0 %copy-start.1 = (bf16[768,256]{1,0:T(8,128)(2,1)S(1)}, bf16[768,256]{1,0:T(8,128)(2,1)}, u32[]{:S(2)}) copy-start(bf16[768,256]{1,0:T(8,128)(2,1)} %param.5) | copy-start | bytes 1179652
  0.0 17.1 %collective-permute-start.5 = (bf16[768,2048]{1,0:T(8,128)(2,1)}, bf16[768,2048]{1,0:T(8,128)(2,1)S(1)}, u32[]{:S(2)}, u32[]{:S(2)}) collective-permute-start(bf16[768,2048]{1,0:T(8,128)(2,1)} %param.4), channel_id=1, source_target_pairs={{0,1},{1,0},{2,3},{3,2},{4,5},{5,4},{6,7},{7,6},{8,9},{9,8},{10,11... | collective-permute-start | bytes 9437192 | tf_op jit(solution)/shard_map/ppermute | solution.py:41
  2.5 16.5 %collective-permute-start = (bf16[1,16,2176]{2,1,0:T(8,128)(2,1)S(1)}, bf16[1,16,2176]{2,1,0:T(8,128)(2,1)S(1)}, u32[]{:S(2)}, u32[]{:S(2)}) collective-permute-start(bf16[1,16,2176]{2,1,0:T(8,128)(2,1)S(1)} %maximum_bitcast_fusion), channel_id=1, source_target_pairs={{0,2},{1,3},{2,0},{3,1},{4,6},{5,7},{6,4},{7,5},{8,10},{9,11},{10,... | collective-permute-start | bytes 208904 | tf_op jit(solution)/shard_map/ppermute | solution.py:41
  5.2 7.8 %collective-permute-start.3 = (bf16[1,16,2176]{2,1,0:T(8,128)(2,1)S(1)}, bf16[1,16,2176]{2,1,0:T(8,128)(2,1)S(1)}, u32[]{:S(2)}, u32[]{:S(2)}) collective-permute-start(bf16[1,16,2176]{2,1,0:T(8,128)(2,1)S(1)} %maximum_bitcast_fusion), channel_id=1, source_target_pairs={{0,12},{1,13},{2,14},{3,15},{4,8},{5,9},{6,10},{7,11},{8,4},{9,5},... | collective-permute-start | bytes 208904 | tf_op jit(solution)/shard_map/ppermute | solution.py:41
  8.8 6.2 %collective-permute-start.2 = (bf16[1,16,2176]{2,1,0:T(8,128)(2,1)S(1)}, bf16[1,16,2176]{2,1,0:T(8,128)(2,1)S(1)}, u32[]{:S(2)}, u32[]{:S(2)}) collective-permute-start(bf16[1,16,2176]{2,1,0:T(8,128)(2,1)S(1)} %maximum_bitcast_fusion), channel_id=1, source_target_pairs={{0,8},{1,9},{2,10},{3,11},{4,12},{5,13},{6,14},{7,15},{8,0},{9,1},... | collective-permute-start | bytes 208904 | tf_op jit(solution)/shard_map/ppermute | solution.py:41
  8.8 6.2 %collective-permute-start.1 = (bf16[1,16,2176]{2,1,0:T(8,128)(2,1)S(1)}, bf16[1,16,2176]{2,1,0:T(8,128)(2,1)S(1)}, u32[]{:S(2)}, u32[]{:S(2)}) collective-permute-start(bf16[1,16,2176]{2,1,0:T(8,128)(2,1)S(1)} %maximum_bitcast_fusion), channel_id=1, source_target_pairs={{0,4},{1,5},{2,6},{3,7},{4,0},{5,1},{6,2},{7,3},{8,12},{9,13},{10,... | collective-permute-start | bytes 208904 | tf_op jit(solution)/shard_map/ppermute | solution.py:41
  13.0 11.8 %collective-permute-start.7 = (bf16[768,256]{1,0:T(8,128)(2,1)S(1)}, bf16[768,256]{1,0:T(8,128)(2,1)S(1)}, u32[]{:S(2)}, u32[]{:S(2)}) collective-permute-start(bf16[768,256]{1,0:T(8,128)(2,1)S(1)} %copy-done.1), channel_id=1, source_target_pairs={{0,1},{1,0},{2,3},{3,2},{4,5},{5,4},{6,7},{7,6},{8,9},{9,8},{10,11... | collective-permute-start | bytes 1179656 | tf_op jit(solution)/shard_map/ppermute | solution.py:41
  15.0 6.6 %collective-permute-start.4 = (bf16[3,16,2176]{2,1,0:T(8,128)(2,1)S(1)}, bf16[3,16,2176]{2,1,0:T(8,128)(2,1)S(1)}, u32[]{:S(2)}, u32[]{:S(2)}) collective-permute-start(bf16[3,16,2176]{2,1,0:T(8,128)(2,1)S(1)} %pad_maximum_fusion.2), channel_id=1, source_target_pairs={{0,2},{1,3},{2,0},{3,1},{4,6},{5,7},{6,4},{7,5},{8,10},{9,11},{10,... | collective-permute-start | bytes 626696 | tf_op jit(solution)/shard_map/ppermute | solution.py:41
  23.2 1.4 %collective-permute-start.6 = (f32[512]{0:T(512)S(1)}, f32[512]{0:T(512)S(1)}, u32[]{:S(2)}, u32[]{:S(2)}) collective-permute-start(f32[512]{0:T(512)S(1)} %fusion.71), channel_id=1, source_target_pairs={{0,1},{1,0},{2,3},{3,2},{4,5},{5,4},{6,7},{7,6},{8,9},{9,8},{10,11... | collective-permute-start | bytes 6152 | tf_op jit(solution)/shard_map/ppermute | solution.py:41
  25.3 6.5 %collective-permute-start.10 = (f32[2,16,384]{2,1,0:T(8,128)S(1)}, f32[2,16,384]{2,1,0:T(8,128)S(1)}, u32[]{:S(2)}, u32[]{:S(2)}) collective-permute-start(f32[2,16,384]{2,1,0:T(8,128)S(1)} %get-tuple-element.18), channel_id=1, source_target_pairs={{0,12},{1,13},{2,14},{3,15},{4,8},{5,9},{6,10},{7,11},{8,4},{9,5},... | collective-permute-start | bytes 147464 | tf_op jit(solution)/shard_map/ppermute | solution.py:41
  28.0 5.4 %collective-permute-start.9 = (f32[2,16,384]{2,1,0:T(8,128)S(1)}, f32[2,16,384]{2,1,0:T(8,128)S(1)}, u32[]{:S(2)}, u32[]{:S(2)}) collective-permute-start(f32[2,16,384]{2,1,0:T(8,128)S(1)} %get-tuple-element.19), channel_id=1, source_target_pairs={{0,8},{1,9},{2,10},{3,11},{4,12},{5,13},{6,14},{7,15},{8,0},{9,1},... | collective-permute-start | bytes 147464 | tf_op jit(solution)/shard_map/ppermute | solution.py:41
  28.0 5.4 %collective-permute-start.8 = (f32[2,16,384]{2,1,0:T(8,128)S(1)}, f32[2,16,384]{2,1,0:T(8,128)S(1)}, u32[]{:S(2)}, u32[]{:S(2)}) collective-permute-start(f32[2,16,384]{2,1,0:T(8,128)S(1)} %get-tuple-element.17), channel_id=1, source_target_pairs={{0,4},{1,5},{2,6},{3,7},{4,0},{5,1},{6,2},{7,3},{8,12},{9,13},{10,... | collective-permute-start | bytes 147464 | tf_op jit(solution)/shard_map/ppermute | solution.py:41
  33.4 3.9 %collective-permute-start.11 = (f32[16,384]{1,0:T(8,128)S(1)}, f32[16,384]{1,0:T(8,128)S(1)}, u32[]{:S(2)}, u32[]{:S(2)}) collective-permute-start(f32[16,384]{1,0:T(8,128)S(1)} %slice_bitcast_fusion.4), channel_id=1, source_target_pairs={{0,2},{1,3},{2,0},{3,1},{4,6},{5,7},{6,4},{7,5},{8,10},{9,11},{10,... | collective-permute-start | bytes 73736 | tf_op jit(solution)/shard_map/ppermute | solution.py:41

commit v22 on v21

--- a/solution.py
+++ b/solution.py
@@ -111,14 +111,14 @@
     values = assays.astype(jnp.float32)
     partial = jnp.concatenate([jnp.sum(values, axis=0), jnp.sum(values * values, axis=0)])
 
-    pair_lib = swap(library, "blk", core)
-    pair_values = swap(assays, "blk", core).astype(jnp.float32)
-
     coded = split3(partial)
     lanes = -(-coded.shape[0] // q_dev)
     lanes += -lanes % 128
     coded = jnp.pad(coded, (0, q_dev * lanes - coded.shape[0])).reshape(q_dev, lanes)
     packet = jnp.concatenate([queries, coded], axis=1)
+    packet, held = lax.optimization_barrier((packet, library))
+    pair_lib = swap(held, "blk", core)
+    pair_values = swap(assays, "blk", core).astype(jnp.float32)
     libs = [jnp.pad(lib, ((0, 0), (0, lanes))) for lib in (library, pair_lib)]
     lib_sqs = [jnp.sum(jnp.square(lib.astype(jnp.float32)), axis=1) for lib in (library, pair_lib)]
     got, parts = gather_rounds(

time: 38.4 us -> 38.3 us (level)
  waiting for transfers between devices: 11.6 us -> 12.4 us
  other arithmetic: 7.39 us -> 6.69 us
    ppermute x12, waiting for transfers between devices: 11.6 us -> 12.4 us  [swap(): return lax.ppermute(x, axis, [(i, i ^ mask) for i in range(count)])]
    broadcast_in_dim x1 -> x0, other arithmetic: 0.85 us -> none  [gather_rounds(): pieces = [packet[None]]]
    concatenate x0 -> x1, other arithmetic: none -> 0.85 us  [shards(): packet = jnp.concatenate([queries, coded], axis=1)]
    unnamed x2 -> x1, other arithmetic: 0.85 us -> 0.01 us
  transfers between devices with their start and end apart: 12 -> 12, of which waited for: 5 -> 5; matrix products, arithmetic and copies ran while one was open for 31% -> 24% of each run, Pallas kernels for 0% -> 0%
where the time goes in v22:
time: 38.3 us; the launch traced here: 38.2 us
  starting transfers between devices  13.2 us (34%)
  waiting for transfers between devices  12.4 us (32%)
  other arithmetic  6.69 us (17%)
  matrix products  5.37 us (14%)
    ppermute x12, starting transfers between devices, swap(): return lax.ppermute(x, axis, [(i, i ^ mask) for i in range(count)])  13.2 us
    ppermute x12, waiting for transfers between devices, swap(): return lax.ppermute(x, axis, [(i, i ^ mask) for i in range(count)])  12.4 us
    dot_general x4, matrix products, piece_weights(): lax.dot_general(rows, lib_ext, (((1,), (1,)), ((), ())), preferred_elemen...  4.87 us
    reduce_sum x2, other arithmetic, shards(): jnp.sum(jnp.square(lib.astype(jnp.float32)), axis=1)  3.25 us
    reduce_sum x1, other arithmetic, shards(): jnp.sum(values, axis=0)  1.29 us
    concatenate x1, other arithmetic, shards(): packet = jnp.concatenate([queries, coded], axis=1)  0.85 us
  transfers between devices with their start and end apart: 12, of which 5 were waited for; matrix products, arithmetic and copies ran while one was open for 24% of the time, Pallas kernels for 0%

profile of v22, /device:TPU:0, one launch (start us, length us, event | category | flops | bytes accessed | tf_op | source)
XLA Modules:
  0.0 38.2 jit_solution(12916581725563384800)
XLA Ops:
  0.0 0.0 copy-start.1
  0.0 0.0 copy-start
  0.0 1.3 %convert_reduce_fusion = (f32[256]{0:T(256)S(1)}, f32[256]{0:T(256)S(1)}) fusion(bf16[768,256]{1,0:T(8,128)(2,1)} %param.5), kind=kLoop, calls=%fused_computation.12 | loop fusion | flops 785920 | bytes 395264 | tf_op jit(solution)/shard_map/reduce_sum | solution.py:112
  1.3 0.8 %pad_maximum_fusion.4 = bf16[16,2176]{1,0:T(8,128)(2,1)S(1)} fusion(bf16[16,128]{1,0:T(8,128)(2,1)S(1)} %fusion.77, bf16[16,2048]{1,0:T(8,128)(2,1)} %param.3), kind=kLoop, calls=%fused_computation.52 | loop fusion | flops 139264 | bytes 139264 | tf_op jit(solution)/shard_map/concatenate | solution.py:118
  2.2 0.5 %collective-permute-start.5 = (bf16[768,2048]{1,0:T(8,128)(2,1)}, bf16[768,2048]{1,0:T(8,128)(2,1)S(1)}, u32[]{:S(2)}, u32[]{:S(2)}) collective-permute-start(bf16[768,2048]{1,0:T(8,128)(2,1)} %param.4), channel_id=1, source_target_pairs={{0,1},{1,0},{2,3},{3,2},{4,5},{5,4},{6,7},{7,6},{8,9},{9,8},{10,11... | collective-permute-start | bytes 9437192 | tf_op jit(solution)/shard_map/ppermute | solution.py:41
  2.7 2.6 %collective-permute-start = (bf16[1,16,2176]{2,1,0:T(8,128)(2,1)S(1)}, bf16[1,16,2176]{2,1,0:T(8,128)(2,1)S(1)}, u32[]{:S(2)}, u32[]{:S(2)}) collective-permute-start(bf16[1,16,2176]{2,1,0:T(8,128)(2,1)S(1)} %bitcast.48), channel_id=1, source_target_pairs={{0,2},{1,3},{2,0},{3,1},{4,6},{5,7},{6,4},{7,5},{8,10},{9,11},{10,... | collective-permute-start | bytes 208904 | tf_op jit(solution)/shard_map/ppermute | solution.py:41
  5.2 3.6 %collective-permute-start.3 = (bf16[1,16,2176]{2,1,0:T(8,128)(2,1)S(1)}, bf16[1,16,2176]{2,1,0:T(8,128)(2,1)S(1)}, u32[]{:S(2)}, u32[]{:S(2)}) collective-permute-start(bf16[1,16,2176]{2,1,0:T(8,128)(2,1)S(1)} %bitcast.49), channel_id=1, source_target_pairs={{0,12},{1,13},{2,14},{3,15},{4,8},{5,9},{6,10},{7,11},{8,4},{9,5},... | collective-permute-start | bytes 208904 | tf_op jit(solution)/shard_map/ppermute | solution.py:41
  8.8 0.0 collective-permute-start.2
  8.8 0.8 %collective-permute-start.1 = (bf16[1,16,2176]{2,1,0:T(8,128)(2,1)S(1)}, bf16[1,16,2176]{2,1,0:T(8,128)(2,1)S(1)}, u32[]{:S(2)}, u32[]{:S(2)}) collective-permute-start(bf16[1,16,2176]{2,1,0:T(8,128)(2,1)S(1)} %bitcast.51), channel_id=1, source_target_pairs={{0,4},{1,5},{2,6},{3,7},{4,0},{5,1},{6,2},{7,3},{8,12},{9,13},{10,... | collective-permute-start | bytes 208904 | tf_op jit(solution)/shard_map/ppermute | solution.py:41
  9.6 2.6 %multiply_reduce_fusion.1 = f32[768]{0:T(1024)S(1)} fusion(bf16[768,2048]{1,0:T(8,128)(2,1)} %param.4), kind=kLoop, calls=%fused_computation.1 | loop fusion | flops 4717824 | bytes 3148800 | tf_op jit(solution)/shard_map/reduce_sum | solution.py:123
  12.2 0.0 collective-permute-done.3
  12.2 0.0 copy-done.1
  12.2 0.1 collective-permute-start.7
  12.3 2.7 %collective-permute-done.2 = bf16[1,16,2176]{2,1,0:T(8,128)(2,1)S(1)} collective-permute-done((bf16[1,16,2176]{2,1,0:T(8,128)(2,1)S(1)}, bf16[1,16,2176]{2,1,0:T(8,128)(2,1)S(1)}, u32[]{:S(2)}, u32[]{:S(2)}) %collective-permute-start.2) | collective-permute-done | bytes 69664 | tf_op jit(solution)/shard_map/ppermute | solution.py:41
  15.0 0.0 collective-permute-done.1
  15.1 0.6 %collective-permute-start.4 = (bf16[3,16,2176]{2,1,0:T(8,128)(2,1)S(1)}, bf16[3,16,2176]{2,1,0:T(8,128)(2,1)S(1)}, u32[]{:S(2)}, u32[]{:S(2)}) collective-permute-start(bf16[3,16,2176]{2,1,0:T(8,128)(2,1)S(1)} %pad_maximum_fusion.2), channel_id=1, source_target_pairs={{0,2},{1,3},{2,0},{3,1},{4,6},{5,7},{6,4},{7,5},{8,10},{9,11},{10,... | collective-permute-start | bytes 626696 | tf_op jit(solution)/shard_map/ppermute | solution.py:41
  15.7 0.2 multiply_reduce_fusion.3
  15.9 0.0 copy-done
  15.9 1.2 %fusion.88 = (f32[64]{0:T(128)S(1)}, bf16[64,768]{1,0:T(8,128)(2,1)S(1)}) fusion(f32[768]{0:T(1024)S(1)} %multiply_reduce_fusion.1, f32[64]{0:T(128)S(1)} %multiply_reduce_fusion.3, bf16[64,2176]{1,0:T(8,128)(2,1)S(1)} %bitcast.43, bf16[768,2048]{1,0:T(8,128)(2,1)S(1)} %copy-done), kind=kOutput, calls=%fused_computation.101 | convolution fusion | flops 214253504 | bytes 3526144 | tf_op jit(solution)/shard_map/dot_general | solution.py:29
  17.1 0.0 collective-permute-done.5
  17.1 0.7 %multiply_reduce_fusion = f32[768]{0:T(1024)S(1)} fusion(bf16[768,2048]{1,0:T(8,128)(2,1)S(1)} %collective-permute-done.5), kind=kLoop, calls=%fused_computation | loop fusion | flops 4717824 | bytes 3148800 | tf_op jit(solution)/shard_map/reduce_sum | solution.py:123
  17.8 1.2 %fusion.87 = (f32[64]{0:T(128)S(1)}, bf16[64,768]{1,0:T(8,128)(2,1)S(1)}) fusion(f32[768]{0:T(1024)S(1)} %multiply_reduce_fusion, f32[64]{0:T(128)S(1)} %multiply_reduce_fusion.3, bf16[64,2176]{1,0:T(8,128)(2,1)S(1)} %bitcast.44, bf16[768,2048]{1,0:T(8,128)(2,1)S(1)} %collective-permute-done.5), kind=kOutput, calls=%fused_computation.100 | convolution fusion | flops 214253504 | bytes 3526144 | tf_op jit(solution)/shard_map/dot_general | solution.py:29
  19.0 0.0 collective-permute-done
  19.0 2.7 %collective-permute-done.4 = bf16[3,16,2176]{2,1,0:T(8,128)(2,1)S(1)} collective-permute-done((bf16[3,16,2176]{2,1,0:T(8,128)(2,1)S(1)}, bf16[3,16,2176]{2,1,0:T(8,128)(2,1)S(1)}, u32[]{:S(2)}, u32[]{:S(2)}) %collective-permute-start.4) | collective-permute-done | bytes 208928 | tf_op jit(solution)/shard_map/ppermute | solution.py:41
  21.8 0.2 multiply_reduce_fusion.2
  21.9 1.2 %fusion.86 = (bf16[64,768]{1,0:T(8,128)(2,1)S(1)}, f32[64]{0:T(128)S(1)}) fusion(f32[768]{0:T(1024)S(1)} %multiply_reduce_fusion.1, f32[64]{0:T(128)S(1)} %multiply_reduce_fusion.2, bf16[64,2176]{1,0:T(8,128)(2,1)S(1)} %bitcast.40, bf16[768,2048]{1,0:T(8,128)(2,1)S(1)} %copy-done), kind=kOutput, calls=%fused_computation.99 | convolution fusion | flops 214253504 | bytes 3526144 | tf_op jit(solution)/shard_map/dot_general | solution.py:29
  23.3 0.1 collective-permute-start.6
  23.3 1.2 %fusion.85 = (bf16[64,768]{1,0:T(8,128)(2,1)S(1)}, f32[64]{0:T(128)S(1)}) fusion(f32[768]{0:T(1024)S(1)} %multiply_reduce_fusion, f32[64]{0:T(128)S(1)} %multiply_reduce_fusion.2, bf16[64,2176]{1,0:T(8,128)(2,1)S(1)} %bitcast.41, bf16[768,2048]{1,0:T(8,128)(2,1)S(1)} %collective-permute-done.5), kind=kOutput, calls=%fused_computation.98 | convolution fusion | flops 214253504 | bytes 3526144 | tf_op jit(solution)/shard_map/dot_general | solution.py:29
  24.6 0.1 pad_maximum_fusion.6
  24.7 0.0 collective-permute-done.6
  24.7 0.3 fusion.11
  24.9 0.0 collective-permute-done.7
  25.0 0.2 convolution_add_fusion
  25.2 0.1 broadcast_in_dim.5
  25.4 2.3 %collective-permute-start.10 = (f32[2,16,384]{2,1,0:T(8,128)S(1)}, f32[2,16,384]{2,1,0:T(8,128)S(1)}, u32[]{:S(2)}, u32[]{:S(2)}) collective-permute-start(f32[2,16,384]{2,1,0:T(8,128)S(1)} %get-tuple-element.22), channel_id=1, source_target_pairs={{0,12},{1,13},{2,14},{3,15},{4,8},{5,9},{6,10},{7,11},{8,4},{9,5},... | collective-permute-start | bytes 147464 | tf_op jit(solution)/shard_map/ppermute | solution.py:41
  27.7 0.0 collective-permute-start.9
  27.7 2.1 %collective-permute-start.8 = (f32[2,16,384]{2,1,0:T(8,128)S(1)}, f32[2,16,384]{2,1,0:T(8,128)S(1)}, u32[]{:S(2)}, u32[]{:S(2)}) collective-permute-start(f32[2,16,384]{2,1,0:T(8,128)S(1)} %get-tuple-element.21), channel_id=1, source_target_pairs={{0,4},{1,5},{2,6},{3,7},{4,0},{5,1},{6,2},{7,3},{8,12},{9,13},{10,... | collective-permute-start | bytes 147464 | tf_op jit(solution)/shard_map/ppermute | solution.py:41
  29.8 2.1 %collective-permute-done.10 = f32[2,16,384]{2,1,0:T(8,128)S(1)} collective-permute-done((f32[2,16,384]{2,1,0:T(8,128)S(1)}, f32[2,16,384]{2,1,0:T(8,128)S(1)}, u32[]{:S(2)}, u32[]{:S(2)}) %collective-permute-start.10) | collective-permute-done | bytes 49184 | tf_op jit(solution)/shard_map/ppermute | solution.py:41
  31.9 1.6 %collective-permute-done.9 = f32[2,16,384]{2,1,0:T(8,128)S(1)} collective-permute-done((f32[2,16,384]{2,1,0:T(8,128)S(1)}, f32[2,16,384]{2,1,0:T(8,128)S(1)}, u32[]{:S(2)}, u32[]{:S(2)}) %collective-permute-start.9) | collective-permute-done | bytes 49184 | tf_op jit(solution)/shard_map/ppermute | solution.py:41
  33.5 0.0 collective-permute-done.8
  33.5 0.6 %collective-permute-start.11 = (f32[16,384]{1,0:T(8,128)S(1)}, f32[16,384]{1,0:T(8,128)S(1)}, u32[]{:S(2)}, u32[]{:S(2)}) collective-permute-start(f32[16,384]{1,0:T(8,128)S(1)} %slice_bitcast_fusion.4), channel_id=1, source_target_pairs={{0,2},{1,3},{2,0},{3,1},{4,6},{5,7},{6,4},{7,5},{8,10},{9,11},{10,... | collective-permute-start | bytes 73736 | tf_op jit(solution)/shard_map/ppermute | solution.py:41
  34.1 3.3 %collective-permute-done.11 = f32[16,384]{1,0:T(8,128)S(1)} collective-permute-done((f32[16,384]{1,0:T(8,128)S(1)}, f32[16,384]{1,0:T(8,128)S(1)}, u32[]{:S(2)}, u32[]{:S(2)}) %collective-permute-start.11) | collective-permute-done | bytes 24608 | tf_op jit(solution)/shard_map/ppermute | solution.py:41
  37.4 0.1 slice_reduce_fusion
  37.5 0.7 %slice_divide_fusion = f32[16,256]{1,0:T(8,128)} fusion(f32[16,384]{1,0:T(8,128)S(1)} %fusion.70, f32[16]{0:T(128)S(1)} %slice_reduce_fusion), kind=kLoop, calls=%fused_computation.65 | loop fusion | flops 4096 | bytes 32832 | tf_op jit(solution)/shard_map/div | solution.py:148
  (24 shorter events, 0.4 us)
Async XLA Ops:
  0.0 12.2 %copy-start.1 = (bf16[768,256]{1,0:T(8,128)(2,1)S(1)}, bf16[768,256]{1,0:T(8,128)(2,1)}, u32[]{:S(2)}) copy-start(bf16[768,256]{1,0:T(8,128)(2,1)} %param.5) | copy-start | bytes 1179652
  0.0 15.8 %copy-start = (bf16[768,2048]{1,0:T(8,128)(2,1)S(1)}, bf16[768,2048]{1,0:T(8,128)(2,1)}, u32[]{:S(2)}) copy-start(bf16[768,2048]{1,0:T(8,128)(2,1)} %param.4) | copy-start | bytes 9437188
  2.2 14.9 %collective-permute-start.5 = (bf16[768,2048]{1,0:T(8,128)(2,1)}, bf16[768,2048]{1,0:T(8,128)(2,1)S(1)}, u32[]{:S(2)}, u32[]{:S(2)}) collective-permute-start(bf16[768,2048]{1,0:T(8,128)(2,1)} %param.4), channel_id=1, source_target_pairs={{0,1},{1,0},{2,3},{3,2},{4,5},{5,4},{6,7},{7,6},{8,9},{9,8},{10,11... | collective-permute-start | bytes 9437192 | tf_op jit(solution)/shard_map/ppermute | solution.py:41
  2.7 16.4 %collective-permute-start = (bf16[1,16,2176]{2,1,0:T(8,128)(2,1)S(1)}, bf16[1,16,2176]{2,1,0:T(8,128)(2,1)S(1)}, u32[]{:S(2)}, u32[]{:S(2)}) collective-permute-start(bf16[1,16,2176]{2,1,0:T(8,128)(2,1)S(1)} %bitcast.48), channel_id=1, source_target_pairs={{0,2},{1,3},{2,0},{3,1},{4,6},{5,7},{6,4},{7,5},{8,10},{9,11},{10,... | collective-permute-start | bytes 208904 | tf_op jit(solution)/shard_map/ppermute | solution.py:41
  5.2 7.0 %collective-permute-start.3 = (bf16[1,16,2176]{2,1,0:T(8,128)(2,1)S(1)}, bf16[1,16,2176]{2,1,0:T(8,128)(2,1)S(1)}, u32[]{:S(2)}, u32[]{:S(2)}) collective-permute-start(bf16[1,16,2176]{2,1,0:T(8,128)(2,1)S(1)} %bitcast.49), channel_id=1, source_target_pairs={{0,12},{1,13},{2,14},{3,15},{4,8},{5,9},{6,10},{7,11},{8,4},{9,5},... | collective-permute-start | bytes 208904 | tf_op jit(solution)/shard_map/ppermute | solution.py:41
  8.8 6.2 %collective-permute-start.2 = (bf16[1,16,2176]{2,1,0:T(8,128)(2,1)S(1)}, bf16[1,16,2176]{2,1,0:T(8,128)(2,1)S(1)}, u32[]{:S(2)}, u32[]{:S(2)}) collective-permute-start(bf16[1,16,2176]{2,1,0:T(8,128)(2,1)S(1)} %bitcast.50), channel_id=1, source_target_pairs={{0,8},{1,9},{2,10},{3,11},{4,12},{5,13},{6,14},{7,15},{8,0},{9,1},... | collective-permute-start | bytes 208904 | tf_op jit(solution)/shard_map/ppermute | solution.py:41
  8.8 6.2 %collective-permute-start.1 = (bf16[1,16,2176]{2,1,0:T(8,128)(2,1)S(1)}, bf16[1,16,2176]{2,1,0:T(8,128)(2,1)S(1)}, u32[]{:S(2)}, u32[]{:S(2)}) collective-permute-start(bf16[1,16,2176]{2,1,0:T(8,128)(2,1)S(1)} %bitcast.51), channel_id=1, source_target_pairs={{0,4},{1,5},{2,6},{3,7},{4,0},{5,1},{6,2},{7,3},{8,12},{9,13},{10,... | collective-permute-start | bytes 208904 | tf_op jit(solution)/shard_map/ppermute | solution.py:41
  12.2 12.7 %collective-permute-start.7 = (bf16[768,256]{1,0:T(8,128)(2,1)S(1)}, bf16[768,256]{1,0:T(8,128)(2,1)S(1)}, u32[]{:S(2)}, u32[]{:S(2)}) collective-permute-start(bf16[768,256]{1,0:T(8,128)(2,1)S(1)} %copy-done.1), channel_id=1, source_target_pairs={{0,1},{1,0},{2,3},{3,2},{4,5},{5,4},{6,7},{7,6},{8,9},{9,8},{10,11... | collective-permute-start | bytes 1179656 | tf_op jit(solution)/shard_map/ppermute | solution.py:41
  15.1 6.7 %collective-permute-start.4 = (bf16[3,16,2176]{2,1,0:T(8,128)(2,1)S(1)}, bf16[3,16,2176]{2,1,0:T(8,128)(2,1)S(1)}, u32[]{:S(2)}, u32[]{:S(2)}) collective-permute-start(bf16[3,16,2176]{2,1,0:T(8,128)(2,1)S(1)} %pad_maximum_fusion.2), channel_id=1, source_target_pairs={{0,2},{1,3},{2,0},{3,1},{4,6},{5,7},{6,4},{7,5},{8,10},{9,11},{10,... | collective-permute-start | bytes 626696 | tf_op jit(solution)/shard_map/ppermute | solution.py:41
  23.3 1.4 %collective-permute-start.6 = (f32[512]{0:T(512)S(1)}, f32[512]{0:T(512)S(1)}, u32[]{:S(2)}, u32[]{:S(2)}) collective-permute-start(f32[512]{0:T(512)S(1)} %fusion.71), channel_id=1, source_target_pairs={{0,1},{1,0},{2,3},{3,2},{4,5},{5,4},{6,7},{7,6},{8,9},{9,8},{10,11... | collective-permute-start | bytes 6152 | tf_op jit(solution)/shard_map/ppermute | solution.py:41
  25.4 6.5 %collective-permute-start.10 = (f32[2,16,384]{2,1,0:T(8,128)S(1)}, f32[2,16,384]{2,1,0:T(8,128)S(1)}, u32[]{:S(2)}, u32[]{:S(2)}) collective-permute-start(f32[2,16,384]{2,1,0:T(8,128)S(1)} %get-tuple-element.22), channel_id=1, source_target_pairs={{0,12},{1,13},{2,14},{3,15},{4,8},{5,9},{6,10},{7,11},{8,4},{9,5},... | collective-permute-start | bytes 147464 | tf_op jit(solution)/shard_map/ppermute | solution.py:41
  27.7 5.8 %collective-permute-start.9 = (f32[2,16,384]{2,1,0:T(8,128)S(1)}, f32[2,16,384]{2,1,0:T(8,128)S(1)}, u32[]{:S(2)}, u32[]{:S(2)}) collective-permute-start(f32[2,16,384]{2,1,0:T(8,128)S(1)} %get-tuple-element.23), channel_id=1, source_target_pairs={{0,8},{1,9},{2,10},{3,11},{4,12},{5,13},{6,14},{7,15},{8,0},{9,1},... | collective-permute-start | bytes 147464 | tf_op jit(solution)/shard_map/ppermute | solution.py:41
  27.7 5.8 %collective-permute-start.8 = (f32[2,16,384]{2,1,0:T(8,128)S(1)}, f32[2,16,384]{2,1,0:T(8,128)S(1)}, u32[]{:S(2)}, u32[]{:S(2)}) collective-permute-start(f32[2,16,384]{2,1,0:T(8,128)S(1)} %get-tuple-element.21), channel_id=1, source_target_pairs={{0,4},{1,5},{2,6},{3,7},{4,0},{5,1},{6,2},{7,3},{8,12},{9,13},{10,... | collective-permute-start | bytes 147464 | tf_op jit(solution)/shard_map/ppermute | solution.py:41
  33.5 3.9 %collective-permute-start.11 = (f32[16,384]{1,0:T(8,128)S(1)}, f32[16,384]{1,0:T(8,128)S(1)}, u32[]{:S(2)}, u32[]{:S(2)}) collective-permute-start(f32[16,384]{1,0:T(8,128)S(1)} %slice_bitcast_fusion.4), channel_id=1, source_target_pairs={{0,2},{1,3},{2,0},{3,1},{4,6},{5,7},{6,4},{7,5},{8,10},{9,11},{10,... | collective-permute-start | bytes 73736 | tf_op jit(solution)/shard_map/ppermute | solution.py:41

commit v23 on v21

--- a/solution.py
+++ b/solution.py
@@ -144,7 +144,9 @@
     sums = sums.reshape(tuple(len(offsets(g)) for g in groups) + sums.shape[1:])
     order = list(range(1, len(groups))) + [0]
     sums = jnp.transpose(sums, order + list(range(len(groups), sums.ndim)))
-    mine = scatter_rounds(sums, "blk", [groups[k] for k in order])
+    bits = [bit for k in order for bit in reversed(groups[k])]
+    sums = sums.reshape((2,) * len(bits) + sums.shape[len(groups):])
+    mine = scatter_rounds(sums, "blk", [[bit] for bit in bits])
     return mine[:, :width] / mine[:, width:width + 1]
 
 

time: 38.4 us -> 42.6 us (1.11)
  waiting for transfers between devices: 11.6 us -> 18.9 us
  starting transfers between devices: 13.3 us -> 10.2 us
    ppermute x12 -> x11, waiting for transfers between devices: 11.6 us -> 18.9 us  [swap(): return lax.ppermute(x, axis, [(i, i ^ mask) for i in range(count)])]
    ppermute x12 -> x11, starting transfers between devices: 13.3 us -> 10.2 us  [swap(): return lax.ppermute(x, axis, [(i, i ^ mask) for i in range(count)])]
  transfers between devices with their start and end apart: 12 -> 11, of which waited for: 5 -> 5; matrix products, arithmetic and copies ran while one was open for 31% -> 28% of each run, Pallas kernels for 0% -> 0%
where the time goes in v23:
time: 42.6 us; the launch traced here: 42.4 us
  waiting for transfers between devices  18.9 us (44%)
  starting transfers between devices  10.2 us (24%)
  other arithmetic  7.39 us (17%)
  matrix products  5.37 us (13%)
    ppermute x11, waiting for transfers between devices, swap(): return lax.ppermute(x, axis, [(i, i ^ mask) for i in range(count)])  18.9 us
    ppermute x11, starting transfers between devices, swap(): return lax.ppermute(x, axis, [(i, i ^ mask) for i in range(count)])  10.2 us
    dot_general x4, matrix products, piece_weights(): lax.dot_general(rows, lib_ext, (((1,), (1,)), ((), ())), preferred_elemen...  4.87 us
    reduce_sum x2, other arithmetic, shards(): jnp.sum(jnp.square(lib.astype(jnp.float32)), axis=1)  3.25 us
    reduce_sum x1, other arithmetic, shards(): jnp.sum(values, axis=0)  1.14 us
  transfers between devices with their start and end apart: 11, of which 5 were waited for; matrix products, arithmetic and copies ran while one was open for 28% of the time, Pallas kernels for 0%

profile of v23, /device:TPU:0, one launch (start us, length us, event | category | flops | bytes accessed | tf_op | source)
XLA Modules:
  0.0 42.4 jit_solution(15285505408547756222)
XLA Ops:
  0.0 0.0 copy-start
  0.0 0.0 copy-start.1
  0.0 0.5 %collective-permute-start.5 = (bf16[768,2048]{1,0:T(8,128)(2,1)}, bf16[768,2048]{1,0:T(8,128)(2,1)S(1)}, u32[]{:S(2)}, u32[]{:S(2)}) collective-permute-start(bf16[768,2048]{1,0:T(8,128)(2,1)} %param.4), channel_id=1, source_target_pairs={{0,1},{1,0},{2,3},{3,2},{4,5},{5,4},{6,7},{7,6},{8,9},{9,8},{10,11... | collective-permute-start | bytes 9437192 | tf_op jit(solution)/shard_map/ppermute | solution.py:41
  0.5 1.1 %convert_reduce_fusion = (f32[256]{0:T(256)S(1)}, f32[256]{0:T(256)S(1)}) fusion(bf16[768,256]{1,0:T(8,128)(2,1)} %param.5), kind=kLoop, calls=%fused_computation.12 | loop fusion | flops 785920 | bytes 395264 | tf_op jit(solution)/shard_map/reduce_sum | solution.py:112
  1.7 0.8 %maximum_bitcast_fusion = bf16[1,16,2176]{2,1,0:T(8,128)(2,1)S(1)} fusion(bf16[16,128]{1,0:T(8,128)(2,1)S(1)} %fusion.75, bf16[16,2048]{1,0:T(8,128)(2,1)} %param.3), kind=kLoop, calls=%fused_computation.53 | loop fusion | flops 139264 | bytes 139264 | tf_op jit(solution)/shard_map/broadcast_in_dim | solution.py:70
  2.5 2.7 %collective-permute-start = (bf16[1,16,2176]{2,1,0:T(8,128)(2,1)S(1)}, bf16[1,16,2176]{2,1,0:T(8,128)(2,1)S(1)}, u32[]{:S(2)}, u32[]{:S(2)}) collective-permute-start(bf16[1,16,2176]{2,1,0:T(8,128)(2,1)S(1)} %maximum_bitcast_fusion), channel_id=1, source_target_pairs={{0,2},{1,3},{2,0},{3,1},{4,6},{5,7},{6,4},{7,5},{8,10},{9,11},{10,... | collective-permute-start | bytes 208904 | tf_op jit(solution)/shard_map/ppermute | solution.py:41
  5.2 3.6 %collective-permute-start.3 = (bf16[1,16,2176]{2,1,0:T(8,128)(2,1)S(1)}, bf16[1,16,2176]{2,1,0:T(8,128)(2,1)S(1)}, u32[]{:S(2)}, u32[]{:S(2)}) collective-permute-start(bf16[1,16,2176]{2,1,0:T(8,128)(2,1)S(1)} %maximum_bitcast_fusion), channel_id=1, source_target_pairs={{0,12},{1,13},{2,14},{3,15},{4,8},{5,9},{6,10},{7,11},{8,4},{9,5},... | collective-permute-start | bytes 208904 | tf_op jit(solution)/shard_map/ppermute | solution.py:41
  8.8 0.0 collective-permute-start.2
  8.8 0.8 %collective-permute-start.1 = (bf16[1,16,2176]{2,1,0:T(8,128)(2,1)S(1)}, bf16[1,16,2176]{2,1,0:T(8,128)(2,1)S(1)}, u32[]{:S(2)}, u32[]{:S(2)}) collective-permute-start(bf16[1,16,2176]{2,1,0:T(8,128)(2,1)S(1)} %maximum_bitcast_fusion), channel_id=1, source_target_pairs={{0,4},{1,5},{2,6},{3,7},{4,0},{5,1},{6,2},{7,3},{8,12},{9,13},{10,... | collective-permute-start | bytes 208904 | tf_op jit(solution)/shard_map/ppermute | solution.py:41
  9.6 0.8 %constant_dynamic-update-slice_fusion.5 = bf16[8,16,2176]{2,1,0:T(8,128)(2,1)S(1)} fusion(bf16[16,128]{1,0:T(8,128)(2,1)S(1)} %fusion.75, bf16[16,2048]{1,0:T(8,128)(2,1)} %param.3), kind=kLoop, calls=%fused_computation.71 | loop fusion | flops 139263 | bytes 139264
  10.4 2.6 %multiply_reduce_fusion.1 = f32[768]{0:T(1024)S(1)} fusion(bf16[768,2048]{1,0:T(8,128)(2,1)} %param.4), kind=kLoop, calls=%fused_computation.1 | loop fusion | flops 4717824 | bytes 3148800 | tf_op jit(solution)/shard_map/reduce_sum | solution.py:123
  13.0 0.0 collective-permute-done.3
  13.0 0.0 copy-done.1
  13.0 0.1 collective-permute-start.7
  13.1 1.9 %collective-permute-done.2 = bf16[1,16,2176]{2,1,0:T(8,128)(2,1)S(1)} collective-permute-done((bf16[1,16,2176]{2,1,0:T(8,128)(2,1)S(1)}, bf16[1,16,2176]{2,1,0:T(8,128)(2,1)S(1)}, u32[]{:S(2)}, u32[]{:S(2)}) %collective-permute-start.2) | collective-permute-done | bytes 69664 | tf_op jit(solution)/shard_map/ppermute | solution.py:41
  15.0 0.0 collective-permute-done.1
  15.0 0.6 %collective-permute-start.4 = (bf16[3,16,2176]{2,1,0:T(8,128)(2,1)S(1)}, bf16[3,16,2176]{2,1,0:T(8,128)(2,1)S(1)}, u32[]{:S(2)}, u32[]{:S(2)}) collective-permute-start(bf16[3,16,2176]{2,1,0:T(8,128)(2,1)S(1)} %pad_maximum_fusion.2), channel_id=1, source_target_pairs={{0,2},{1,3},{2,0},{3,1},{4,6},{5,7},{6,4},{7,5},{8,10},{9,11},{10,... | collective-permute-start | bytes 626696 | tf_op jit(solution)/shard_map/ppermute | solution.py:41
  15.6 0.2 multiply_reduce_fusion.3
  15.8 0.0 copy-done
  15.8 1.2 %fusion.86 = (f32[64]{0:T(128)S(1)}, bf16[64,768]{1,0:T(8,128)(2,1)S(1)}) fusion(f32[768]{0:T(1024)S(1)} %multiply_reduce_fusion.1, f32[64]{0:T(128)S(1)} %multiply_reduce_fusion.3, bf16[64,2176]{1,0:T(8,128)(2,1)S(1)} %bitcast.37, bf16[768,2048]{1,0:T(8,128)(2,1)S(1)} %copy-done), kind=kOutput, calls=%fused_computation.98 | convolution fusion | flops 214253504 | bytes 3526144 | tf_op jit(solution)/shard_map/dot_general | solution.py:29
  17.1 0.0 collective-permute-done.5
  17.1 0.7 %multiply_reduce_fusion = f32[768]{0:T(1024)S(1)} fusion(bf16[768,2048]{1,0:T(8,128)(2,1)S(1)} %collective-permute-done.5), kind=kLoop, calls=%fused_computation | loop fusion | flops 4717824 | bytes 3148800 | tf_op jit(solution)/shard_map/reduce_sum | solution.py:123
  17.8 1.2 %fusion.85 = (f32[64]{0:T(128)S(1)}, bf16[64,768]{1,0:T(8,128)(2,1)S(1)}) fusion(f32[768]{0:T(1024)S(1)} %multiply_reduce_fusion, f32[64]{0:T(128)S(1)} %multiply_reduce_fusion.3, bf16[64,2176]{1,0:T(8,128)(2,1)S(1)} %bitcast.38, bf16[768,2048]{1,0:T(8,128)(2,1)S(1)} %collective-permute-done.5), kind=kOutput, calls=%fused_computation.97 | convolution fusion | flops 214253504 | bytes 3526144 | tf_op jit(solution)/shard_map/dot_general | solution.py:29
  19.0 0.0 collective-permute-done
  19.0 2.7 %collective-permute-done.4 = bf16[3,16,2176]{2,1,0:T(8,128)(2,1)S(1)} collective-permute-done((bf16[3,16,2176]{2,1,0:T(8,128)(2,1)S(1)}, bf16[3,16,2176]{2,1,0:T(8,128)(2,1)S(1)}, u32[]{:S(2)}, u32[]{:S(2)}) %collective-permute-start.4) | collective-permute-done | bytes 208928 | tf_op jit(solution)/shard_map/ppermute | solution.py:41
  21.7 0.2 multiply_reduce_fusion.2
  21.8 1.2 %fusion.84 = (bf16[64,768]{1,0:T(8,128)(2,1)S(1)}, f32[64]{0:T(128)S(1)}) fusion(f32[768]{0:T(1024)S(1)} %multiply_reduce_fusion.1, f32[64]{0:T(128)S(1)} %multiply_reduce_fusion.2, bf16[64,2176]{1,0:T(8,128)(2,1)S(1)} %bitcast.34, bf16[768,2048]{1,0:T(8,128)(2,1)S(1)} %copy-done), kind=kOutput, calls=%fused_computation.96 | convolution fusion | flops 214253504 | bytes 3526144 | tf_op jit(solution)/shard_map/dot_general | solution.py:29
  23.2 0.1 collective-permute-start.6
  23.3 1.2 %fusion.83 = (bf16[64,768]{1,0:T(8,128)(2,1)S(1)}, f32[64]{0:T(128)S(1)}) fusion(f32[768]{0:T(1024)S(1)} %multiply_reduce_fusion, f32[64]{0:T(128)S(1)} %multiply_reduce_fusion.2, bf16[64,2176]{1,0:T(8,128)(2,1)S(1)} %bitcast.35, bf16[768,2048]{1,0:T(8,128)(2,1)S(1)} %collective-permute-done.5), kind=kOutput, calls=%fused_computation.95 | convolution fusion | flops 214253504 | bytes 3526144 | tf_op jit(solution)/shard_map/dot_general | solution.py:29
  24.5 0.1 pad_maximum_fusion.5
  24.6 0.0 collective-permute-done.6
  24.6 0.3 fusion.11
  24.8 0.0 collective-permute-done.7
  24.9 0.2 convolution_add_fusion
  25.1 0.1 broadcast_in_dim.5
  25.3 1.3 %collective-permute-start.8 = (f32[2,2,16,384]{3,2,1,0:T(8,128)S(1)}, f32[2,2,16,384]{3,2,1,0:T(8,128)S(1)}, u32[]{:S(2)}, u32[]{:S(2)}) collective-permute-start(f32[2,2,16,384]{3,2,1,0:T(8,128)S(1)} %slice.73), channel_id=1, source_target_pairs={{0,8},{1,9},{2,10},{3,11},{4,12},{5,13},{6,14},{7,15},{8,0},{9,1},... | collective-permute-start | bytes 294920 | tf_op jit(solution)/shard_map/ppermute | solution.py:41
  26.6 6.9 %collective-permute-done.8 = f32[2,2,16,384]{3,2,1,0:T(8,128)S(1)} collective-permute-done((f32[2,2,16,384]{3,2,1,0:T(8,128)S(1)}, f32[2,2,16,384]{3,2,1,0:T(8,128)S(1)}, u32[]{:S(2)}, u32[]{:S(2)}) %collective-permute-start.8) | collective-permute-done | bytes 98336 | tf_op jit(solution)/shard_map/ppermute | solution.py:41
  33.5 0.1 collective-permute-start.9
  33.6 4.1 %collective-permute-done.9 = f32[2,16,384]{2,1,0:T(8,128)S(1)} collective-permute-done((f32[2,16,384]{2,1,0:T(8,128)S(1)}, f32[2,16,384]{2,1,0:T(8,128)S(1)}, u32[]{:S(2)}, u32[]{:S(2)}) %collective-permute-start.9) | collective-permute-done | bytes 49184 | tf_op jit(solution)/shard_map/ppermute | solution.py:41
  37.7 0.6 %collective-permute-start.10 = (f32[16,384]{1,0:T(8,128)S(1)}, f32[16,384]{1,0:T(8,128)S(1)}, u32[]{:S(2)}, u32[]{:S(2)}) collective-permute-start(f32[16,384]{1,0:T(8,128)S(1)} %slice_bitcast_fusion.2), channel_id=1, source_target_pairs={{0,2},{1,3},{2,0},{3,1},{4,6},{5,7},{6,4},{7,5},{8,10},{9,11},{10,... | collective-permute-start | bytes 73736 | tf_op jit(solution)/shard_map/ppermute | solution.py:41
  38.3 3.3 %collective-permute-done.10 = f32[16,384]{1,0:T(8,128)S(1)} collective-permute-done((f32[16,384]{1,0:T(8,128)S(1)}, f32[16,384]{1,0:T(8,128)S(1)}, u32[]{:S(2)}, u32[]{:S(2)}) %collective-permute-start.10) | collective-permute-done | bytes 24608 | tf_op jit(solution)/shard_map/ppermute | solution.py:41
  41.6 0.1 slice_reduce_fusion
  41.7 0.7 %slice_divide_fusion = f32[16,256]{1,0:T(8,128)} fusion(f32[16,384]{1,0:T(8,128)S(1)} %fusion.68, f32[16]{0:T(128)S(1)} %slice_reduce_fusion), kind=kLoop, calls=%fused_computation.62 | loop fusion | flops 4096 | bytes 32832 | tf_op jit(solution)/shard_map/div | solution.py:150
  (25 shorter events, 0.4 us)
Async XLA Ops:
  0.0 15.8 %copy-start = (bf16[768,2048]{1,0:T(8,128)(2,1)S(1)}, bf16[768,2048]{1,0:T(8,128)(2,1)}, u32[]{:S(2)}) copy-start(bf16[768,2048]{1,0:T(8,128)(2,1)} %param.4) | copy-start | bytes 9437188
  0.0 13.0 %copy-start.1 = (bf16[768,256]{1,0:T(8,128)(2,1)S(1)}, bf16[768,256]{1,0:T(8,128)(2,1)}, u32[]{:S(2)}) copy-start(bf16[768,256]{1,0:T(8,128)(2,1)} %param.5) | copy-start | bytes 1179652
  0.0 17.1 %collective-permute-start.5 = (bf16[768,2048]{1,0:T(8,128)(2,1)}, bf16[768,2048]{1,0:T(8,128)(2,1)S(1)}, u32[]{:S(2)}, u32[]{:S(2)}) collective-permute-start(bf16[768,2048]{1,0:T(8,128)(2,1)} %param.4), channel_id=1, source_target_pairs={{0,1},{1,0},{2,3},{3,2},{4,5},{5,4},{6,7},{7,6},{8,9},{9,8},{10,11... | collective-permute-start | bytes 9437192 | tf_op jit(solution)/shard_map/ppermute | solution.py:41
  2.5 16.5 %collective-permute-start = (bf16[1,16,2176]{2,1,0:T(8,128)(2,1)S(1)}, bf16[1,16,2176]{2,1,0:T(8,128)(2,1)S(1)}, u32[]{:S(2)}, u32[]{:S(2)}) collective-permute-start(bf16[1,16,2176]{2,1,0:T(8,128)(2,1)S(1)} %maximum_bitcast_fusion), channel_id=1, source_target_pairs={{0,2},{1,3},{2,0},{3,1},{4,6},{5,7},{6,4},{7,5},{8,10},{9,11},{10,... | collective-permute-start | bytes 208904 | tf_op jit(solution)/shard_map/ppermute | solution.py:41
  5.2 7.8 %collective-permute-start.3 = (bf16[1,16,2176]{2,1,0:T(8,128)(2,1)S(1)}, bf16[1,16,2176]{2,1,0:T(8,128)(2,1)S(1)}, u32[]{:S(2)}, u32[]{:S(2)}) collective-permute-start(bf16[1,16,2176]{2,1,0:T(8,128)(2,1)S(1)} %maximum_bitcast_fusion), channel_id=1, source_target_pairs={{0,12},{1,13},{2,14},{3,15},{4,8},{5,9},{6,10},{7,11},{8,4},{9,5},... | collective-permute-start | bytes 208904 | tf_op jit(solution)/shard_map/ppermute | solution.py:41
  8.8 6.2 %collective-permute-start.2 = (bf16[1,16,2176]{2,1,0:T(8,128)(2,1)S(1)}, bf16[1,16,2176]{2,1,0:T(8,128)(2,1)S(1)}, u32[]{:S(2)}, u32[]{:S(2)}) collective-permute-start(bf16[1,16,2176]{2,1,0:T(8,128)(2,1)S(1)} %maximum_bitcast_fusion), channel_id=1, source_target_pairs={{0,8},{1,9},{2,10},{3,11},{4,12},{5,13},{6,14},{7,15},{8,0},{9,1},... | collective-permute-start | bytes 208904 | tf_op jit(solution)/shard_map/ppermute | solution.py:41
  8.8 6.2 %collective-permute-start.1 = (bf16[1,16,2176]{2,1,0:T(8,128)(2,1)S(1)}, bf16[1,16,2176]{2,1,0:T(8,128)(2,1)S(1)}, u32[]{:S(2)}, u32[]{:S(2)}) collective-permute-start(bf16[1,16,2176]{2,1,0:T(8,128)(2,1)S(1)} %maximum_bitcast_fusion), channel_id=1, source_target_pairs={{0,4},{1,5},{2,6},{3,7},{4,0},{5,1},{6,2},{7,3},{8,12},{9,13},{10,... | collective-permute-start | bytes 208904 | tf_op jit(solution)/shard_map/ppermute | solution.py:41
  13.0 11.8 %collective-permute-start.7 = (bf16[768,256]{1,0:T(8,128)(2,1)S(1)}, bf16[768,256]{1,0:T(8,128)(2,1)S(1)}, u32[]{:S(2)}, u32[]{:S(2)}) collective-permute-start(bf16[768,256]{1,0:T(8,128)(2,1)S(1)} %copy-done.1), channel_id=1, source_target_pairs={{0,1},{1,0},{2,3},{3,2},{4,5},{5,4},{6,7},{7,6},{8,9},{9,8},{10,11... | collective-permute-start | bytes 1179656 | tf_op jit(solution)/shard_map/ppermute | solution.py:41
  15.0 6.6 %collective-permute-start.4 = (bf16[3,16,2176]{2,1,0:T(8,128)(2,1)S(1)}, bf16[3,16,2176]{2,1,0:T(8,128)(2,1)S(1)}, u32[]{:S(2)}, u32[]{:S(2)}) collective-permute-start(bf16[3,16,2176]{2,1,0:T(8,128)(2,1)S(1)} %pad_maximum_fusion.2), channel_id=1, source_target_pairs={{0,2},{1,3},{2,0},{3,1},{4,6},{5,7},{6,4},{7,5},{8,10},{9,11},{10,... | collective-permute-start | bytes 626696 | tf_op jit(solution)/shard_map/ppermute | solution.py:41
  23.2 1.4 %collective-permute-start.6 = (f32[512]{0:T(512)S(1)}, f32[512]{0:T(512)S(1)}, u32[]{:S(2)}, u32[]{:S(2)}) collective-permute-start(f32[512]{0:T(512)S(1)} %fusion.69), channel_id=1, source_target_pairs={{0,1},{1,0},{2,3},{3,2},{4,5},{5,4},{6,7},{7,6},{8,9},{9,8},{10,11... | collective-permute-start | bytes 6152 | tf_op jit(solution)/shard_map/ppermute | solution.py:41
  25.3 8.3 %collective-permute-start.8 = (f32[2,2,16,384]{3,2,1,0:T(8,128)S(1)}, f32[2,2,16,384]{3,2,1,0:T(8,128)S(1)}, u32[]{:S(2)}, u32[]{:S(2)}) collective-permute-start(f32[2,2,16,384]{3,2,1,0:T(8,128)S(1)} %slice.73), channel_id=1, source_target_pairs={{0,8},{1,9},{2,10},{3,11},{4,12},{5,13},{6,14},{7,15},{8,0},{9,1},... | collective-permute-start | bytes 294920 | tf_op jit(solution)/shard_map/ppermute | solution.py:41
  33.5 4.2 %collective-permute-start.9 = (f32[2,16,384]{2,1,0:T(8,128)S(1)}, f32[2,16,384]{2,1,0:T(8,128)S(1)}, u32[]{:S(2)}, u32[]{:S(2)}) collective-permute-start(f32[2,16,384]{2,1,0:T(8,128)S(1)} %slice_bitcast_fusion), channel_id=1, source_target_pairs={{0,4},{1,5},{2,6},{3,7},{4,0},{5,1},{6,2},{7,3},{8,12},{9,13},{10,... | collective-permute-start | bytes 147464 | tf_op jit(solution)/shard_map/ppermute | solution.py:41
  37.7 3.9 %collective-permute-start.10 = (f32[16,384]{1,0:T(8,128)S(1)}, f32[16,384]{1,0:T(8,128)S(1)}, u32[]{:S(2)}, u32[]{:S(2)}) collective-permute-start(f32[16,384]{1,0:T(8,128)S(1)} %slice_bitcast_fusion.2), channel_id=1, source_target_pairs={{0,2},{1,3},{2,0},{3,1},{4,6},{5,7},{6,4},{7,5},{8,10},{9,11},{10,... | collective-permute-start | bytes 73736 | tf_op jit(solution)/shard_map/ppermute | solution.py:41

commit v24 on v21

--- a/solution.py
+++ b/solution.py
@@ -133,11 +133,13 @@
     mean = col_sum / total
     spread = col_sq / total - mean * mean
     scale = lax.rsqrt(spread + EPS)
-    numer = 0.0
-    for k, vals in enumerate((values, pair_values)):
-        zvals = ((vals - mean) * scale).astype(jnp.bfloat16)
-        weight_b = jnp.concatenate([p[0][k] for p in parts], axis=0)
-        numer = numer + jnp.dot(weight_b, zvals, preferred_element_type=jnp.float32)
+    zvals = jnp.concatenate(
+        [((vals - mean) * scale).astype(jnp.bfloat16) for vals in (values, pair_values)], axis=0
+    )
+    weight_b = jnp.concatenate(
+        [jnp.concatenate([p[0][k] for p in parts], axis=0) for k in range(2)], axis=1
+    )
+    numer = jnp.dot(weight_b, zvals, preferred_element_type=jnp.float32)
     denom = jnp.concatenate([p[1] for p in parts], axis=0)
     den = jnp.broadcast_to(denom[:, None], (denom.shape[0], 128))
     sums = jnp.concatenate([numer, den], axis=1).reshape(lineage, q_dev, width + 128)

time: 38.4 us -> 38.3 us (level)
  no operation moved by 1% of the time
where the time goes in v24:
time: 38.3 us; the launch traced here: 38.1 us
  starting transfers between devices  13.3 us (35%)
  waiting for transfers between devices  11.6 us (30%)
  other arithmetic  7.6 us (20%)
  matrix products  5.14 us (13%)
    ppermute x12, starting transfers between devices, swap(): return lax.ppermute(x, axis, [(i, i ^ mask) for i in range(count)])  13.3 us
    ppermute x12, waiting for transfers between devices, swap(): return lax.ppermute(x, axis, [(i, i ^ mask) for i in range(count)])  11.6 us
    dot_general x4, matrix products, piece_weights(): lax.dot_general(rows, lib_ext, (((1,), (1,)), ((), ())), preferred_elemen...  4.87 us
    reduce_sum x2, other arithmetic, shards(): jnp.sum(jnp.square(lib.astype(jnp.float32)), axis=1)  3.25 us
    reduce_sum x1, other arithmetic, shards(): jnp.sum(values, axis=0)  1.14 us
    unnamed x2, other arithmetic  0.85 us
    broadcast_in_dim x1, other arithmetic, gather_rounds(): pieces = [packet[None]]  0.85 us
  transfers between devices with their start and end apart: 12, of which 5 were waited for; matrix products, arithmetic and copies ran while one was open for 31% of the time, Pallas kernels for 0%

profile of v24, /device:TPU:0, one launch (start us, length us, event | category | flops | bytes accessed | tf_op | source)
XLA Modules:
  0.0 38.1 jit_solution(16982394776426035711)
XLA Ops:
  0.0 0.0 copy-start
  0.0 0.0 copy-start.1
  0.0 0.5 %collective-permute-start.5 = (bf16[768,2048]{1,0:T(8,128)(2,1)}, bf16[768,2048]{1,0:T(8,128)(2,1)S(1)}, u32[]{:S(2)}, u32[]{:S(2)}) collective-permute-start(bf16[768,2048]{1,0:T(8,128)(2,1)} %param.4), channel_id=1, source_target_pairs={{0,1},{1,0},{2,3},{3,2},{4,5},{5,4},{6,7},{7,6},{8,9},{9,8},{10,11... | collective-permute-start | bytes 9437192 | tf_op jit(solution)/shard_map/ppermute | solution.py:41
  0.5 1.1 %convert_reduce_fusion = (f32[256]{0:T(256)S(1)}, f32[256]{0:T(256)S(1)}) fusion(bf16[768,256]{1,0:T(8,128)(2,1)} %param.5), kind=kLoop, calls=%fused_computation.12 | loop fusion | flops 785920 | bytes 395264 | tf_op jit(solution)/shard_map/reduce_sum | solution.py:112
  1.7 0.8 %maximum_bitcast_fusion = bf16[1,16,2176]{2,1,0:T(8,128)(2,1)S(1)} fusion(bf16[16,128]{1,0:T(8,128)(2,1)S(1)} %fusion.76, bf16[16,2048]{1,0:T(8,128)(2,1)} %param.3), kind=kLoop, calls=%fused_computation.51 | loop fusion | flops 139264 | bytes 139264 | tf_op jit(solution)/shard_map/broadcast_in_dim | solution.py:70
  2.5 2.7 %collective-permute-start = (bf16[1,16,2176]{2,1,0:T(8,128)(2,1)S(1)}, bf16[1,16,2176]{2,1,0:T(8,128)(2,1)S(1)}, u32[]{:S(2)}, u32[]{:S(2)}) collective-permute-start(bf16[1,16,2176]{2,1,0:T(8,128)(2,1)S(1)} %maximum_bitcast_fusion), channel_id=1, source_target_pairs={{0,2},{1,3},{2,0},{3,1},{4,6},{5,7},{6,4},{7,5},{8,10},{9,11},{10,... | collective-permute-start | bytes 208904 | tf_op jit(solution)/shard_map/ppermute | solution.py:41
  5.2 3.6 %collective-permute-start.3 = (bf16[1,16,2176]{2,1,0:T(8,128)(2,1)S(1)}, bf16[1,16,2176]{2,1,0:T(8,128)(2,1)S(1)}, u32[]{:S(2)}, u32[]{:S(2)}) collective-permute-start(bf16[1,16,2176]{2,1,0:T(8,128)(2,1)S(1)} %maximum_bitcast_fusion), channel_id=1, source_target_pairs={{0,12},{1,13},{2,14},{3,15},{4,8},{5,9},{6,10},{7,11},{8,4},{9,5},... | collective-permute-start | bytes 208904 | tf_op jit(solution)/shard_map/ppermute | solution.py:41
  8.8 0.0 collective-permute-start.2
  8.8 0.8 %collective-permute-start.1 = (bf16[1,16,2176]{2,1,0:T(8,128)(2,1)S(1)}, bf16[1,16,2176]{2,1,0:T(8,128)(2,1)S(1)}, u32[]{:S(2)}, u32[]{:S(2)}) collective-permute-start(bf16[1,16,2176]{2,1,0:T(8,128)(2,1)S(1)} %maximum_bitcast_fusion), channel_id=1, source_target_pairs={{0,4},{1,5},{2,6},{3,7},{4,0},{5,1},{6,2},{7,3},{8,12},{9,13},{10,... | collective-permute-start | bytes 208904 | tf_op jit(solution)/shard_map/ppermute | solution.py:41
  9.6 0.8 %constant_dynamic-update-slice_fusion.5 = bf16[8,16,2176]{2,1,0:T(8,128)(2,1)S(1)} fusion(bf16[16,128]{1,0:T(8,128)(2,1)S(1)} %fusion.76, bf16[16,2048]{1,0:T(8,128)(2,1)} %param.3), kind=kLoop, calls=%fused_computation.73 | loop fusion | flops 139263 | bytes 139264
  10.4 2.6 %multiply_reduce_fusion.1 = f32[768]{0:T(1024)S(1)} fusion(bf16[768,2048]{1,0:T(8,128)(2,1)} %param.4), kind=kLoop, calls=%fused_computation.1 | loop fusion | flops 4717824 | bytes 3148800 | tf_op jit(solution)/shard_map/reduce_sum | solution.py:123
  13.0 0.0 collective-permute-done.3
  13.0 0.0 copy-done.1
  13.0 0.1 collective-permute-start.7
  13.1 1.9 %collective-permute-done.2 = bf16[1,16,2176]{2,1,0:T(8,128)(2,1)S(1)} collective-permute-done((bf16[1,16,2176]{2,1,0:T(8,128)(2,1)S(1)}, bf16[1,16,2176]{2,1,0:T(8,128)(2,1)S(1)}, u32[]{:S(2)}, u32[]{:S(2)}) %collective-permute-start.2) | collective-permute-done | bytes 69664 | tf_op jit(solution)/shard_map/ppermute | solution.py:41
  15.0 0.0 collective-permute-done.1
  15.0 0.6 %collective-permute-start.4 = (bf16[3,16,2176]{2,1,0:T(8,128)(2,1)S(1)}, bf16[3,16,2176]{2,1,0:T(8,128)(2,1)S(1)}, u32[]{:S(2)}, u32[]{:S(2)}) collective-permute-start(bf16[3,16,2176]{2,1,0:T(8,128)(2,1)S(1)} %pad_maximum_fusion.2), channel_id=1, source_target_pairs={{0,2},{1,3},{2,0},{3,1},{4,6},{5,7},{6,4},{7,5},{8,10},{9,11},{10,... | collective-permute-start | bytes 626696 | tf_op jit(solution)/shard_map/ppermute | solution.py:41
  15.6 0.2 multiply_reduce_fusion.3
  15.8 0.0 copy-done
  15.8 1.2 %fusion.86 = (f32[64]{0:T(128)S(1)}, bf16[64,768]{1,0:T(8,128)(2,1)S(1)}) fusion(f32[768]{0:T(1024)S(1)} %multiply_reduce_fusion.1, f32[64]{0:T(128)S(1)} %multiply_reduce_fusion.3, bf16[64,2176]{1,0:T(8,128)(2,1)S(1)} %bitcast.45, bf16[768,2048]{1,0:T(8,128)(2,1)S(1)} %copy-done), kind=kOutput, calls=%fused_computation.99 | convolution fusion | flops 214253504 | bytes 3526144 | tf_op jit(solution)/shard_map/dot_general | solution.py:29
  17.1 0.0 collective-permute-done.5
  17.1 0.7 %multiply_reduce_fusion = f32[768]{0:T(1024)S(1)} fusion(bf16[768,2048]{1,0:T(8,128)(2,1)S(1)} %collective-permute-done.5), kind=kLoop, calls=%fused_computation | loop fusion | flops 4717824 | bytes 3148800 | tf_op jit(solution)/shard_map/reduce_sum | solution.py:123
  17.8 1.2 %fusion.85 = (f32[64]{0:T(128)S(1)}, bf16[64,768]{1,0:T(8,128)(2,1)S(1)}) fusion(f32[768]{0:T(1024)S(1)} %multiply_reduce_fusion, f32[64]{0:T(128)S(1)} %multiply_reduce_fusion.3, bf16[64,2176]{1,0:T(8,128)(2,1)S(1)} %bitcast.46, bf16[768,2048]{1,0:T(8,128)(2,1)S(1)} %collective-permute-done.5), kind=kOutput, calls=%fused_computation.98 | convolution fusion | flops 214253504 | bytes 3526144 | tf_op jit(solution)/shard_map/dot_general | solution.py:29
  19.0 0.0 collective-permute-done
  19.0 2.7 %collective-permute-done.4 = bf16[3,16,2176]{2,1,0:T(8,128)(2,1)S(1)} collective-permute-done((bf16[3,16,2176]{2,1,0:T(8,128)(2,1)S(1)}, bf16[3,16,2176]{2,1,0:T(8,128)(2,1)S(1)}, u32[]{:S(2)}, u32[]{:S(2)}) %collective-permute-start.4) | collective-permute-done | bytes 208928 | tf_op jit(solution)/shard_map/ppermute | solution.py:41
  21.7 0.2 multiply_reduce_fusion.2
  21.8 1.2 %fusion.83 = (bf16[64,768]{1,0:T(8,128)(2,1)S(1)}, f32[64]{0:T(128)S(1)}) fusion(f32[768]{0:T(1024)S(1)} %multiply_reduce_fusion.1, f32[64]{0:T(128)S(1)} %multiply_reduce_fusion.2, bf16[64,2176]{1,0:T(8,128)(2,1)S(1)} %bitcast.42, bf16[768,2048]{1,0:T(8,128)(2,1)S(1)} %copy-done), kind=kOutput, calls=%fused_computation.96 | convolution fusion | flops 214253504 | bytes 3526144 | tf_op jit(solution)/shard_map/dot_general | solution.py:29
  23.2 0.1 collective-permute-start.6
  23.3 1.2 %fusion.84 = (bf16[64,768]{1,0:T(8,128)(2,1)S(1)}, f32[64]{0:T(128)S(1)}) fusion(f32[768]{0:T(1024)S(1)} %multiply_reduce_fusion, f32[64]{0:T(128)S(1)} %multiply_reduce_fusion.2, bf16[64,2176]{1,0:T(8,128)(2,1)S(1)} %bitcast.43, bf16[768,2048]{1,0:T(8,128)(2,1)S(1)} %collective-permute-done.5), kind=kOutput, calls=%fused_computation.97 | convolution fusion | flops 214253504 | bytes 3526144 | tf_op jit(solution)/shard_map/dot_general | solution.py:29
  24.5 0.1 pad_maximum_fusion.5
  24.6 0.0 collective-permute-done.6
  24.6 0.0 collective-permute-done.7
  24.6 0.2 fusion.10
  24.8 0.3 fusion.11
  25.1 0.1 broadcast_in_dim.5
  25.2 2.8 %collective-permute-start.10 = (f32[2,16,384]{2,1,0:T(8,128)S(1)}, f32[2,16,384]{2,1,0:T(8,128)S(1)}, u32[]{:S(2)}, u32[]{:S(2)}) collective-permute-start(f32[2,16,384]{2,1,0:T(8,128)S(1)} %get-tuple-element.18), channel_id=1, source_target_pairs={{0,12},{1,13},{2,14},{3,15},{4,8},{5,9},{6,10},{7,11},{8,4},{9,5},... | collective-permute-start | bytes 147464 | tf_op jit(solution)/shard_map/ppermute | solution.py:41
  28.0 0.0 collective-permute-start.9
  28.0 1.7 %collective-permute-start.8 = (f32[2,16,384]{2,1,0:T(8,128)S(1)}, f32[2,16,384]{2,1,0:T(8,128)S(1)}, u32[]{:S(2)}, u32[]{:S(2)}) collective-permute-start(f32[2,16,384]{2,1,0:T(8,128)S(1)} %get-tuple-element.17), channel_id=1, source_target_pairs={{0,4},{1,5},{2,6},{3,7},{4,0},{5,1},{6,2},{7,3},{8,12},{9,13},{10,... | collective-permute-start | bytes 147464 | tf_op jit(solution)/shard_map/ppermute | solution.py:41
  29.7 2.0 %collective-permute-done.10 = f32[2,16,384]{2,1,0:T(8,128)S(1)} collective-permute-done((f32[2,16,384]{2,1,0:T(8,128)S(1)}, f32[2,16,384]{2,1,0:T(8,128)S(1)}, u32[]{:S(2)}, u32[]{:S(2)}) %collective-permute-start.10) | collective-permute-done | bytes 49184 | tf_op jit(solution)/shard_map/ppermute | solution.py:41
  31.7 1.7 %collective-permute-done.9 = f32[2,16,384]{2,1,0:T(8,128)S(1)} collective-permute-done((f32[2,16,384]{2,1,0:T(8,128)S(1)}, f32[2,16,384]{2,1,0:T(8,128)S(1)}, u32[]{:S(2)}, u32[]{:S(2)}) %collective-permute-start.9) | collective-permute-done | bytes 49184 | tf_op jit(solution)/shard_map/ppermute | solution.py:41
  33.4 0.0 collective-permute-done.8
  33.4 0.6 %collective-permute-start.11 = (f32[16,384]{1,0:T(8,128)S(1)}, f32[16,384]{1,0:T(8,128)S(1)}, u32[]{:S(2)}, u32[]{:S(2)}) collective-permute-start(f32[16,384]{1,0:T(8,128)S(1)} %slice_bitcast_fusion.4), channel_id=1, source_target_pairs={{0,2},{1,3},{2,0},{3,1},{4,6},{5,7},{6,4},{7,5},{8,10},{9,11},{10,... | collective-permute-start | bytes 73736 | tf_op jit(solution)/shard_map/ppermute | solution.py:41
  34.0 3.3 %collective-permute-done.11 = f32[16,384]{1,0:T(8,128)S(1)} collective-permute-done((f32[16,384]{1,0:T(8,128)S(1)}, f32[16,384]{1,0:T(8,128)S(1)}, u32[]{:S(2)}, u32[]{:S(2)}) %collective-permute-start.11) | collective-permute-done | bytes 24608 | tf_op jit(solution)/shard_map/ppermute | solution.py:41
  37.3 0.1 slice_reduce_fusion
  37.4 0.7 %slice_divide_fusion = f32[16,256]{1,0:T(8,128)} fusion(f32[16,384]{1,0:T(8,128)S(1)} %fusion.69, f32[16]{0:T(128)S(1)} %slice_reduce_fusion), kind=kLoop, calls=%fused_computation.64 | loop fusion | flops 4096 | bytes 32832 | tf_op jit(solution)/shard_map/div | solution.py:150
  (23 shorter events, 0.4 us)
Async XLA Ops:
  0.0 15.8 %copy-start = (bf16[768,2048]{1,0:T(8,128)(2,1)S(1)}, bf16[768,2048]{1,0:T(8,128)(2,1)}, u32[]{:S(2)}) copy-start(bf16[768,2048]{1,0:T(8,128)(2,1)} %param.4) | copy-start | bytes 9437188
  0.0 13.0 %copy-start.1 = (bf16[768,256]{1,0:T(8,128)(2,1)S(1)}, bf16[768,256]{1,0:T(8,128)(2,1)}, u32[]{:S(2)}) copy-start(bf16[768,256]{1,0:T(8,128)(2,1)} %param.5) | copy-start | bytes 1179652
  0.0 17.1 %collective-permute-start.5 = (bf16[768,2048]{1,0:T(8,128)(2,1)}, bf16[768,2048]{1,0:T(8,128)(2,1)S(1)}, u32[]{:S(2)}, u32[]{:S(2)}) collective-permute-start(bf16[768,2048]{1,0:T(8,128)(2,1)} %param.4), channel_id=1, source_target_pairs={{0,1},{1,0},{2,3},{3,2},{4,5},{5,4},{6,7},{7,6},{8,9},{9,8},{10,11... | collective-permute-start | bytes 9437192 | tf_op jit(solution)/shard_map/ppermute | solution.py:41
  2.5 16.5 %collective-permute-start = (bf16[1,16,2176]{2,1,0:T(8,128)(2,1)S(1)}, bf16[1,16,2176]{2,1,0:T(8,128)(2,1)S(1)}, u32[]{:S(2)}, u32[]{:S(2)}) collective-permute-start(bf16[1,16,2176]{2,1,0:T(8,128)(2,1)S(1)} %maximum_bitcast_fusion), channel_id=1, source_target_pairs={{0,2},{1,3},{2,0},{3,1},{4,6},{5,7},{6,4},{7,5},{8,10},{9,11},{10,... | collective-permute-start | bytes 208904 | tf_op jit(solution)/shard_map/ppermute | solution.py:41
  5.2 7.8 %collective-permute-start.3 = (bf16[1,16,2176]{2,1,0:T(8,128)(2,1)S(1)}, bf16[1,16,2176]{2,1,0:T(8,128)(2,1)S(1)}, u32[]{:S(2)}, u32[]{:S(2)}) collective-permute-start(bf16[1,16,2176]{2,1,0:T(8,128)(2,1)S(1)} %maximum_bitcast_fusion), channel_id=1, source_target_pairs={{0,12},{1,13},{2,14},{3,15},{4,8},{5,9},{6,10},{7,11},{8,4},{9,5},... | collective-permute-start | bytes 208904 | tf_op jit(solution)/shard_map/ppermute | solution.py:41
  8.8 6.2 %collective-permute-start.2 = (bf16[1,16,2176]{2,1,0:T(8,128)(2,1)S(1)}, bf16[1,16,2176]{2,1,0:T(8,128)(2,1)S(1)}, u32[]{:S(2)}, u32[]{:S(2)}) collective-permute-start(bf16[1,16,2176]{2,1,0:T(8,128)(2,1)S(1)} %maximum_bitcast_fusion), channel_id=1, source_target_pairs={{0,8},{1,9},{2,10},{3,11},{4,12},{5,13},{6,14},{7,15},{8,0},{9,1},... | collective-permute-start | bytes 208904 | tf_op jit(solution)/shard_map/ppermute | solution.py:41
  8.8 6.2 %collective-permute-start.1 = (bf16[1,16,2176]{2,1,0:T(8,128)(2,1)S(1)}, bf16[1,16,2176]{2,1,0:T(8,128)(2,1)S(1)}, u32[]{:S(2)}, u32[]{:S(2)}) collective-permute-start(bf16[1,16,2176]{2,1,0:T(8,128)(2,1)S(1)} %maximum_bitcast_fusion), channel_id=1, source_target_pairs={{0,4},{1,5},{2,6},{3,7},{4,0},{5,1},{6,2},{7,3},{8,12},{9,13},{10,... | collective-permute-start | bytes 208904 | tf_op jit(solution)/shard_map/ppermute | solution.py:41
  13.0 11.6 %collective-permute-start.7 = (bf16[768,256]{1,0:T(8,128)(2,1)S(1)}, bf16[768,256]{1,0:T(8,128)(2,1)S(1)}, u32[]{:S(2)}, u32[]{:S(2)}) collective-permute-start(bf16[768,256]{1,0:T(8,128)(2,1)S(1)} %copy-done.1), channel_id=1, source_target_pairs={{0,1},{1,0},{2,3},{3,2},{4,5},{5,4},{6,7},{7,6},{8,9},{9,8},{10,11... | collective-permute-start | bytes 1179656 | tf_op jit(solution)/shard_map/ppermute | solution.py:41
  15.0 6.6 %collective-permute-start.4 = (bf16[3,16,2176]{2,1,0:T(8,128)(2,1)S(1)}, bf16[3,16,2176]{2,1,0:T(8,128)(2,1)S(1)}, u32[]{:S(2)}, u32[]{:S(2)}) collective-permute-start(bf16[3,16,2176]{2,1,0:T(8,128)(2,1)S(1)} %pad_maximum_fusion.2), channel_id=1, source_target_pairs={{0,2},{1,3},{2,0},{3,1},{4,6},{5,7},{6,4},{7,5},{8,10},{9,11},{10,... | collective-permute-start | bytes 626696 | tf_op jit(solution)/shard_map/ppermute | solution.py:41
  23.2 1.4 %collective-permute-start.6 = (f32[512]{0:T(512)S(1)}, f32[512]{0:T(512)S(1)}, u32[]{:S(2)}, u32[]{:S(2)}) collective-permute-start(f32[512]{0:T(512)S(1)} %fusion.70), channel_id=1, source_target_pairs={{0,1},{1,0},{2,3},{3,2},{4,5},{5,4},{6,7},{7,6},{8,9},{9,8},{10,11... | collective-permute-start | bytes 6152 | tf_op jit(solution)/shard_map/ppermute | solution.py:41
  25.2 6.5 %collective-permute-start.10 = (f32[2,16,384]{2,1,0:T(8,128)S(1)}, f32[2,16,384]{2,1,0:T(8,128)S(1)}, u32[]{:S(2)}, u32[]{:S(2)}) collective-permute-start(f32[2,16,384]{2,1,0:T(8,128)S(1)} %get-tuple-element.18), channel_id=1, source_target_pairs={{0,12},{1,13},{2,14},{3,15},{4,8},{5,9},{6,10},{7,11},{8,4},{9,5},... | collective-permute-start | bytes 147464 | tf_op jit(solution)/shard_map/ppermute | solution.py:41
  28.0 5.4 %collective-permute-start.9 = (f32[2,16,384]{2,1,0:T(8,128)S(1)}, f32[2,16,384]{2,1,0:T(8,128)S(1)}, u32[]{:S(2)}, u32[]{:S(2)}) collective-permute-start(f32[2,16,384]{2,1,0:T(8,128)S(1)} %get-tuple-element.19), channel_id=1, source_target_pairs={{0,8},{1,9},{2,10},{3,11},{4,12},{5,13},{6,14},{7,15},{8,0},{9,1},... | collective-permute-start | bytes 147464 | tf_op jit(solution)/shard_map/ppermute | solution.py:41
  28.0 5.4 %collective-permute-start.8 = (f32[2,16,384]{2,1,0:T(8,128)S(1)}, f32[2,16,384]{2,1,0:T(8,128)S(1)}, u32[]{:S(2)}, u32[]{:S(2)}) collective-permute-start(f32[2,16,384]{2,1,0:T(8,128)S(1)} %get-tuple-element.17), channel_id=1, source_target_pairs={{0,4},{1,5},{2,6},{3,7},{4,0},{5,1},{6,2},{7,3},{8,12},{9,13},{10,... | collective-permute-start | bytes 147464 | tf_op jit(solution)/shard_map/ppermute | solution.py:41
  33.4 3.9 %collective-permute-start.11 = (f32[16,384]{1,0:T(8,128)S(1)}, f32[16,384]{1,0:T(8,128)S(1)}, u32[]{:S(2)}, u32[]{:S(2)}) collective-permute-start(f32[16,384]{1,0:T(8,128)S(1)} %slice_bitcast_fusion.4), channel_id=1, source_target_pairs={{0,2},{1,3},{2,0},{3,1},{4,6},{5,7},{6,4},{7,5},{8,10},{9,11},{10,... | collective-permute-start | bytes 73736 | tf_op jit(solution)/shard_map/ppermute | solution.py:41

commit v25 on v21

--- a/solution.py
+++ b/solution.py
@@ -81,8 +81,6 @@
         if r + 1 < len(rounds):
             early = [swap(cat(pieces), axis, m) for m in offsets(rounds[r + 1])[1:]]
             mark = len(pieces)
-        if results:
-            got, results[-1] = lax.optimization_barrier((got, results[-1]))
         got = [piece for pair in got for piece in pair]
         pieces += got
         fresh += got

time: 38.4 us -> 40.4 us (1.052)
  starting transfers between devices: 13.3 us -> 14.6 us
  waiting for transfers between devices: 11.6 us -> 12.2 us
    ppermute x12, starting transfers between devices: 13.3 us -> 14.6 us  [swap(): return lax.ppermute(x, axis, [(i, i ^ mask) for i in range(count)])]
    ppermute x12, waiting for transfers between devices: 11.6 us -> 12.2 us  [swap(): return lax.ppermute(x, axis, [(i, i ^ mask) for i in range(count)])]
  transfers between devices with their start and end apart: 12 -> 12, of which waited for: 5 -> 6; matrix products, arithmetic and copies ran while one was open for 31% -> 24% of each run, Pallas kernels for 0% -> 0%
where the time goes in v25:
time: 40.4 us; the launch traced here: 40.2 us
  starting transfers between devices  14.6 us (36%)
  waiting for transfers between devices  12.2 us (30%)
  other arithmetic  7.54 us (19%)
  matrix products  5.36 us (13%)
    ppermute x12, starting transfers between devices, swap(): return lax.ppermute(x, axis, [(i, i ^ mask) for i in range(count)])  14.6 us
    ppermute x12, waiting for transfers between devices, swap(): return lax.ppermute(x, axis, [(i, i ^ mask) for i in range(count)])  12.2 us
    dot_general x4, matrix products, piece_weights(): lax.dot_general(rows, lib_ext, (((1,), (1,)), ((), ())), preferred_elemen...  4.86 us
    reduce_sum x2, other arithmetic, shards(): jnp.sum(jnp.square(lib.astype(jnp.float32)), axis=1)  3.25 us
    reduce_sum x1, other arithmetic, shards(): jnp.sum(values, axis=0)  1.29 us
    unnamed x2, other arithmetic  0.85 us
    broadcast_in_dim x1, other arithmetic, gather_rounds(): fresh = [packet[None]]  0.85 us
  transfers between devices with their start and end apart: 12, of which 6 were waited for; matrix products, arithmetic and copies ran while one was open for 24% of the time, Pallas kernels for 0%

profile of v25, /device:TPU:0, one launch (start us, length us, event | category | flops | bytes accessed | tf_op | source)
XLA Modules:
  0.0 40.2 jit_solution(9023727589109535040)
XLA Ops:
  0.0 0.0 copy-start.1
  0.0 0.0 copy-start
  0.0 1.3 %convert_reduce_fusion = (f32[256]{0:T(256)S(1)}, f32[256]{0:T(256)S(1)}) fusion(bf16[768,256]{1,0:T(8,128)(2,1)} %param.5), kind=kLoop, calls=%fused_computation.12 | loop fusion | flops 785920 | bytes 395264 | tf_op jit(solution)/shard_map/reduce_sum | solution.py:110
  1.3 0.8 %maximum_bitcast_fusion = bf16[1,16,2176]{2,1,0:T(8,128)(2,1)S(1)} fusion(bf16[16,128]{1,0:T(8,128)(2,1)S(1)} %fusion.77, bf16[16,2048]{1,0:T(8,128)(2,1)} %param.3), kind=kLoop, calls=%fused_computation.52 | loop fusion | flops 139264 | bytes 139264 | tf_op jit(solution)/shard_map/broadcast_in_dim | solution.py:72
  2.2 3.1 %collective-permute-start = (bf16[1,16,2176]{2,1,0:T(8,128)(2,1)S(1)}, bf16[1,16,2176]{2,1,0:T(8,128)(2,1)S(1)}, u32[]{:S(2)}, u32[]{:S(2)}) collective-permute-start(bf16[1,16,2176]{2,1,0:T(8,128)(2,1)S(1)} %maximum_bitcast_fusion), channel_id=1, source_target_pairs={{0,4},{1,5},{2,6},{3,7},{4,0},{5,1},{6,2},{7,3},{8,12},{9,13},{10,... | collective-permute-start | bytes 208904 | tf_op jit(solution)/shard_map/ppermute | solution.py:41
  5.2 2.6 %collective-permute-start.1 = (bf16[1,16,2176]{2,1,0:T(8,128)(2,1)S(1)}, bf16[1,16,2176]{2,1,0:T(8,128)(2,1)S(1)}, u32[]{:S(2)}, u32[]{:S(2)}) collective-permute-start(bf16[1,16,2176]{2,1,0:T(8,128)(2,1)S(1)} %maximum_bitcast_fusion), channel_id=1, source_target_pairs={{0,8},{1,9},{2,10},{3,11},{4,12},{5,13},{6,14},{7,15},{8,0},{9,1},... | collective-permute-start | bytes 208904 | tf_op jit(solution)/shard_map/ppermute | solution.py:41
  7.8 0.0 collective-permute-start.2
  7.8 1.7 %collective-permute-start.3 = (bf16[1,16,2176]{2,1,0:T(8,128)(2,1)S(1)}, bf16[1,16,2176]{2,1,0:T(8,128)(2,1)S(1)}, u32[]{:S(2)}, u32[]{:S(2)}) collective-permute-start(bf16[1,16,2176]{2,1,0:T(8,128)(2,1)S(1)} %maximum_bitcast_fusion), channel_id=1, source_target_pairs={{0,2},{1,3},{2,0},{3,1},{4,6},{5,7},{6,4},{7,5},{8,10},{9,11},{10,... | collective-permute-start | bytes 208904 | tf_op jit(solution)/shard_map/ppermute | solution.py:41
  9.6 0.0 collective-permute-start.6
  9.6 0.8 %constant_dynamic-update-slice_fusion.5 = bf16[8,16,2176]{2,1,0:T(8,128)(2,1)S(1)} fusion(bf16[16,128]{1,0:T(8,128)(2,1)S(1)} %fusion.77, bf16[16,2048]{1,0:T(8,128)(2,1)} %param.3), kind=kLoop, calls=%fused_computation.74 | loop fusion | flops 139263 | bytes 139264
  10.4 2.6 %multiply_reduce_fusion.1 = f32[768]{0:T(1024)S(1)} fusion(bf16[768,2048]{1,0:T(8,128)(2,1)} %param.4), kind=kLoop, calls=%fused_computation.1 | loop fusion | flops 4717824 | bytes 3148800 | tf_op jit(solution)/shard_map/reduce_sum | solution.py:121
  13.0 0.0 collective-permute-done
  13.0 0.0 copy-done.1
  13.0 0.6 %collective-permute-start.7 = (bf16[768,256]{1,0:T(8,128)(2,1)S(1)}, bf16[768,256]{1,0:T(8,128)(2,1)S(1)}, u32[]{:S(2)}, u32[]{:S(2)}) collective-permute-start(bf16[768,256]{1,0:T(8,128)(2,1)S(1)} %copy-done.1), channel_id=1, source_target_pairs={{0,1},{1,0},{2,3},{3,2},{4,5},{5,4},{6,7},{7,6},{8,9},{9,8},{10,11... | collective-permute-start | bytes 1179656 | tf_op jit(solution)/shard_map/ppermute | solution.py:41
  13.6 0.0 collective-permute-done.1
  13.6 0.5 %collective-permute-done.2 = bf16[1,16,2176]{2,1,0:T(8,128)(2,1)S(1)} collective-permute-done((bf16[1,16,2176]{2,1,0:T(8,128)(2,1)S(1)}, bf16[1,16,2176]{2,1,0:T(8,128)(2,1)S(1)}, u32[]{:S(2)}, u32[]{:S(2)}) %collective-permute-start.2) | collective-permute-done | bytes 69664 | tf_op jit(solution)/shard_map/ppermute | solution.py:41
  14.1 1.6 %collective-permute-start.4 = (bf16[3,16,2176]{2,1,0:T(8,128)(2,1)S(1)}, bf16[3,16,2176]{2,1,0:T(8,128)(2,1)S(1)}, u32[]{:S(2)}, u32[]{:S(2)}) collective-permute-start(bf16[3,16,2176]{2,1,0:T(8,128)(2,1)S(1)} %pad_maximum_fusion.2), channel_id=1, source_target_pairs={{0,2},{1,3},{2,0},{3,1},{4,6},{5,7},{6,4},{7,5},{8,10},{9,11},{10,... | collective-permute-start | bytes 626696 | tf_op jit(solution)/shard_map/ppermute | solution.py:41
  15.7 0.2 multiply_reduce_fusion.3
  15.9 0.0 collective-permute-done.3
  15.9 0.0 copy-done
  15.9 1.2 %fusion.87 = (bf16[64,768]{1,0:T(8,128)(2,1)S(1)}, f32[64]{0:T(128)S(1)}) fusion(f32[768]{0:T(1024)S(1)} %multiply_reduce_fusion.1, f32[64]{0:T(128)S(1)} %multiply_reduce_fusion.3, bf16[64,2176]{1,0:T(8,128)(2,1)S(1)} %bitcast.42, bf16[768,2048]{1,0:T(8,128)(2,1)S(1)} %copy-done), kind=kOutput, calls=%fused_computation.100 | convolution fusion | flops 214253504 | bytes 3526144 | tf_op jit(solution)/shard_map/dot_general | solution.py:29
  17.1 3.6 %collective-permute-done.4 = bf16[3,16,2176]{2,1,0:T(8,128)(2,1)S(1)} collective-permute-done((bf16[3,16,2176]{2,1,0:T(8,128)(2,1)S(1)}, bf16[3,16,2176]{2,1,0:T(8,128)(2,1)S(1)}, u32[]{:S(2)}, u32[]{:S(2)}) %collective-permute-start.4) | collective-permute-done | bytes 208928 | tf_op jit(solution)/shard_map/ppermute | solution.py:41
  20.9 0.1 collective-permute-start.5
  21.0 0.2 multiply_reduce_fusion.2
  21.2 1.2 %fusion.88 = (bf16[64,768]{1,0:T(8,128)(2,1)S(1)}, f32[64]{0:T(128)S(1)}) fusion(f32[768]{0:T(1024)S(1)} %multiply_reduce_fusion.1, f32[64]{0:T(128)S(1)} %multiply_reduce_fusion.2, bf16[64,2176]{1,0:T(8,128)(2,1)S(1)} %bitcast.45, bf16[768,2048]{1,0:T(8,128)(2,1)S(1)} %copy-done), kind=kOutput, calls=%fused_computation.101 | convolution fusion | flops 214253504 | bytes 3526144 | tf_op jit(solution)/shard_map/dot_general | solution.py:29
  22.4 0.0 collective-permute-done.5
  22.4 0.2 fusion.11
  22.7 0.0 collective-permute-done.6
  22.7 0.7 %multiply_reduce_fusion = f32[768]{0:T(1024)S(1)} fusion(bf16[768,2048]{1,0:T(8,128)(2,1)S(1)} %collective-permute-done.6), kind=kLoop, calls=%fused_computation | loop fusion | flops 4717824 | bytes 3148800 | tf_op jit(solution)/shard_map/reduce_sum | solution.py:121
  23.3 1.2 %fusion.85 = (bf16[64,768]{1,0:T(8,128)(2,1)S(1)}, f32[64]{0:T(128)S(1)}) fusion(f32[768]{0:T(1024)S(1)} %multiply_reduce_fusion, f32[64]{0:T(128)S(1)} %multiply_reduce_fusion.3, bf16[64,2176]{1,0:T(8,128)(2,1)S(1)} %bitcast.43, bf16[768,2048]{1,0:T(8,128)(2,1)S(1)} %collective-permute-done.6), kind=kOutput, calls=%fused_computation.98 | convolution fusion | flops 214253504 | bytes 3526144 | tf_op jit(solution)/shard_map/dot_general | solution.py:29
  24.6 1.2 %fusion.86 = (bf16[64,768]{1,0:T(8,128)(2,1)S(1)}, f32[64]{0:T(128)S(1)}) fusion(f32[768]{0:T(1024)S(1)} %multiply_reduce_fusion, f32[64]{0:T(128)S(1)} %multiply_reduce_fusion.2, bf16[64,2176]{1,0:T(8,128)(2,1)S(1)} %bitcast.46, bf16[768,2048]{1,0:T(8,128)(2,1)S(1)} %collective-permute-done.6), kind=kOutput, calls=%fused_computation.99 | convolution fusion | flops 214253504 | bytes 3526144 | tf_op jit(solution)/shard_map/dot_general | solution.py:29
  25.8 0.1 pad_maximum_fusion.5
  25.9 0.0 collective-permute-done.7
  25.9 0.3 convolution_add_fusion
  26.1 0.1 broadcast_in_dim.5
  26.3 3.7 %collective-permute-start.10 = (f32[2,16,384]{2,1,0:T(8,128)S(1)}, f32[2,16,384]{2,1,0:T(8,128)S(1)}, u32[]{:S(2)}, u32[]{:S(2)}) collective-permute-start(f32[2,16,384]{2,1,0:T(8,128)S(1)} %get-tuple-element.8), channel_id=1, source_target_pairs={{0,12},{1,13},{2,14},{3,15},{4,8},{5,9},{6,10},{7,11},{8,4},{9,5},... | collective-permute-start | bytes 147464 | tf_op jit(solution)/shard_map/ppermute | solution.py:41
  30.0 0.0 collective-permute-start.8
  30.0 0.8 %collective-permute-start.9 = (f32[2,16,384]{2,1,0:T(8,128)S(1)}, f32[2,16,384]{2,1,0:T(8,128)S(1)}, u32[]{:S(2)}, u32[]{:S(2)}) collective-permute-start(f32[2,16,384]{2,1,0:T(8,128)S(1)} %get-tuple-element.9), channel_id=1, source_target_pairs={{0,8},{1,9},{2,10},{3,11},{4,12},{5,13},{6,14},{7,15},{8,0},{9,1},... | collective-permute-start | bytes 147464 | tf_op jit(solution)/shard_map/ppermute | solution.py:41
  30.7 2.0 %collective-permute-done.10 = f32[2,16,384]{2,1,0:T(8,128)S(1)} collective-permute-done((f32[2,16,384]{2,1,0:T(8,128)S(1)}, f32[2,16,384]{2,1,0:T(8,128)S(1)}, u32[]{:S(2)}, u32[]{:S(2)}) %collective-permute-start.10) | collective-permute-done | bytes 49184 | tf_op jit(solution)/shard_map/ppermute | solution.py:41
  32.8 2.3 %collective-permute-done.8 = f32[2,16,384]{2,1,0:T(8,128)S(1)} collective-permute-done((f32[2,16,384]{2,1,0:T(8,128)S(1)}, f32[2,16,384]{2,1,0:T(8,128)S(1)}, u32[]{:S(2)}, u32[]{:S(2)}) %collective-permute-start.8) | collective-permute-done | bytes 49184 | tf_op jit(solution)/shard_map/ppermute | solution.py:41
  35.1 0.4 collective-permute-done.9
  35.5 0.6 %collective-permute-start.11 = (f32[16,384]{1,0:T(8,128)S(1)}, f32[16,384]{1,0:T(8,128)S(1)}, u32[]{:S(2)}, u32[]{:S(2)}) collective-permute-start(f32[16,384]{1,0:T(8,128)S(1)} %slice_bitcast_fusion.4), channel_id=1, source_target_pairs={{0,2},{1,3},{2,0},{3,1},{4,6},{5,7},{6,4},{7,5},{8,10},{9,11},{10,... | collective-permute-start | bytes 73736 | tf_op jit(solution)/shard_map/ppermute | solution.py:41
  36.1 3.3 %collective-permute-done.11 = f32[16,384]{1,0:T(8,128)S(1)} collective-permute-done((f32[16,384]{1,0:T(8,128)S(1)}, f32[16,384]{1,0:T(8,128)S(1)}, u32[]{:S(2)}, u32[]{:S(2)}) %collective-permute-start.11) | collective-permute-done | bytes 24608 | tf_op jit(solution)/shard_map/ppermute | solution.py:41
  39.4 0.1 slice_reduce_fusion
  39.5 0.7 %slice_divide_fusion = f32[16,256]{1,0:T(8,128)} fusion(f32[16,384]{1,0:T(8,128)S(1)} %fusion.70, f32[16]{0:T(128)S(1)} %slice_reduce_fusion), kind=kLoop, calls=%fused_computation.65 | loop fusion | flops 4096 | bytes 32832 | tf_op jit(solution)/shard_map/div | solution.py:146
  (23 shorter events, 0.4 us)
Async XLA Ops:
  0.0 13.0 %copy-start.1 = (bf16[768,256]{1,0:T(8,128)(2,1)S(1)}, bf16[768,256]{1,0:T(8,128)(2,1)}, u32[]{:S(2)}) copy-start(bf16[768,256]{1,0:T(8,128)(2,1)} %param.5) | copy-start | bytes 1179652
  0.0 15.9 %copy-start = (bf16[768,2048]{1,0:T(8,128)(2,1)S(1)}, bf16[768,2048]{1,0:T(8,128)(2,1)}, u32[]{:S(2)}) copy-start(bf16[768,2048]{1,0:T(8,128)(2,1)} %param.4) | copy-start | bytes 9437188
  2.2 10.8 %collective-permute-start = (bf16[1,16,2176]{2,1,0:T(8,128)(2,1)S(1)}, bf16[1,16,2176]{2,1,0:T(8,128)(2,1)S(1)}, u32[]{:S(2)}, u32[]{:S(2)}) collective-permute-start(bf16[1,16,2176]{2,1,0:T(8,128)(2,1)S(1)} %maximum_bitcast_fusion), channel_id=1, source_target_pairs={{0,4},{1,5},{2,6},{3,7},{4,0},{5,1},{6,2},{7,3},{8,12},{9,13},{10,... | collective-permute-start | bytes 208904 | tf_op jit(solution)/shard_map/ppermute | solution.py:41
  5.2 8.3 %collective-permute-start.1 = (bf16[1,16,2176]{2,1,0:T(8,128)(2,1)S(1)}, bf16[1,16,2176]{2,1,0:T(8,128)(2,1)S(1)}, u32[]{:S(2)}, u32[]{:S(2)}) collective-permute-start(bf16[1,16,2176]{2,1,0:T(8,128)(2,1)S(1)} %maximum_bitcast_fusion), channel_id=1, source_target_pairs={{0,8},{1,9},{2,10},{3,11},{4,12},{5,13},{6,14},{7,15},{8,0},{9,1},... | collective-permute-start | bytes 208904 | tf_op jit(solution)/shard_map/ppermute | solution.py:41
  7.8 6.2 %collective-permute-start.2 = (bf16[1,16,2176]{2,1,0:T(8,128)(2,1)S(1)}, bf16[1,16,2176]{2,1,0:T(8,128)(2,1)S(1)}, u32[]{:S(2)}, u32[]{:S(2)}) collective-permute-start(bf16[1,16,2176]{2,1,0:T(8,128)(2,1)S(1)} %maximum_bitcast_fusion), channel_id=1, source_target_pairs={{0,12},{1,13},{2,14},{3,15},{4,8},{5,9},{6,10},{7,11},{8,4},{9,5},... | collective-permute-start | bytes 208904 | tf_op jit(solution)/shard_map/ppermute | solution.py:41
  7.8 8.1 %collective-permute-start.3 = (bf16[1,16,2176]{2,1,0:T(8,128)(2,1)S(1)}, bf16[1,16,2176]{2,1,0:T(8,128)(2,1)S(1)}, u32[]{:S(2)}, u32[]{:S(2)}) collective-permute-start(bf16[1,16,2176]{2,1,0:T(8,128)(2,1)S(1)} %maximum_bitcast_fusion), channel_id=1, source_target_pairs={{0,2},{1,3},{2,0},{3,1},{4,6},{5,7},{6,4},{7,5},{8,10},{9,11},{10,... | collective-permute-start | bytes 208904 | tf_op jit(solution)/shard_map/ppermute | solution.py:41
  9.6 13.1 %collective-permute-start.6 = (bf16[768,2048]{1,0:T(8,128)(2,1)}, bf16[768,2048]{1,0:T(8,128)(2,1)S(1)}, u32[]{:S(2)}, u32[]{:S(2)}) collective-permute-start(bf16[768,2048]{1,0:T(8,128)(2,1)} %param.4), channel_id=1, source_target_pairs={{0,1},{1,0},{2,3},{3,2},{4,5},{5,4},{6,7},{7,6},{8,9},{9,8},{10,11... | collective-permute-start | bytes 9437192 | tf_op jit(solution)/shard_map/ppermute | solution.py:41
  13.0 12.9 %collective-permute-start.7 = (bf16[768,256]{1,0:T(8,128)(2,1)S(1)}, bf16[768,256]{1,0:T(8,128)(2,1)S(1)}, u32[]{:S(2)}, u32[]{:S(2)}) collective-permute-start(bf16[768,256]{1,0:T(8,128)(2,1)S(1)} %copy-done.1), channel_id=1, source_target_pairs={{0,1},{1,0},{2,3},{3,2},{4,5},{5,4},{6,7},{7,6},{8,9},{9,8},{10,11... | collective-permute-start | bytes 1179656 | tf_op jit(solution)/shard_map/ppermute | solution.py:41
  14.1 6.7 %collective-permute-start.4 = (bf16[3,16,2176]{2,1,0:T(8,128)(2,1)S(1)}, bf16[3,16,2176]{2,1,0:T(8,128)(2,1)S(1)}, u32[]{:S(2)}, u32[]{:S(2)}) collective-permute-start(bf16[3,16,2176]{2,1,0:T(8,128)(2,1)S(1)} %pad_maximum_fusion.2), channel_id=1, source_target_pairs={{0,2},{1,3},{2,0},{3,1},{4,6},{5,7},{6,4},{7,5},{8,10},{9,11},{10,... | collective-permute-start | bytes 626696 | tf_op jit(solution)/shard_map/ppermute | solution.py:41
  20.9 1.5 %collective-permute-start.5 = (f32[512]{0:T(512)S(1)}, f32[512]{0:T(512)S(1)}, u32[]{:S(2)}, u32[]{:S(2)}) collective-permute-start(f32[512]{0:T(512)S(1)} %fusion.71), channel_id=1, source_target_pairs={{0,1},{1,0},{2,3},{3,2},{4,5},{5,4},{6,7},{7,6},{8,9},{9,8},{10,11... | collective-permute-start | bytes 6152 | tf_op jit(solution)/shard_map/ppermute | solution.py:41
  26.3 6.5 %collective-permute-start.10 = (f32[2,16,384]{2,1,0:T(8,128)S(1)}, f32[2,16,384]{2,1,0:T(8,128)S(1)}, u32[]{:S(2)}, u32[]{:S(2)}) collective-permute-start(f32[2,16,384]{2,1,0:T(8,128)S(1)} %get-tuple-element.8), channel_id=1, source_target_pairs={{0,12},{1,13},{2,14},{3,15},{4,8},{5,9},{6,10},{7,11},{8,4},{9,5},... | collective-permute-start | bytes 147464 | tf_op jit(solution)/shard_map/ppermute | solution.py:41
  30.0 5.1 %collective-permute-start.8 = (f32[2,16,384]{2,1,0:T(8,128)S(1)}, f32[2,16,384]{2,1,0:T(8,128)S(1)}, u32[]{:S(2)}, u32[]{:S(2)}) collective-permute-start(f32[2,16,384]{2,1,0:T(8,128)S(1)} %get-tuple-element.7), channel_id=1, source_target_pairs={{0,4},{1,5},{2,6},{3,7},{4,0},{5,1},{6,2},{7,3},{8,12},{9,13},{10,... | collective-permute-start | bytes 147464 | tf_op jit(solution)/shard_map/ppermute | solution.py:41
  30.0 5.5 %collective-permute-start.9 = (f32[2,16,384]{2,1,0:T(8,128)S(1)}, f32[2,16,384]{2,1,0:T(8,128)S(1)}, u32[]{:S(2)}, u32[]{:S(2)}) collective-permute-start(f32[2,16,384]{2,1,0:T(8,128)S(1)} %get-tuple-element.9), channel_id=1, source_target_pairs={{0,8},{1,9},{2,10},{3,11},{4,12},{5,13},{6,14},{7,15},{8,0},{9,1},... | collective-permute-start | bytes 147464 | tf_op jit(solution)/shard_map/ppermute | solution.py:41
  35.5 3.9 %collective-permute-start.11 = (f32[16,384]{1,0:T(8,128)S(1)}, f32[16,384]{1,0:T(8,128)S(1)}, u32[]{:S(2)}, u32[]{:S(2)}) collective-permute-start(f32[16,384]{1,0:T(8,128)S(1)} %slice_bitcast_fusion.4), channel_id=1, source_target_pairs={{0,2},{1,3},{2,0},{3,1},{4,6},{5,7},{6,4},{7,5},{8,10},{9,11},{10,... | collective-permute-start | bytes 73736 | tf_op jit(solution)/shard_map/ppermute | solution.py:41

commit v26 on v21

--- a/solution.py
+++ b/solution.py
@@ -119,6 +119,7 @@
     lanes += -lanes % 128
     coded = jnp.pad(coded, (0, q_dev * lanes - coded.shape[0])).reshape(q_dev, lanes)
     packet = jnp.concatenate([queries, coded], axis=1)
+    pair_lib, pair_values = lax.optimization_barrier((pair_lib, pair_values))
     libs = [jnp.pad(lib, ((0, 0), (0, lanes))) for lib in (library, pair_lib)]
     lib_sqs = [jnp.sum(jnp.square(lib.astype(jnp.float32)), axis=1) for lib in (library, pair_lib)]
     got, parts = gather_rounds(

time: 38.4 us -> 39.2 us (1.021)
  waiting for transfers between devices: 11.6 us -> 12.3 us
    ppermute x12, waiting for transfers between devices: 11.6 us -> 12.3 us  [swap(): return lax.ppermute(x, axis, [(i, i ^ mask) for i in range(count)])]
  transfers between devices with their start and end apart: 12 -> 12, of which waited for: 5 -> 7; matrix products, arithmetic and copies ran while one was open for 31% -> 23% of each run, Pallas kernels for 0% -> 0%
where the time goes in v26:
time: 39.2 us; the launch traced here: 38.9 us
  starting transfers between devices  13.3 us (34%)
  waiting for transfers between devices  12.3 us (31%)
  other arithmetic  7.44 us (19%)
  matrix products  5.35 us (14%)
    ppermute x12, starting transfers between devices, swap(): return lax.ppermute(x, axis, [(i, i ^ mask) for i in range(count)])  13.3 us
    ppermute x12, waiting for transfers between devices, swap(): return lax.ppermute(x, axis, [(i, i ^ mask) for i in range(count)])  12.3 us
    dot_general x4, matrix products, piece_weights(): lax.dot_general(rows, lib_ext, (((1,), (1,)), ((), ())), preferred_elemen...  4.87 us
    reduce_sum x2, other arithmetic, shards(): jnp.sum(jnp.square(lib.astype(jnp.float32)), axis=1)  3.25 us
    reduce_sum x1, other arithmetic, shards(): jnp.sum(values, axis=0)  1.14 us
    unnamed x2, other arithmetic  0.85 us
    broadcast_in_dim x1, other arithmetic, gather_rounds(): pieces = [packet[None]]  0.85 us
  transfers between devices with their start and end apart: 12, of which 7 were waited for; matrix products, arithmetic and copies ran while one was open for 23% of the time, Pallas kernels for 0%

profile of v26, /device:TPU:0, one launch (start us, length us, event | category | flops | bytes accessed | tf_op | source)
XLA Modules:
  0.0 38.9 jit_solution(16957420813745840631)
XLA Ops:
  0.0 0.0 copy-start
  0.0 0.0 copy-start.1
  0.0 0.5 %collective-permute-start.5 = (bf16[768,2048]{1,0:T(8,128)(2,1)}, bf16[768,2048]{1,0:T(8,128)(2,1)S(1)}, u32[]{:S(2)}, u32[]{:S(2)}) collective-permute-start(bf16[768,2048]{1,0:T(8,128)(2,1)} %param.4), channel_id=1, source_target_pairs={{0,1},{1,0},{2,3},{3,2},{4,5},{5,4},{6,7},{7,6},{8,9},{9,8},{10,11... | collective-permute-start | bytes 9437192 | tf_op jit(solution)/shard_map/ppermute | solution.py:41
  0.5 1.1 %convert_reduce_fusion = (f32[256]{0:T(256)S(1)}, f32[256]{0:T(256)S(1)}) fusion(bf16[768,256]{1,0:T(8,128)(2,1)} %param.5), kind=kLoop, calls=%fused_computation.12 | loop fusion | flops 785920 | bytes 395264 | tf_op jit(solution)/shard_map/reduce_sum | solution.py:112
  1.7 0.8 %maximum_bitcast_fusion = bf16[1,16,2176]{2,1,0:T(8,128)(2,1)S(1)} fusion(bf16[16,128]{1,0:T(8,128)(2,1)S(1)} %fusion.77, bf16[16,2048]{1,0:T(8,128)(2,1)} %param.3), kind=kLoop, calls=%fused_computation.52 | loop fusion | flops 139264 | bytes 139264 | tf_op jit(solution)/shard_map/broadcast_in_dim | solution.py:70
  2.5 2.7 %collective-permute-start = (bf16[1,16,2176]{2,1,0:T(8,128)(2,1)S(1)}, bf16[1,16,2176]{2,1,0:T(8,128)(2,1)S(1)}, u32[]{:S(2)}, u32[]{:S(2)}) collective-permute-start(bf16[1,16,2176]{2,1,0:T(8,128)(2,1)S(1)} %maximum_bitcast_fusion), channel_id=1, source_target_pairs={{0,2},{1,3},{2,0},{3,1},{4,6},{5,7},{6,4},{7,5},{8,10},{9,11},{10,... | collective-permute-start | bytes 208904 | tf_op jit(solution)/shard_map/ppermute | solution.py:41
  5.2 3.6 %collective-permute-start.3 = (bf16[1,16,2176]{2,1,0:T(8,128)(2,1)S(1)}, bf16[1,16,2176]{2,1,0:T(8,128)(2,1)S(1)}, u32[]{:S(2)}, u32[]{:S(2)}) collective-permute-start(bf16[1,16,2176]{2,1,0:T(8,128)(2,1)S(1)} %maximum_bitcast_fusion), channel_id=1, source_target_pairs={{0,12},{1,13},{2,14},{3,15},{4,8},{5,9},{6,10},{7,11},{8,4},{9,5},... | collective-permute-start | bytes 208904 | tf_op jit(solution)/shard_map/ppermute | solution.py:41
  8.8 0.0 collective-permute-start.2
  8.8 0.8 %collective-permute-start.1 = (bf16[1,16,2176]{2,1,0:T(8,128)(2,1)S(1)}, bf16[1,16,2176]{2,1,0:T(8,128)(2,1)S(1)}, u32[]{:S(2)}, u32[]{:S(2)}) collective-permute-start(bf16[1,16,2176]{2,1,0:T(8,128)(2,1)S(1)} %maximum_bitcast_fusion), channel_id=1, source_target_pairs={{0,4},{1,5},{2,6},{3,7},{4,0},{5,1},{6,2},{7,3},{8,12},{9,13},{10,... | collective-permute-start | bytes 208904 | tf_op jit(solution)/shard_map/ppermute | solution.py:41
  9.6 0.8 %constant_dynamic-update-slice_fusion.5 = bf16[8,16,2176]{2,1,0:T(8,128)(2,1)S(1)} fusion(bf16[16,128]{1,0:T(8,128)(2,1)S(1)} %fusion.77, bf16[16,2048]{1,0:T(8,128)(2,1)} %param.3), kind=kLoop, calls=%fused_computation.74 | loop fusion | flops 139263 | bytes 139264
  10.4 2.6 %multiply_reduce_fusion.1 = f32[768]{0:T(1024)S(1)} fusion(bf16[768,2048]{1,0:T(8,128)(2,1)} %param.4), kind=kLoop, calls=%fused_computation.1 | loop fusion | flops 4717824 | bytes 3148800 | tf_op jit(solution)/shard_map/reduce_sum | solution.py:124
  13.0 0.0 collective-permute-done.3
  13.0 0.0 copy-done.1
  13.0 0.1 collective-permute-start.6
  13.1 1.9 %collective-permute-done.2 = bf16[1,16,2176]{2,1,0:T(8,128)(2,1)S(1)} collective-permute-done((bf16[1,16,2176]{2,1,0:T(8,128)(2,1)S(1)}, bf16[1,16,2176]{2,1,0:T(8,128)(2,1)S(1)}, u32[]{:S(2)}, u32[]{:S(2)}) %collective-permute-start.2) | collective-permute-done | bytes 69664 | tf_op jit(solution)/shard_map/ppermute | solution.py:41
  15.0 0.0 collective-permute-done.1
  15.0 0.6 %collective-permute-start.4 = (bf16[3,16,2176]{2,1,0:T(8,128)(2,1)S(1)}, bf16[3,16,2176]{2,1,0:T(8,128)(2,1)S(1)}, u32[]{:S(2)}, u32[]{:S(2)}) collective-permute-start(bf16[3,16,2176]{2,1,0:T(8,128)(2,1)S(1)} %pad_maximum_fusion.2), channel_id=1, source_target_pairs={{0,2},{1,3},{2,0},{3,1},{4,6},{5,7},{6,4},{7,5},{8,10},{9,11},{10,... | collective-permute-start | bytes 626696 | tf_op jit(solution)/shard_map/ppermute | solution.py:41
  15.6 0.2 multiply_reduce_fusion.3
  15.8 0.0 copy-done
  15.8 1.2 %fusion.88 = (f32[64]{0:T(128)S(1)}, bf16[64,768]{1,0:T(8,128)(2,1)S(1)}) fusion(f32[768]{0:T(1024)S(1)} %multiply_reduce_fusion.1, f32[64]{0:T(128)S(1)} %multiply_reduce_fusion.3, bf16[64,2176]{1,0:T(8,128)(2,1)S(1)} %bitcast.42, bf16[768,2048]{1,0:T(8,128)(2,1)S(1)} %copy-done), kind=kOutput, calls=%fused_computation.101 | convolution fusion | flops 214253504 | bytes 3526144 | tf_op jit(solution)/shard_map/dot_general | solution.py:29
  17.1 0.0 collective-permute-done.6
  17.1 0.1 convert_element_type.52
  17.1 0.0 collective-permute-done.5
  17.1 0.7 %multiply_reduce_fusion = f32[768]{0:T(1024)S(1)} fusion(bf16[768,2048]{1,0:T(8,128)(2,1)S(1)} %collective-permute-done.5), kind=kLoop, calls=%fused_computation | loop fusion | flops 4717824 | bytes 3148800 | tf_op jit(solution)/shard_map/reduce_sum | solution.py:124
  17.8 1.2 %fusion.87 = (f32[64]{0:T(128)S(1)}, bf16[64,768]{1,0:T(8,128)(2,1)S(1)}) fusion(f32[768]{0:T(1024)S(1)} %multiply_reduce_fusion, f32[64]{0:T(128)S(1)} %multiply_reduce_fusion.3, bf16[64,2176]{1,0:T(8,128)(2,1)S(1)} %bitcast.43, bf16[768,2048]{1,0:T(8,128)(2,1)S(1)} %collective-permute-done.5), kind=kOutput, calls=%fused_computation.100 | convolution fusion | flops 214253504 | bytes 3526144 | tf_op jit(solution)/shard_map/dot_general | solution.py:29
  19.1 0.0 collective-permute-done
  19.1 2.6 %collective-permute-done.4 = bf16[3,16,2176]{2,1,0:T(8,128)(2,1)S(1)} collective-permute-done((bf16[3,16,2176]{2,1,0:T(8,128)(2,1)S(1)}, bf16[3,16,2176]{2,1,0:T(8,128)(2,1)S(1)}, u32[]{:S(2)}, u32[]{:S(2)}) %collective-permute-start.4) | collective-permute-done | bytes 208928 | tf_op jit(solution)/shard_map/ppermute | solution.py:41
  21.7 0.2 multiply_reduce_fusion.2
  21.8 1.2 %fusion.86 = (bf16[64,768]{1,0:T(8,128)(2,1)S(1)}, f32[64]{0:T(128)S(1)}) fusion(f32[768]{0:T(1024)S(1)} %multiply_reduce_fusion.1, f32[64]{0:T(128)S(1)} %multiply_reduce_fusion.2, bf16[64,2176]{1,0:T(8,128)(2,1)S(1)} %bitcast.45, bf16[768,2048]{1,0:T(8,128)(2,1)S(1)} %copy-done), kind=kOutput, calls=%fused_computation.99 | convolution fusion | flops 214253504 | bytes 3526144 | tf_op jit(solution)/shard_map/dot_general | solution.py:29
  23.1 1.2 %fusion.85 = (bf16[64,768]{1,0:T(8,128)(2,1)S(1)}, f32[64]{0:T(128)S(1)}) fusion(f32[768]{0:T(1024)S(1)} %multiply_reduce_fusion, f32[64]{0:T(128)S(1)} %multiply_reduce_fusion.2, bf16[64,2176]{1,0:T(8,128)(2,1)S(1)} %bitcast.46, bf16[768,2048]{1,0:T(8,128)(2,1)S(1)} %collective-permute-done.5), kind=kOutput, calls=%fused_computation.98 | convolution fusion | flops 214253504 | bytes 3526144 | tf_op jit(solution)/shard_map/dot_general | solution.py:29
  24.4 0.1 collective-permute-start.7
  24.5 0.1 pad_maximum_fusion.5
  24.6 1.1 %collective-permute-done.7 = f32[512]{0:T(512)S(1)} collective-permute-done((f32[512]{0:T(512)S(1)}, f32[512]{0:T(512)S(1)}, u32[]{:S(2)}, u32[]{:S(2)}) %collective-permute-start.7) | collective-permute-done | bytes 2080 | tf_op jit(solution)/shard_map/ppermute | solution.py:41
  25.6 0.2 fusion.11
  25.9 0.2 convolution_add_fusion
  26.1 0.1 broadcast_in_dim.5
  26.3 2.8 %collective-permute-start.10 = (f32[2,16,384]{2,1,0:T(8,128)S(1)}, f32[2,16,384]{2,1,0:T(8,128)S(1)}, u32[]{:S(2)}, u32[]{:S(2)}) collective-permute-start(f32[2,16,384]{2,1,0:T(8,128)S(1)} %get-tuple-element.22), channel_id=1, source_target_pairs={{0,12},{1,13},{2,14},{3,15},{4,8},{5,9},{6,10},{7,11},{8,4},{9,5},... | collective-permute-start | bytes 147464 | tf_op jit(solution)/shard_map/ppermute | solution.py:41
  29.1 0.0 collective-permute-start.9
  29.1 1.7 %collective-permute-start.8 = (f32[2,16,384]{2,1,0:T(8,128)S(1)}, f32[2,16,384]{2,1,0:T(8,128)S(1)}, u32[]{:S(2)}, u32[]{:S(2)}) collective-permute-start(f32[2,16,384]{2,1,0:T(8,128)S(1)} %get-tuple-element.21), channel_id=1, source_target_pairs={{0,4},{1,5},{2,6},{3,7},{4,0},{5,1},{6,2},{7,3},{8,12},{9,13},{10,... | collective-permute-start | bytes 147464 | tf_op jit(solution)/shard_map/ppermute | solution.py:41
  30.7 1.9 %collective-permute-done.10 = f32[2,16,384]{2,1,0:T(8,128)S(1)} collective-permute-done((f32[2,16,384]{2,1,0:T(8,128)S(1)}, f32[2,16,384]{2,1,0:T(8,128)S(1)}, u32[]{:S(2)}, u32[]{:S(2)}) %collective-permute-start.10) | collective-permute-done | bytes 49184 | tf_op jit(solution)/shard_map/ppermute | solution.py:41
  32.6 1.5 %collective-permute-done.9 = f32[2,16,384]{2,1,0:T(8,128)S(1)} collective-permute-done((f32[2,16,384]{2,1,0:T(8,128)S(1)}, f32[2,16,384]{2,1,0:T(8,128)S(1)}, u32[]{:S(2)}, u32[]{:S(2)}) %collective-permute-start.9) | collective-permute-done | bytes 49184 | tf_op jit(solution)/shard_map/ppermute | solution.py:41
  34.1 0.1 collective-permute-done.8
  34.2 0.6 %collective-permute-start.11 = (f32[16,384]{1,0:T(8,128)S(1)}, f32[16,384]{1,0:T(8,128)S(1)}, u32[]{:S(2)}, u32[]{:S(2)}) collective-permute-start(f32[16,384]{1,0:T(8,128)S(1)} %slice_bitcast_fusion.4), channel_id=1, source_target_pairs={{0,2},{1,3},{2,0},{3,1},{4,6},{5,7},{6,4},{7,5},{8,10},{9,11},{10,... | collective-permute-start | bytes 73736 | tf_op jit(solution)/shard_map/ppermute | solution.py:41
  34.8 3.3 %collective-permute-done.11 = f32[16,384]{1,0:T(8,128)S(1)} collective-permute-done((f32[16,384]{1,0:T(8,128)S(1)}, f32[16,384]{1,0:T(8,128)S(1)}, u32[]{:S(2)}, u32[]{:S(2)}) %collective-permute-start.11) | collective-permute-done | bytes 24608 | tf_op jit(solution)/shard_map/ppermute | solution.py:41
  38.1 0.1 slice_reduce_fusion
  38.3 0.7 %slice_divide_fusion = f32[16,256]{1,0:T(8,128)} fusion(f32[16,384]{1,0:T(8,128)S(1)} %fusion.70, f32[16]{0:T(128)S(1)} %slice_reduce_fusion), kind=kLoop, calls=%fused_computation.65 | loop fusion | flops 4096 | bytes 32832 | tf_op jit(solution)/shard_map/div | solution.py:149
  (23 shorter events, 0.4 us)
Async XLA Ops:
  0.0 15.8 %copy-start = (bf16[768,2048]{1,0:T(8,128)(2,1)S(1)}, bf16[768,2048]{1,0:T(8,128)(2,1)}, u32[]{:S(2)}) copy-start(bf16[768,2048]{1,0:T(8,128)(2,1)} %param.4) | copy-start | bytes 9437188
  0.0 13.0 %copy-start.1 = (bf16[768,256]{1,0:T(8,128)(2,1)S(1)}, bf16[768,256]{1,0:T(8,128)(2,1)}, u32[]{:S(2)}) copy-start(bf16[768,256]{1,0:T(8,128)(2,1)} %param.5) | copy-start | bytes 1179652
  0.0 17.1 %collective-permute-start.5 = (bf16[768,2048]{1,0:T(8,128)(2,1)}, bf16[768,2048]{1,0:T(8,128)(2,1)S(1)}, u32[]{:S(2)}, u32[]{:S(2)}) collective-permute-start(bf16[768,2048]{1,0:T(8,128)(2,1)} %param.4), channel_id=1, source_target_pairs={{0,1},{1,0},{2,3},{3,2},{4,5},{5,4},{6,7},{7,6},{8,9},{9,8},{10,11... | collective-permute-start | bytes 9437192 | tf_op jit(solution)/shard_map/ppermute | solution.py:41
  2.5 16.5 %collective-permute-start = (bf16[1,16,2176]{2,1,0:T(8,128)(2,1)S(1)}, bf16[1,16,2176]{2,1,0:T(8,128)(2,1)S(1)}, u32[]{:S(2)}, u32[]{:S(2)}) collective-permute-start(bf16[1,16,2176]{2,1,0:T(8,128)(2,1)S(1)} %maximum_bitcast_fusion), channel_id=1, source_target_pairs={{0,2},{1,3},{2,0},{3,1},{4,6},{5,7},{6,4},{7,5},{8,10},{9,11},{10,... | collective-permute-start | bytes 208904 | tf_op jit(solution)/shard_map/ppermute | solution.py:41
  5.2 7.8 %collective-permute-start.3 = (bf16[1,16,2176]{2,1,0:T(8,128)(2,1)S(1)}, bf16[1,16,2176]{2,1,0:T(8,128)(2,1)S(1)}, u32[]{:S(2)}, u32[]{:S(2)}) collective-permute-start(bf16[1,16,2176]{2,1,0:T(8,128)(2,1)S(1)} %maximum_bitcast_fusion), channel_id=1, source_target_pairs={{0,12},{1,13},{2,14},{3,15},{4,8},{5,9},{6,10},{7,11},{8,4},{9,5},... | collective-permute-start | bytes 208904 | tf_op jit(solution)/shard_map/ppermute | solution.py:41
  8.8 6.2 %collective-permute-start.2 = (bf16[1,16,2176]{2,1,0:T(8,128)(2,1)S(1)}, bf16[1,16,2176]{2,1,0:T(8,128)(2,1)S(1)}, u32[]{:S(2)}, u32[]{:S(2)}) collective-permute-start(bf16[1,16,2176]{2,1,0:T(8,128)(2,1)S(1)} %maximum_bitcast_fusion), channel_id=1, source_target_pairs={{0,8},{1,9},{2,10},{3,11},{4,12},{5,13},{6,14},{7,15},{8,0},{9,1},... | collective-permute-start | bytes 208904 | tf_op jit(solution)/shard_map/ppermute | solution.py:41
  8.8 6.2 %collective-permute-start.1 = (bf16[1,16,2176]{2,1,0:T(8,128)(2,1)S(1)}, bf16[1,16,2176]{2,1,0:T(8,128)(2,1)S(1)}, u32[]{:S(2)}, u32[]{:S(2)}) collective-permute-start(bf16[1,16,2176]{2,1,0:T(8,128)(2,1)S(1)} %maximum_bitcast_fusion), channel_id=1, source_target_pairs={{0,4},{1,5},{2,6},{3,7},{4,0},{5,1},{6,2},{7,3},{8,12},{9,13},{10,... | collective-permute-start | bytes 208904 | tf_op jit(solution)/shard_map/ppermute | solution.py:41
  13.0 4.0 %collective-permute-start.6 = (bf16[768,256]{1,0:T(8,128)(2,1)S(1)}, bf16[768,256]{1,0:T(8,128)(2,1)S(1)}, u32[]{:S(2)}, u32[]{:S(2)}) collective-permute-start(bf16[768,256]{1,0:T(8,128)(2,1)S(1)} %copy-done.1), channel_id=1, source_target_pairs={{0,1},{1,0},{2,3},{3,2},{4,5},{5,4},{6,7},{7,6},{8,9},{9,8},{10,11... | collective-permute-start | bytes 1179656 | tf_op jit(solution)/shard_map/ppermute | solution.py:41
  15.0 6.6 %collective-permute-start.4 = (bf16[3,16,2176]{2,1,0:T(8,128)(2,1)S(1)}, bf16[3,16,2176]{2,1,0:T(8,128)(2,1)S(1)}, u32[]{:S(2)}, u32[]{:S(2)}) collective-permute-start(bf16[3,16,2176]{2,1,0:T(8,128)(2,1)S(1)} %pad_maximum_fusion.2), channel_id=1, source_target_pairs={{0,2},{1,3},{2,0},{3,1},{4,6},{5,7},{6,4},{7,5},{8,10},{9,11},{10,... | collective-permute-start | bytes 626696 | tf_op jit(solution)/shard_map/ppermute | solution.py:41
  24.4 1.2 %collective-permute-start.7 = (f32[512]{0:T(512)S(1)}, f32[512]{0:T(512)S(1)}, u32[]{:S(2)}, u32[]{:S(2)}) collective-permute-start(f32[512]{0:T(512)S(1)} %fusion.71), channel_id=1, source_target_pairs={{0,1},{1,0},{2,3},{3,2},{4,5},{5,4},{6,7},{7,6},{8,9},{9,8},{10,11... | collective-permute-start | bytes 6152 | tf_op jit(solution)/shard_map/ppermute | solution.py:41
  26.3 6.3 %collective-permute-start.10 = (f32[2,16,384]{2,1,0:T(8,128)S(1)}, f32[2,16,384]{2,1,0:T(8,128)S(1)}, u32[]{:S(2)}, u32[]{:S(2)}) collective-permute-start(f32[2,16,384]{2,1,0:T(8,128)S(1)} %get-tuple-element.22), channel_id=1, source_target_pairs={{0,12},{1,13},{2,14},{3,15},{4,8},{5,9},{6,10},{7,11},{8,4},{9,5},... | collective-permute-start | bytes 147464 | tf_op jit(solution)/shard_map/ppermute | solution.py:41
  29.1 5.0 %collective-permute-start.9 = (f32[2,16,384]{2,1,0:T(8,128)S(1)}, f32[2,16,384]{2,1,0:T(8,128)S(1)}, u32[]{:S(2)}, u32[]{:S(2)}) collective-permute-start(f32[2,16,384]{2,1,0:T(8,128)S(1)} %get-tuple-element.23), channel_id=1, source_target_pairs={{0,8},{1,9},{2,10},{3,11},{4,12},{5,13},{6,14},{7,15},{8,0},{9,1},... | collective-permute-start | bytes 147464 | tf_op jit(solution)/shard_map/ppermute | solution.py:41
  29.1 5.1 %collective-permute-start.8 = (f32[2,16,384]{2,1,0:T(8,128)S(1)}, f32[2,16,384]{2,1,0:T(8,128)S(1)}, u32[]{:S(2)}, u32[]{:S(2)}) collective-permute-start(f32[2,16,384]{2,1,0:T(8,128)S(1)} %get-tuple-element.21), channel_id=1, source_target_pairs={{0,4},{1,5},{2,6},{3,7},{4,0},{5,1},{6,2},{7,3},{8,12},{9,13},{10,... | collective-permute-start | bytes 147464 | tf_op jit(solution)/shard_map/ppermute | solution.py:41
  34.2 3.9 %collective-permute-start.11 = (f32[16,384]{1,0:T(8,128)S(1)}, f32[16,384]{1,0:T(8,128)S(1)}, u32[]{:S(2)}, u32[]{:S(2)}) collective-permute-start(f32[16,384]{1,0:T(8,128)S(1)} %slice_bitcast_fusion.4), channel_id=1, source_target_pairs={{0,2},{1,3},{2,0},{3,1},{4,6},{5,7},{6,4},{7,5},{8,10},{9,11},{10,... | collective-permute-start | bytes 73736 | tf_op jit(solution)/shard_map/ppermute | solution.py:41

commit v27 on v21

--- a/solution.py
+++ b/solution.py
@@ -139,13 +139,13 @@
         weight_b = jnp.concatenate([p[0][k] for p in parts], axis=0)
         numer = numer + jnp.dot(weight_b, zvals, preferred_element_type=jnp.float32)
     denom = jnp.concatenate([p[1] for p in parts], axis=0)
-    den = jnp.broadcast_to(denom[:, None], (denom.shape[0], 128))
-    sums = jnp.concatenate([numer, den], axis=1).reshape(lineage, q_dev, width + 128)
+    den = jnp.broadcast_to(denom[:, None], (denom.shape[0], width))
+    sums = jnp.concatenate([numer, den], axis=1).reshape(lineage, q_dev, 2 * width)
     sums = sums.reshape(tuple(len(offsets(g)) for g in groups) + sums.shape[1:])
     order = list(range(1, len(groups))) + [0]
     sums = jnp.transpose(sums, order + list(range(len(groups), sums.ndim)))
     mine = scatter_rounds(sums, "blk", [groups[k] for k in order])
-    return mine[:, :width] / mine[:, width:width + 1]
+    return mine[:, :width] / mine[:, width:]
 
 
 def solution(mesh):

time: 38.4 us -> 39.3 us (1.023)
  waiting for transfers between devices: 11.6 us -> 12.7 us
    ppermute x12, waiting for transfers between devices: 11.6 us -> 12.7 us  [swap(): return lax.ppermute(x, axis, [(i, i ^ mask) for i in range(count)])]
  transfers between devices with their start and end apart: 12 -> 12, of which waited for: 5 -> 5; matrix products, arithmetic and copies ran while one was open for 31% -> 30% of each run, Pallas kernels for 0% -> 0%
where the time goes in v27:
time: 39.3 us; the launch traced here: 39.1 us
  starting transfers between devices  13.3 us (34%)
  waiting for transfers between devices  12.7 us (32%)
  other arithmetic  7.32 us (19%)
  matrix products  5.37 us (14%)
    ppermute x12, starting transfers between devices, swap(): return lax.ppermute(x, axis, [(i, i ^ mask) for i in range(count)])  13.3 us
    ppermute x12, waiting for transfers between devices, swap(): return lax.ppermute(x, axis, [(i, i ^ mask) for i in range(count)])  12.7 us
    dot_general x4, matrix products, piece_weights(): lax.dot_general(rows, lib_ext, (((1,), (1,)), ((), ())), preferred_elemen...  4.87 us
    reduce_sum x2, other arithmetic, shards(): jnp.sum(jnp.square(lib.astype(jnp.float32)), axis=1)  3.25 us
    reduce_sum x1, other arithmetic, shards(): jnp.sum(values, axis=0)  1.14 us
    unnamed x2, other arithmetic  0.85 us
    broadcast_in_dim x1, other arithmetic, gather_rounds(): pieces = [packet[None]]  0.85 us
  transfers between devices with their start and end apart: 12, of which 5 were waited for; matrix products, arithmetic and copies ran while one was open for 30% of the time, Pallas kernels for 0%

profile of v27, /device:TPU:0, one launch (start us, length us, event | category | flops | bytes accessed | tf_op | source)
XLA Modules:
  0.0 39.1 jit_solution(15060814054731474979)
XLA Ops:
  0.0 0.0 copy-start
  0.0 0.0 copy-start.1
  0.0 0.5 %collective-permute-start.5 = (bf16[768,2048]{1,0:T(8,128)(2,1)}, bf16[768,2048]{1,0:T(8,128)(2,1)S(1)}, u32[]{:S(2)}, u32[]{:S(2)}) collective-permute-start(bf16[768,2048]{1,0:T(8,128)(2,1)} %param.4), channel_id=1, source_target_pairs={{0,1},{1,0},{2,3},{3,2},{4,5},{5,4},{6,7},{7,6},{8,9},{9,8},{10,11... | collective-permute-start | bytes 9437192 | tf_op jit(solution)/shard_map/ppermute | solution.py:41
  0.5 1.1 %convert_reduce_fusion = (f32[256]{0:T(256)S(1)}, f32[256]{0:T(256)S(1)}) fusion(bf16[768,256]{1,0:T(8,128)(2,1)} %param.5), kind=kLoop, calls=%fused_computation.12 | loop fusion | flops 785920 | bytes 395264 | tf_op jit(solution)/shard_map/reduce_sum | solution.py:112
  1.7 0.8 %maximum_bitcast_fusion = bf16[1,16,2176]{2,1,0:T(8,128)(2,1)S(1)} fusion(bf16[16,128]{1,0:T(8,128)(2,1)S(1)} %fusion.77, bf16[16,2048]{1,0:T(8,128)(2,1)} %param.3), kind=kLoop, calls=%fused_computation.52 | loop fusion | flops 139264 | bytes 139264 | tf_op jit(solution)/shard_map/broadcast_in_dim | solution.py:70
  2.5 2.7 %collective-permute-start = (bf16[1,16,2176]{2,1,0:T(8,128)(2,1)S(1)}, bf16[1,16,2176]{2,1,0:T(8,128)(2,1)S(1)}, u32[]{:S(2)}, u32[]{:S(2)}) collective-permute-start(bf16[1,16,2176]{2,1,0:T(8,128)(2,1)S(1)} %maximum_bitcast_fusion), channel_id=1, source_target_pairs={{0,2},{1,3},{2,0},{3,1},{4,6},{5,7},{6,4},{7,5},{8,10},{9,11},{10,... | collective-permute-start | bytes 208904 | tf_op jit(solution)/shard_map/ppermute | solution.py:41
  5.2 3.6 %collective-permute-start.3 = (bf16[1,16,2176]{2,1,0:T(8,128)(2,1)S(1)}, bf16[1,16,2176]{2,1,0:T(8,128)(2,1)S(1)}, u32[]{:S(2)}, u32[]{:S(2)}) collective-permute-start(bf16[1,16,2176]{2,1,0:T(8,128)(2,1)S(1)} %maximum_bitcast_fusion), channel_id=1, source_target_pairs={{0,12},{1,13},{2,14},{3,15},{4,8},{5,9},{6,10},{7,11},{8,4},{9,5},... | collective-permute-start | bytes 208904 | tf_op jit(solution)/shard_map/ppermute | solution.py:41
  8.8 0.0 collective-permute-start.2
  8.8 0.8 %collective-permute-start.1 = (bf16[1,16,2176]{2,1,0:T(8,128)(2,1)S(1)}, bf16[1,16,2176]{2,1,0:T(8,128)(2,1)S(1)}, u32[]{:S(2)}, u32[]{:S(2)}) collective-permute-start(bf16[1,16,2176]{2,1,0:T(8,128)(2,1)S(1)} %maximum_bitcast_fusion), channel_id=1, source_target_pairs={{0,4},{1,5},{2,6},{3,7},{4,0},{5,1},{6,2},{7,3},{8,12},{9,13},{10,... | collective-permute-start | bytes 208904 | tf_op jit(solution)/shard_map/ppermute | solution.py:41
  9.6 0.8 %constant_dynamic-update-slice_fusion.5 = bf16[8,16,2176]{2,1,0:T(8,128)(2,1)S(1)} fusion(bf16[16,128]{1,0:T(8,128)(2,1)S(1)} %fusion.77, bf16[16,2048]{1,0:T(8,128)(2,1)} %param.3), kind=kLoop, calls=%fused_computation.74 | loop fusion | flops 139263 | bytes 139264
  10.4 2.6 %multiply_reduce_fusion.1 = f32[768]{0:T(1024)S(1)} fusion(bf16[768,2048]{1,0:T(8,128)(2,1)} %param.4), kind=kLoop, calls=%fused_computation.1 | loop fusion | flops 4717824 | bytes 3148800 | tf_op jit(solution)/shard_map/reduce_sum | solution.py:123
  13.0 0.0 collective-permute-done.3
  13.0 0.0 copy-done.1
  13.0 0.1 collective-permute-start.7
  13.1 1.9 %collective-permute-done.2 = bf16[1,16,2176]{2,1,0:T(8,128)(2,1)S(1)} collective-permute-done((bf16[1,16,2176]{2,1,0:T(8,128)(2,1)S(1)}, bf16[1,16,2176]{2,1,0:T(8,128)(2,1)S(1)}, u32[]{:S(2)}, u32[]{:S(2)}) %collective-permute-start.2) | collective-permute-done | bytes 69664 | tf_op jit(solution)/shard_map/ppermute | solution.py:41
  15.0 0.0 collective-permute-done.1
  15.0 0.6 %collective-permute-start.4 = (bf16[3,16,2176]{2,1,0:T(8,128)(2,1)S(1)}, bf16[3,16,2176]{2,1,0:T(8,128)(2,1)S(1)}, u32[]{:S(2)}, u32[]{:S(2)}) collective-permute-start(bf16[3,16,2176]{2,1,0:T(8,128)(2,1)S(1)} %pad_maximum_fusion.3), channel_id=1, source_target_pairs={{0,2},{1,3},{2,0},{3,1},{4,6},{5,7},{6,4},{7,5},{8,10},{9,11},{10,... | collective-permute-start | bytes 626696 | tf_op jit(solution)/shard_map/ppermute | solution.py:41
  15.6 0.2 multiply_reduce_fusion.3
  15.8 0.0 copy-done
  15.8 1.2 %fusion.88 = (f32[64]{0:T(128)S(1)}, bf16[64,768]{1,0:T(8,128)(2,1)S(1)}) fusion(f32[768]{0:T(1024)S(1)} %multiply_reduce_fusion.1, f32[64]{0:T(128)S(1)} %multiply_reduce_fusion.3, bf16[64,2176]{1,0:T(8,128)(2,1)S(1)} %bitcast.45, bf16[768,2048]{1,0:T(8,128)(2,1)S(1)} %copy-done), kind=kOutput, calls=%fused_computation.100 | convolution fusion | flops 214253504 | bytes 3526144 | tf_op jit(solution)/shard_map/dot_general | solution.py:29
  17.1 0.0 collective-permute-done.5
  17.1 0.7 %multiply_reduce_fusion = f32[768]{0:T(1024)S(1)} fusion(bf16[768,2048]{1,0:T(8,128)(2,1)S(1)} %collective-permute-done.5), kind=kLoop, calls=%fused_computation | loop fusion | flops 4717824 | bytes 3148800 | tf_op jit(solution)/shard_map/reduce_sum | solution.py:123
  17.8 1.2 %fusion.87 = (f32[64]{0:T(128)S(1)}, bf16[64,768]{1,0:T(8,128)(2,1)S(1)}) fusion(f32[768]{0:T(1024)S(1)} %multiply_reduce_fusion, f32[64]{0:T(128)S(1)} %multiply_reduce_fusion.3, bf16[64,2176]{1,0:T(8,128)(2,1)S(1)} %bitcast.46, bf16[768,2048]{1,0:T(8,128)(2,1)S(1)} %collective-permute-done.5), kind=kOutput, calls=%fused_computation.99 | convolution fusion | flops 214253504 | bytes 3526144 | tf_op jit(solution)/shard_map/dot_general | solution.py:29
  19.0 0.0 collective-permute-done
  19.0 2.7 %collective-permute-done.4 = bf16[3,16,2176]{2,1,0:T(8,128)(2,1)S(1)} collective-permute-done((bf16[3,16,2176]{2,1,0:T(8,128)(2,1)S(1)}, bf16[3,16,2176]{2,1,0:T(8,128)(2,1)S(1)}, u32[]{:S(2)}, u32[]{:S(2)}) %collective-permute-start.4) | collective-permute-done | bytes 208928 | tf_op jit(solution)/shard_map/ppermute | solution.py:41
  21.7 0.2 multiply_reduce_fusion.2
  21.8 1.2 %fusion.86 = (bf16[64,768]{1,0:T(8,128)(2,1)S(1)}, f32[64]{0:T(128)S(1)}) fusion(f32[768]{0:T(1024)S(1)} %multiply_reduce_fusion.1, f32[64]{0:T(128)S(1)} %multiply_reduce_fusion.2, bf16[64,2176]{1,0:T(8,128)(2,1)S(1)} %bitcast.42, bf16[768,2048]{1,0:T(8,128)(2,1)S(1)} %copy-done), kind=kOutput, calls=%fused_computation.98 | convolution fusion | flops 214253504 | bytes 3526144 | tf_op jit(solution)/shard_map/dot_general | solution.py:29
  23.2 0.1 collective-permute-start.6
  23.3 1.2 %fusion.85 = (bf16[64,768]{1,0:T(8,128)(2,1)S(1)}, f32[64]{0:T(128)S(1)}) fusion(f32[768]{0:T(1024)S(1)} %multiply_reduce_fusion, f32[64]{0:T(128)S(1)} %multiply_reduce_fusion.2, bf16[64,2176]{1,0:T(8,128)(2,1)S(1)} %bitcast.43, bf16[768,2048]{1,0:T(8,128)(2,1)S(1)} %collective-permute-done.5), kind=kOutput, calls=%fused_computation.97 | convolution fusion | flops 214253504 | bytes 3526144 | tf_op jit(solution)/shard_map/dot_general | solution.py:29
  24.5 0.1 pad_maximum_fusion.5
  24.6 0.0 collective-permute-done.6
  24.6 0.3 fusion.11
  24.8 0.0 collective-permute-done.7
  24.9 0.2 convolution_add_fusion
  25.1 0.1 broadcast_in_dim.5
  25.3 2.8 %collective-permute-start.10 = (f32[2,16,512]{2,1,0:T(8,128)S(1)}, f32[2,16,512]{2,1,0:T(8,128)S(1)}, u32[]{:S(2)}, u32[]{:S(2)}) collective-permute-start(f32[2,16,512]{2,1,0:T(8,128)S(1)} %get-tuple-element.18), channel_id=1, source_target_pairs={{0,12},{1,13},{2,14},{3,15},{4,8},{5,9},{6,10},{7,11},{8,4},{9,5},... | collective-permute-start | bytes 196616 | tf_op jit(solution)/shard_map/ppermute | solution.py:41
  28.1 0.0 collective-permute-start.9
  28.1 1.7 %collective-permute-start.8 = (f32[2,16,512]{2,1,0:T(8,128)S(1)}, f32[2,16,512]{2,1,0:T(8,128)S(1)}, u32[]{:S(2)}, u32[]{:S(2)}) collective-permute-start(f32[2,16,512]{2,1,0:T(8,128)S(1)} %get-tuple-element.17), channel_id=1, source_target_pairs={{0,4},{1,5},{2,6},{3,7},{4,0},{5,1},{6,2},{7,3},{8,12},{9,13},{10,... | collective-permute-start | bytes 196616 | tf_op jit(solution)/shard_map/ppermute | solution.py:41
  29.7 2.4 %collective-permute-done.10 = f32[2,16,512]{2,1,0:T(8,128)S(1)} collective-permute-done((f32[2,16,512]{2,1,0:T(8,128)S(1)}, f32[2,16,512]{2,1,0:T(8,128)S(1)}, u32[]{:S(2)}, u32[]{:S(2)}) %collective-permute-start.10) | collective-permute-done | bytes 65568 | tf_op jit(solution)/shard_map/ppermute | solution.py:41
  32.1 2.3 %collective-permute-done.9 = f32[2,16,512]{2,1,0:T(8,128)S(1)} collective-permute-done((f32[2,16,512]{2,1,0:T(8,128)S(1)}, f32[2,16,512]{2,1,0:T(8,128)S(1)}, u32[]{:S(2)}, u32[]{:S(2)}) %collective-permute-start.9) | collective-permute-done | bytes 65568 | tf_op jit(solution)/shard_map/ppermute | solution.py:41
  34.4 0.0 collective-permute-done.8
  34.5 0.6 %collective-permute-start.11 = (f32[16,512]{1,0:T(8,128)S(1)}, f32[16,512]{1,0:T(8,128)S(1)}, u32[]{:S(2)}, u32[]{:S(2)}) collective-permute-start(f32[16,512]{1,0:T(8,128)S(1)} %slice_bitcast_fusion.4), channel_id=1, source_target_pairs={{0,2},{1,3},{2,0},{3,1},{4,6},{5,7},{6,4},{7,5},{8,10},{9,11},{10,... | collective-permute-start | bytes 98312 | tf_op jit(solution)/shard_map/ppermute | solution.py:41
  35.0 3.4 %collective-permute-done.11 = f32[16,512]{1,0:T(8,128)S(1)} collective-permute-done((f32[16,512]{1,0:T(8,128)S(1)}, f32[16,512]{1,0:T(8,128)S(1)}, u32[]{:S(2)}, u32[]{:S(2)}) %collective-permute-start.11) | collective-permute-done | bytes 32800 | tf_op jit(solution)/shard_map/ppermute | solution.py:41
  38.5 0.6 %slice_divide_fusion = f32[16,256]{1,0:T(8,128)} fusion(f32[16,512]{1,0:T(8,128)S(1)} %fusion.70), kind=kLoop, calls=%fused_computation.65 | loop fusion | flops 4096 | bytes 49152 | tf_op jit(solution)/shard_map/div | solution.py:148
  (23 shorter events, 0.4 us)
Async XLA Ops:
  0.0 15.8 %copy-start = (bf16[768,2048]{1,0:T(8,128)(2,1)S(1)}, bf16[768,2048]{1,0:T(8,128)(2,1)}, u32[]{:S(2)}) copy-start(bf16[768,2048]{1,0:T(8,128)(2,1)} %param.4) | copy-start | bytes 9437188
  0.0 13.0 %copy-start.1 = (bf16[768,256]{1,0:T(8,128)(2,1)S(1)}, bf16[768,256]{1,0:T(8,128)(2,1)}, u32[]{:S(2)}) copy-start(bf16[768,256]{1,0:T(8,128)(2,1)} %param.5) | copy-start | bytes 1179652
  0.0 17.1 %collective-permute-start.5 = (bf16[768,2048]{1,0:T(8,128)(2,1)}, bf16[768,2048]{1,0:T(8,128)(2,1)S(1)}, u32[]{:S(2)}, u32[]{:S(2)}) collective-permute-start(bf16[768,2048]{1,0:T(8,128)(2,1)} %param.4), channel_id=1, source_target_pairs={{0,1},{1,0},{2,3},{3,2},{4,5},{5,4},{6,7},{7,6},{8,9},{9,8},{10,11... | collective-permute-start | bytes 9437192 | tf_op jit(solution)/shard_map/ppermute | solution.py:41
  2.5 16.5 %collective-permute-start = (bf16[1,16,2176]{2,1,0:T(8,128)(2,1)S(1)}, bf16[1,16,2176]{2,1,0:T(8,128)(2,1)S(1)}, u32[]{:S(2)}, u32[]{:S(2)}) collective-permute-start(bf16[1,16,2176]{2,1,0:T(8,128)(2,1)S(1)} %maximum_bitcast_fusion), channel_id=1, source_target_pairs={{0,2},{1,3},{2,0},{3,1},{4,6},{5,7},{6,4},{7,5},{8,10},{9,11},{10,... | collective-permute-start | bytes 208904 | tf_op jit(solution)/shard_map/ppermute | solution.py:41
  5.2 7.8 %collective-permute-start.3 = (bf16[1,16,2176]{2,1,0:T(8,128)(2,1)S(1)}, bf16[1,16,2176]{2,1,0:T(8,128)(2,1)S(1)}, u32[]{:S(2)}, u32[]{:S(2)}) collective-permute-start(bf16[1,16,2176]{2,1,0:T(8,128)(2,1)S(1)} %maximum_bitcast_fusion), channel_id=1, source_target_pairs={{0,12},{1,13},{2,14},{3,15},{4,8},{5,9},{6,10},{7,11},{8,4},{9,5},... | collective-permute-start | bytes 208904 | tf_op jit(solution)/shard_map/ppermute | solution.py:41
  8.8 6.2 %collective-permute-start.2 = (bf16[1,16,2176]{2,1,0:T(8,128)(2,1)S(1)}, bf16[1,16,2176]{2,1,0:T(8,128)(2,1)S(1)}, u32[]{:S(2)}, u32[]{:S(2)}) collective-permute-start(bf16[1,16,2176]{2,1,0:T(8,128)(2,1)S(1)} %maximum_bitcast_fusion), channel_id=1, source_target_pairs={{0,8},{1,9},{2,10},{3,11},{4,12},{5,13},{6,14},{7,15},{8,0},{9,1},... | collective-permute-start | bytes 208904 | tf_op jit(solution)/shard_map/ppermute | solution.py:41
  8.8 6.2 %collective-permute-start.1 = (bf16[1,16,2176]{2,1,0:T(8,128)(2,1)S(1)}, bf16[1,16,2176]{2,1,0:T(8,128)(2,1)S(1)}, u32[]{:S(2)}, u32[]{:S(2)}) collective-permute-start(bf16[1,16,2176]{2,1,0:T(8,128)(2,1)S(1)} %maximum_bitcast_fusion), channel_id=1, source_target_pairs={{0,4},{1,5},{2,6},{3,7},{4,0},{5,1},{6,2},{7,3},{8,12},{9,13},{10,... | collective-permute-start | bytes 208904 | tf_op jit(solution)/shard_map/ppermute | solution.py:41
  13.0 11.8 %collective-permute-start.7 = (bf16[768,256]{1,0:T(8,128)(2,1)S(1)}, bf16[768,256]{1,0:T(8,128)(2,1)S(1)}, u32[]{:S(2)}, u32[]{:S(2)}) collective-permute-start(bf16[768,256]{1,0:T(8,128)(2,1)S(1)} %copy-done.1), channel_id=1, source_target_pairs={{0,1},{1,0},{2,3},{3,2},{4,5},{5,4},{6,7},{7,6},{8,9},{9,8},{10,11... | collective-permute-start | bytes 1179656 | tf_op jit(solution)/shard_map/ppermute | solution.py:41
  15.0 6.6 %collective-permute-start.4 = (bf16[3,16,2176]{2,1,0:T(8,128)(2,1)S(1)}, bf16[3,16,2176]{2,1,0:T(8,128)(2,1)S(1)}, u32[]{:S(2)}, u32[]{:S(2)}) collective-permute-start(bf16[3,16,2176]{2,1,0:T(8,128)(2,1)S(1)} %pad_maximum_fusion.3), channel_id=1, source_target_pairs={{0,2},{1,3},{2,0},{3,1},{4,6},{5,7},{6,4},{7,5},{8,10},{9,11},{10,... | collective-permute-start | bytes 626696 | tf_op jit(solution)/shard_map/ppermute | solution.py:41
  23.2 1.4 %collective-permute-start.6 = (f32[512]{0:T(512)S(1)}, f32[512]{0:T(512)S(1)}, u32[]{:S(2)}, u32[]{:S(2)}) collective-permute-start(f32[512]{0:T(512)S(1)} %fusion.71), channel_id=1, source_target_pairs={{0,1},{1,0},{2,3},{3,2},{4,5},{5,4},{6,7},{7,6},{8,9},{9,8},{10,11... | collective-permute-start | bytes 6152 | tf_op jit(solution)/shard_map/ppermute | solution.py:41
  25.3 6.9 %collective-permute-start.10 = (f32[2,16,512]{2,1,0:T(8,128)S(1)}, f32[2,16,512]{2,1,0:T(8,128)S(1)}, u32[]{:S(2)}, u32[]{:S(2)}) collective-permute-start(f32[2,16,512]{2,1,0:T(8,128)S(1)} %get-tuple-element.18), channel_id=1, source_target_pairs={{0,12},{1,13},{2,14},{3,15},{4,8},{5,9},{6,10},{7,11},{8,4},{9,5},... | collective-permute-start | bytes 196616 | tf_op jit(solution)/shard_map/ppermute | solution.py:41
  28.1 6.4 %collective-permute-start.9 = (f32[2,16,512]{2,1,0:T(8,128)S(1)}, f32[2,16,512]{2,1,0:T(8,128)S(1)}, u32[]{:S(2)}, u32[]{:S(2)}) collective-permute-start(f32[2,16,512]{2,1,0:T(8,128)S(1)} %get-tuple-element.19), channel_id=1, source_target_pairs={{0,8},{1,9},{2,10},{3,11},{4,12},{5,13},{6,14},{7,15},{8,0},{9,1},... | collective-permute-start | bytes 196616 | tf_op jit(solution)/shard_map/ppermute | solution.py:41
  28.1 6.4 %collective-permute-start.8 = (f32[2,16,512]{2,1,0:T(8,128)S(1)}, f32[2,16,512]{2,1,0:T(8,128)S(1)}, u32[]{:S(2)}, u32[]{:S(2)}) collective-permute-start(f32[2,16,512]{2,1,0:T(8,128)S(1)} %get-tuple-element.17), channel_id=1, source_target_pairs={{0,4},{1,5},{2,6},{3,7},{4,0},{5,1},{6,2},{7,3},{8,12},{9,13},{10,... | collective-permute-start | bytes 196616 | tf_op jit(solution)/shard_map/ppermute | solution.py:41
  34.5 4.0 %collective-permute-start.11 = (f32[16,512]{1,0:T(8,128)S(1)}, f32[16,512]{1,0:T(8,128)S(1)}, u32[]{:S(2)}, u32[]{:S(2)}) collective-permute-start(f32[16,512]{1,0:T(8,128)S(1)} %slice_bitcast_fusion.4), channel_id=1, source_target_pairs={{0,2},{1,3},{2,0},{3,1},{4,6},{5,7},{6,4},{7,5},{8,10},{9,11},{10,... | collective-permute-start | bytes 98312 | tf_op jit(solution)/shard_map/ppermute | solution.py:41
